TPU v7x, 256 devices: a whole 4x4x8 slice. The times are simulated.
256 devices in a mesh: tm: 32 (over z, x), sensor: 8 (over y, core).
Axes of the slice: x: 4, y: 4, z: 8, core: 2. Of those that a mesh axis runs over, the one named last changes fastest.
Arguments:
- observations: bfloat16 [8192, 32768], P('tm', 'sensor'), may hold values from -6 to 6
- obs_list: int32 [8192, 128], P('tm', 'sensor'), may hold values from -1 to 255, as said below
- gain_rows: bfloat16 [32768, 1024], P('sensor'), may hold values from -0.0048828125 to 0.0048828125
- decay: float32 [8192, 1024], P('tm'), may hold values from 0 to 1
- smooth_gain: float32 [8192, 1024], P('tm'), may hold values from 0 to 1
- model_rate: float32 [1024], replicated, may hold values from 0.5 to 1
- first_state: float32 [1024], replicated, may hold values from -6 to 6
Outputs:
- filtered: float32 [8192, 1024], P('tm', 'sensor')
- smoothed: float32 [8192, 1024], P('tm', 'sensor')
Inputs may be any that keep to these rules, and one draw needn't show every extreme that they name: `obs_list`: in row t the 16 slots of sensor index j name distinct blocks from j * 32 to (j + 1) * 32 - 1; -1 marks an empty slot; slots of lower sensor indices are emptier.
All inputs are finite; a program needn't handle non-finite values.
Results may differ from a plain program's by a relative error of at most 0.0003.
Values sent between devices are 32-bit elements; how exact they have to be, the bound alone decides.
No kernel may reach another device: no remote copies, remote signals or barrier semaphores. Data moves between devices by JAX's collectives and lax.ppermute only.
A program may use at most 64 MiB of HBM per device.

v0:
```python
import jax
import jax.numpy as jnp
from jax import lax
from jax.sharding import PartitionSpec as P


def prefix(part, axis, combine, identity, reverse):
    count = lax.axis_size(axis)
    place = lax.axis_index(axis)
    ahead = count - 1 - place if reverse else place
    gathered = jax.tree.map(lambda a: lax.all_gather(a, axis), part)
    state = jax.tree.map(lambda a, e: jnp.zeros_like(a) + jnp.asarray(e, a.dtype), part, identity)

    def one(hop, state):
        source = count - 1 - hop if reverse else hop
        return combine(
            state, jax.tree.map(lambda a: lax.dynamic_index_in_dim(a, source, 0, False), gathered)
        )

    return lax.fori_loop(0, ahead, one, state)


def link(earlier, later):
    return (later[0] * earlier[0], later[0] * earlier[1] + later[1])


def per_device(observations, obs_list, gain_rows, decay, smooth_gain, model_rate, first_state):
    sensor_count = lax.axis_size("sensor")
    sensor_index = lax.axis_index("sensor")
    time_index = lax.axis_index("tm")
    rows_here = observations.shape[0]
    block_count = observations.shape[1] // 128
    own_blocks = sensor_index * block_count + jnp.arange(block_count, dtype=jnp.int32)
    listed = jnp.any(obs_list[:, :, None] == own_blocks[None, None, :], axis=1).astype(jnp.float32)
    weighted = (
        (observations.reshape(rows_here, block_count, 128) * listed[:, :, None])
        .reshape(rows_here, block_count * 128)
        .astype(jnp.bfloat16)
    )
    partial_sum = jnp.dot(weighted, gain_rows, preferred_element_type=jnp.float32)
    width = gain_rows.shape[1] // sensor_count
    inflow = lax.psum_scatter(partial_sum, "sensor", scatter_dimension=1, tiled=True)
    start_col = sensor_index * width
    factors = lax.dynamic_slice_in_dim(decay, start_col, width, 1)
    gains = lax.dynamic_slice_in_dim(smooth_gain, start_col, width, 1)
    rates = lax.dynamic_slice_in_dim(model_rate, start_col, width, 0)
    initial = lax.dynamic_slice_in_dim(first_state, start_col, width, 0)
    identity = (jnp.ones((width,), jnp.float32), jnp.zeros((width,), jnp.float32))
    prod_fwd, local_fwd = lax.associative_scan(link, (factors, inflow), axis=0)
    carry_prod, carry_state = prefix((prod_fwd[-1], local_fwd[-1]), "tm", link, identity, False)
    entering = carry_prod * initial + carry_state
    filtered = local_fwd + prod_fwd * entering[None, :]
    hour_ids = time_index * rows_here + jnp.arange(rows_here, dtype=jnp.int32)
    total_hours = rows_here * lax.axis_size("tm")
    step_gain = jnp.where((hour_ids == total_hours - 1)[:, None], jnp.float32(0.0), gains)
    offset = filtered - step_gain * rates[None, :] * filtered
    prod_back, local_back = lax.associative_scan(link, (step_gain, offset), axis=0, reverse=True)
    _, after_state = prefix((prod_back[0], local_back[0]), "tm", link, identity, True)
    smoothed = local_back + prod_back * after_state[None, :]
    return (filtered, smoothed)


def solution(mesh):
    in_specs = (
        P("tm", "sensor"),
        P("tm", "sensor"),
        P("sensor", None),
        P("tm", None),
        P("tm", None),
        P(),
        P(),
    )
    out_specs = (P("tm", "sensor"), P("tm", "sensor"))
    return jax.shard_map(
        per_device, mesh=mesh, in_specs=in_specs, out_specs=out_specs, check_vma=False
    )
```

profile of v0, /device:TPU:8, one launch (start us, length us, event | category | flops | bytes accessed | tf_op | source)
XLA Modules:
  0.0 220.8 jit_solution(1037110100710104763)
XLA Ops:
  7.2 0.0 copy-start
  7.2 0.0 copy-start.2
  7.2 0.0 reduce-scatter.2.cloned.1.call-start
  7.3 1.0 compare_reduce_fusion
  8.3 0.1 copy.11
  8.4 1.1 mul.245
  9.5 0.0 copy-done.2
  9.5 8.7 %fusion.1 = f32[256,1024]{1,0:T(8,128)} fusion(bf16[4096,1024]{1,0:T(8,128)(2,1)} %param.13, f32[32,8,32,128]{3,2,1,0:T(8,128)S(1)} %bitcast.40, bf16[256,4096]{1,0:T(8,128)(2,1)S(1)} %copy-done.2), kind=kOutput, calls=%fused_computation.8 | convolution fusion | flops 2150629376 | bytes 15728640 | tf_op jit(solution)/shard_map/dot_general | solution.py:40
  18.2 0.0 reduce-scatter.2.cloned.1.call-update
  18.2 0.0 copy-done
  18.3 0.8 dynamic_slice.37
  19.1 34.0 %reduce-scatter.2.cloned.1.call-done = f32[256,128]{1,0:T(8,128)} async-done(((f32[256,1024]{1,0:T(8,128)}), f32[256,128]{1,0:T(8,128)}) %reduce-scatter.2.cloned.1.call-update) | async-done | bytes 131088 | tf_op jit(solution)/shard_map/reduce_scatter | solution.py:42
  53.1 0.0 copy-start.1
  53.1 0.0 slice-start
  53.1 1.0 slice.498
  54.1 0.9 slice.497
  56.6 0.0 copy-done.1
  56.7 40.2 %all-gather = f32[32,1,128]{2,1,0:T(1,128)S(1)} all-gather(f32[1,1,128]{2,1,0:T(1,128)S(1)} %add_bitcast_fusion.3), channel_id=1, replica_groups=mesh['tm'=32,'sensor'=8] {'tm'}, dimensions={0}, use_global_device_ids=true | all-gather | bytes 16896 | tf_op jit(solution)/shard_map/all_gather | solution.py:11
  97.0 0.0 slice-done
  97.0 36.6 %all-gather.1 = f32[32,1,128]{2,1,0:T(1,128)S(1)} all-gather(f32[1,1,128]{2,1,0:T(1,128)S(1)} %add_bitcast_fusion.2), channel_id=1, replica_groups=mesh['tm'=32,'sensor'=8] {'tm'}, dimensions={0}, use_global_device_ids=true | all-gather | bytes 16896 | tf_op jit(solution)/shard_map/all_gather | solution.py:11
  133.7 0.8 multiply_add_fusion.20
  134.5 1.6 multiply_subtract_fusion
  138.2 0.1 rev.8
  138.3 0.1 rev.9
  138.4 37.8 %all-gather.2 = f32[32,1,128]{2,1,0:T(1,128)S(1)} all-gather(f32[1,1,128]{2,1,0:T(1,128)S(1)} %add_bitcast_fusion.1), channel_id=1, replica_groups=mesh['tm'=32,'sensor'=8] {'tm'}, dimensions={0}, use_global_device_ids=true | all-gather | bytes 16896 | tf_op jit(solution)/shard_map/all_gather | solution.py:11
  176.2 35.8 %all-gather.3 = f32[32,1,128]{2,1,0:T(1,128)S(1)} all-gather(f32[1,1,128]{2,1,0:T(1,128)S(1)} %add_bitcast_fusion), channel_id=1, replica_groups=mesh['tm'=32,'sensor'=8] {'tm'}, dimensions={0}, use_global_device_ids=true | all-gather | bytes 16896 | tf_op jit(solution)/shard_map/all_gather | solution.py:11
  212.0 1.2 while.27
  213.2 0.7 multiply_add_fusion
  (293 shorter events, 3.3 us)
Async XLA Ops:
  7.2 11.1 %copy-start = (f32[256,1024]{1,0:T(8,128)S(1)}, f32[256,1024]{1,0:T(8,128)}, u32[]{:S(2)}) copy-start(f32[256,1024]{1,0:T(8,128)} %param.14) | copy-start | bytes 3145732
  7.2 2.3 %copy-start.2 = (bf16[256,4096]{1,0:T(8,128)(2,1)S(1)}, bf16[256,4096]{1,0:T(8,128)(2,1)}, u32[]{:S(2)}) copy-start(bf16[256,4096]{1,0:T(8,128)(2,1)} %param.11) | copy-start | bytes 6291460
  7.2 45.9 %reduce-scatter.2.cloned.1.call-start = ((), (), s32[]{:S(2)}) async-start(), calls=%async_computation.1 | async-start | bytes 1179648 | tf_op jit(solution)/shard_map/reduce_scatter | solution.py:42
  53.1 3.5 %copy-start.1 = (f32[256,128]{1,0:T(8,128)S(1)}, f32[256,128]{1,0:T(8,128)}, u32[]{:S(2)}) copy-start(f32[256,128]{1,0:T(8,128)} %reduce-scatter.2.cloned.1.call-done) | copy-start | bytes 393220
  53.1 43.9 %slice-start = ((f32[256,128]{1,0:T(8,128)}), f32[1,128]{1,0:T(1,128)S(1)}, s32[]{:S(2)}) async-start(f32[256,128]{1,0:T(8,128)} %reduce-scatter.2.cloned.1.call-done), calls=%async_computation.2 | async-start | bytes 1024 | tf_op jit(solution)/shard_map/slice | solution.py:49
Sparse Core Ops, SparseCore 0:
  18.3 34.7 reduce-scatter.1
where the time goes:
time: 224 us; the launch traced here: 221 us
  blocking collectives  151 us (67%)
  waiting for transfers between devices  34 us (15%)
  between operations  15.4 us (7%)
  matrix products  8.68 us (4%)
  local copies, waits for them, and re-layouts  6 us (3%)
  other arithmetic  5.43 us (2%)
    all_gather x4, blocking collectives, prefix(): gathered = jax.tree.map(lambda a: lax.all_gather(a, axis), part)  151 us
    reduce_scatter x1, waiting for transfers between devices, per_device(): lax.psum_scatter(partial_sum, 'sensor', scatter_dimension=1, tiled=True)  34 us
    dot_general x1, matrix products, per_device(): jnp.dot(weighted, gain_rows, preferred_element_type=jnp.float32)  8.68 us
  transfers between devices with their start and end apart: 1, of which 1 were waited for; matrix products, arithmetic and copies ran while one was open for 0% of the time, Pallas kernels for 0%

commit v1 on v0

v1 whole, which is shorter than its diff:
```python
import jax
import jax.numpy as jnp
from jax import lax
from jax.sharding import PartitionSpec as P


def link(earlier, later):
    return (later[0] * earlier[0], later[0] * earlier[1] + later[1])


def sensor_reduce_scatter(partial, width):
    count = lax.axis_size("sensor")
    chips = count // 2
    j = lax.axis_index("sensor")
    chip = j // 2
    core = j % 2
    rows = partial.shape[0]
    split = partial.reshape(rows, chips, 2, width)
    send = lax.dynamic_index_in_dim(split, 1 - core, 2, False)
    keep = lax.dynamic_index_in_dim(split, core, 2, False)
    chip_sum = keep + lax.ppermute(send, "sensor", [(i, i ^ 1) for i in range(count)])
    total = lax.dynamic_index_in_dim(chip_sum, chip, 1, False)
    for shift in range(1, chips):
        piece = lax.dynamic_index_in_dim(chip_sum, (chip + shift) % chips, 1, False)
        perm = [(i, (((i // 2) + shift) % chips) * 2 + i % 2) for i in range(count)]
        total = total + lax.ppermute(piece, "sensor", perm)
    return total


def gather_tm(x):
    count = lax.axis_size("tm")
    place = lax.axis_index("tm")
    held = x[None]
    step = 1
    while step < count:
        other = lax.ppermute(held, "tm", [(i, i ^ step) for i in range(count)])
        low = (place & step) == 0
        held = jnp.where(
            low, jnp.concatenate([held, other], 0), jnp.concatenate([other, held], 0)
        )
        step *= 2
    return held


def per_device(observations, obs_list, gain_rows, decay, smooth_gain, model_rate, first_state):
    sensor_count = lax.axis_size("sensor")
    sensor_index = lax.axis_index("sensor")
    time_index = lax.axis_index("tm")
    time_count = lax.axis_size("tm")
    rows_here = observations.shape[0]
    block_count = observations.shape[1] // 128
    own_blocks = sensor_index * block_count + jnp.arange(block_count, dtype=jnp.int32)
    listed = jnp.any(obs_list[:, :, None] == own_blocks[None, None, :], axis=1).astype(jnp.float32)
    weighted = (
        (observations.reshape(rows_here, block_count, 128) * listed[:, :, None])
        .reshape(rows_here, block_count * 128)
        .astype(jnp.bfloat16)
    )
    partial_sum = jnp.dot(weighted, gain_rows, preferred_element_type=jnp.float32)
    width = gain_rows.shape[1] // sensor_count
    inflow = sensor_reduce_scatter(partial_sum, width)
    start_col = sensor_index * width
    factors = lax.dynamic_slice_in_dim(decay, start_col, width, 1)
    gains = lax.dynamic_slice_in_dim(smooth_gain, start_col, width, 1)
    rates = lax.dynamic_slice_in_dim(model_rate, start_col, width, 0)
    initial = lax.dynamic_slice_in_dim(first_state, start_col, width, 0)
    hour_ids = time_index * rows_here + jnp.arange(rows_here, dtype=jnp.int32)
    total_hours = rows_here * time_count
    step_gain = jnp.where((hour_ids == total_hours - 1)[:, None], jnp.float32(0.0), gains)
    scale = step_gain * rates[None, :]

    prod_fwd, local_fwd = lax.associative_scan(link, (factors, inflow), axis=0)
    off_local = local_fwd - scale * local_fwd
    off_prod = prod_fwd - scale * prod_fwd
    prod_back, back = lax.associative_scan(
        link,
        (jnp.concatenate([step_gain, step_gain], 1), jnp.concatenate([off_local, off_prod], 1)),
        axis=0,
        reverse=True,
    )
    prod_back = prod_back[:, :width]
    back_local = back[:, :width]
    back_prod = back[:, width:]

    summary = jnp.stack(
        [prod_fwd[-1], local_fwd[-1], prod_back[0], back_local[0], back_prod[0]], 0
    )
    every = gather_tm(summary)
    entering = [initial]
    for k in range(time_count - 1):
        entering.append(every[k, 0] * entering[-1] + every[k, 1])
    after = [jnp.zeros_like(initial)]
    for k in range(time_count - 1, 0, -1):
        after.append(every[k, 3] + every[k, 4] * entering[k] + every[k, 2] * after[-1])
    after = after[::-1]
    entering_here = lax.dynamic_index_in_dim(jnp.stack(entering, 0), time_index, 0, False)
    after_here = lax.dynamic_index_in_dim(jnp.stack(after, 0), time_index, 0, False)

    filtered = local_fwd + prod_fwd * entering_here[None, :]
    smoothed = back_local + back_prod * entering_here[None, :] + prod_back * after_here[None, :]
    return (filtered, smoothed)


def solution(mesh):
    in_specs = (
        P("tm", "sensor"),
        P("tm", "sensor"),
        P("sensor", None),
        P("tm", None),
        P("tm", None),
        P(),
        P(),
    )
    out_specs = (P("tm", "sensor"), P("tm", "sensor"))
    return jax.shard_map(
        per_device, mesh=mesh, in_specs=in_specs, out_specs=out_specs, check_vma=False
    )
```

time: 224 us -> 72 us (0.32); the launches traced: 221 us -> 71.5 us
  blocking collectives: 151 us -> 0 us
  starting transfers between devices: 0.04 us -> 18.6 us
  waiting for transfers between devices: 34 us -> 19.3 us
  between operations: 15.4 us -> 2.27 us
  local copies, waits for them, and re-layouts: 6 us -> 18.3 us
    all_gather x4 -> x0, blocking collectives: 151 us -> none  [prefix(): gathered = jax.tree.map(lambda a: lax.all_gather(a, axis), part)]
    reduce_scatter x1 -> x0, waiting for transfers between devices: 34 us -> none  [per_device(): lax.psum_scatter(partial_sum, 'sensor', scatter_dimension=1, tiled=True)]
    ppermute x0 -> x9, waiting for transfers between devices: none -> 19.3 us  [the longest x5 12.2 us: gather_tm(): other = lax.ppermute(held, 'tm', [(i, i ^ step) for i in range(count)])]
    ppermute x0 -> x9, starting transfers between devices: none -> 18.6 us  [the longest x5 13.5 us: gather_tm(): other = lax.ppermute(held, 'tm', [(i, i ^ step) for i in range(count)])]
    dot_general x0 -> x1, local copies, waits for them, and re-layouts: none -> 11.3 us  [per_device(): jnp.dot(weighted, gain_rows, preferred_element_type=jnp.float32)]
  transfers between devices with their start and end apart: 1 -> 9, of which waited for: 1 -> 9; matrix products, arithmetic and copies ran while one was open for 0% -> 3% of each run, Pallas kernels for 0% -> 0%
where the time goes in v1:
time: 72 us; the launch traced here: 71.5 us
  waiting for transfers between devices  19.3 us (27%)
  starting transfers between devices  18.6 us (26%)
  local copies, waits for them, and re-layouts  18.3 us (25%)
  matrix products  8.16 us (11%)
  other arithmetic  4.85 us (7%)
  between operations  2.27 us (3%)
    ppermute x5, starting transfers between devices, gather_tm(): other = lax.ppermute(held, 'tm', [(i, i ^ step) for i in range(count)])  13.5 us
    ppermute x5, waiting for transfers between devices, gather_tm(): other = lax.ppermute(held, 'tm', [(i, i ^ step) for i in range(count)])  12.2 us
    dot_general x1, local copies, waits for them, and re-layouts, per_device(): jnp.dot(weighted, gain_rows, preferred_element_type=jnp.float32)  11.3 us
    dot_general x1, matrix products, per_device(): jnp.dot(weighted, gain_rows, preferred_element_type=jnp.float32)  8.16 us
    ppermute x3, waiting for transfers between devices, sensor_reduce_scatter(): total = total + lax.ppermute(piece, 'sensor', perm)  5.38 us
    ppermute x3, starting transfers between devices, sensor_reduce_scatter(): total = total + lax.ppermute(piece, 'sensor', perm)  5 us
    slice x56, local copies, waits for them, and re-layouts, per_device(): lax.associative_scan(link, (jnp.concatenate([step_gain, step_gain], 1), j...  1.89 us
    ppermute x1, waiting for transfers between devices, sensor_reduce_scatter(): lax.ppermute(send, 'sensor', [(i, i ^ 1) for i in range(count)])  1.77 us
  transfers between devices with their start and end apart: 9, of which 9 were waited for; matrix products, arithmetic and copies ran while one was open for 3% of the time, Pallas kernels for 0%

profile of v1, /device:TPU:8, one launch (start us, length us, event | category | flops | bytes accessed | tf_op | source)
XLA Modules:
  0.0 71.5 jit_solution(9664331515461411177)
XLA Ops:
  0.7 0.9 %compare_reduce_fusion = pred[256,32]{0,1:T(8,128)(4,1)S(1)} fusion(s32[256,16]{0,1:T(8,128)} %param.8, s32[32]{0:T(128)S(1)} %iota_add_fusion), kind=kLoop, calls=%fused_computation.6 | loop fusion | flops 253952 | bytes 24704 | tf_op jit(solution)/shard_map/reduce_or | solution.py:53
  1.7 11.3 %copy.14 = bf16[1024,4096]{1,0:T(8,128)(2,1)} copy(bf16[1024,4096]{0,1:T(8,128)(2,1)} %bitcast.1126) | data formatting | bytes 16777216 | tf_op jit(solution)/shard_map/dot_general | solution.py:59
  13.0 1.1 %mul.523 = f32[256,32,128]{2,1,0:T(8,128)S(1)} broadcast(f32[256,32]{1,0:T(8,128)S(1)} %copy.11), dimensions={0,1} | broadcast | bytes 4227072 | tf_op jit(solution)/shard_map/mul | solution.py:55
  14.2 0.5 copy-done.1
  14.6 8.2 %fusion.2 = f32[256,4,2,128]{3,0,2,1:T(8,128)S(1)} fusion(bf16[4,2,128,4096]{3,2,1,0:T(8,128)(2,1)} %bitcast.1127, f32[32,8,32,128]{3,2,1,0:T(8,128)S(1)} %bitcast.1128, bf16[256,4096]{1,0:T(8,128)(2,1)S(1)} %copy-done.1), kind=kOutput, calls=%fused_computation.3 | convolution fusion | flops 2150629376 | bytes 15728640 | tf_op jit(solution)/shard_map/dot_general | solution.py:59
  23.1 1.8 %collective-permute-done = f32[256,4,128]{2,0,1:T(8,128)S(1)} collective-permute-done((f32[256,4,128]{2,0,1:T(8,128)S(1)}, f32[256,4,128]{2,0,1:T(8,128)S(1)}, u32[]{:S(2)}, u32[]{:S(2)}) %collective-permute-start) | collective-permute-done | bytes 524320 | tf_op jit(solution)/shard_map/ppermute | solution.py:21
  24.9 1.7 %collective-permute-start.1 = (f32[256,128]{1,0:T(8,128)S(1)}, f32[256,128]{1,0:T(8,128)S(1)}, u32[]{:S(2)}, u32[]{:S(2)}) collective-permute-start(f32[256,128]{1,0:T(8,128)S(1)} %get-tuple-element.71), channel_id=1, source_target_pairs={{0,2},{1,3},{2,4},{3,5},{4,6},{5,7},{6,0},{7,1},{8,10},{9,11},{10,... | collective-permute-start | bytes 393224 | tf_op jit(solution)/shard_map/ppermute | solution.py:26
  26.6 2.6 %collective-permute-start.2 = (f32[256,128]{1,0:T(8,128)S(1)}, f32[256,128]{1,0:T(8,128)S(1)}, u32[]{:S(2)}, u32[]{:S(2)}) collective-permute-start(f32[256,128]{1,0:T(8,128)S(1)} %get-tuple-element.73), channel_id=1, source_target_pairs={{0,4},{1,5},{2,6},{3,7},{4,0},{5,1},{6,2},{7,3},{8,12},{9,13},{10,... | collective-permute-start | bytes 393224 | tf_op jit(solution)/shard_map/ppermute | solution.py:26
  29.2 0.7 collective-permute-start.3
  30.0 0.8 %dynamic_slice.48 = f32[128]{0:T(128)S(1)} dynamic-slice(f32[1024]{0:T(1024)} %param.12, s32[]{:T(128)S(6)} %select_n.109), dynamic_slice_sizes={128} | dynamic-slice | bytes 1028 | tf_op jit(solution)/shard_map/dynamic_slice | solution.py:65
  30.8 0.7 %collective-permute-done.1 = f32[256,128]{1,0:T(8,128)S(1)} collective-permute-done((f32[256,128]{1,0:T(8,128)S(1)}, f32[256,128]{1,0:T(8,128)S(1)}, u32[]{:S(2)}, u32[]{:S(2)}) %collective-permute-start.1) | collective-permute-done | bytes 131104 | tf_op jit(solution)/shard_map/ppermute | solution.py:26
  31.5 2.9 %collective-permute-done.2 = f32[256,128]{1,0:T(8,128)S(1)} collective-permute-done((f32[256,128]{1,0:T(8,128)S(1)}, f32[256,128]{1,0:T(8,128)S(1)}, u32[]{:S(2)}, u32[]{:S(2)}) %collective-permute-start.2) | collective-permute-done | bytes 131104 | tf_op jit(solution)/shard_map/ppermute | solution.py:26
  34.5 1.7 %collective-permute-done.3 = f32[256,128]{1,0:T(8,128)S(1)} collective-permute-done((f32[256,128]{1,0:T(8,128)S(1)}, f32[256,128]{1,0:T(8,128)S(1)}, u32[]{:S(2)}, u32[]{:S(2)}) %collective-permute-start.3) | collective-permute-done | bytes 131104 | tf_op jit(solution)/shard_map/ppermute | solution.py:26
  38.0 1.0 %multiply_subtract_fusion.1 = (f32[256,128]{1,0:T(8,128)S(1)}, f32[256,128]{1,0:T(8,128)S(1)}, f32[256,128]{1,0:T(8,128)S(1)}) fusion(f32[128]{0:T(128)S(1)} %dynamic_slice.48, f32[256,1024]{1,0:T(8,128)} %param.11, s32[]{:T(128)S(6)} %select_n.109, pred[256]{0:T(512)(128)(4,1)S(1)} %add_compare_fusion, f32[256,128]{1,0:T(8,128)S(1)} %pad.210, ...), kind=kLoop, calls=%fused_computation.14 | loop fusion | flops 163840 | bytes 787204 | tf_op jit(solution)/shard_map/sub | solution.py:73
  39.1 0.1 slice.1102
  41.0 0.1 slice.1139
  41.1 0.1 slice.1061
  42.1 0.1 slice.1140
  42.2 0.1 slice.1062
  42.7 0.9 %collective-permute-start.4 = (f32[1,5,128]{2,1,0:T(8,128)S(1)}, f32[1,5,128]{2,1,0:T(8,128)S(1)}, u32[]{:S(2)}, u32[]{:S(2)}) collective-permute-start(f32[1,5,128]{2,1,0:T(8,128)S(1)} %bitcast.1129), channel_id=1, source_target_pairs={{0,8},{8,0},{16,24},{24,16},{32,40},{40,32},{48,56},{56,48},{64,72... | collective-permute-start | bytes 7688 | tf_op jit(solution)/shard_map/ppermute | solution.py:36
  43.6 2.8 %collective-permute-done.4 = f32[1,5,128]{2,1,0:T(8,128)S(1)} collective-permute-done((f32[1,5,128]{2,1,0:T(8,128)S(1)}, f32[1,5,128]{2,1,0:T(8,128)S(1)}, u32[]{:S(2)}, u32[]{:S(2)}) %collective-permute-start.4) | collective-permute-done | bytes 2592 | tf_op jit(solution)/shard_map/ppermute | solution.py:36
  46.4 2.3 %collective-permute-start.5 = (f32[2,5,128]{2,1,0:T(8,128)S(1)}, f32[2,5,128]{2,1,0:T(8,128)S(1)}, u32[]{:S(2)}, u32[]{:S(2)}) collective-permute-start(f32[2,5,128]{2,1,0:T(8,128)S(1)} %maximum_select_fusion.4), channel_id=1, source_target_pairs={{0,16},{8,24},{16,0},{24,8},{32,48},{40,56},{48,32},{56,40},{64,80... | collective-permute-start | bytes 15368 | tf_op jit(solution)/shard_map/ppermute | solution.py:36
  48.7 2.8 %collective-permute-done.5 = f32[2,5,128]{2,1,0:T(8,128)S(1)} collective-permute-done((f32[2,5,128]{2,1,0:T(8,128)S(1)}, f32[2,5,128]{2,1,0:T(8,128)S(1)}, u32[]{:S(2)}, u32[]{:S(2)}) %collective-permute-start.5) | collective-permute-done | bytes 5152 | tf_op jit(solution)/shard_map/ppermute | solution.py:36
  51.6 1.2 %collective-permute-start.6 = (f32[4,5,128]{2,1,0:T(8,128)S(1)}, f32[4,5,128]{2,1,0:T(8,128)S(1)}, u32[]{:S(2)}, u32[]{:S(2)}) collective-permute-start(f32[4,5,128]{2,1,0:T(8,128)S(1)} %maximum_select_fusion.3), channel_id=1, source_target_pairs={{0,32},{8,40},{16,48},{24,56},{32,0},{40,8},{48,16},{56,24},{64,96... | collective-permute-start | bytes 30728 | tf_op jit(solution)/shard_map/ppermute | solution.py:36
  52.8 0.8 %dynamic-slice_bitcast_fusion.4 = f32[1,128]{1,0:T(1,128)S(1)} fusion(f32[1024]{0:T(1024)} %param.13, s32[]{:T(128)S(6)} %select_n.109), kind=kLoop, calls=%fused_computation.482 | loop fusion | bytes 1028 | tf_op jit(solution)/shard_map/stack | solution.py:96
  53.5 2.1 %collective-permute-done.6 = f32[4,5,128]{2,1,0:T(8,128)S(1)} collective-permute-done((f32[4,5,128]{2,1,0:T(8,128)S(1)}, f32[4,5,128]{2,1,0:T(8,128)S(1)}, u32[]{:S(2)}, u32[]{:S(2)}) %collective-permute-start.6) | collective-permute-done | bytes 10272 | tf_op jit(solution)/shard_map/ppermute | solution.py:36
  55.7 2.2 %collective-permute-start.7 = (f32[8,5,128]{2,1,0:T(8,128)S(1)}, f32[8,5,128]{2,1,0:T(8,128)S(1)}, u32[]{:S(2)}, u32[]{:S(2)}) collective-permute-start(f32[8,5,128]{2,1,0:T(8,128)S(1)} %maximum_select_fusion.2), channel_id=1, source_target_pairs={{0,64},{8,72},{16,80},{24,88},{32,96},{40,104},{48,112},{56,120},{... | collective-permute-start | bytes 61448 | tf_op jit(solution)/shard_map/ppermute | solution.py:36
  57.9 2.5 %collective-permute-done.7 = f32[8,5,128]{2,1,0:T(8,128)S(1)} collective-permute-done((f32[8,5,128]{2,1,0:T(8,128)S(1)}, f32[8,5,128]{2,1,0:T(8,128)S(1)}, u32[]{:S(2)}, u32[]{:S(2)}) %collective-permute-start.7) | collective-permute-done | bytes 20512 | tf_op jit(solution)/shard_map/ppermute | solution.py:36
  60.5 6.8 %collective-permute-start.8 = (f32[16,5,128]{2,1,0:T(8,128)S(1)}, f32[16,5,128]{2,1,0:T(8,128)S(1)}, u32[]{:S(2)}, u32[]{:S(2)}) collective-permute-start(f32[16,5,128]{2,1,0:T(8,128)S(1)} %maximum_select_fusion.1), channel_id=1, source_target_pairs={{0,128},{8,136},{16,144},{24,152},{32,160},{40,168},{48,176},{56,1... | collective-permute-start | bytes 122888 | tf_op jit(solution)/shard_map/ppermute | solution.py:36
  67.6 1.9 %collective-permute-done.8 = f32[16,5,128]{2,1,0:T(8,128)S(1)} collective-permute-done((f32[16,5,128]{2,1,0:T(8,128)S(1)}, f32[16,5,128]{2,1,0:T(8,128)S(1)}, u32[]{:S(2)}, u32[]{:S(2)}) %collective-permute-start.8) | collective-permute-done | bytes 40992 | tf_op jit(solution)/shard_map/ppermute | solution.py:36
  69.6 1.0 %fusion.210 = (f32[1,128]{1,0:T(1,128)S(1)}, f32[128]{0:T(128)S(1)}, f32[128]{0:T(128)S(1)}, f32[128]{0:T(128)S(1)}, f32[128]{0:T(128)S(1)}, /*index=5*/f32[128]...) fusion(f32[32,5,128]{2,1,0:T(8,128)S(1)} %maximum_select_fusion, ...), kind=kLoop, calls=%fused_computation.480 | loop fusion | flops 23808 | bytes 111620 | tf_op jit(solution)/shard_map/stack | solution.py:97
  70.8 0.7 %multiply_add_fusion = (f32[256,128]{1,0:T(8,128)}, f32[256,128]{1,0:T(8,128)}) fusion(f32[256,128]{1,0:T(8,128)S(1)} %slice.1210, f32[256,128]{1,0:T(8,128)S(1)} %slice.1206, f32[256,128]{1,0:T(8,128)S(1)} %slice.1208, f32[128]{0:T(128)S(1)} %fusion.23, f32[128]{0:T(128)S(1)} %fusion.22, f32[256,128]{1,0:T(8,128)S(1)} %get-tuple-element.66, ...), kind=kLoop, calls=%fused_computation.25 | loop fusion | flops 196608 | bytes 918528 | tf_op jit(solution)/shard_map/add | solution.py:100
  (283 shorter events, 4.6 us)
Async XLA Ops:
  0.6 22.4 %copy-start = (f32[256,1024]{1,0:T(8,128)S(1)}, f32[256,1024]{1,0:T(8,128)}, u32[]{:S(2)}) copy-start(f32[256,1024]{1,0:T(8,128)} %param.10) | copy-start | bytes 3145732
  13.0 1.6 %copy-start.1 = (bf16[256,4096]{1,0:T(8,128)(2,1)S(1)}, bf16[256,4096]{1,0:T(8,128)(2,1)}, u32[]{:S(2)}) copy-start(bf16[256,4096]{1,0:T(8,128)(2,1)} %param.7) | copy-start | bytes 6291460
  22.8 2.0 %collective-permute-start = (f32[256,4,128]{2,0,1:T(8,128)S(1)}, f32[256,4,128]{2,0,1:T(8,128)S(1)}, u32[]{:S(2)}, u32[]{:S(2)}) collective-permute-start(f32[256,4,128]{2,0,1:T(8,128)S(1)} %dynamic-slice_bitcast_fusion), channel_id=1, source_target_pairs={{0,1},{1,0},{2,3},{3,2},{4,5},{5,4},{6,7},{7,6},{8,9},{9,8},{10,11... | collective-permute-start | bytes 1572872 | tf_op jit(solution)/shard_map/ppermute | solution.py:21
  24.9 6.6 %collective-permute-start.1 = (f32[256,128]{1,0:T(8,128)S(1)}, f32[256,128]{1,0:T(8,128)S(1)}, u32[]{:S(2)}, u32[]{:S(2)}) collective-permute-start(f32[256,128]{1,0:T(8,128)S(1)} %get-tuple-element.71), channel_id=1, source_target_pairs={{0,2},{1,3},{2,4},{3,5},{4,6},{5,7},{6,0},{7,1},{8,10},{9,11},{10,... | collective-permute-start | bytes 393224 | tf_op jit(solution)/shard_map/ppermute | solution.py:26
  26.6 7.9 %collective-permute-start.2 = (f32[256,128]{1,0:T(8,128)S(1)}, f32[256,128]{1,0:T(8,128)S(1)}, u32[]{:S(2)}, u32[]{:S(2)}) collective-permute-start(f32[256,128]{1,0:T(8,128)S(1)} %get-tuple-element.73), channel_id=1, source_target_pairs={{0,4},{1,5},{2,6},{3,7},{4,0},{5,1},{6,2},{7,3},{8,12},{9,13},{10,... | collective-permute-start | bytes 393224 | tf_op jit(solution)/shard_map/ppermute | solution.py:26
  29.2 6.9 %collective-permute-start.3 = (f32[256,128]{1,0:T(8,128)S(1)}, f32[256,128]{1,0:T(8,128)S(1)}, u32[]{:S(2)}, u32[]{:S(2)}) collective-permute-start(f32[256,128]{1,0:T(8,128)S(1)} %get-tuple-element.72), channel_id=1, source_target_pairs={{0,6},{1,7},{2,0},{3,1},{4,2},{5,3},{6,4},{7,5},{8,14},{9,15},{10,... | collective-permute-start | bytes 393224 | tf_op jit(solution)/shard_map/ppermute | solution.py:26
  42.7 3.7 %collective-permute-start.4 = (f32[1,5,128]{2,1,0:T(8,128)S(1)}, f32[1,5,128]{2,1,0:T(8,128)S(1)}, u32[]{:S(2)}, u32[]{:S(2)}) collective-permute-start(f32[1,5,128]{2,1,0:T(8,128)S(1)} %bitcast.1129), channel_id=1, source_target_pairs={{0,8},{8,0},{16,24},{24,16},{32,40},{40,32},{48,56},{56,48},{64,72... | collective-permute-start | bytes 7688 | tf_op jit(solution)/shard_map/ppermute | solution.py:36
  46.4 5.2 %collective-permute-start.5 = (f32[2,5,128]{2,1,0:T(8,128)S(1)}, f32[2,5,128]{2,1,0:T(8,128)S(1)}, u32[]{:S(2)}, u32[]{:S(2)}) collective-permute-start(f32[2,5,128]{2,1,0:T(8,128)S(1)} %maximum_select_fusion.4), channel_id=1, source_target_pairs={{0,16},{8,24},{16,0},{24,8},{32,48},{40,56},{48,32},{56,40},{64,80... | collective-permute-start | bytes 15368 | tf_op jit(solution)/shard_map/ppermute | solution.py:36
  51.6 4.1 %collective-permute-start.6 = (f32[4,5,128]{2,1,0:T(8,128)S(1)}, f32[4,5,128]{2,1,0:T(8,128)S(1)}, u32[]{:S(2)}, u32[]{:S(2)}) collective-permute-start(f32[4,5,128]{2,1,0:T(8,128)S(1)} %maximum_select_fusion.3), channel_id=1, source_target_pairs={{0,32},{8,40},{16,48},{24,56},{32,0},{40,8},{48,16},{56,24},{64,96... | collective-permute-start | bytes 30728 | tf_op jit(solution)/shard_map/ppermute | solution.py:36
  55.7 4.8 %collective-permute-start.7 = (f32[8,5,128]{2,1,0:T(8,128)S(1)}, f32[8,5,128]{2,1,0:T(8,128)S(1)}, u32[]{:S(2)}, u32[]{:S(2)}) collective-permute-start(f32[8,5,128]{2,1,0:T(8,128)S(1)} %maximum_select_fusion.2), channel_id=1, source_target_pairs={{0,64},{8,72},{16,80},{24,88},{32,96},{40,104},{48,112},{56,120},{... | collective-permute-start | bytes 61448 | tf_op jit(solution)/shard_map/ppermute | solution.py:36
  60.5 9.1 %collective-permute-start.8 = (f32[16,5,128]{2,1,0:T(8,128)S(1)}, f32[16,5,128]{2,1,0:T(8,128)S(1)}, u32[]{:S(2)}, u32[]{:S(2)}) collective-permute-start(f32[16,5,128]{2,1,0:T(8,128)S(1)} %maximum_select_fusion.1), channel_id=1, source_target_pairs={{0,128},{8,136},{16,144},{24,152},{32,160},{40,168},{48,176},{56,1... | collective-permute-start | bytes 122888 | tf_op jit(solution)/shard_map/ppermute | solution.py:36

commit v2 on v1

--- a/solution.py
+++ b/solution.py
@@ -14,16 +14,18 @@
     j = lax.axis_index("sensor")
     chip = j // 2
     core = j % 2
-    rows = partial.shape[0]
-    split = partial.reshape(rows, chips, 2, width)
-    send = lax.dynamic_index_in_dim(split, 1 - core, 2, False)
-    keep = lax.dynamic_index_in_dim(split, core, 2, False)
+
+    def piece(index):
+        return lax.dynamic_slice_in_dim(partial, index * width, width, 1)
+
+    send = jnp.stack([piece(2 * c + 1 - core) for c in range(chips)], 0)
+    keep = jnp.stack([piece(2 * c + core) for c in range(chips)], 0)
     chip_sum = keep + lax.ppermute(send, "sensor", [(i, i ^ 1) for i in range(count)])
-    total = lax.dynamic_index_in_dim(chip_sum, chip, 1, False)
+    total = lax.dynamic_index_in_dim(chip_sum, chip, 0, False)
     for shift in range(1, chips):
-        piece = lax.dynamic_index_in_dim(chip_sum, (chip + shift) % chips, 1, False)
+        part = lax.dynamic_index_in_dim(chip_sum, (chip + shift) % chips, 0, False)
         perm = [(i, (((i // 2) + shift) % chips) * 2 + i % 2) for i in range(count)]
-        total = total + lax.ppermute(piece, "sensor", perm)
+        total = total + lax.ppermute(part, "sensor", perm)
     return total
 
 

time: 72 us -> 60.4 us (0.84)
  local copies, waits for them, and re-layouts: 18.3 us -> 6.65 us
    dot_general x1 -> x0, local copies, waits for them, and re-layouts: 11.3 us -> none  [per_device(): jnp.dot(weighted, gain_rows, preferred_element_type=jnp.float32)]
where the time goes in v2:
time: 60.4 us; the launch traced here: 59.7 us
  waiting for transfers between devices  19.4 us (32%)
  starting transfers between devices  18.7 us (31%)
  matrix products  7.71 us (13%)
  local copies, waits for them, and re-layouts  6.65 us (11%)
  other arithmetic  4.96 us (8%)
  between operations  2.31 us (4%)
    ppermute x5, starting transfers between devices, gather_tm(): other = lax.ppermute(held, 'tm', [(i, i ^ step) for i in range(count)])  13.6 us
    ppermute x5, waiting for transfers between devices, gather_tm(): other = lax.ppermute(held, 'tm', [(i, i ^ step) for i in range(count)])  12.2 us
    dot_general x1, matrix products, per_device(): jnp.dot(weighted, gain_rows, preferred_element_type=jnp.float32)  7.71 us
    ppermute x3, waiting for transfers between devices, sensor_reduce_scatter(): total = total + lax.ppermute(part, 'sensor', perm)  5.38 us
    ppermute x3, starting transfers between devices, sensor_reduce_scatter(): total = total + lax.ppermute(part, 'sensor', perm)  5.01 us
    slice x56, local copies, waits for them, and re-layouts, per_device(): lax.associative_scan(link, (jnp.concatenate([step_gain, step_gain], 1), j...  1.89 us
    ppermute x1, waiting for transfers between devices, sensor_reduce_scatter(): lax.ppermute(send, 'sensor', [(i, i ^ 1) for i in range(count)])  1.78 us
  transfers between devices with their start and end apart: 9, of which 9 were waited for; matrix products, arithmetic and copies ran while one was open for 3% of the time, Pallas kernels for 0%

profile of v2, /device:TPU:8, one launch (start us, length us, event | category | flops | bytes accessed | tf_op | source)
XLA Modules:
  0.0 59.7 jit_solution(13761387459983137111)
XLA Ops:
  0.7 1.0 %compare_reduce_fusion = pred[256,32]{0,1:T(8,128)(4,1)S(1)} fusion(s32[256,16]{0,1:T(8,128)} %param.8, s32[32]{0:T(128)S(1)} %iota_add_fusion), kind=kLoop, calls=%fused_computation.5 | loop fusion | flops 253952 | bytes 24704 | tf_op jit(solution)/shard_map/reduce_or | solution.py:55
  1.8 1.1 %mul.547 = f32[256,32,128]{2,1,0:T(8,128)S(1)} broadcast(f32[256,32]{1,0:T(8,128)S(1)} %copy.10), dimensions={0,1} | broadcast | bytes 4227072 | tf_op jit(solution)/shard_map/mul | solution.py:57
  3.0 7.7 %fusion.1 = f32[256,1024]{1,0:T(8,128)S(1)} fusion(bf16[4096,1024]{1,0:T(8,128)(2,1)} %param.9, f32[32,8,32,128]{3,2,1,0:T(8,128)S(1)} %bitcast.1129, bf16[256,4096]{1,0:T(8,128)(2,1)S(1)} %copy-done.1), kind=kOutput, calls=%fused_computation.2 | convolution fusion | flops 2150629376 | bytes 15728640 | tf_op jit(solution)/shard_map/dot_general | solution.py:61
  10.7 0.2 dynamic-slice_bitcast_fusion.10
  11.1 1.8 %collective-permute-done = f32[4,256,128]{2,1,0:T(8,128)S(1)} collective-permute-done((f32[4,256,128]{2,1,0:T(8,128)S(1)}, f32[4,256,128]{2,1,0:T(8,128)S(1)}, u32[]{:S(2)}, u32[]{:S(2)}) %collective-permute-start) | collective-permute-done | bytes 524320 | tf_op jit(solution)/shard_map/ppermute | solution.py:23
  13.0 1.7 %collective-permute-start.1 = (f32[256,128]{1,0:T(8,128)S(1)}, f32[256,128]{1,0:T(8,128)S(1)}, u32[]{:S(2)}, u32[]{:S(2)}) collective-permute-start(f32[256,128]{1,0:T(8,128)S(1)} %get-tuple-element.79), channel_id=1, source_target_pairs={{0,2},{1,3},{2,4},{3,5},{4,6},{5,7},{6,0},{7,1},{8,10},{9,11},{10,... | collective-permute-start | bytes 393224 | tf_op jit(solution)/shard_map/ppermute | solution.py:28
  14.7 2.6 %collective-permute-start.2 = (f32[256,128]{1,0:T(8,128)S(1)}, f32[256,128]{1,0:T(8,128)S(1)}, u32[]{:S(2)}, u32[]{:S(2)}) collective-permute-start(f32[256,128]{1,0:T(8,128)S(1)} %get-tuple-element.81), channel_id=1, source_target_pairs={{0,4},{1,5},{2,6},{3,7},{4,0},{5,1},{6,2},{7,3},{8,12},{9,13},{10,... | collective-permute-start | bytes 393224 | tf_op jit(solution)/shard_map/ppermute | solution.py:28
  17.3 0.7 %collective-permute-start.3 = (f32[256,128]{1,0:T(8,128)S(1)}, f32[256,128]{1,0:T(8,128)S(1)}, u32[]{:S(2)}, u32[]{:S(2)}) collective-permute-start(f32[256,128]{1,0:T(8,128)S(1)} %get-tuple-element.80), channel_id=1, source_target_pairs={{0,6},{1,7},{2,0},{3,1},{4,2},{5,3},{6,4},{7,5},{8,14},{9,15},{10,... | collective-permute-start | bytes 393224 | tf_op jit(solution)/shard_map/ppermute | solution.py:28
  18.1 0.8 %dynamic_slice.71 = f32[128]{0:T(128)S(1)} dynamic-slice(f32[1024]{0:T(1024)} %param.12, s32[]{:T(128)S(6)} %select_n.132), dynamic_slice_sizes={128} | dynamic-slice | bytes 1028 | tf_op jit(solution)/shard_map/dynamic_slice | solution.py:67
  18.9 0.7 %collective-permute-done.1 = f32[256,128]{1,0:T(8,128)S(1)} collective-permute-done((f32[256,128]{1,0:T(8,128)S(1)}, f32[256,128]{1,0:T(8,128)S(1)}, u32[]{:S(2)}, u32[]{:S(2)}) %collective-permute-start.1) | collective-permute-done | bytes 131104 | tf_op jit(solution)/shard_map/ppermute | solution.py:28
  19.6 2.9 %collective-permute-done.2 = f32[256,128]{1,0:T(8,128)S(1)} collective-permute-done((f32[256,128]{1,0:T(8,128)S(1)}, f32[256,128]{1,0:T(8,128)S(1)}, u32[]{:S(2)}, u32[]{:S(2)}) %collective-permute-start.2) | collective-permute-done | bytes 131104 | tf_op jit(solution)/shard_map/ppermute | solution.py:28
  22.5 1.7 %collective-permute-done.3 = f32[256,128]{1,0:T(8,128)S(1)} collective-permute-done((f32[256,128]{1,0:T(8,128)S(1)}, f32[256,128]{1,0:T(8,128)S(1)}, u32[]{:S(2)}, u32[]{:S(2)}) %collective-permute-start.3) | collective-permute-done | bytes 131104 | tf_op jit(solution)/shard_map/ppermute | solution.py:28
  26.1 1.0 %multiply_subtract_fusion.1 = (f32[256,128]{1,0:T(8,128)S(1)}, f32[256,128]{1,0:T(8,128)S(1)}, f32[256,128]{1,0:T(8,128)S(1)}) fusion(f32[128]{0:T(128)S(1)} %dynamic_slice.71, f32[256,1024]{1,0:T(8,128)} %param.11, s32[]{:T(128)S(6)} %select_n.132, pred[256]{0:T(512)(128)(4,1)S(1)} %add_compare_fusion, f32[256,128]{1,0:T(8,128)S(1)} %pad.210, ...), kind=kLoop, calls=%fused_computation.13 | loop fusion | flops 163840 | bytes 787204 | tf_op jit(solution)/shard_map/sub | solution.py:75
  27.2 0.1 slice.1102
  27.3 0.1 slice.1104
  27.4 0.1 slice.1063
  27.5 0.1 slice.1065
  30.2 0.1 slice.1140
  30.3 0.1 slice.1062
  30.8 1.1 %collective-permute-start.4 = (f32[1,5,128]{2,1,0:T(8,128)S(1)}, f32[1,5,128]{2,1,0:T(8,128)S(1)}, u32[]{:S(2)}, u32[]{:S(2)}) collective-permute-start(f32[1,5,128]{2,1,0:T(8,128)S(1)} %bitcast.1130), channel_id=1, source_target_pairs={{0,8},{8,0},{16,24},{24,16},{32,40},{40,32},{48,56},{56,48},{64,72... | collective-permute-start | bytes 7688 | tf_op jit(solution)/shard_map/ppermute | solution.py:38
  31.8 2.8 %collective-permute-done.4 = f32[1,5,128]{2,1,0:T(8,128)S(1)} collective-permute-done((f32[1,5,128]{2,1,0:T(8,128)S(1)}, f32[1,5,128]{2,1,0:T(8,128)S(1)}, u32[]{:S(2)}, u32[]{:S(2)}) %collective-permute-start.4) | collective-permute-done | bytes 2592 | tf_op jit(solution)/shard_map/ppermute | solution.py:38
  34.7 2.3 %collective-permute-start.5 = (f32[2,5,128]{2,1,0:T(8,128)S(1)}, f32[2,5,128]{2,1,0:T(8,128)S(1)}, u32[]{:S(2)}, u32[]{:S(2)}) collective-permute-start(f32[2,5,128]{2,1,0:T(8,128)S(1)} %maximum_select_fusion.4), channel_id=1, source_target_pairs={{0,16},{8,24},{16,0},{24,8},{32,48},{40,56},{48,32},{56,40},{64,80... | collective-permute-start | bytes 15368 | tf_op jit(solution)/shard_map/ppermute | solution.py:38
  37.0 2.8 %collective-permute-done.5 = f32[2,5,128]{2,1,0:T(8,128)S(1)} collective-permute-done((f32[2,5,128]{2,1,0:T(8,128)S(1)}, f32[2,5,128]{2,1,0:T(8,128)S(1)}, u32[]{:S(2)}, u32[]{:S(2)}) %collective-permute-start.5) | collective-permute-done | bytes 5152 | tf_op jit(solution)/shard_map/ppermute | solution.py:38
  39.8 1.2 %collective-permute-start.6 = (f32[4,5,128]{2,1,0:T(8,128)S(1)}, f32[4,5,128]{2,1,0:T(8,128)S(1)}, u32[]{:S(2)}, u32[]{:S(2)}) collective-permute-start(f32[4,5,128]{2,1,0:T(8,128)S(1)} %maximum_select_fusion.3), channel_id=1, source_target_pairs={{0,32},{8,40},{16,48},{24,56},{32,0},{40,8},{48,16},{56,24},{64,96... | collective-permute-start | bytes 30728 | tf_op jit(solution)/shard_map/ppermute | solution.py:38
  41.0 0.8 %dynamic-slice_bitcast_fusion.11 = f32[1,128]{1,0:T(1,128)S(1)} fusion(f32[1024]{0:T(1024)} %param.13, s32[]{:T(128)S(6)} %select_n.132), kind=kLoop, calls=%fused_computation.489 | loop fusion | bytes 1028 | tf_op jit(solution)/shard_map/stack | solution.py:98
  41.8 2.1 %collective-permute-done.6 = f32[4,5,128]{2,1,0:T(8,128)S(1)} collective-permute-done((f32[4,5,128]{2,1,0:T(8,128)S(1)}, f32[4,5,128]{2,1,0:T(8,128)S(1)}, u32[]{:S(2)}, u32[]{:S(2)}) %collective-permute-start.6) | collective-permute-done | bytes 10272 | tf_op jit(solution)/shard_map/ppermute | solution.py:38
  43.9 2.2 %collective-permute-start.7 = (f32[8,5,128]{2,1,0:T(8,128)S(1)}, f32[8,5,128]{2,1,0:T(8,128)S(1)}, u32[]{:S(2)}, u32[]{:S(2)}) collective-permute-start(f32[8,5,128]{2,1,0:T(8,128)S(1)} %maximum_select_fusion.2), channel_id=1, source_target_pairs={{0,64},{8,72},{16,80},{24,88},{32,96},{40,104},{48,112},{56,120},{... | collective-permute-start | bytes 61448 | tf_op jit(solution)/shard_map/ppermute | solution.py:38
  46.2 2.6 %collective-permute-done.7 = f32[8,5,128]{2,1,0:T(8,128)S(1)} collective-permute-done((f32[8,5,128]{2,1,0:T(8,128)S(1)}, f32[8,5,128]{2,1,0:T(8,128)S(1)}, u32[]{:S(2)}, u32[]{:S(2)}) %collective-permute-start.7) | collective-permute-done | bytes 20512 | tf_op jit(solution)/shard_map/ppermute | solution.py:38
  48.7 6.8 %collective-permute-start.8 = (f32[16,5,128]{2,1,0:T(8,128)S(1)}, f32[16,5,128]{2,1,0:T(8,128)S(1)}, u32[]{:S(2)}, u32[]{:S(2)}) collective-permute-start(f32[16,5,128]{2,1,0:T(8,128)S(1)} %maximum_select_fusion.1), channel_id=1, source_target_pairs={{0,128},{8,136},{16,144},{24,152},{32,160},{40,168},{48,176},{56,1... | collective-permute-start | bytes 122888 | tf_op jit(solution)/shard_map/ppermute | solution.py:38
  55.9 1.9 %collective-permute-done.8 = f32[16,5,128]{2,1,0:T(8,128)S(1)} collective-permute-done((f32[16,5,128]{2,1,0:T(8,128)S(1)}, f32[16,5,128]{2,1,0:T(8,128)S(1)}, u32[]{:S(2)}, u32[]{:S(2)}) %collective-permute-start.8) | collective-permute-done | bytes 40992 | tf_op jit(solution)/shard_map/ppermute | solution.py:38
  57.8 1.0 %fusion.209 = (f32[1,128]{1,0:T(1,128)S(1)}, f32[128]{0:T(128)S(1)}, f32[128]{0:T(128)S(1)}, f32[128]{0:T(128)S(1)}, f32[128]{0:T(128)S(1)}, /*index=5*/f32[128]...) fusion(f32[32,5,128]{2,1,0:T(8,128)S(1)} %maximum_select_fusion, ...), kind=kLoop, calls=%fused_computation.487 | loop fusion | flops 23808 | bytes 111620 | tf_op jit(solution)/shard_map/stack | solution.py:99
  59.0 0.7 %multiply_add_fusion = (f32[256,128]{1,0:T(8,128)}, f32[256,128]{1,0:T(8,128)}) fusion(f32[256,128]{1,0:T(8,128)S(1)} %slice.1210, f32[256,128]{1,0:T(8,128)S(1)} %slice.1206, f32[256,128]{1,0:T(8,128)S(1)} %slice.1208, f32[128]{0:T(128)S(1)} %fusion.22, f32[128]{0:T(128)S(1)} %fusion.21, f32[256,128]{1,0:T(8,128)S(1)} %get-tuple-element.66, ...), kind=kLoop, calls=%fused_computation.24 | loop fusion | flops 196608 | bytes 918528 | tf_op jit(solution)/shard_map/add | solution.py:102
  (283 shorter events, 4.5 us)
Async XLA Ops:
  0.6 10.5 %copy-start = (f32[256,1024]{1,0:T(8,128)S(1)}, f32[256,1024]{1,0:T(8,128)}, u32[]{:S(2)}) copy-start(f32[256,1024]{1,0:T(8,128)} %param.10) | copy-start | bytes 3145732
  0.6 2.3 %copy-start.1 = (bf16[256,4096]{1,0:T(8,128)(2,1)S(1)}, bf16[256,4096]{1,0:T(8,128)(2,1)}, u32[]{:S(2)}) copy-start(bf16[256,4096]{1,0:T(8,128)(2,1)} %param.7) | copy-start | bytes 6291460
  10.9 2.0 %collective-permute-start = (f32[4,256,128]{2,1,0:T(8,128)S(1)}, f32[4,256,128]{2,1,0:T(8,128)S(1)}, u32[]{:S(2)}, u32[]{:S(2)}) collective-permute-start(f32[4,256,128]{2,1,0:T(8,128)S(1)} %pad_maximum_fusion), channel_id=1, source_target_pairs={{0,1},{1,0},{2,3},{3,2},{4,5},{5,4},{6,7},{7,6},{8,9},{9,8},{10,11... | collective-permute-start | bytes 1572872 | tf_op jit(solution)/shard_map/ppermute | solution.py:23
  13.0 6.6 %collective-permute-start.1 = (f32[256,128]{1,0:T(8,128)S(1)}, f32[256,128]{1,0:T(8,128)S(1)}, u32[]{:S(2)}, u32[]{:S(2)}) collective-permute-start(f32[256,128]{1,0:T(8,128)S(1)} %get-tuple-element.79), channel_id=1, source_target_pairs={{0,2},{1,3},{2,4},{3,5},{4,6},{5,7},{6,0},{7,1},{8,10},{9,11},{10,... | collective-permute-start | bytes 393224 | tf_op jit(solution)/shard_map/ppermute | solution.py:28
  14.7 7.9 %collective-permute-start.2 = (f32[256,128]{1,0:T(8,128)S(1)}, f32[256,128]{1,0:T(8,128)S(1)}, u32[]{:S(2)}, u32[]{:S(2)}) collective-permute-start(f32[256,128]{1,0:T(8,128)S(1)} %get-tuple-element.81), channel_id=1, source_target_pairs={{0,4},{1,5},{2,6},{3,7},{4,0},{5,1},{6,2},{7,3},{8,12},{9,13},{10,... | collective-permute-start | bytes 393224 | tf_op jit(solution)/shard_map/ppermute | solution.py:28
  17.3 6.9 %collective-permute-start.3 = (f32[256,128]{1,0:T(8,128)S(1)}, f32[256,128]{1,0:T(8,128)S(1)}, u32[]{:S(2)}, u32[]{:S(2)}) collective-permute-start(f32[256,128]{1,0:T(8,128)S(1)} %get-tuple-element.80), channel_id=1, source_target_pairs={{0,6},{1,7},{2,0},{3,1},{4,2},{5,3},{6,4},{7,5},{8,14},{9,15},{10,... | collective-permute-start | bytes 393224 | tf_op jit(solution)/shard_map/ppermute | solution.py:28
  30.8 3.9 %collective-permute-start.4 = (f32[1,5,128]{2,1,0:T(8,128)S(1)}, f32[1,5,128]{2,1,0:T(8,128)S(1)}, u32[]{:S(2)}, u32[]{:S(2)}) collective-permute-start(f32[1,5,128]{2,1,0:T(8,128)S(1)} %bitcast.1130), channel_id=1, source_target_pairs={{0,8},{8,0},{16,24},{24,16},{32,40},{40,32},{48,56},{56,48},{64,72... | collective-permute-start | bytes 7688 | tf_op jit(solution)/shard_map/ppermute | solution.py:38
  34.7 5.2 %collective-permute-start.5 = (f32[2,5,128]{2,1,0:T(8,128)S(1)}, f32[2,5,128]{2,1,0:T(8,128)S(1)}, u32[]{:S(2)}, u32[]{:S(2)}) collective-permute-start(f32[2,5,128]{2,1,0:T(8,128)S(1)} %maximum_select_fusion.4), channel_id=1, source_target_pairs={{0,16},{8,24},{16,0},{24,8},{32,48},{40,56},{48,32},{56,40},{64,80... | collective-permute-start | bytes 15368 | tf_op jit(solution)/shard_map/ppermute | solution.py:38
  39.8 4.1 %collective-permute-start.6 = (f32[4,5,128]{2,1,0:T(8,128)S(1)}, f32[4,5,128]{2,1,0:T(8,128)S(1)}, u32[]{:S(2)}, u32[]{:S(2)}) collective-permute-start(f32[4,5,128]{2,1,0:T(8,128)S(1)} %maximum_select_fusion.3), channel_id=1, source_target_pairs={{0,32},{8,40},{16,48},{24,56},{32,0},{40,8},{48,16},{56,24},{64,96... | collective-permute-start | bytes 30728 | tf_op jit(solution)/shard_map/ppermute | solution.py:38
  43.9 4.8 %collective-permute-start.7 = (f32[8,5,128]{2,1,0:T(8,128)S(1)}, f32[8,5,128]{2,1,0:T(8,128)S(1)}, u32[]{:S(2)}, u32[]{:S(2)}) collective-permute-start(f32[8,5,128]{2,1,0:T(8,128)S(1)} %maximum_select_fusion.2), channel_id=1, source_target_pairs={{0,64},{8,72},{16,80},{24,88},{32,96},{40,104},{48,112},{56,120},{... | collective-permute-start | bytes 61448 | tf_op jit(solution)/shard_map/ppermute | solution.py:38
  48.7 9.0 %collective-permute-start.8 = (f32[16,5,128]{2,1,0:T(8,128)S(1)}, f32[16,5,128]{2,1,0:T(8,128)S(1)}, u32[]{:S(2)}, u32[]{:S(2)}) collective-permute-start(f32[16,5,128]{2,1,0:T(8,128)S(1)} %maximum_select_fusion.1), channel_id=1, source_target_pairs={{0,128},{8,136},{16,144},{24,152},{32,160},{40,168},{48,176},{56,1... | collective-permute-start | bytes 122888 | tf_op jit(solution)/shard_map/ppermute | solution.py:38

commit v3 on v2

--- a/solution.py
+++ b/solution.py
@@ -1,11 +1,64 @@
 import jax
 import jax.numpy as jnp
 from jax import lax
+from jax.experimental import pallas as pl
+from jax.experimental.pallas import tpu as pltpu
 from jax.sharding import PartitionSpec as P
 
 
-def link(earlier, later):
-    return (later[0] * earlier[0], later[0] * earlier[1] + later[1])
+SUB = 8
+
+
+def _chunk_scan(a, x, rows, reverse):
+    sub = lax.broadcasted_iota(jnp.int32, a.shape, 0) % SUB
+    for k in (1, 2, 4):
+        shift = rows - k if reverse else k
+        prev_a = pltpu.roll(a, shift, 0)
+        prev_x = [pltpu.roll(v, shift, 0) for v in x]
+        inside = sub < SUB - k if reverse else sub >= k
+        x = [jnp.where(inside, a * p + v, v) for p, v in zip(prev_x, x)]
+        a = jnp.where(inside, a * prev_a, a)
+    return a, x
+
+
+def _carry(a, x, out_a, out_x, rows, reverse):
+    chunks = rows // SUB
+    order = range(chunks - 1, -1, -1) if reverse else range(chunks)
+    edge = 0 if reverse else SUB - 1
+    carry_a = None
+    for i in order:
+        ca = a[i * SUB:(i + 1) * SUB]
+        cx = [v[i * SUB:(i + 1) * SUB] for v in x]
+        if carry_a is not None:
+            cx = [c * px + v for c, px, v in zip([ca] * len(cx), carry_x, cx)]
+            ca = ca * carry_a
+        if out_a is not None:
+            out_a[i * SUB:(i + 1) * SUB, :] = ca
+        for o, v in zip(out_x, cx):
+            o[i * SUB:(i + 1) * SUB, :] = v
+        carry_a = jnp.broadcast_to(ca[edge:edge + 1], ca.shape)
+        carry_x = [jnp.broadcast_to(v[edge:edge + 1], v.shape) for v in cx]
+
+
+def scan_kernel(a_ref, u_ref, g_ref, s_ref, pf_ref, lf_ref, pb_ref, bl_ref, bp_ref):
+    rows = a_ref.shape[0]
+    a, (u,) = _chunk_scan(a_ref[...], [u_ref[...]], rows, False)
+    _carry(a, [u], pf_ref, [lf_ref], rows, False)
+    scale = s_ref[...]
+    lf = lf_ref[...]
+    pf = pf_ref[...]
+    g, (ol, op) = _chunk_scan(g_ref[...], [lf - scale * lf, pf - scale * pf], rows, True)
+    _carry(g, [ol, op], pb_ref, [bl_ref, bp_ref], rows, True)
+
+
+def local_scans(factors, inflow, step_gain, scale):
+    shape = jax.ShapeDtypeStruct(factors.shape, jnp.float32)
+    rows, cols = factors.shape
+    return pl.pallas_call(
+        scan_kernel,
+        out_shape=[shape] * 5,
+        cost_estimate=pl.CostEstimate(flops=40 * rows * cols, bytes_accessed=36 * rows * cols, transcendentals=0),
+    )(factors, inflow, step_gain, scale)
 
 
 def sensor_reduce_scatter(partial, width):
@@ -71,18 +124,9 @@
     step_gain = jnp.where((hour_ids == total_hours - 1)[:, None], jnp.float32(0.0), gains)
     scale = step_gain * rates[None, :]
 
-    prod_fwd, local_fwd = lax.associative_scan(link, (factors, inflow), axis=0)
-    off_local = local_fwd - scale * local_fwd
-    off_prod = prod_fwd - scale * prod_fwd
-    prod_back, back = lax.associative_scan(
-        link,
-        (jnp.concatenate([step_gain, step_gain], 1), jnp.concatenate([off_local, off_prod], 1)),
-        axis=0,
-        reverse=True,
+    prod_fwd, local_fwd, prod_back, back_local, back_prod = local_scans(
+        factors, inflow, step_gain, scale
     )
-    prod_back = prod_back[:, :width]
-    back_local = back[:, :width]
-    back_prod = back[:, width:]
 
     summary = jnp.stack(
         [prod_fwd[-1], local_fwd[-1], prod_back[0], back_local[0], back_prod[0]], 0

time: 60.4 us -> 61.5 us (1.018)
  Pallas kernels: 0 us -> 2.44 us
  other arithmetic: 4.96 us -> 6.5 us
  between operations: 2.31 us -> 0.88 us
  waiting for transfers between devices: 19.4 us -> 18 us
    pallas_call x0 -> x1, Pallas kernels: none -> 2.44 us  [local_scans(): pl.pallas_call(scan_kernel, out_shape=[shape] * 5, cost_estimate=pl.CostE...]
    mul x14 -> x1, other arithmetic: 0.16 us -> 1.81 us  [per_device(): scale = step_gain * rates[None, :]]
    add x1, other arithmetic: 0.74 us -> 1.9 us  [per_device(): back_local + back_prod * entering_here[None, :]]
    sub x2 -> x0, other arithmetic: 1.04 us -> none  [the longest x1 1.01 us: per_device(): off_local = local_fwd - scale * local_fwd]
    ppermute x3, waiting for transfers between devices: 5.38 us -> 4.41 us  [sensor_reduce_scatter(): total = total + lax.ppermute(part, 'sensor', perm)]
    ppermute x1, waiting for transfers between devices: 1.78 us -> 1.04 us  [sensor_reduce_scatter(): lax.ppermute(send, 'sensor', [(i, i ^ 1) for i in range(count)])]
    pad x56 -> x0, local copies, waits for them, and re-layouts: 0.67 us -> none  [the longest x28 0.41 us: per_device(): lax.associative_scan(link, (jnp.concatenate([step_gain, step_gain], 1), j...]
    add x1, other arithmetic: 0.03 us -> 0.67 us  [sensor_reduce_scatter(): total = total + lax.ppermute(part, 'sensor', perm)]
  transfers between devices with their start and end apart: 9 -> 9, of which waited for: 9 -> 8; matrix products, arithmetic and copies ran while one was open for 3% -> 5% of each run, Pallas kernels for 0% -> 0%
where the time goes in v3:
time: 61.5 us; the launch traced here: 60.7 us
  starting transfers between devices  18.6 us (30%)
  waiting for transfers between devices  18 us (29%)
  matrix products  7.7 us (13%)
  local copies, waits for them, and re-layouts  6.58 us (11%)
  other arithmetic  6.5 us (11%)
  Pallas kernels  2.44 us (4%)
  between operations  0.88 us (1%)
    ppermute x5, starting transfers between devices, gather_tm(): other = lax.ppermute(held, 'tm', [(i, i ^ step) for i in range(count)])  13.5 us
    ppermute x5, waiting for transfers between devices, gather_tm(): other = lax.ppermute(held, 'tm', [(i, i ^ step) for i in range(count)])  12.5 us
    dot_general x1, matrix products, per_device(): jnp.dot(weighted, gain_rows, preferred_element_type=jnp.float32)  7.7 us
    ppermute x3, starting transfers between devices, sensor_reduce_scatter(): total = total + lax.ppermute(part, 'sensor', perm)  5.01 us
    ppermute x3, waiting for transfers between devices, sensor_reduce_scatter(): total = total + lax.ppermute(part, 'sensor', perm)  4.41 us
    pallas_call x1, Pallas kernels, local_scans(): pl.pallas_call(scan_kernel, out_shape=[shape] * 5, cost_estimate=pl.CostE...  2.44 us
    add x1, other arithmetic, per_device(): back_local + back_prod * entering_here[None, :]  1.9 us
    mul x1, other arithmetic, per_device(): scale = step_gain * rates[None, :]  1.81 us
  transfers between devices with their start and end apart: 9, of which 8 were waited for; matrix products, arithmetic and copies ran while one was open for 5% of the time, Pallas kernels for 0%

profile of v3, /device:TPU:8, one launch (start us, length us, event | category | flops | bytes accessed | tf_op | source)
XLA Modules:
  0.0 60.7 jit_solution(14728284151437207157)
XLA Ops:
  0.7 1.0 %compare_reduce_fusion = pred[256,32]{0,1:T(8,128)(4,1)S(1)} fusion(s32[256,16]{0,1:T(8,128)} %param.8, s32[32]{0:T(128)S(1)} %iota_add_fusion), kind=kLoop, calls=%fused_computation.5 | loop fusion | flops 253952 | bytes 24704 | tf_op jit(solution)/shard_map/reduce_or | solution.py:108
  1.8 1.1 %mul.362 = f32[256,32,128]{2,1,0:T(8,128)S(1)} broadcast(f32[256,32]{1,0:T(8,128)S(1)} %copy.10), dimensions={0,1} | broadcast | bytes 4227072 | tf_op jit(solution)/shard_map/mul | solution.py:110
  3.0 7.7 %fusion.1 = f32[256,1024]{1,0:T(8,128)S(1)} fusion(bf16[4096,1024]{1,0:T(8,128)(2,1)} %param.9, f32[32,8,32,128]{3,2,1,0:T(8,128)S(1)} %bitcast.1129, bf16[256,4096]{1,0:T(8,128)(2,1)S(1)} %copy-done), kind=kOutput, calls=%fused_computation.2 | convolution fusion | flops 2150629376 | bytes 15728640 | tf_op jit(solution)/shard_map/dot_general | solution.py:114
  10.7 0.2 dynamic-slice_bitcast_fusion.10
  11.1 0.8 %dynamic_slice.70 = f32[128]{0:T(128)S(1)} dynamic-slice(f32[1024]{0:T(1024)} %param.12, s32[]{:T(128)S(6)} %select_n.115), dynamic_slice_sizes={128} | dynamic-slice | bytes 1028 | tf_op jit(solution)/shard_map/dynamic_slice | solution.py:120
  11.8 1.0 %collective-permute-done = f32[4,256,128]{2,1,0:T(8,128)S(1)} collective-permute-done((f32[4,256,128]{2,1,0:T(8,128)S(1)}, f32[4,256,128]{2,1,0:T(8,128)S(1)}, u32[]{:S(2)}, u32[]{:S(2)}) %collective-permute-start) | collective-permute-done | bytes 524320 | tf_op jit(solution)/shard_map/ppermute | solution.py:76
  13.0 1.7 %collective-permute-start.1 = (f32[256,128]{1,0:T(8,128)S(1)}, f32[256,128]{1,0:T(8,128)S(1)}, u32[]{:S(2)}, u32[]{:S(2)}) collective-permute-start(f32[256,128]{1,0:T(8,128)S(1)} %get-tuple-element.84), channel_id=1, source_target_pairs={{0,2},{1,3},{2,4},{3,5},{4,6},{5,7},{6,0},{7,1},{8,10},{9,11},{10,... | collective-permute-start | bytes 393224 | tf_op jit(solution)/shard_map/ppermute | solution.py:81
  14.6 2.6 %collective-permute-start.2 = (f32[256,128]{1,0:T(8,128)S(1)}, f32[256,128]{1,0:T(8,128)S(1)}, u32[]{:S(2)}, u32[]{:S(2)}) collective-permute-start(f32[256,128]{1,0:T(8,128)S(1)} %get-tuple-element.86), channel_id=1, source_target_pairs={{0,4},{1,5},{2,6},{3,7},{4,0},{5,1},{6,2},{7,3},{8,12},{9,13},{10,... | collective-permute-start | bytes 393224 | tf_op jit(solution)/shard_map/ppermute | solution.py:81
  17.3 0.7 %collective-permute-start.3 = (f32[256,128]{1,0:T(8,128)S(1)}, f32[256,128]{1,0:T(8,128)S(1)}, u32[]{:S(2)}, u32[]{:S(2)}) collective-permute-start(f32[256,128]{1,0:T(8,128)S(1)} %get-tuple-element.85), channel_id=1, source_target_pairs={{0,6},{1,7},{2,0},{3,1},{4,2},{5,3},{6,4},{7,5},{8,14},{9,15},{10,... | collective-permute-start | bytes 393224 | tf_op jit(solution)/shard_map/ppermute | solution.py:81
  18.0 1.8 %broadcast_multiply_fusion = (f32[256,128]{1,0:T(8,128)}, f32[256,128]{1,0:T(8,128)}, f32[256,128]{1,0:T(8,128)}) fusion(f32[128]{0:T(128)S(1)} %dynamic_slice.70, f32[256,1024]{1,0:T(8,128)} %param.11, s32[]{:T(128)S(6)} %select_n.115, pred[256]{0:T(512)(128)(4,1)S(1)} %add_compare_fusion, f32[256,1024]{1,0:T(8,128)} %param.10), kind=kLoop, calls=%fused_computation.25 | loop fusion | flops 65536 | bytes 656132 | tf_op jit(solution)/shard_map/mul | solution.py:125
  19.8 2.7 %collective-permute-done.2 = f32[256,128]{1,0:T(8,128)S(1)} collective-permute-done((f32[256,128]{1,0:T(8,128)S(1)}, f32[256,128]{1,0:T(8,128)S(1)}, u32[]{:S(2)}, u32[]{:S(2)}) %collective-permute-start.2) | collective-permute-done | bytes 131104 | tf_op jit(solution)/shard_map/ppermute | solution.py:81
  22.5 1.7 %collective-permute-done.3 = f32[256,128]{1,0:T(8,128)S(1)} collective-permute-done((f32[256,128]{1,0:T(8,128)S(1)}, f32[256,128]{1,0:T(8,128)S(1)}, u32[]{:S(2)}, u32[]{:S(2)}) %collective-permute-start.3) | collective-permute-done | bytes 131104 | tf_op jit(solution)/shard_map/ppermute | solution.py:81
  24.2 0.7 %fusion.4.u_ref = f32[256,128]{1,0:T(8,128)} fusion(f32[256,128]{1,0:T(8,128)S(1)} %collective-permute-done.3, f32[256,128]{1,0:T(8,128)S(1)} %collective-permute-done.2, f32[256,128]{1,0:T(8,128)S(1)} %collective-permute-done.1, f32[4,256,128]{2,1,0:T(8,128)S(1)} %maximum_add_fusion, s32[]{:T(128)S(6)} %select_n.126), kind=kLoop, calls=%fused_computation.9 | loop fusion | flops 98304 | bytes 655364 | tf_op jit(solution)/shard_map/add | solution.py:81
  24.9 2.4 %shard_map.86 = (f32[256,128]{1,0:T(8,128)}, f32[256,128]{1,0:T(8,128)}, f32[256,128]{1,0:T(8,128)}, f32[256,128]{1,0:T(8,128)}, f32[256,128]{1,0:T(8,128)}) custom-call(f32[256,128]{1,0:T(8,128)} %get-tuple-element.89.a_ref, f32[256,128]{1,0:T(8,128)} %fusion.4.u_ref, f32[256,128]{1,0:T(8,128)} %get-tuple-element.75.g_ref, f32[256,128]{1,0:T(8,128)} %get-tuple-element.74.s_ref), custom_call_target="tpu_custom_call" | custom-call | flops 1310720 | bytes 1179648 | tf_op jit(solution)/shard_map/pallas_call | solution.py:57
  27.3 0.7 %slice.480 = f32[1,128]{1,0:T(1,128)S(1)} slice(f32[256,128]{1,0:T(8,128)} %get-tuple-element.8), slice={[255:256], [0:128]} | slice | bytes 1024 | tf_op jit(solution)/shard_map/slice | solution.py:132
  28.0 0.7 %slice.481 = f32[1,128]{1,0:T(1,128)S(1)} slice(f32[256,128]{1,0:T(8,128)} %get-tuple-element.7), slice={[255:256], [0:128]} | slice | bytes 1024 | tf_op jit(solution)/shard_map/slice | solution.py:132
  28.7 0.7 %slice.482 = f32[1,128]{1,0:T(1,128)S(1)} slice(f32[256,128]{1,0:T(8,128)} %get-tuple-element.9), slice={[0:1], [0:128]} | slice | bytes 1024 | tf_op jit(solution)/shard_map/slice | solution.py:132
  29.3 0.7 %slice.483 = f32[1,128]{1,0:T(1,128)S(1)} slice(f32[256,128]{1,0:T(8,128)} %get-tuple-element.10), slice={[0:1], [0:128]} | slice | bytes 1024 | tf_op jit(solution)/shard_map/slice | solution.py:132
  30.0 0.7 %slice.484 = f32[1,128]{1,0:T(1,128)S(1)} slice(f32[256,128]{1,0:T(8,128)} %get-tuple-element.11), slice={[0:1], [0:128]} | slice | bytes 1024 | tf_op jit(solution)/shard_map/slice | solution.py:132
  30.7 0.9 %collective-permute-start.4 = (f32[1,5,128]{2,1,0:T(8,128)S(1)}, f32[1,5,128]{2,1,0:T(8,128)S(1)}, u32[]{:S(2)}, u32[]{:S(2)}) collective-permute-start(f32[1,5,128]{2,1,0:T(8,128)S(1)} %bitcast.1130), channel_id=1, source_target_pairs={{0,8},{8,0},{16,24},{24,16},{32,40},{40,32},{48,56},{56,48},{64,72... | collective-permute-start | bytes 7688 | tf_op jit(solution)/shard_map/ppermute | solution.py:91
  31.6 2.8 %collective-permute-done.4 = f32[1,5,128]{2,1,0:T(8,128)S(1)} collective-permute-done((f32[1,5,128]{2,1,0:T(8,128)S(1)}, f32[1,5,128]{2,1,0:T(8,128)S(1)}, u32[]{:S(2)}, u32[]{:S(2)}) %collective-permute-start.4) | collective-permute-done | bytes 2592 | tf_op jit(solution)/shard_map/ppermute | solution.py:91
  34.4 2.3 %collective-permute-start.5 = (f32[2,5,128]{2,1,0:T(8,128)S(1)}, f32[2,5,128]{2,1,0:T(8,128)S(1)}, u32[]{:S(2)}, u32[]{:S(2)}) collective-permute-start(f32[2,5,128]{2,1,0:T(8,128)S(1)} %maximum_select_fusion.4), channel_id=1, source_target_pairs={{0,16},{8,24},{16,0},{24,8},{32,48},{40,56},{48,32},{56,40},{64,80... | collective-permute-start | bytes 15368 | tf_op jit(solution)/shard_map/ppermute | solution.py:91
  36.8 2.8 %collective-permute-done.5 = f32[2,5,128]{2,1,0:T(8,128)S(1)} collective-permute-done((f32[2,5,128]{2,1,0:T(8,128)S(1)}, f32[2,5,128]{2,1,0:T(8,128)S(1)}, u32[]{:S(2)}, u32[]{:S(2)}) %collective-permute-start.5) | collective-permute-done | bytes 5152 | tf_op jit(solution)/shard_map/ppermute | solution.py:91
  39.6 1.2 %collective-permute-start.6 = (f32[4,5,128]{2,1,0:T(8,128)S(1)}, f32[4,5,128]{2,1,0:T(8,128)S(1)}, u32[]{:S(2)}, u32[]{:S(2)}) collective-permute-start(f32[4,5,128]{2,1,0:T(8,128)S(1)} %maximum_select_fusion.3), channel_id=1, source_target_pairs={{0,32},{8,40},{16,48},{24,56},{32,0},{40,8},{48,16},{56,24},{64,96... | collective-permute-start | bytes 30728 | tf_op jit(solution)/shard_map/ppermute | solution.py:91
  40.8 2.8 %collective-permute-done.6 = f32[4,5,128]{2,1,0:T(8,128)S(1)} collective-permute-done((f32[4,5,128]{2,1,0:T(8,128)S(1)}, f32[4,5,128]{2,1,0:T(8,128)S(1)}, u32[]{:S(2)}, u32[]{:S(2)}) %collective-permute-start.6) | collective-permute-done | bytes 10272 | tf_op jit(solution)/shard_map/ppermute | solution.py:91
  43.7 2.2 %collective-permute-start.7 = (f32[8,5,128]{2,1,0:T(8,128)S(1)}, f32[8,5,128]{2,1,0:T(8,128)S(1)}, u32[]{:S(2)}, u32[]{:S(2)}) collective-permute-start(f32[8,5,128]{2,1,0:T(8,128)S(1)} %maximum_select_fusion.2), channel_id=1, source_target_pairs={{0,64},{8,72},{16,80},{24,88},{32,96},{40,104},{48,112},{56,120},{... | collective-permute-start | bytes 61448 | tf_op jit(solution)/shard_map/ppermute | solution.py:91
  45.9 2.6 %collective-permute-done.7 = f32[8,5,128]{2,1,0:T(8,128)S(1)} collective-permute-done((f32[8,5,128]{2,1,0:T(8,128)S(1)}, f32[8,5,128]{2,1,0:T(8,128)S(1)}, u32[]{:S(2)}, u32[]{:S(2)}) %collective-permute-start.7) | collective-permute-done | bytes 20512 | tf_op jit(solution)/shard_map/ppermute | solution.py:91
  48.5 6.8 %collective-permute-start.8 = (f32[16,5,128]{2,1,0:T(8,128)S(1)}, f32[16,5,128]{2,1,0:T(8,128)S(1)}, u32[]{:S(2)}, u32[]{:S(2)}) collective-permute-start(f32[16,5,128]{2,1,0:T(8,128)S(1)} %maximum_select_fusion.1), channel_id=1, source_target_pairs={{0,128},{8,136},{16,144},{24,152},{32,160},{40,168},{48,176},{56,1... | collective-permute-start | bytes 122888 | tf_op jit(solution)/shard_map/ppermute | solution.py:91
  55.3 0.8 %dynamic-slice_bitcast_fusion.11 = f32[1,128]{1,0:T(1,128)S(1)} fusion(f32[1024]{0:T(1024)} %param.13, s32[]{:T(128)S(6)} %select_n.115), kind=kLoop, calls=%fused_computation.378 | loop fusion | bytes 1028 | tf_op jit(solution)/shard_map/stack | solution.py:142
  56.1 1.5 %collective-permute-done.8 = f32[16,5,128]{2,1,0:T(8,128)S(1)} collective-permute-done((f32[16,5,128]{2,1,0:T(8,128)S(1)}, f32[16,5,128]{2,1,0:T(8,128)S(1)}, u32[]{:S(2)}, u32[]{:S(2)}) %collective-permute-start.8) | collective-permute-done | bytes 40992 | tf_op jit(solution)/shard_map/ppermute | solution.py:91
  57.6 1.0 %fusion.193 = (f32[1,128]{1,0:T(1,128)S(1)}, f32[128]{0:T(128)S(1)}, f32[128]{0:T(128)S(1)}, f32[128]{0:T(128)S(1)}, f32[128]{0:T(128)S(1)}, /*index=5*/f32[128]...) fusion(f32[32,5,128]{2,1,0:T(8,128)S(1)} %maximum_select_fusion, ...), kind=kLoop, calls=%fused_computation.377 | loop fusion | flops 23808 | bytes 111620 | tf_op jit(solution)/shard_map/stack | solution.py:143
  58.8 1.9 %multiply_add_fusion = (f32[256,128]{1,0:T(8,128)}, f32[256,128]{1,0:T(8,128)}) fusion(f32[256,128]{1,0:T(8,128)} %get-tuple-element.9, f32[256,128]{1,0:T(8,128)} %get-tuple-element.10, f32[256,128]{1,0:T(8,128)} %get-tuple-element.11, f32[128]{0:T(128)S(1)} %fusion.6, f32[128]{0:T(128)S(1)} %fusion.5, f32[256,128]{1,0:T(8,128)} %get-tuple-element.7, ...), kind=kLoop, calls=%fused_computation.10 | loop fusion | flops 196608 | bytes 918528 | tf_op jit(solution)/shard_map/add | solution.py:146
  (22 shorter events, 0.6 us)
Async XLA Ops:
  0.6 2.3 %copy-start = (bf16[256,4096]{1,0:T(8,128)(2,1)S(1)}, bf16[256,4096]{1,0:T(8,128)(2,1)}, u32[]{:S(2)}) copy-start(bf16[256,4096]{1,0:T(8,128)(2,1)} %param.7) | copy-start | bytes 6291460
  10.9 2.0 %collective-permute-start = (f32[4,256,128]{2,1,0:T(8,128)S(1)}, f32[4,256,128]{2,1,0:T(8,128)S(1)}, u32[]{:S(2)}, u32[]{:S(2)}) collective-permute-start(f32[4,256,128]{2,1,0:T(8,128)S(1)} %pad_maximum_fusion), channel_id=1, source_target_pairs={{0,1},{1,0},{2,3},{3,2},{4,5},{5,4},{6,7},{7,6},{8,9},{9,8},{10,11... | collective-permute-start | bytes 1572872 | tf_op jit(solution)/shard_map/ppermute | solution.py:76
  13.0 6.8 %collective-permute-start.1 = (f32[256,128]{1,0:T(8,128)S(1)}, f32[256,128]{1,0:T(8,128)S(1)}, u32[]{:S(2)}, u32[]{:S(2)}) collective-permute-start(f32[256,128]{1,0:T(8,128)S(1)} %get-tuple-element.84), channel_id=1, source_target_pairs={{0,2},{1,3},{2,4},{3,5},{4,6},{5,7},{6,0},{7,1},{8,10},{9,11},{10,... | collective-permute-start | bytes 393224 | tf_op jit(solution)/shard_map/ppermute | solution.py:81
  14.6 7.9 %collective-permute-start.2 = (f32[256,128]{1,0:T(8,128)S(1)}, f32[256,128]{1,0:T(8,128)S(1)}, u32[]{:S(2)}, u32[]{:S(2)}) collective-permute-start(f32[256,128]{1,0:T(8,128)S(1)} %get-tuple-element.86), channel_id=1, source_target_pairs={{0,4},{1,5},{2,6},{3,7},{4,0},{5,1},{6,2},{7,3},{8,12},{9,13},{10,... | collective-permute-start | bytes 393224 | tf_op jit(solution)/shard_map/ppermute | solution.py:81
  17.3 6.9 %collective-permute-start.3 = (f32[256,128]{1,0:T(8,128)S(1)}, f32[256,128]{1,0:T(8,128)S(1)}, u32[]{:S(2)}, u32[]{:S(2)}) collective-permute-start(f32[256,128]{1,0:T(8,128)S(1)} %get-tuple-element.85), channel_id=1, source_target_pairs={{0,6},{1,7},{2,0},{3,1},{4,2},{5,3},{6,4},{7,5},{8,14},{9,15},{10,... | collective-permute-start | bytes 393224 | tf_op jit(solution)/shard_map/ppermute | solution.py:81
  30.7 3.7 %collective-permute-start.4 = (f32[1,5,128]{2,1,0:T(8,128)S(1)}, f32[1,5,128]{2,1,0:T(8,128)S(1)}, u32[]{:S(2)}, u32[]{:S(2)}) collective-permute-start(f32[1,5,128]{2,1,0:T(8,128)S(1)} %bitcast.1130), channel_id=1, source_target_pairs={{0,8},{8,0},{16,24},{24,16},{32,40},{40,32},{48,56},{56,48},{64,72... | collective-permute-start | bytes 7688 | tf_op jit(solution)/shard_map/ppermute | solution.py:91
  34.4 5.2 %collective-permute-start.5 = (f32[2,5,128]{2,1,0:T(8,128)S(1)}, f32[2,5,128]{2,1,0:T(8,128)S(1)}, u32[]{:S(2)}, u32[]{:S(2)}) collective-permute-start(f32[2,5,128]{2,1,0:T(8,128)S(1)} %maximum_select_fusion.4), channel_id=1, source_target_pairs={{0,16},{8,24},{16,0},{24,8},{32,48},{40,56},{48,32},{56,40},{64,80... | collective-permute-start | bytes 15368 | tf_op jit(solution)/shard_map/ppermute | solution.py:91
  39.6 4.1 %collective-permute-start.6 = (f32[4,5,128]{2,1,0:T(8,128)S(1)}, f32[4,5,128]{2,1,0:T(8,128)S(1)}, u32[]{:S(2)}, u32[]{:S(2)}) collective-permute-start(f32[4,5,128]{2,1,0:T(8,128)S(1)} %maximum_select_fusion.3), channel_id=1, source_target_pairs={{0,32},{8,40},{16,48},{24,56},{32,0},{40,8},{48,16},{56,24},{64,96... | collective-permute-start | bytes 30728 | tf_op jit(solution)/shard_map/ppermute | solution.py:91
  43.7 4.8 %collective-permute-start.7 = (f32[8,5,128]{2,1,0:T(8,128)S(1)}, f32[8,5,128]{2,1,0:T(8,128)S(1)}, u32[]{:S(2)}, u32[]{:S(2)}) collective-permute-start(f32[8,5,128]{2,1,0:T(8,128)S(1)} %maximum_select_fusion.2), channel_id=1, source_target_pairs={{0,64},{8,72},{16,80},{24,88},{32,96},{40,104},{48,112},{56,120},{... | collective-permute-start | bytes 61448 | tf_op jit(solution)/shard_map/ppermute | solution.py:91
  48.5 9.1 %collective-permute-start.8 = (f32[16,5,128]{2,1,0:T(8,128)S(1)}, f32[16,5,128]{2,1,0:T(8,128)S(1)}, u32[]{:S(2)}, u32[]{:S(2)}) collective-permute-start(f32[16,5,128]{2,1,0:T(8,128)S(1)} %maximum_select_fusion.1), channel_id=1, source_target_pairs={{0,128},{8,136},{16,144},{24,152},{32,160},{40,168},{48,176},{56,1... | collective-permute-start | bytes 122888 | tf_op jit(solution)/shard_map/ppermute | solution.py:91

commit v4 on v3

--- a/solution.py
+++ b/solution.py
@@ -40,7 +40,7 @@
         carry_x = [jnp.broadcast_to(v[edge:edge + 1], v.shape) for v in cx]
 
 
-def scan_kernel(a_ref, u_ref, g_ref, s_ref, pf_ref, lf_ref, pb_ref, bl_ref, bp_ref):
+def scan_kernel(a_ref, u_ref, g_ref, s_ref, pf_ref, lf_ref, pb_ref, bl_ref, bp_ref, sum_ref):
     rows = a_ref.shape[0]
     a, (u,) = _chunk_scan(a_ref[...], [u_ref[...]], rows, False)
     _carry(a, [u], pf_ref, [lf_ref], rows, False)
@@ -49,6 +49,12 @@
     pf = pf_ref[...]
     g, (ol, op) = _chunk_scan(g_ref[...], [lf - scale * lf, pf - scale * pf], rows, True)
     _carry(g, [ol, op], pb_ref, [bl_ref, bp_ref], rows, True)
+    sum_ref[...] = jnp.zeros_like(sum_ref)
+    sum_ref[0:1, :] = pf_ref[rows - 1:rows, :]
+    sum_ref[1:2, :] = lf_ref[rows - 1:rows, :]
+    sum_ref[2:3, :] = pb_ref[0:1, :]
+    sum_ref[3:4, :] = bl_ref[0:1, :]
+    sum_ref[4:5, :] = bp_ref[0:1, :]
 
 
 def local_scans(factors, inflow, step_gain, scale):
@@ -56,9 +62,38 @@
     rows, cols = factors.shape
     return pl.pallas_call(
         scan_kernel,
-        out_shape=[shape] * 5,
+        out_shape=[shape] * 5 + [jax.ShapeDtypeStruct((SUB, cols), jnp.float32)],
         cost_estimate=pl.CostEstimate(flops=40 * rows * cols, bytes_accessed=36 * rows * cols, transcendentals=0),
     )(factors, inflow, step_gain, scale)
+
+
+def combine_kernel(every_ref, init_ref, pf_ref, lf_ref, pb_ref, bl_ref, bp_ref, f_ref, s_ref):
+    count = every_ref.shape[0]
+    place = lax.axis_index("tm")
+    entering = [init_ref[...]]
+    for k in range(count - 1):
+        tile = every_ref[k]
+        entering.append(tile[0:1] * entering[-1] + tile[1:2])
+    after = jnp.zeros_like(entering[0])
+    e_here = jnp.where(place == count - 1, entering[count - 1], 0.0)
+    y_here = jnp.zeros_like(after)
+    for k in range(count - 1, 0, -1):
+        tile = every_ref[k]
+        after = tile[3:4] + tile[4:5] * entering[k] + tile[2:3] * after
+        e_here = jnp.where(place == k - 1, entering[k - 1], e_here)
+        y_here = jnp.where(place == k - 1, after, y_here)
+    f_ref[...] = lf_ref[...] + pf_ref[...] * e_here
+    s_ref[...] = bl_ref[...] + bp_ref[...] * e_here + pb_ref[...] * y_here
+
+
+def combine(every, initial, pf, lf, pb, bl, bp):
+    rows, cols = pf.shape
+    shape = jax.ShapeDtypeStruct(pf.shape, jnp.float32)
+    return pl.pallas_call(
+        combine_kernel,
+        out_shape=[shape, shape],
+        cost_estimate=pl.CostEstimate(flops=5 * rows * cols, bytes_accessed=28 * rows * cols, transcendentals=0),
+    )(every, initial, pf, lf, pb, bl, bp)
 
 
 def sensor_reduce_scatter(partial, width):
@@ -124,26 +159,13 @@
     step_gain = jnp.where((hour_ids == total_hours - 1)[:, None], jnp.float32(0.0), gains)
     scale = step_gain * rates[None, :]
 
-    prod_fwd, local_fwd, prod_back, back_local, back_prod = local_scans(
+    prod_fwd, local_fwd, prod_back, back_local, back_prod, summary = local_scans(
         factors, inflow, step_gain, scale
     )
-
-    summary = jnp.stack(
-        [prod_fwd[-1], local_fwd[-1], prod_back[0], back_local[0], back_prod[0]], 0
+    every = gather_tm(summary)
+    filtered, smoothed = combine(
+        every, initial[None, :], prod_fwd, local_fwd, prod_back, back_local, back_prod
     )
-    every = gather_tm(summary)
-    entering = [initial]
-    for k in range(time_count - 1):
-        entering.append(every[k, 0] * entering[-1] + every[k, 1])
-    after = [jnp.zeros_like(initial)]
-    for k in range(time_count - 1, 0, -1):
-        after.append(every[k, 3] + every[k, 4] * entering[k] + every[k, 2] * after[-1])
-    after = after[::-1]
-    entering_here = lax.dynamic_index_in_dim(jnp.stack(entering, 0), time_index, 0, False)
-    after_here = lax.dynamic_index_in_dim(jnp.stack(after, 0), time_index, 0, False)
-
-    filtered = local_fwd + prod_fwd * entering_here[None, :]
-    smoothed = back_local + back_prod * entering_here[None, :] + prod_back * after_here[None, :]
     return (filtered, smoothed)
 
 

time: 61.5 us -> 58.2 us (0.946)
  local copies, waits for them, and re-layouts: 6.58 us -> 2.76 us
  Pallas kernels: 2.44 us -> 4.53 us
  other arithmetic: 6.5 us -> 5.04 us
    slice x5 -> x0, local copies, waits for them, and re-layouts: 3.4 us -> none  [the longest x1 0.69 us: per_device(): back_prod[0]]
    pallas_call x1 -> x2, Pallas kernels: 2.44 us -> 4.53 us  [the longest x1 2.45 us: local_scans(): pl.pallas_call(scan_kernel, out_shape=[shape] * 5 + [jax.ShapeDtypeStruct...]
    add x1 -> x0, other arithmetic: 1.9 us -> none  [per_device(): back_local + back_prod * entering_here[None, :]]
    select_n x5, other arithmetic: 0.04 us -> 1.44 us  [gather_tm(): jnp.where(low, jnp.concatenate([held, other], 0), jnp.concatenate([other,...]
    another operation x1 -> x0, other arithmetic: 0.98 us -> none  [per_device(): jnp.stack(after, 0)]
    another operation x5 -> x0, local copies, waits for them, and re-layouts: 0.97 us -> none  [the longest x2 0.85 us: per_device(): jnp.stack(entering, 0)]
where the time goes in v4:
time: 58.2 us; the launch traced here: 57.8 us
  starting transfers between devices  18.5 us (32%)
  waiting for transfers between devices  18.4 us (32%)
  matrix products  7.73 us (13%)
  other arithmetic  5.04 us (9%)
  Pallas kernels  4.53 us (8%)
  local copies, waits for them, and re-layouts  2.76 us (5%)
  between operations  0.86 us (1%)
    ppermute x5, starting transfers between devices, gather_tm(): other = lax.ppermute(held, 'tm', [(i, i ^ step) for i in range(count)])  13.4 us
    ppermute x5, waiting for transfers between devices, gather_tm(): other = lax.ppermute(held, 'tm', [(i, i ^ step) for i in range(count)])  12.9 us
    dot_general x1, matrix products, per_device(): jnp.dot(weighted, gain_rows, preferred_element_type=jnp.float32)  7.73 us
    ppermute x3, starting transfers between devices, sensor_reduce_scatter(): total = total + lax.ppermute(part, 'sensor', perm)  5.01 us
    ppermute x3, waiting for transfers between devices, sensor_reduce_scatter(): total = total + lax.ppermute(part, 'sensor', perm)  4.41 us
    pallas_call x1, Pallas kernels, local_scans(): pl.pallas_call(scan_kernel, out_shape=[shape] * 5 + [jax.ShapeDtypeStruct...  2.45 us
    pallas_call x1, Pallas kernels, combine(): pl.pallas_call(combine_kernel, out_shape=[shape, shape], cost_estimate=pl...  2.08 us
    mul x1, other arithmetic, per_device(): scale = step_gain * rates[None, :]  1.81 us
  transfers between devices with their start and end apart: 9, of which 8 were waited for; matrix products, arithmetic and copies ran while one was open for 5% of the time, Pallas kernels for 0%

profile of v4, /device:TPU:8, one launch (start us, length us, event | category | flops | bytes accessed | tf_op | source)
XLA Modules:
  0.0 57.8 jit_solution(8863818502245273228)
XLA Ops:
  0.6 0.0 copy-start
  0.7 1.0 %compare_reduce_fusion = pred[256,32]{0,1:T(8,128)(4,1)S(1)} fusion(s32[256,16]{0,1:T(8,128)} %param.8, s32[32]{0:T(128)S(1)} %iota_add_fusion), kind=kLoop, calls=%fused_computation.5 | loop fusion | flops 253952 | bytes 24704 | tf_op jit(solution)/shard_map/reduce_or | solution.py:143
  1.7 0.1 copy.10
  1.8 1.1 %mul.54 = f32[256,32,128]{2,1,0:T(8,128)S(1)} broadcast(f32[256,32]{1,0:T(8,128)S(1)} %copy.10), dimensions={0,1} | broadcast | bytes 4227072 | tf_op jit(solution)/shard_map/mul | solution.py:145
  3.0 7.7 %fusion.1 = f32[256,1024]{1,0:T(8,128)S(1)} fusion(bf16[4096,1024]{1,0:T(8,128)(2,1)} %param.9, f32[32,8,32,128]{3,2,1,0:T(8,128)S(1)} %bitcast.38, bf16[256,4096]{1,0:T(8,128)(2,1)S(1)} %copy-done.1), kind=kOutput, calls=%fused_computation.2 | convolution fusion | flops 2150629376 | bytes 15728640 | tf_op jit(solution)/shard_map/dot_general | solution.py:149
  10.7 0.2 dynamic-slice_bitcast_fusion.10
  10.9 0.1 collective-permute-start
  11.1 0.8 %dynamic_slice.63 = f32[128]{0:T(128)S(1)} dynamic-slice(f32[1024]{0:T(1024)} %param.12, s32[]{:T(128)S(6)} %select_n.115), dynamic_slice_sizes={128} | dynamic-slice | bytes 1028 | tf_op jit(solution)/shard_map/dynamic_slice | solution.py:155
  11.9 1.0 %collective-permute-done = f32[4,256,128]{2,1,0:T(8,128)S(1)} collective-permute-done((f32[4,256,128]{2,1,0:T(8,128)S(1)}, f32[4,256,128]{2,1,0:T(8,128)S(1)}, u32[]{:S(2)}, u32[]{:S(2)}) %collective-permute-start) | collective-permute-done | bytes 524320 | tf_op jit(solution)/shard_map/ppermute | solution.py:111
  12.9 0.1 maximum_add_fusion
  13.0 1.7 %collective-permute-start.1 = (f32[256,128]{1,0:T(8,128)S(1)}, f32[256,128]{1,0:T(8,128)S(1)}, u32[]{:S(2)}, u32[]{:S(2)}) collective-permute-start(f32[256,128]{1,0:T(8,128)S(1)} %get-tuple-element.24), channel_id=1, source_target_pairs={{0,2},{1,3},{2,4},{3,5},{4,6},{5,7},{6,0},{7,1},{8,10},{9,11},{10,... | collective-permute-start | bytes 393224 | tf_op jit(solution)/shard_map/ppermute | solution.py:116
  14.7 2.6 %collective-permute-start.2 = (f32[256,128]{1,0:T(8,128)S(1)}, f32[256,128]{1,0:T(8,128)S(1)}, u32[]{:S(2)}, u32[]{:S(2)}) collective-permute-start(f32[256,128]{1,0:T(8,128)S(1)} %get-tuple-element.26), channel_id=1, source_target_pairs={{0,4},{1,5},{2,6},{3,7},{4,0},{5,1},{6,2},{7,3},{8,12},{9,13},{10,... | collective-permute-start | bytes 393224 | tf_op jit(solution)/shard_map/ppermute | solution.py:116
  17.3 0.7 %collective-permute-start.3 = (f32[256,128]{1,0:T(8,128)S(1)}, f32[256,128]{1,0:T(8,128)S(1)}, u32[]{:S(2)}, u32[]{:S(2)}) collective-permute-start(f32[256,128]{1,0:T(8,128)S(1)} %get-tuple-element.25), channel_id=1, source_target_pairs={{0,6},{1,7},{2,0},{3,1},{4,2},{5,3},{6,4},{7,5},{8,14},{9,15},{10,... | collective-permute-start | bytes 393224 | tf_op jit(solution)/shard_map/ppermute | solution.py:116
  18.0 1.8 %broadcast_multiply_fusion = (f32[256,128]{1,0:T(8,128)}, f32[256,128]{1,0:T(8,128)}, f32[256,128]{1,0:T(8,128)}) fusion(f32[128]{0:T(128)S(1)} %dynamic_slice.63, f32[256,1024]{1,0:T(8,128)} %param.11, s32[]{:T(128)S(6)} %select_n.115, pred[256]{0:T(512)(128)(4,1)S(1)} %add_compare_fusion, f32[256,1024]{1,0:T(8,128)} %param.10), kind=kLoop, calls=%fused_computation.23 | loop fusion | flops 65536 | bytes 656132 | tf_op jit(solution)/shard_map/mul | solution.py:160
  19.8 2.7 %collective-permute-done.2 = f32[256,128]{1,0:T(8,128)S(1)} collective-permute-done((f32[256,128]{1,0:T(8,128)S(1)}, f32[256,128]{1,0:T(8,128)S(1)}, u32[]{:S(2)}, u32[]{:S(2)}) %collective-permute-start.2) | collective-permute-done | bytes 131104 | tf_op jit(solution)/shard_map/ppermute | solution.py:116
  22.5 1.7 %collective-permute-done.3 = f32[256,128]{1,0:T(8,128)S(1)} collective-permute-done((f32[256,128]{1,0:T(8,128)S(1)}, f32[256,128]{1,0:T(8,128)S(1)}, u32[]{:S(2)}, u32[]{:S(2)}) %collective-permute-start.3) | collective-permute-done | bytes 131104 | tf_op jit(solution)/shard_map/ppermute | solution.py:116
  24.2 0.7 %fusion.4.u_ref = f32[256,128]{1,0:T(8,128)} fusion(f32[256,128]{1,0:T(8,128)S(1)} %collective-permute-done.3, f32[256,128]{1,0:T(8,128)S(1)} %collective-permute-done.2, f32[256,128]{1,0:T(8,128)S(1)} %collective-permute-done.1, f32[4,256,128]{2,1,0:T(8,128)S(1)} %maximum_add_fusion, s32[]{:T(128)S(6)} %select_n.126), kind=kLoop, calls=%fused_computation.9 | loop fusion | flops 98304 | bytes 655364 | tf_op jit(solution)/shard_map/add | solution.py:116
  24.9 2.5 %shard_map.86 = (f32[256,128]{1,0:T(8,128)}, f32[256,128]{1,0:T(8,128)}, f32[256,128]{1,0:T(8,128)}, f32[256,128]{1,0:T(8,128)}, f32[256,128]{1,0:T(8,128)}, /*index=5*/f32[8,128]{1,0:T(8,128)}) custom-call(f32[256,128]{1,0:T(8,128)} %get-tuple-element.27.a_ref, f32[256,128]{1,0:T(8,128)} %fusion.4.u_ref, f32[256,128]{1,0:T(8,128)} %get-tuple-element.15.g_ref, ...), custom_call_target="tpu_custom_call" | custom-call | flops 1310720 | bytes 1179648 | tf_op jit(solution)/shard_map/pallas_call | solution.py:63
  27.4 0.8 %collective-permute-start.4 = (f32[1,8,128]{2,1,0:T(8,128)}, f32[1,8,128]{2,1,0:T(8,128)S(1)}, u32[]{:S(2)}, u32[]{:S(2)}) collective-permute-start(f32[1,8,128]{2,1,0:T(8,128)} %bitcast.39), channel_id=1, source_target_pairs={{0,8},{8,0},{16,24},{24,16},{32,40},{40,32},{48,56},{56,48},{64,72... | collective-permute-start | bytes 12296 | tf_op jit(solution)/shard_map/ppermute | solution.py:126
  28.2 3.0 %collective-permute-done.4 = f32[1,8,128]{2,1,0:T(8,128)S(1)} collective-permute-done((f32[1,8,128]{2,1,0:T(8,128)}, f32[1,8,128]{2,1,0:T(8,128)S(1)}, u32[]{:S(2)}, u32[]{:S(2)}) %collective-permute-start.4) | collective-permute-done | bytes 4128 | tf_op jit(solution)/shard_map/ppermute | solution.py:126
  31.2 0.8 %maximum_select_fusion.4 = f32[2,8,128]{2,1,0:T(8,128)S(1)} fusion(f32[1,8,128]{2,1,0:T(8,128)S(1)} %collective-permute-done.4, f32[1,8,128]{2,1,0:T(8,128)} %bitcast.40, pred[]{:T(512)S(6)} %eq.47), kind=kLoop, calls=%fused_computation.26 | loop fusion | flops 6144 | bytes 16385 | tf_op jit(solution)/shard_map/jit(_where)/select_n | solution.py:128
  32.0 2.3 %collective-permute-start.5 = (f32[2,8,128]{2,1,0:T(8,128)S(1)}, f32[2,8,128]{2,1,0:T(8,128)S(1)}, u32[]{:S(2)}, u32[]{:S(2)}) collective-permute-start(f32[2,8,128]{2,1,0:T(8,128)S(1)} %maximum_select_fusion.4), channel_id=1, source_target_pairs={{0,16},{8,24},{16,0},{24,8},{32,48},{40,56},{48,32},{56,40},{64,80... | collective-permute-start | bytes 24584 | tf_op jit(solution)/shard_map/ppermute | solution.py:126
  34.3 2.8 %collective-permute-done.5 = f32[2,8,128]{2,1,0:T(8,128)S(1)} collective-permute-done((f32[2,8,128]{2,1,0:T(8,128)S(1)}, f32[2,8,128]{2,1,0:T(8,128)S(1)}, u32[]{:S(2)}, u32[]{:S(2)}) %collective-permute-start.5) | collective-permute-done | bytes 8224 | tf_op jit(solution)/shard_map/ppermute | solution.py:126
  37.1 1.2 %collective-permute-start.6 = (f32[4,8,128]{2,1,0:T(8,128)S(1)}, f32[4,8,128]{2,1,0:T(8,128)S(1)}, u32[]{:S(2)}, u32[]{:S(2)}) collective-permute-start(f32[4,8,128]{2,1,0:T(8,128)S(1)} %maximum_select_fusion.3), channel_id=1, source_target_pairs={{0,32},{8,40},{16,48},{24,56},{32,0},{40,8},{48,16},{56,24},{64,96... | collective-permute-start | bytes 49160 | tf_op jit(solution)/shard_map/ppermute | solution.py:126
  38.4 2.9 %collective-permute-done.6 = f32[4,8,128]{2,1,0:T(8,128)S(1)} collective-permute-done((f32[4,8,128]{2,1,0:T(8,128)S(1)}, f32[4,8,128]{2,1,0:T(8,128)S(1)}, u32[]{:S(2)}, u32[]{:S(2)}) %collective-permute-start.6) | collective-permute-done | bytes 16416 | tf_op jit(solution)/shard_map/ppermute | solution.py:126
  41.2 2.2 %collective-permute-start.7 = (f32[8,8,128]{2,1,0:T(8,128)S(1)}, f32[8,8,128]{2,1,0:T(8,128)S(1)}, u32[]{:S(2)}, u32[]{:S(2)}) collective-permute-start(f32[8,8,128]{2,1,0:T(8,128)S(1)} %maximum_select_fusion.2), channel_id=1, source_target_pairs={{0,64},{8,72},{16,80},{24,88},{32,96},{40,104},{48,112},{56,120},{... | collective-permute-start | bytes 98312 | tf_op jit(solution)/shard_map/ppermute | solution.py:126
  43.5 2.6 %collective-permute-done.7 = f32[8,8,128]{2,1,0:T(8,128)S(1)} collective-permute-done((f32[8,8,128]{2,1,0:T(8,128)S(1)}, f32[8,8,128]{2,1,0:T(8,128)S(1)}, u32[]{:S(2)}, u32[]{:S(2)}) %collective-permute-start.7) | collective-permute-done | bytes 32800 | tf_op jit(solution)/shard_map/ppermute | solution.py:126
  46.0 6.8 %collective-permute-start.8 = (f32[16,8,128]{2,1,0:T(8,128)S(1)}, f32[16,8,128]{2,1,0:T(8,128)S(1)}, u32[]{:S(2)}, u32[]{:S(2)}) collective-permute-start(f32[16,8,128]{2,1,0:T(8,128)S(1)} %maximum_select_fusion.1), channel_id=1, source_target_pairs={{0,128},{8,136},{16,144},{24,152},{32,160},{40,168},{48,176},{56,1... | collective-permute-start | bytes 196616 | tf_op jit(solution)/shard_map/ppermute | solution.py:126
  52.8 0.6 dynamic-slice_bitcast_fusion.11.init_ref
  53.4 1.7 %collective-permute-done.8 = f32[16,8,128]{2,1,0:T(8,128)S(1)} collective-permute-done((f32[16,8,128]{2,1,0:T(8,128)S(1)}, f32[16,8,128]{2,1,0:T(8,128)S(1)}, u32[]{:S(2)}, u32[]{:S(2)}) %collective-permute-start.8) | collective-permute-done | bytes 65568 | tf_op jit(solution)/shard_map/ppermute | solution.py:126
  55.1 0.7 %maximum_select_fusion.every_ref = f32[32,8,128]{2,1,0:T(8,128)} fusion(f32[16,8,128]{2,1,0:T(8,128)S(1)} %collective-permute-done.8, f32[16,8,128]{2,1,0:T(8,128)S(1)} %maximum_select_fusion.1, pred[]{:T(512)S(6)} %eq.43), kind=kLoop, calls=%fused_computation.6 | loop fusion | flops 98304 | bytes 262145 | tf_op jit(solution)/shard_map/jit(_where)/select_n | solution.py:128
  55.8 2.1 %shard_map.87 = (f32[256,128]{1,0:T(8,128)}, f32[256,128]{1,0:T(8,128)}) custom-call(f32[32,8,128]{2,1,0:T(8,128)} %maximum_select_fusion.every_ref, f32[1,128]{1,0:T(1,128)} %dynamic-slice_bitcast_fusion.11.init_ref, f32[256,128]{1,0:T(8,128)} %get-tuple-element.9.pf_ref, f32[256,128]{1,0:T(8,128)} %get-tuple-element.10.lf_ref, ...), custom_call_target="tpu_custom_call" | custom-call | flops 163840 | bytes 917504 | tf_op jit(solution)/shard_map/pallas_call | solution.py:92
  (12 shorter events, 0.1 us)
Async XLA Ops:
  0.6 52.2 %copy-start = (f32[1024]{0:T(1024)S(1)}, f32[1024]{0:T(1024)}, u32[]{:S(2)}) copy-start(f32[1024]{0:T(1024)} %param.13) | copy-start | bytes 12292
  0.6 2.3 %copy-start.1 = (bf16[256,4096]{1,0:T(8,128)(2,1)S(1)}, bf16[256,4096]{1,0:T(8,128)(2,1)}, u32[]{:S(2)}) copy-start(bf16[256,4096]{1,0:T(8,128)(2,1)} %param.7) | copy-start | bytes 6291460
  10.9 2.0 %collective-permute-start = (f32[4,256,128]{2,1,0:T(8,128)S(1)}, f32[4,256,128]{2,1,0:T(8,128)S(1)}, u32[]{:S(2)}, u32[]{:S(2)}) collective-permute-start(f32[4,256,128]{2,1,0:T(8,128)S(1)} %pad_maximum_fusion), channel_id=1, source_target_pairs={{0,1},{1,0},{2,3},{3,2},{4,5},{5,4},{6,7},{7,6},{8,9},{9,8},{10,11... | collective-permute-start | bytes 1572872 | tf_op jit(solution)/shard_map/ppermute | solution.py:111
  13.0 6.8 %collective-permute-start.1 = (f32[256,128]{1,0:T(8,128)S(1)}, f32[256,128]{1,0:T(8,128)S(1)}, u32[]{:S(2)}, u32[]{:S(2)}) collective-permute-start(f32[256,128]{1,0:T(8,128)S(1)} %get-tuple-element.24), channel_id=1, source_target_pairs={{0,2},{1,3},{2,4},{3,5},{4,6},{5,7},{6,0},{7,1},{8,10},{9,11},{10,... | collective-permute-start | bytes 393224 | tf_op jit(solution)/shard_map/ppermute | solution.py:116
  14.7 7.9 %collective-permute-start.2 = (f32[256,128]{1,0:T(8,128)S(1)}, f32[256,128]{1,0:T(8,128)S(1)}, u32[]{:S(2)}, u32[]{:S(2)}) collective-permute-start(f32[256,128]{1,0:T(8,128)S(1)} %get-tuple-element.26), channel_id=1, source_target_pairs={{0,4},{1,5},{2,6},{3,7},{4,0},{5,1},{6,2},{7,3},{8,12},{9,13},{10,... | collective-permute-start | bytes 393224 | tf_op jit(solution)/shard_map/ppermute | solution.py:116
  17.3 6.9 %collective-permute-start.3 = (f32[256,128]{1,0:T(8,128)S(1)}, f32[256,128]{1,0:T(8,128)S(1)}, u32[]{:S(2)}, u32[]{:S(2)}) collective-permute-start(f32[256,128]{1,0:T(8,128)S(1)} %get-tuple-element.25), channel_id=1, source_target_pairs={{0,6},{1,7},{2,0},{3,1},{4,2},{5,3},{6,4},{7,5},{8,14},{9,15},{10,... | collective-permute-start | bytes 393224 | tf_op jit(solution)/shard_map/ppermute | solution.py:116
  27.4 3.8 %collective-permute-start.4 = (f32[1,8,128]{2,1,0:T(8,128)}, f32[1,8,128]{2,1,0:T(8,128)S(1)}, u32[]{:S(2)}, u32[]{:S(2)}) collective-permute-start(f32[1,8,128]{2,1,0:T(8,128)} %bitcast.39), channel_id=1, source_target_pairs={{0,8},{8,0},{16,24},{24,16},{32,40},{40,32},{48,56},{56,48},{64,72... | collective-permute-start | bytes 12296 | tf_op jit(solution)/shard_map/ppermute | solution.py:126
  32.0 5.2 %collective-permute-start.5 = (f32[2,8,128]{2,1,0:T(8,128)S(1)}, f32[2,8,128]{2,1,0:T(8,128)S(1)}, u32[]{:S(2)}, u32[]{:S(2)}) collective-permute-start(f32[2,8,128]{2,1,0:T(8,128)S(1)} %maximum_select_fusion.4), channel_id=1, source_target_pairs={{0,16},{8,24},{16,0},{24,8},{32,48},{40,56},{48,32},{56,40},{64,80... | collective-permute-start | bytes 24584 | tf_op jit(solution)/shard_map/ppermute | solution.py:126
  37.1 4.1 %collective-permute-start.6 = (f32[4,8,128]{2,1,0:T(8,128)S(1)}, f32[4,8,128]{2,1,0:T(8,128)S(1)}, u32[]{:S(2)}, u32[]{:S(2)}) collective-permute-start(f32[4,8,128]{2,1,0:T(8,128)S(1)} %maximum_select_fusion.3), channel_id=1, source_target_pairs={{0,32},{8,40},{16,48},{24,56},{32,0},{40,8},{48,16},{56,24},{64,96... | collective-permute-start | bytes 49160 | tf_op jit(solution)/shard_map/ppermute | solution.py:126
  41.2 4.8 %collective-permute-start.7 = (f32[8,8,128]{2,1,0:T(8,128)S(1)}, f32[8,8,128]{2,1,0:T(8,128)S(1)}, u32[]{:S(2)}, u32[]{:S(2)}) collective-permute-start(f32[8,8,128]{2,1,0:T(8,128)S(1)} %maximum_select_fusion.2), channel_id=1, source_target_pairs={{0,64},{8,72},{16,80},{24,88},{32,96},{40,104},{48,112},{56,120},{... | collective-permute-start | bytes 98312 | tf_op jit(solution)/shard_map/ppermute | solution.py:126
  46.0 9.0 %collective-permute-start.8 = (f32[16,8,128]{2,1,0:T(8,128)S(1)}, f32[16,8,128]{2,1,0:T(8,128)S(1)}, u32[]{:S(2)}, u32[]{:S(2)}) collective-permute-start(f32[16,8,128]{2,1,0:T(8,128)S(1)} %maximum_select_fusion.1), channel_id=1, source_target_pairs={{0,128},{8,136},{16,144},{24,152},{32,160},{40,168},{48,176},{56,1... | collective-permute-start | bytes 196616 | tf_op jit(solution)/shard_map/ppermute | solution.py:126

commit v5 on v4

--- a/solution.py
+++ b/solution.py
@@ -96,18 +96,56 @@
     )(every, initial, pf, lf, pb, bl, bp)
 
 
-def sensor_reduce_scatter(partial, width):
+def matmul_kernel(core_ref, obs_ref, listed_ref, gain_ref, keep_ref, send_ref, lhs_ref):
+    @pl.when(pl.program_id(0) == 0)
+    def _():
+        for b in range(listed_ref.shape[1]):
+            cols = pl.ds(128 * b, 128)
+            block = obs_ref[:, cols]
+            lhs_ref[:, cols] = jnp.where(listed_ref[:, b:b + 1] > 0, block, jnp.zeros_like(block))
+
+    prod = jnp.dot(lhs_ref[...], gain_ref[...], preferred_element_type=jnp.float32)
+    half = prod.shape[1] // 2
+    even = core_ref[0] == 0
+    keep_ref[0] = jnp.where(even, prod[:, :half], prod[:, half:])
+    send_ref[0] = jnp.where(even, prod[:, half:], prod[:, :half])
+
+
+def listed_matmul(core, observations, listed, gain_rows):
+    rows, depth = observations.shape
+    modes = gain_rows.shape[1]
+    tile = 256
+    tiles = modes // tile
+    piece = jax.ShapeDtypeStruct((tiles, rows, tile // 2), jnp.float32)
+    return pl.pallas_call(
+        matmul_kernel,
+        grid=(tiles,),
+        in_specs=[
+            pl.BlockSpec(memory_space=pltpu.SMEM),
+            pl.BlockSpec((rows, depth), lambda j: (0, 0)),
+            pl.BlockSpec((rows, listed.shape[1]), lambda j: (0, 0)),
+            pl.BlockSpec((depth, tile), lambda j: (0, j)),
+        ],
+        out_specs=[
+            pl.BlockSpec((1, rows, tile // 2), lambda j: (j, 0, 0)),
+            pl.BlockSpec((1, rows, tile // 2), lambda j: (j, 0, 0)),
+        ],
+        out_shape=[piece, piece],
+        scratch_shapes=[pltpu.VMEM((rows, depth), jnp.bfloat16)],
+        compiler_params=pltpu.CompilerParams(dimension_semantics=("arbitrary",)),
+        cost_estimate=pl.CostEstimate(
+            flops=2 * rows * depth * modes,
+            bytes_accessed=2 * rows * depth + 2 * depth * modes + 4 * rows * modes,
+            transcendentals=0,
+        ),
+    )(core, observations, listed, gain_rows)
+
+
+def sensor_reduce_scatter(keep, send):
     count = lax.axis_size("sensor")
     chips = count // 2
     j = lax.axis_index("sensor")
     chip = j // 2
-    core = j % 2
-
-    def piece(index):
-        return lax.dynamic_slice_in_dim(partial, index * width, width, 1)
-
-    send = jnp.stack([piece(2 * c + 1 - core) for c in range(chips)], 0)
-    keep = jnp.stack([piece(2 * c + core) for c in range(chips)], 0)
     chip_sum = keep + lax.ppermute(send, "sensor", [(i, i ^ 1) for i in range(count)])
     total = lax.dynamic_index_in_dim(chip_sum, chip, 0, False)
     for shift in range(1, chips):
@@ -141,14 +179,10 @@
     block_count = observations.shape[1] // 128
     own_blocks = sensor_index * block_count + jnp.arange(block_count, dtype=jnp.int32)
     listed = jnp.any(obs_list[:, :, None] == own_blocks[None, None, :], axis=1).astype(jnp.float32)
-    weighted = (
-        (observations.reshape(rows_here, block_count, 128) * listed[:, :, None])
-        .reshape(rows_here, block_count * 128)
-        .astype(jnp.bfloat16)
-    )
-    partial_sum = jnp.dot(weighted, gain_rows, preferred_element_type=jnp.float32)
+    core = (sensor_index % 2).astype(jnp.int32)[None]
+    keep, send = listed_matmul(core, observations, listed, gain_rows)
     width = gain_rows.shape[1] // sensor_count
-    inflow = sensor_reduce_scatter(partial_sum, width)
+    inflow = sensor_reduce_scatter(keep, send)
     start_col = sensor_index * width
     factors = lax.dynamic_slice_in_dim(decay, start_col, width, 1)
     gains = lax.dynamic_slice_in_dim(smooth_gain, start_col, width, 1)

time: 58.2 us -> 59 us (1.014)
  Pallas kernels: 4.53 us -> 12.7 us
  matrix products: 7.73 us -> 0 us
  other arithmetic: 5.04 us -> 5.9 us
    pallas_call x0 -> x1, Pallas kernels: none -> 8.18 us  [listed_matmul(): pl.pallas_call(matmul_kernel, grid=(tiles,), in_specs=[pl.BlockSpec(memor...]
    dot_general x1 -> x0, matrix products: 7.73 us -> none  [per_device(): jnp.dot(weighted, gain_rows, preferred_element_type=jnp.float32)]
    mul x1 -> x0, local copies, waits for them, and re-layouts: 1.14 us -> none  [per_device(): observations.reshape(rows_here, block_count, 128) * listed[:, :, None]]
    add x1, other arithmetic: 0.05 us -> 1.12 us  [sensor_reduce_scatter(): keep + lax.ppermute(send, 'sensor', [(i, i ^ 1) for i in range(count)])]
    convert_element_type x1, local copies, waits for them, and re-layouts: 0.1 us -> 0.76 us  [per_device(): jnp.any(obs_list[:, :, None] == own_blocks[None, None, :], axis=1)]
where the time goes in v5:
time: 59 us; the launch traced here: 58.5 us
  waiting for transfers between devices  18.6 us (32%)
  starting transfers between devices  18.4 us (31%)
  Pallas kernels  12.7 us (22%)
  other arithmetic  5.9 us (10%)
  local copies, waits for them, and re-layouts  2.21 us (4%)
  between operations  0.69 us (1%)
    ppermute x5, starting transfers between devices, gather_tm(): other = lax.ppermute(held, 'tm', [(i, i ^ step) for i in range(count)])  13.4 us
    ppermute x5, waiting for transfers between devices, gather_tm(): other = lax.ppermute(held, 'tm', [(i, i ^ step) for i in range(count)])  12.9 us
    pallas_call x1, Pallas kernels, listed_matmul(): pl.pallas_call(matmul_kernel, grid=(tiles,), in_specs=[pl.BlockSpec(memor...  8.18 us
    ppermute x3, starting transfers between devices, sensor_reduce_scatter(): total = total + lax.ppermute(part, 'sensor', perm)  5 us
    ppermute x3, waiting for transfers between devices, sensor_reduce_scatter(): total = total + lax.ppermute(part, 'sensor', perm)  4.42 us
    pallas_call x1, Pallas kernels, local_scans(): pl.pallas_call(scan_kernel, out_shape=[shape] * 5 + [jax.ShapeDtypeStruct...  2.43 us
    pallas_call x1, Pallas kernels, combine(): pl.pallas_call(combine_kernel, out_shape=[shape, shape], cost_estimate=pl...  2.08 us
    mul x1, other arithmetic, per_device(): scale = step_gain * rates[None, :]  1.8 us
  transfers between devices with their start and end apart: 9, of which 8 were waited for; matrix products, arithmetic and copies ran while one was open for 5% of the time, Pallas kernels for 0%

profile of v5, /device:TPU:8, one launch (start us, length us, event | category | flops | bytes accessed | tf_op | source)
XLA Modules:
  0.0 58.5 jit_solution(17803730388719207029)
XLA Ops:
  0.6 0.0 copy-start
  0.7 0.9 %compare_reduce_fusion = pred[256,32]{0,1:T(8,128)(4,1)S(1)} fusion(s32[256,16]{0,1:T(8,128)} %param.8, s32[32]{0:T(128)S(1)} %iota_add_fusion), kind=kLoop, calls=%fused_computation | loop fusion | flops 253952 | bytes 24704 | tf_op jit(solution)/shard_map/reduce_or | solution.py:181
  1.5 0.8 %copy.11.listed_ref = f32[256,32]{1,0:T(8,128)} copy(f32[256,32]{0,1:T(8,128)S(1)} %convert_element_type.3) | data formatting | bytes 65536 | tf_op jit(solution)/shard_map/convert_element_type | solution.py:181
  2.3 8.2 %shard_map.86 = (f32[4,256,128]{2,1,0:T(8,128)}, f32[4,256,128]{2,1,0:T(8,128)}) custom-call(s32[1]{0:T(128)} %bitcast.core_ref, bf16[256,4096]{1,0:T(8,128)(2,1)} %obs_ref.1, f32[256,32]{1,0:T(8,128)} %copy.11.listed_ref, bf16[4096,1024]{1,0:T(8,128)(2,1)} %gain_ref.1), custom_call_target="tpu_custom_call" | custom-call | flops 2147483648 | bytes 11534336 | tf_op jit(solution)/shard_map/pallas_call | solution.py:120
  10.5 0.0 collective-permute-start
  10.5 0.8 %dynamic_slice.31 = f32[128]{0:T(128)S(1)} dynamic-slice(f32[1024]{0:T(1024)} %param.12, s32[]{:T(128)S(6)} %select_n.91), dynamic_slice_sizes={128} | dynamic-slice | bytes 1028 | tf_op jit(solution)/shard_map/dynamic_slice | solution.py:189
  11.3 1.4 %collective-permute-done = f32[4,256,128]{2,1,0:T(8,128)S(1)} collective-permute-done((f32[4,256,128]{2,1,0:T(8,128)}, f32[4,256,128]{2,1,0:T(8,128)S(1)}, u32[]{:S(2)}, u32[]{:S(2)}) %collective-permute-start) | collective-permute-done | bytes 524320 | tf_op jit(solution)/shard_map/ppermute | solution.py:149
  12.6 1.1 %add.78 = f32[4,256,128]{2,1,0:T(8,128)S(1)} add(f32[4,256,128]{2,1,0:T(8,128)} %get-tuple-element.10, f32[4,256,128]{2,1,0:T(8,128)S(1)} %collective-permute-done) | non-fusion elementwise | flops 131072 | bytes 1572864 | tf_op jit(solution)/shard_map/add | solution.py:149
  13.8 1.7 %collective-permute-start.1 = (f32[256,128]{1,0:T(8,128)S(1)}, f32[256,128]{1,0:T(8,128)S(1)}, u32[]{:S(2)}, u32[]{:S(2)}) collective-permute-start(f32[256,128]{1,0:T(8,128)S(1)} %get-tuple-element.20), channel_id=1, source_target_pairs={{0,2},{1,3},{2,4},{3,5},{4,6},{5,7},{6,0},{7,1},{8,10},{9,11},{10,... | collective-permute-start | bytes 393224 | tf_op jit(solution)/shard_map/ppermute | solution.py:154
  15.4 2.6 %collective-permute-start.2 = (f32[256,128]{1,0:T(8,128)S(1)}, f32[256,128]{1,0:T(8,128)S(1)}, u32[]{:S(2)}, u32[]{:S(2)}) collective-permute-start(f32[256,128]{1,0:T(8,128)S(1)} %get-tuple-element.22), channel_id=1, source_target_pairs={{0,4},{1,5},{2,6},{3,7},{4,0},{5,1},{6,2},{7,3},{8,12},{9,13},{10,... | collective-permute-start | bytes 393224 | tf_op jit(solution)/shard_map/ppermute | solution.py:154
  18.1 0.7 %collective-permute-start.3 = (f32[256,128]{1,0:T(8,128)S(1)}, f32[256,128]{1,0:T(8,128)S(1)}, u32[]{:S(2)}, u32[]{:S(2)}) collective-permute-start(f32[256,128]{1,0:T(8,128)S(1)} %get-tuple-element.21), channel_id=1, source_target_pairs={{0,6},{1,7},{2,0},{3,1},{4,2},{5,3},{6,4},{7,5},{8,14},{9,15},{10,... | collective-permute-start | bytes 393224 | tf_op jit(solution)/shard_map/ppermute | solution.py:154
  18.8 1.8 %broadcast_multiply_fusion = (f32[256,128]{1,0:T(8,128)}, f32[256,128]{1,0:T(8,128)}, f32[256,128]{1,0:T(8,128)}) fusion(f32[128]{0:T(128)S(1)} %dynamic_slice.31, f32[256,1024]{1,0:T(8,128)} %param.11, s32[]{:T(128)S(6)} %select_n.91, pred[256]{0:T(512)(128)(4,1)S(1)} %add_compare_fusion, f32[256,1024]{1,0:T(8,128)} %param.10), kind=kLoop, calls=%fused_computation.10 | loop fusion | flops 65536 | bytes 656132 | tf_op jit(solution)/shard_map/mul | solution.py:194
  20.6 0.0 collective-permute-done.1
  20.6 2.7 %collective-permute-done.2 = f32[256,128]{1,0:T(8,128)S(1)} collective-permute-done((f32[256,128]{1,0:T(8,128)S(1)}, f32[256,128]{1,0:T(8,128)S(1)}, u32[]{:S(2)}, u32[]{:S(2)}) %collective-permute-start.2) | collective-permute-done | bytes 131104 | tf_op jit(solution)/shard_map/ppermute | solution.py:154
  23.3 1.7 %collective-permute-done.3 = f32[256,128]{1,0:T(8,128)S(1)} collective-permute-done((f32[256,128]{1,0:T(8,128)S(1)}, f32[256,128]{1,0:T(8,128)S(1)}, u32[]{:S(2)}, u32[]{:S(2)}) %collective-permute-start.3) | collective-permute-done | bytes 131104 | tf_op jit(solution)/shard_map/ppermute | solution.py:154
  25.0 0.7 %fusion.1.u_ref = f32[256,128]{1,0:T(8,128)} fusion(f32[256,128]{1,0:T(8,128)S(1)} %collective-permute-done.3, f32[256,128]{1,0:T(8,128)S(1)} %collective-permute-done.2, f32[256,128]{1,0:T(8,128)S(1)} %collective-permute-done.1, f32[4,256,128]{2,1,0:T(8,128)S(1)} %add.78, s32[]{:T(128)S(6)} %select_n.94), kind=kLoop, calls=%fused_computation.4 | loop fusion | flops 98304 | bytes 655364 | tf_op jit(solution)/shard_map/add | solution.py:154
  25.7 2.4 %shard_map.87 = (f32[256,128]{1,0:T(8,128)}, f32[256,128]{1,0:T(8,128)}, f32[256,128]{1,0:T(8,128)}, f32[256,128]{1,0:T(8,128)}, f32[256,128]{1,0:T(8,128)}, /*index=5*/f32[8,128]{1,0:T(8,128)}) custom-call(f32[256,128]{1,0:T(8,128)} %get-tuple-element.23.a_ref, f32[256,128]{1,0:T(8,128)} %fusion.1.u_ref, f32[256,128]{1,0:T(8,128)} %get-tuple-element.19.g_ref, ...), custom_call_target="tpu_custom_call" | custom-call | flops 1310720 | bytes 1179648 | tf_op jit(solution)/shard_map/pallas_call | solution.py:63
  28.1 0.8 %collective-permute-start.4 = (f32[1,8,128]{2,1,0:T(8,128)}, f32[1,8,128]{2,1,0:T(8,128)S(1)}, u32[]{:S(2)}, u32[]{:S(2)}) collective-permute-start(f32[1,8,128]{2,1,0:T(8,128)} %bitcast.16), channel_id=1, source_target_pairs={{0,8},{8,0},{16,24},{24,16},{32,40},{40,32},{48,56},{56,48},{64,72... | collective-permute-start | bytes 12296 | tf_op jit(solution)/shard_map/ppermute | solution.py:164
  28.9 3.0 %collective-permute-done.4 = f32[1,8,128]{2,1,0:T(8,128)S(1)} collective-permute-done((f32[1,8,128]{2,1,0:T(8,128)}, f32[1,8,128]{2,1,0:T(8,128)S(1)}, u32[]{:S(2)}, u32[]{:S(2)}) %collective-permute-start.4) | collective-permute-done | bytes 4128 | tf_op jit(solution)/shard_map/ppermute | solution.py:164
  31.9 0.8 %maximum_select_fusion.4 = f32[2,8,128]{2,1,0:T(8,128)S(1)} fusion(f32[1,8,128]{2,1,0:T(8,128)S(1)} %collective-permute-done.4, f32[1,8,128]{2,1,0:T(8,128)} %bitcast.17, pred[]{:T(512)S(6)} %eq.47), kind=kLoop, calls=%fused_computation.13 | loop fusion | flops 6144 | bytes 16385 | tf_op jit(solution)/shard_map/jit(_where)/select_n | solution.py:166
  32.7 2.3 %collective-permute-start.5 = (f32[2,8,128]{2,1,0:T(8,128)S(1)}, f32[2,8,128]{2,1,0:T(8,128)S(1)}, u32[]{:S(2)}, u32[]{:S(2)}) collective-permute-start(f32[2,8,128]{2,1,0:T(8,128)S(1)} %maximum_select_fusion.4), channel_id=1, source_target_pairs={{0,16},{8,24},{16,0},{24,8},{32,48},{40,56},{48,32},{56,40},{64,80... | collective-permute-start | bytes 24584 | tf_op jit(solution)/shard_map/ppermute | solution.py:164
  35.0 2.8 %collective-permute-done.5 = f32[2,8,128]{2,1,0:T(8,128)S(1)} collective-permute-done((f32[2,8,128]{2,1,0:T(8,128)S(1)}, f32[2,8,128]{2,1,0:T(8,128)S(1)}, u32[]{:S(2)}, u32[]{:S(2)}) %collective-permute-start.5) | collective-permute-done | bytes 8224 | tf_op jit(solution)/shard_map/ppermute | solution.py:164
  37.8 1.2 %collective-permute-start.6 = (f32[4,8,128]{2,1,0:T(8,128)S(1)}, f32[4,8,128]{2,1,0:T(8,128)S(1)}, u32[]{:S(2)}, u32[]{:S(2)}) collective-permute-start(f32[4,8,128]{2,1,0:T(8,128)S(1)} %maximum_select_fusion.3), channel_id=1, source_target_pairs={{0,32},{8,40},{16,48},{24,56},{32,0},{40,8},{48,16},{56,24},{64,96... | collective-permute-start | bytes 49160 | tf_op jit(solution)/shard_map/ppermute | solution.py:164
  39.1 2.9 %collective-permute-done.6 = f32[4,8,128]{2,1,0:T(8,128)S(1)} collective-permute-done((f32[4,8,128]{2,1,0:T(8,128)S(1)}, f32[4,8,128]{2,1,0:T(8,128)S(1)}, u32[]{:S(2)}, u32[]{:S(2)}) %collective-permute-start.6) | collective-permute-done | bytes 16416 | tf_op jit(solution)/shard_map/ppermute | solution.py:164
  41.9 2.2 %collective-permute-start.7 = (f32[8,8,128]{2,1,0:T(8,128)S(1)}, f32[8,8,128]{2,1,0:T(8,128)S(1)}, u32[]{:S(2)}, u32[]{:S(2)}) collective-permute-start(f32[8,8,128]{2,1,0:T(8,128)S(1)} %maximum_select_fusion.2), channel_id=1, source_target_pairs={{0,64},{8,72},{16,80},{24,88},{32,96},{40,104},{48,112},{56,120},{... | collective-permute-start | bytes 98312 | tf_op jit(solution)/shard_map/ppermute | solution.py:164
  44.2 2.6 %collective-permute-done.7 = f32[8,8,128]{2,1,0:T(8,128)S(1)} collective-permute-done((f32[8,8,128]{2,1,0:T(8,128)S(1)}, f32[8,8,128]{2,1,0:T(8,128)S(1)}, u32[]{:S(2)}, u32[]{:S(2)}) %collective-permute-start.7) | collective-permute-done | bytes 32800 | tf_op jit(solution)/shard_map/ppermute | solution.py:164
  46.8 6.8 %collective-permute-start.8 = (f32[16,8,128]{2,1,0:T(8,128)S(1)}, f32[16,8,128]{2,1,0:T(8,128)S(1)}, u32[]{:S(2)}, u32[]{:S(2)}) collective-permute-start(f32[16,8,128]{2,1,0:T(8,128)S(1)} %maximum_select_fusion.1), channel_id=1, source_target_pairs={{0,128},{8,136},{16,144},{24,152},{32,160},{40,168},{48,176},{56,1... | collective-permute-start | bytes 196616 | tf_op jit(solution)/shard_map/ppermute | solution.py:164
  53.6 0.0 copy-done
  53.6 0.6 %dynamic-slice_bitcast_fusion.3.init_ref = f32[1,128]{1,0:T(1,128)} fusion(f32[1024]{0:T(1024)S(1)} %copy-done, s32[]{:T(128)S(6)} %select_n.91), kind=kLoop, calls=%fused_computation.16 | loop fusion | bytes 1028 | tf_op jit(solution)/shard_map/broadcast_in_dim | solution.py:201
  54.2 1.6 %collective-permute-done.8 = f32[16,8,128]{2,1,0:T(8,128)S(1)} collective-permute-done((f32[16,8,128]{2,1,0:T(8,128)S(1)}, f32[16,8,128]{2,1,0:T(8,128)S(1)}, u32[]{:S(2)}, u32[]{:S(2)}) %collective-permute-start.8) | collective-permute-done | bytes 65568 | tf_op jit(solution)/shard_map/ppermute | solution.py:164
  55.8 0.7 %maximum_select_fusion.every_ref = f32[32,8,128]{2,1,0:T(8,128)} fusion(f32[16,8,128]{2,1,0:T(8,128)S(1)} %collective-permute-done.8, f32[16,8,128]{2,1,0:T(8,128)S(1)} %maximum_select_fusion.1, pred[]{:T(512)S(6)} %eq.43), kind=kLoop, calls=%fused_computation.1 | loop fusion | flops 98304 | bytes 262145 | tf_op jit(solution)/shard_map/jit(_where)/select_n | solution.py:166
  56.5 2.1 %shard_map.88 = (f32[256,128]{1,0:T(8,128)}, f32[256,128]{1,0:T(8,128)}) custom-call(f32[32,8,128]{2,1,0:T(8,128)} %maximum_select_fusion.every_ref, f32[1,128]{1,0:T(1,128)} %dynamic-slice_bitcast_fusion.3.init_ref, f32[256,128]{1,0:T(8,128)} %get-tuple-element.13.pf_ref, f32[256,128]{1,0:T(8,128)} %get-tuple-element.14.lf_ref, ...), custom_call_target="tpu_custom_call" | custom-call | flops 163840 | bytes 917504 | tf_op jit(solution)/shard_map/pallas_call | solution.py:92
  (7 shorter events, 0.1 us)
Async XLA Ops:
  0.6 52.9 %copy-start = (f32[1024]{0:T(1024)S(1)}, f32[1024]{0:T(1024)}, u32[]{:S(2)}) copy-start(f32[1024]{0:T(1024)} %param.13) | copy-start | bytes 12292
  10.5 2.1 %collective-permute-start = (f32[4,256,128]{2,1,0:T(8,128)}, f32[4,256,128]{2,1,0:T(8,128)S(1)}, u32[]{:S(2)}, u32[]{:S(2)}) collective-permute-start(f32[4,256,128]{2,1,0:T(8,128)} %get-tuple-element.11), channel_id=1, source_target_pairs={{0,1},{1,0},{2,3},{3,2},{4,5},{5,4},{6,7},{7,6},{8,9},{9,8},{10,11... | collective-permute-start | bytes 1572872 | tf_op jit(solution)/shard_map/ppermute | solution.py:149
  13.8 6.8 %collective-permute-start.1 = (f32[256,128]{1,0:T(8,128)S(1)}, f32[256,128]{1,0:T(8,128)S(1)}, u32[]{:S(2)}, u32[]{:S(2)}) collective-permute-start(f32[256,128]{1,0:T(8,128)S(1)} %get-tuple-element.20), channel_id=1, source_target_pairs={{0,2},{1,3},{2,4},{3,5},{4,6},{5,7},{6,0},{7,1},{8,10},{9,11},{10,... | collective-permute-start | bytes 393224 | tf_op jit(solution)/shard_map/ppermute | solution.py:154
  15.4 7.9 %collective-permute-start.2 = (f32[256,128]{1,0:T(8,128)S(1)}, f32[256,128]{1,0:T(8,128)S(1)}, u32[]{:S(2)}, u32[]{:S(2)}) collective-permute-start(f32[256,128]{1,0:T(8,128)S(1)} %get-tuple-element.22), channel_id=1, source_target_pairs={{0,4},{1,5},{2,6},{3,7},{4,0},{5,1},{6,2},{7,3},{8,12},{9,13},{10,... | collective-permute-start | bytes 393224 | tf_op jit(solution)/shard_map/ppermute | solution.py:154
  18.1 6.9 %collective-permute-start.3 = (f32[256,128]{1,0:T(8,128)S(1)}, f32[256,128]{1,0:T(8,128)S(1)}, u32[]{:S(2)}, u32[]{:S(2)}) collective-permute-start(f32[256,128]{1,0:T(8,128)S(1)} %get-tuple-element.21), channel_id=1, source_target_pairs={{0,6},{1,7},{2,0},{3,1},{4,2},{5,3},{6,4},{7,5},{8,14},{9,15},{10,... | collective-permute-start | bytes 393224 | tf_op jit(solution)/shard_map/ppermute | solution.py:154
  28.1 3.8 %collective-permute-start.4 = (f32[1,8,128]{2,1,0:T(8,128)}, f32[1,8,128]{2,1,0:T(8,128)S(1)}, u32[]{:S(2)}, u32[]{:S(2)}) collective-permute-start(f32[1,8,128]{2,1,0:T(8,128)} %bitcast.16), channel_id=1, source_target_pairs={{0,8},{8,0},{16,24},{24,16},{32,40},{40,32},{48,56},{56,48},{64,72... | collective-permute-start | bytes 12296 | tf_op jit(solution)/shard_map/ppermute | solution.py:164
  32.7 5.2 %collective-permute-start.5 = (f32[2,8,128]{2,1,0:T(8,128)S(1)}, f32[2,8,128]{2,1,0:T(8,128)S(1)}, u32[]{:S(2)}, u32[]{:S(2)}) collective-permute-start(f32[2,8,128]{2,1,0:T(8,128)S(1)} %maximum_select_fusion.4), channel_id=1, source_target_pairs={{0,16},{8,24},{16,0},{24,8},{32,48},{40,56},{48,32},{56,40},{64,80... | collective-permute-start | bytes 24584 | tf_op jit(solution)/shard_map/ppermute | solution.py:164
  37.8 4.1 %collective-permute-start.6 = (f32[4,8,128]{2,1,0:T(8,128)S(1)}, f32[4,8,128]{2,1,0:T(8,128)S(1)}, u32[]{:S(2)}, u32[]{:S(2)}) collective-permute-start(f32[4,8,128]{2,1,0:T(8,128)S(1)} %maximum_select_fusion.3), channel_id=1, source_target_pairs={{0,32},{8,40},{16,48},{24,56},{32,0},{40,8},{48,16},{56,24},{64,96... | collective-permute-start | bytes 49160 | tf_op jit(solution)/shard_map/ppermute | solution.py:164
  41.9 4.8 %collective-permute-start.7 = (f32[8,8,128]{2,1,0:T(8,128)S(1)}, f32[8,8,128]{2,1,0:T(8,128)S(1)}, u32[]{:S(2)}, u32[]{:S(2)}) collective-permute-start(f32[8,8,128]{2,1,0:T(8,128)S(1)} %maximum_select_fusion.2), channel_id=1, source_target_pairs={{0,64},{8,72},{16,80},{24,88},{32,96},{40,104},{48,112},{56,120},{... | collective-permute-start | bytes 98312 | tf_op jit(solution)/shard_map/ppermute | solution.py:164
  46.8 9.0 %collective-permute-start.8 = (f32[16,8,128]{2,1,0:T(8,128)S(1)}, f32[16,8,128]{2,1,0:T(8,128)S(1)}, u32[]{:S(2)}, u32[]{:S(2)}) collective-permute-start(f32[16,8,128]{2,1,0:T(8,128)S(1)} %maximum_select_fusion.1), channel_id=1, source_target_pairs={{0,128},{8,136},{16,144},{24,152},{32,160},{40,168},{48,176},{56,1... | collective-permute-start | bytes 196616 | tf_op jit(solution)/shard_map/ppermute | solution.py:164

commit v6 on v5

--- a/solution.py
+++ b/solution.py
@@ -157,17 +157,8 @@
 
 def gather_tm(x):
     count = lax.axis_size("tm")
-    place = lax.axis_index("tm")
-    held = x[None]
-    step = 1
-    while step < count:
-        other = lax.ppermute(held, "tm", [(i, i ^ step) for i in range(count)])
-        low = (place & step) == 0
-        held = jnp.where(
-            low, jnp.concatenate([held, other], 0), jnp.concatenate([other, held], 0)
-        )
-        step *= 2
-    return held
+    copies = jnp.broadcast_to(x[None], (count,) + x.shape)
+    return lax.all_to_all(copies, "tm", 0, 0, tiled=True)
 
 
 def per_device(observations, obs_list, gain_rows, decay, smooth_gain, model_rate, first_state):

time: 59 us -> 53.8 us (0.912)
  waiting for transfers between devices: 18.6 us -> 15.6 us
  starting transfers between devices: 18.4 us -> 15.6 us
  local copies, waits for them, and re-layouts: 2.21 us -> 4.19 us
  other arithmetic: 5.9 us -> 4.48 us
    ppermute x5 -> x0, starting transfers between devices: 13.4 us -> none  [gather_tm(): other = lax.ppermute(held, 'tm', [(i, i ^ step) for i in range(count)])]
    ppermute x5 -> x0, waiting for transfers between devices: 12.9 us -> none  [gather_tm(): other = lax.ppermute(held, 'tm', [(i, i ^ step) for i in range(count)])]
    all_to_all x0 -> x1, starting transfers between devices: none -> 10.6 us  [gather_tm(): return lax.all_to_all(copies, 'tm', 0, 0, tiled=True)]
    all_to_all x0 -> x1, waiting for transfers between devices: none -> 9.88 us  [gather_tm(): return lax.all_to_all(copies, 'tm', 0, 0, tiled=True)]
    select_n x5 -> x0, other arithmetic: 1.42 us -> none  [gather_tm(): jnp.where(low, jnp.concatenate([held, other], 0), jnp.concatenate([other,...]
    broadcast_in_dim x0 -> x1, local copies, waits for them, and re-layouts: none -> 1.34 us  [gather_tm(): copies = jnp.broadcast_to(x[None], (count,) + x.shape)]
    unnamed x2 -> x4, local copies, waits for them, and re-layouts: 0.01 us -> 0.66 us
  transfers between devices with their start and end apart: 9 -> 5, of which waited for: 8 -> 4; matrix products, arithmetic and copies ran while one was open for 5% -> 6% of each run, Pallas kernels for 0% -> 0%
where the time goes in v6:
time: 53.8 us; the launch traced here: 53.4 us
  starting transfers between devices  15.6 us (29%)
  waiting for transfers between devices  15.6 us (29%)
  Pallas kernels  12.7 us (24%)
  other arithmetic  4.48 us (8%)
  local copies, waits for them, and re-layouts  4.19 us (8%)
  between operations  0.7 us (1%)
    all_to_all x1, starting transfers between devices, gather_tm(): return lax.all_to_all(copies, 'tm', 0, 0, tiled=True)  10.6 us
    all_to_all x1, waiting for transfers between devices, gather_tm(): return lax.all_to_all(copies, 'tm', 0, 0, tiled=True)  9.88 us
    pallas_call x1, Pallas kernels, listed_matmul(): pl.pallas_call(matmul_kernel, grid=(tiles,), in_specs=[pl.BlockSpec(memor...  8.19 us
    ppermute x3, starting transfers between devices, sensor_reduce_scatter(): total = total + lax.ppermute(part, 'sensor', perm)  5 us
    ppermute x3, waiting for transfers between devices, sensor_reduce_scatter(): total = total + lax.ppermute(part, 'sensor', perm)  4.41 us
    pallas_call x1, Pallas kernels, local_scans(): pl.pallas_call(scan_kernel, out_shape=[shape] * 5 + [jax.ShapeDtypeStruct...  2.44 us
    pallas_call x1, Pallas kernels, combine(): pl.pallas_call(combine_kernel, out_shape=[shape, shape], cost_estimate=pl...  2.08 us
    mul x1, other arithmetic, per_device(): scale = step_gain * rates[None, :]  1.81 us
  transfers between devices with their start and end apart: 5, of which 4 were waited for; matrix products, arithmetic and copies ran while one was open for 6% of the time, Pallas kernels for 0%

profile of v6, /device:TPU:8, one launch (start us, length us, event | category | flops | bytes accessed | tf_op | source)
XLA Modules:
  0.0 53.4 jit_solution(4192217623862887217)
XLA Ops:
  0.6 0.0 copy-start
  0.7 0.9 %compare_reduce_fusion = pred[256,32]{0,1:T(8,128)(4,1)S(1)} fusion(s32[256,16]{0,1:T(8,128)} %param.8, s32[32]{0:T(128)S(1)} %iota_add_fusion), kind=kLoop, calls=%fused_computation | loop fusion | flops 253952 | bytes 24704 | tf_op jit(solution)/shard_map/reduce_or | solution.py:172
  1.5 0.8 %copy.11.listed_ref = f32[256,32]{1,0:T(8,128)} copy(f32[256,32]{0,1:T(8,128)S(1)} %convert_element_type.3) | data formatting | bytes 65536 | tf_op jit(solution)/shard_map/convert_element_type | solution.py:172
  2.3 8.2 %shard_map.86 = (f32[4,256,128]{2,1,0:T(8,128)}, f32[4,256,128]{2,1,0:T(8,128)}) custom-call(s32[1]{0:T(128)} %bitcast.core_ref, bf16[256,4096]{1,0:T(8,128)(2,1)} %obs_ref.1, f32[256,32]{1,0:T(8,128)} %copy.11.listed_ref, bf16[4096,1024]{1,0:T(8,128)(2,1)} %gain_ref.1), custom_call_target="tpu_custom_call" | custom-call | flops 2147483648 | bytes 11534336 | tf_op jit(solution)/shard_map/pallas_call | solution.py:120
  10.5 0.0 collective-permute-start
  10.5 0.8 %dynamic_slice.31 = f32[128]{0:T(128)S(1)} dynamic-slice(f32[1024]{0:T(1024)} %param.12, s32[]{:T(128)S(6)} %select_n.46), dynamic_slice_sizes={128} | dynamic-slice | bytes 1028 | tf_op jit(solution)/shard_map/dynamic_slice | solution.py:180
  11.3 1.4 %collective-permute-done = f32[4,256,128]{2,1,0:T(8,128)S(1)} collective-permute-done((f32[4,256,128]{2,1,0:T(8,128)}, f32[4,256,128]{2,1,0:T(8,128)S(1)}, u32[]{:S(2)}, u32[]{:S(2)}) %collective-permute-start) | collective-permute-done | bytes 524320 | tf_op jit(solution)/shard_map/ppermute | solution.py:149
  12.6 1.1 %add.78 = f32[4,256,128]{2,1,0:T(8,128)S(1)} add(f32[4,256,128]{2,1,0:T(8,128)} %get-tuple-element.10, f32[4,256,128]{2,1,0:T(8,128)S(1)} %collective-permute-done) | non-fusion elementwise | flops 131072 | bytes 1572864 | tf_op jit(solution)/shard_map/add | solution.py:149
  13.8 1.7 %collective-permute-start.1 = (f32[256,128]{1,0:T(8,128)S(1)}, f32[256,128]{1,0:T(8,128)S(1)}, u32[]{:S(2)}, u32[]{:S(2)}) collective-permute-start(f32[256,128]{1,0:T(8,128)S(1)} %get-tuple-element.20), channel_id=1, source_target_pairs={{0,2},{1,3},{2,4},{3,5},{4,6},{5,7},{6,0},{7,1},{8,10},{9,11},{10,... | collective-permute-start | bytes 393224 | tf_op jit(solution)/shard_map/ppermute | solution.py:154
  15.4 2.6 %collective-permute-start.2 = (f32[256,128]{1,0:T(8,128)S(1)}, f32[256,128]{1,0:T(8,128)S(1)}, u32[]{:S(2)}, u32[]{:S(2)}) collective-permute-start(f32[256,128]{1,0:T(8,128)S(1)} %get-tuple-element.22), channel_id=1, source_target_pairs={{0,4},{1,5},{2,6},{3,7},{4,0},{5,1},{6,2},{7,3},{8,12},{9,13},{10,... | collective-permute-start | bytes 393224 | tf_op jit(solution)/shard_map/ppermute | solution.py:154
  18.1 0.7 %collective-permute-start.3 = (f32[256,128]{1,0:T(8,128)S(1)}, f32[256,128]{1,0:T(8,128)S(1)}, u32[]{:S(2)}, u32[]{:S(2)}) collective-permute-start(f32[256,128]{1,0:T(8,128)S(1)} %get-tuple-element.21), channel_id=1, source_target_pairs={{0,6},{1,7},{2,0},{3,1},{4,2},{5,3},{6,4},{7,5},{8,14},{9,15},{10,... | collective-permute-start | bytes 393224 | tf_op jit(solution)/shard_map/ppermute | solution.py:154
  18.8 1.8 %broadcast_multiply_fusion = (f32[256,128]{1,0:T(8,128)}, f32[256,128]{1,0:T(8,128)}, f32[256,128]{1,0:T(8,128)}) fusion(f32[128]{0:T(128)S(1)} %dynamic_slice.31, f32[256,1024]{1,0:T(8,128)} %param.11, s32[]{:T(128)S(6)} %select_n.46, pred[256]{0:T(512)(128)(4,1)S(1)} %add_compare_fusion, f32[256,1024]{1,0:T(8,128)} %param.10), kind=kLoop, calls=%fused_computation.8 | loop fusion | flops 65536 | bytes 656132 | tf_op jit(solution)/shard_map/mul | solution.py:185
  20.6 0.0 collective-permute-done.1
  20.6 2.7 %collective-permute-done.2 = f32[256,128]{1,0:T(8,128)S(1)} collective-permute-done((f32[256,128]{1,0:T(8,128)S(1)}, f32[256,128]{1,0:T(8,128)S(1)}, u32[]{:S(2)}, u32[]{:S(2)}) %collective-permute-start.2) | collective-permute-done | bytes 131104 | tf_op jit(solution)/shard_map/ppermute | solution.py:154
  23.3 1.7 %collective-permute-done.3 = f32[256,128]{1,0:T(8,128)S(1)} collective-permute-done((f32[256,128]{1,0:T(8,128)S(1)}, f32[256,128]{1,0:T(8,128)S(1)}, u32[]{:S(2)}, u32[]{:S(2)}) %collective-permute-start.3) | collective-permute-done | bytes 131104 | tf_op jit(solution)/shard_map/ppermute | solution.py:154
  25.0 0.7 %fusion.1.u_ref = f32[256,128]{1,0:T(8,128)} fusion(f32[256,128]{1,0:T(8,128)S(1)} %collective-permute-done.3, f32[256,128]{1,0:T(8,128)S(1)} %collective-permute-done.2, f32[256,128]{1,0:T(8,128)S(1)} %collective-permute-done.1, f32[4,256,128]{2,1,0:T(8,128)S(1)} %add.78, s32[]{:T(128)S(6)} %select_n.49), kind=kLoop, calls=%fused_computation.3 | loop fusion | flops 98304 | bytes 655364 | tf_op jit(solution)/shard_map/add | solution.py:154
  25.7 2.4 %shard_map.87 = (f32[256,128]{1,0:T(8,128)}, f32[256,128]{1,0:T(8,128)}, f32[256,128]{1,0:T(8,128)}, f32[256,128]{1,0:T(8,128)}, f32[256,128]{1,0:T(8,128)}, /*index=5*/f32[8,128]{1,0:T(8,128)}) custom-call(f32[256,128]{1,0:T(8,128)} %get-tuple-element.23.a_ref, f32[256,128]{1,0:T(8,128)} %fusion.1.u_ref, f32[256,128]{1,0:T(8,128)} %get-tuple-element.19.g_ref, ...), custom_call_target="tpu_custom_call" | custom-call | flops 1310720 | bytes 1179648 | tf_op jit(solution)/shard_map/pallas_call | solution.py:63
  28.1 1.3 %broadcast_in_dim.31 = f32[32,8,128]{2,1,0:T(8,128)} broadcast(f32[8,128]{1,0:T(8,128)} %get-tuple-element.12), dimensions={1,2} | broadcast | bytes 135168 | tf_op jit(solution)/shard_map/broadcast_in_dim | solution.py:160
  29.5 10.6 %all-to-all-start = ((f32[32,8,128]{2,1,0:T(8,128)}), f32[32,8,128]{2,1,0:T(8,128)S(1)}, u32[]{:S(2)}, u32[]{:S(2)}) async-start(f32[32,8,128]{2,1,0:T(8,128)} %broadcast_in_dim.31), calls=%async_computation | async-start | bytes 262144 | tf_op jit(solution)/shard_map/all_to_all | solution.py:161
  40.1 0.0 copy-done
  40.1 0.7 %dynamic-slice_bitcast_fusion.3.init_ref = f32[1,128]{1,0:T(1,128)} fusion(f32[1024]{0:T(1024)S(1)} %copy-done, s32[]{:T(128)S(6)} %select_n.46), kind=kLoop, calls=%fused_computation.11 | loop fusion | bytes 1028 | tf_op jit(solution)/shard_map/broadcast_in_dim | solution.py:192
  40.8 9.9 %all-to-all-done.every_ref = f32[32,8,128]{2,1,0:T(8,128)S(1)} async-done(((f32[32,8,128]{2,1,0:T(8,128)}), f32[32,8,128]{2,1,0:T(8,128)S(1)}, u32[]{:S(2)}, u32[]{:S(2)}) %all-to-all-start) | async-done | bytes 131104 | tf_op jit(solution)/shard_map/all_to_all | solution.py:161
  50.6 0.0 copy-start.1
  50.6 0.6 %copy-done.1 = f32[32,8,128]{2,1,0:T(8,128)} copy-done((f32[32,8,128]{2,1,0:T(8,128)}, f32[32,8,128]{2,1,0:T(8,128)S(1)}, u32[]{:S(2)}) %copy-start.1) | copy-done | bytes 131096
  51.3 2.1 %shard_map.88 = (f32[256,128]{1,0:T(8,128)}, f32[256,128]{1,0:T(8,128)}) custom-call(f32[32,8,128]{2,1,0:T(8,128)} %copy-done.1, f32[1,128]{1,0:T(1,128)} %dynamic-slice_bitcast_fusion.3.init_ref, f32[256,128]{1,0:T(8,128)} %get-tuple-element.13.pf_ref, f32[256,128]{1,0:T(8,128)} %get-tuple-element.14.lf_ref, f32[256,128]{1,0:T(8,128)} %get-tuple-element.15.pb_ref, ...), custom_call_target="tpu_custom_call" | custom-call | flops 163840 | bytes 917504 | tf_op jit(solution)/shard_map/pallas_call | solution.py:92
  (4 shorter events, 0.1 us)
Async XLA Ops:
  0.6 39.5 %copy-start = (f32[1024]{0:T(1024)S(1)}, f32[1024]{0:T(1024)}, u32[]{:S(2)}) copy-start(f32[1024]{0:T(1024)} %param.13) | copy-start | bytes 12292
  10.5 2.1 %collective-permute-start = (f32[4,256,128]{2,1,0:T(8,128)}, f32[4,256,128]{2,1,0:T(8,128)S(1)}, u32[]{:S(2)}, u32[]{:S(2)}) collective-permute-start(f32[4,256,128]{2,1,0:T(8,128)} %get-tuple-element.11), channel_id=1, source_target_pairs={{0,1},{1,0},{2,3},{3,2},{4,5},{5,4},{6,7},{7,6},{8,9},{9,8},{10,11... | collective-permute-start | bytes 1572872 | tf_op jit(solution)/shard_map/ppermute | solution.py:149
  13.8 6.8 %collective-permute-start.1 = (f32[256,128]{1,0:T(8,128)S(1)}, f32[256,128]{1,0:T(8,128)S(1)}, u32[]{:S(2)}, u32[]{:S(2)}) collective-permute-start(f32[256,128]{1,0:T(8,128)S(1)} %get-tuple-element.20), channel_id=1, source_target_pairs={{0,2},{1,3},{2,4},{3,5},{4,6},{5,7},{6,0},{7,1},{8,10},{9,11},{10,... | collective-permute-start | bytes 393224 | tf_op jit(solution)/shard_map/ppermute | solution.py:154
  15.4 7.9 %collective-permute-start.2 = (f32[256,128]{1,0:T(8,128)S(1)}, f32[256,128]{1,0:T(8,128)S(1)}, u32[]{:S(2)}, u32[]{:S(2)}) collective-permute-start(f32[256,128]{1,0:T(8,128)S(1)} %get-tuple-element.22), channel_id=1, source_target_pairs={{0,4},{1,5},{2,6},{3,7},{4,0},{5,1},{6,2},{7,3},{8,12},{9,13},{10,... | collective-permute-start | bytes 393224 | tf_op jit(solution)/shard_map/ppermute | solution.py:154
  18.1 6.9 %collective-permute-start.3 = (f32[256,128]{1,0:T(8,128)S(1)}, f32[256,128]{1,0:T(8,128)S(1)}, u32[]{:S(2)}, u32[]{:S(2)}) collective-permute-start(f32[256,128]{1,0:T(8,128)S(1)} %get-tuple-element.21), channel_id=1, source_target_pairs={{0,6},{1,7},{2,0},{3,1},{4,2},{5,3},{6,4},{7,5},{8,14},{9,15},{10,... | collective-permute-start | bytes 393224 | tf_op jit(solution)/shard_map/ppermute | solution.py:154
  29.5 21.2 %all-to-all-start = ((f32[32,8,128]{2,1,0:T(8,128)}), f32[32,8,128]{2,1,0:T(8,128)S(1)}, u32[]{:S(2)}, u32[]{:S(2)}) async-start(f32[32,8,128]{2,1,0:T(8,128)} %broadcast_in_dim.31), calls=%async_computation | async-start | bytes 262144 | tf_op jit(solution)/shard_map/all_to_all | solution.py:161
  50.6 0.7 %copy-start.1 = (f32[32,8,128]{2,1,0:T(8,128)}, f32[32,8,128]{2,1,0:T(8,128)S(1)}, u32[]{:S(2)}) copy-start(f32[32,8,128]{2,1,0:T(8,128)S(1)} %all-to-all-done.every_ref) | copy-start | bytes 393220

commit v7 on v6

--- a/solution.py
+++ b/solution.py
@@ -40,31 +40,35 @@
         carry_x = [jnp.broadcast_to(v[edge:edge + 1], v.shape) for v in cx]
 
 
-def scan_kernel(a_ref, u_ref, g_ref, s_ref, pf_ref, lf_ref, pb_ref, bl_ref, bp_ref, sum_ref):
+def scan_kernel(a_ref, own_ref, r1_ref, r2_ref, r3_ref, g_ref, s_ref, pf_ref, lf_ref, pb_ref, bl_ref,
+                bp_ref, sum_ref):
     rows = a_ref.shape[0]
-    a, (u,) = _chunk_scan(a_ref[...], [u_ref[...]], rows, False)
+    inflow = ((own_ref[...] + r1_ref[...]) + r2_ref[...]) + r3_ref[...]
+    a, (u,) = _chunk_scan(a_ref[...], [inflow], rows, False)
     _carry(a, [u], pf_ref, [lf_ref], rows, False)
     scale = s_ref[...]
     lf = lf_ref[...]
     pf = pf_ref[...]
     g, (ol, op) = _chunk_scan(g_ref[...], [lf - scale * lf, pf - scale * pf], rows, True)
     _carry(g, [ol, op], pb_ref, [bl_ref, bp_ref], rows, True)
-    sum_ref[...] = jnp.zeros_like(sum_ref)
-    sum_ref[0:1, :] = pf_ref[rows - 1:rows, :]
-    sum_ref[1:2, :] = lf_ref[rows - 1:rows, :]
-    sum_ref[2:3, :] = pb_ref[0:1, :]
-    sum_ref[3:4, :] = bl_ref[0:1, :]
-    sum_ref[4:5, :] = bp_ref[0:1, :]
-
-
-def local_scans(factors, inflow, step_gain, scale):
+    sub = lax.broadcasted_iota(jnp.int32, (SUB, pf_ref.shape[1]), 0)
+    tile = jnp.zeros((SUB, pf_ref.shape[1]), jnp.float32)
+    for row, value in enumerate(
+        [pf_ref[rows - 1:rows, :], lf_ref[rows - 1:rows, :], pb_ref[0:1, :], bl_ref[0:1, :], bp_ref[0:1, :]]
+    ):
+        tile = jnp.where(sub == row, jnp.broadcast_to(value, tile.shape), tile)
+    for k in range(sum_ref.shape[0]):
+        sum_ref[k] = tile
+
+
+def local_scans(factors, parts, step_gain, scale, blocks):
     shape = jax.ShapeDtypeStruct(factors.shape, jnp.float32)
     rows, cols = factors.shape
     return pl.pallas_call(
         scan_kernel,
-        out_shape=[shape] * 5 + [jax.ShapeDtypeStruct((SUB, cols), jnp.float32)],
-        cost_estimate=pl.CostEstimate(flops=40 * rows * cols, bytes_accessed=36 * rows * cols, transcendentals=0),
-    )(factors, inflow, step_gain, scale)
+        out_shape=[shape] * 5 + [jax.ShapeDtypeStruct((blocks, SUB, cols), jnp.float32)],
+        cost_estimate=pl.CostEstimate(flops=40 * rows * cols, bytes_accessed=48 * rows * cols, transcendentals=0),
+    )(factors, *parts, step_gain, scale)
 
 
 def combine_kernel(every_ref, init_ref, pf_ref, lf_ref, pb_ref, bl_ref, bp_ref, f_ref, s_ref):
@@ -147,17 +151,15 @@
     j = lax.axis_index("sensor")
     chip = j // 2
     chip_sum = keep + lax.ppermute(send, "sensor", [(i, i ^ 1) for i in range(count)])
-    total = lax.dynamic_index_in_dim(chip_sum, chip, 0, False)
+    parts = [lax.dynamic_index_in_dim(chip_sum, chip, 0, False)]
     for shift in range(1, chips):
         part = lax.dynamic_index_in_dim(chip_sum, (chip + shift) % chips, 0, False)
         perm = [(i, (((i // 2) + shift) % chips) * 2 + i % 2) for i in range(count)]
-        total = total + lax.ppermute(part, "sensor", perm)
-    return total
-
-
-def gather_tm(x):
-    count = lax.axis_size("tm")
-    copies = jnp.broadcast_to(x[None], (count,) + x.shape)
+        parts.append(lax.ppermute(part, "sensor", perm))
+    return parts
+
+
+def gather_tm(copies):
     return lax.all_to_all(copies, "tm", 0, 0, tiled=True)
 
 
@@ -173,7 +175,7 @@
     core = (sensor_index % 2).astype(jnp.int32)[None]
     keep, send = listed_matmul(core, observations, listed, gain_rows)
     width = gain_rows.shape[1] // sensor_count
-    inflow = sensor_reduce_scatter(keep, send)
+    parts = sensor_reduce_scatter(keep, send)
     start_col = sensor_index * width
     factors = lax.dynamic_slice_in_dim(decay, start_col, width, 1)
     gains = lax.dynamic_slice_in_dim(smooth_gain, start_col, width, 1)
@@ -185,7 +187,7 @@
     scale = step_gain * rates[None, :]
 
     prod_fwd, local_fwd, prod_back, back_local, back_prod, summary = local_scans(
-        factors, inflow, step_gain, scale
+        factors, parts, step_gain, scale, time_count
     )
     every = gather_tm(summary)
     filtered, smoothed = combine(

time: 53.8 us -> 53.2 us (0.989)
  local copies, waits for them, and re-layouts: 4.19 us -> 5.44 us
  waiting for transfers between devices: 15.6 us -> 14.5 us
  other arithmetic: 4.48 us -> 3.78 us
    broadcast_in_dim x1 -> x0, local copies, waits for them, and re-layouts: 1.34 us -> none  [gather_tm(): copies = jnp.broadcast_to(x[None], (count,) + x.shape)]
    add x1 -> x0, other arithmetic: 0.68 us -> none  [sensor_reduce_scatter(): total = total + lax.ppermute(part, 'sensor', perm)]
    dynamic_slice x0 -> x1, local copies, waits for them, and re-layouts: none -> 0.67 us  [per_device(): factors = lax.dynamic_slice_in_dim(decay, start_col, width, 1)]
    squeeze x1, local copies, waits for them, and re-layouts: 0.03 us -> 0.7 us  [sensor_reduce_scatter(): part = lax.dynamic_index_in_dim(chip_sum, (chip + shift) % chips, 0, False)]
    unnamed x4 -> x10, local copies, waits for them, and re-layouts: 0.66 us -> 1.31 us
    broadcast_in_dim x1, local copies, waits for them, and re-layouts: 0.65 us -> 1.25 us  [per_device(): initial[None, :]]
    ppermute x3, waiting for transfers between devices: 4.41 us -> 3.82 us  [sensor_reduce_scatter(): parts.append(lax.ppermute(part, 'sensor', perm))]
    all_to_all x1, waiting for transfers between devices: 9.88 us -> 9.29 us  [gather_tm(): return lax.all_to_all(copies, 'tm', 0, 0, tiled=True)]
  transfers between devices with their start and end apart: 5 -> 5, of which waited for: 4 -> 4; matrix products, arithmetic and copies ran while one was open for 6% -> 8% of each run, Pallas kernels for 0% -> 0%
where the time goes in v7:
time: 53.2 us; the launch traced here: 52.8 us
  starting transfers between devices  15.5 us (29%)
  waiting for transfers between devices  14.5 us (27%)
  Pallas kernels  12.9 us (24%)
  local copies, waits for them, and re-layouts  5.44 us (10%)
  other arithmetic  3.78 us (7%)
  between operations  0.69 us (1%)
    all_to_all x1, starting transfers between devices, gather_tm(): return lax.all_to_all(copies, 'tm', 0, 0, tiled=True)  10.5 us
    all_to_all x1, waiting for transfers between devices, gather_tm(): return lax.all_to_all(copies, 'tm', 0, 0, tiled=True)  9.29 us
    pallas_call x1, Pallas kernels, listed_matmul(): pl.pallas_call(matmul_kernel, grid=(tiles,), in_specs=[pl.BlockSpec(memor...  8.19 us
    ppermute x3, starting transfers between devices, sensor_reduce_scatter(): parts.append(lax.ppermute(part, 'sensor', perm))  4.93 us
    ppermute x3, waiting for transfers between devices, sensor_reduce_scatter(): parts.append(lax.ppermute(part, 'sensor', perm))  3.82 us
    pallas_call x1, Pallas kernels, local_scans(): pl.pallas_call(scan_kernel, out_shape=[shape] * 5 + [jax.ShapeDtypeStruct...  2.67 us
    pallas_call x1, Pallas kernels, combine(): pl.pallas_call(combine_kernel, out_shape=[shape, shape], cost_estimate=pl...  2.08 us
    mul x1, other arithmetic, per_device(): scale = step_gain * rates[None, :]  1.72 us
  transfers between devices with their start and end apart: 5, of which 4 were waited for; matrix products, arithmetic and copies ran while one was open for 8% of the time, Pallas kernels for 0%

profile of v7, /device:TPU:8, one launch (start us, length us, event | category | flops | bytes accessed | tf_op | source)
XLA Modules:
  0.0 52.8 jit_solution(15469502108444834876)
XLA Ops:
  0.6 0.0 copy-start
  0.7 0.9 %compare_reduce_fusion = pred[256,32]{0,1:T(8,128)(4,1)S(1)} fusion(s32[256,16]{0,1:T(8,128)} %param.8, s32[32]{0:T(128)S(1)} %iota_add_fusion), kind=kLoop, calls=%fused_computation | loop fusion | flops 253952 | bytes 24704 | tf_op jit(solution)/shard_map/reduce_or | solution.py:174
  1.6 0.8 %copy.11.listed_ref = f32[256,32]{1,0:T(8,128)} copy(f32[256,32]{0,1:T(8,128)S(1)} %convert_element_type.3) | data formatting | bytes 65536 | tf_op jit(solution)/shard_map/convert_element_type | solution.py:174
  2.4 8.2 %shard_map.86 = (f32[4,256,128]{2,1,0:T(8,128)}, f32[4,256,128]{2,1,0:T(8,128)}) custom-call(s32[1]{0:T(128)} %bitcast.core_ref, bf16[256,4096]{1,0:T(8,128)(2,1)} %obs_ref.1, f32[256,32]{1,0:T(8,128)} %copy.11.listed_ref, bf16[4096,1024]{1,0:T(8,128)(2,1)} %gain_ref.1), custom_call_target="tpu_custom_call" | custom-call | flops 2147483648 | bytes 11534336 | tf_op jit(solution)/shard_map/pallas_call | solution.py:124
  10.6 0.0 collective-permute-start
  10.6 0.8 %dynamic_slice.31 = f32[128]{0:T(128)S(1)} dynamic-slice(f32[1024]{0:T(1024)} %param.12, s32[]{:T(128)S(6)} %select_n.46), dynamic_slice_sizes={128} | dynamic-slice | bytes 1028 | tf_op jit(solution)/shard_map/dynamic_slice | solution.py:182
  11.3 1.4 %collective-permute-done = f32[4,256,128]{2,1,0:T(8,128)S(1)} collective-permute-done((f32[4,256,128]{2,1,0:T(8,128)}, f32[4,256,128]{2,1,0:T(8,128)S(1)}, u32[]{:S(2)}, u32[]{:S(2)}) %collective-permute-start) | collective-permute-done | bytes 524320 | tf_op jit(solution)/shard_map/ppermute | solution.py:153
  12.7 1.1 %add.69 = f32[4,256,128]{2,1,0:T(8,128)S(1)} add(f32[4,256,128]{2,1,0:T(8,128)} %get-tuple-element.10, f32[4,256,128]{2,1,0:T(8,128)S(1)} %collective-permute-done) | non-fusion elementwise | flops 131072 | bytes 1572864 | tf_op jit(solution)/shard_map/add | solution.py:153
  13.8 0.7 %dynamic-slice_bitcast_fusion = (f32[256,128]{1,0:T(8,128)S(1)}, f32[256,128]{1,0:T(8,128)S(1)}, f32[256,128]{1,0:T(8,128)S(1)}, f32[256,128]{1,0:T(8,128)}) fusion(f32[4,256,128]{2,1,0:T(8,128)S(1)} %add.69, s32[]{:T(128)S(6)} %select_n.55, s32[]{:T(128)S(6)} %select_n.53, s32[]{:T(128)S(6)} %select_n.51, s32[]{:T(128)S(6)} %select_n.49), kind=kLoop, calls=%fused_computation.2 | loop fusion | bytes 1048592 | tf_op jit(solution)/shard_map/jit(dynamic_index_in_dim)/squeeze | solution.py:156
  14.5 1.6 %collective-permute-start.1 = (f32[256,128]{1,0:T(8,128)S(1)}, f32[256,128]{1,0:T(8,128)S(1)}, u32[]{:S(2)}, u32[]{:S(2)}) collective-permute-start(f32[256,128]{1,0:T(8,128)S(1)} %get-tuple-element.22), channel_id=1, source_target_pairs={{0,2},{1,3},{2,4},{3,5},{4,6},{5,7},{6,0},{7,1},{8,10},{9,11},{10,... | collective-permute-start | bytes 393224 | tf_op jit(solution)/shard_map/ppermute | solution.py:158
  16.1 2.6 %collective-permute-start.2 = (f32[256,128]{1,0:T(8,128)S(1)}, f32[256,128]{1,0:T(8,128)S(1)}, u32[]{:S(2)}, u32[]{:S(2)}) collective-permute-start(f32[256,128]{1,0:T(8,128)S(1)} %get-tuple-element.21), channel_id=1, source_target_pairs={{0,4},{1,5},{2,6},{3,7},{4,0},{5,1},{6,2},{7,3},{8,12},{9,13},{10,... | collective-permute-start | bytes 393224 | tf_op jit(solution)/shard_map/ppermute | solution.py:158
  18.7 0.7 %collective-permute-start.3 = (f32[256,128]{1,0:T(8,128)S(1)}, f32[256,128]{1,0:T(8,128)S(1)}, u32[]{:S(2)}, u32[]{:S(2)}) collective-permute-start(f32[256,128]{1,0:T(8,128)S(1)} %get-tuple-element.20), channel_id=1, source_target_pairs={{0,6},{1,7},{2,0},{3,1},{4,2},{5,3},{6,4},{7,5},{8,14},{9,15},{10,... | collective-permute-start | bytes 393224 | tf_op jit(solution)/shard_map/ppermute | solution.py:158
  19.4 1.7 %broadcast_multiply_fusion = (f32[256,128]{1,0:T(8,128)}, f32[256,128]{1,0:T(8,128)}) fusion(f32[128]{0:T(128)S(1)} %dynamic_slice.31, f32[256,1024]{1,0:T(8,128)} %param.11, s32[]{:T(128)S(6)} %select_n.46, pred[256]{0:T(512)(128)(4,1)S(1)} %add_compare_fusion), kind=kLoop, calls=%fused_computation.6 | loop fusion | flops 65536 | bytes 393988 | tf_op jit(solution)/shard_map/mul | solution.py:187
  21.1 0.0 copy-done
  21.2 0.7 %constant_dynamic-slice_fusion.a_ref = f32[256,128]{1,0:T(8,128)} fusion(f32[256,1024]{1,0:T(8,128)S(1)} %copy-done, s32[]{:T(128)S(6)} %select_n.46), kind=kLoop, calls=%fused_computation.7 | loop fusion | bytes 262148 | tf_op jit(solution)/shard_map/dynamic_slice | solution.py:180
  21.8 0.0 collective-permute-done.1.r1_ref
  21.8 0.0 copy-start.2
  21.8 2.1 %collective-permute-done.2.r2_ref = f32[256,128]{1,0:T(8,128)S(1)} collective-permute-done((f32[256,128]{1,0:T(8,128)S(1)}, f32[256,128]{1,0:T(8,128)S(1)}, u32[]{:S(2)}, u32[]{:S(2)}) %collective-permute-start.2) | collective-permute-done | bytes 131104 | tf_op jit(solution)/shard_map/ppermute | solution.py:158
  23.9 0.0 copy-start.3
  24.0 1.7 %collective-permute-done.3.r3_ref = f32[256,128]{1,0:T(8,128)S(1)} collective-permute-done((f32[256,128]{1,0:T(8,128)S(1)}, f32[256,128]{1,0:T(8,128)S(1)}, u32[]{:S(2)}, u32[]{:S(2)}) %collective-permute-start.3) | collective-permute-done | bytes 131104 | tf_op jit(solution)/shard_map/ppermute | solution.py:158
  25.6 0.0 copy-start.4
  25.6 0.0 copy-done.2
  25.6 0.0 copy-done.3
  25.7 0.6 %copy-done.4 = f32[256,128]{1,0:T(8,128)} copy-done((f32[256,128]{1,0:T(8,128)}, f32[256,128]{1,0:T(8,128)S(1)}, u32[]{:S(2)}) %copy-start.4) | copy-done | bytes 131096
  26.3 2.7 %shard_map.87 = (f32[256,128]{1,0:T(8,128)}, f32[256,128]{1,0:T(8,128)}, f32[256,128]{1,0:T(8,128)}, f32[256,128]{1,0:T(8,128)}, f32[256,128]{1,0:T(8,128)}, /*index=5*/f32[32,8,128]{2,1,0:T(8,128)}) custom-call(f32[256,128]{1,0:T(8,128)} %constant_dynamic-slice_fusion.a_ref, f32[256,128]{1,0:T(8,128)} %get-tuple-element.23.own_ref, f32[256,128]{1,0:T(8,128)} %copy-done.2, ...), custom_call_target="tpu_custom_call" | custom-call | flops 1310720 | bytes 1572864 | tf_op jit(solution)/shard_map/pallas_call | solution.py:67
  29.0 10.5 %all-to-all-start = ((f32[32,8,128]{2,1,0:T(8,128)}), f32[32,8,128]{2,1,0:T(8,128)S(1)}, u32[]{:S(2)}, u32[]{:S(2)}) async-start(f32[32,8,128]{2,1,0:T(8,128)} %get-tuple-element.12), calls=%async_computation | async-start | bytes 262144 | tf_op jit(solution)/shard_map/all_to_all | solution.py:163
  39.5 1.2 %dynamic-slice_bitcast_fusion.4.init_ref = f32[1,128]{1,0:T(1,128)} fusion(f32[1024]{0:T(1024)} %param.13, s32[]{:T(128)S(6)} %select_n.46), kind=kLoop, calls=%fused_computation.9 | loop fusion | bytes 1028 | tf_op jit(solution)/shard_map/broadcast_in_dim | solution.py:194
  40.7 9.3 %all-to-all-done.every_ref = f32[32,8,128]{2,1,0:T(8,128)S(1)} async-done(((f32[32,8,128]{2,1,0:T(8,128)}), f32[32,8,128]{2,1,0:T(8,128)S(1)}, u32[]{:S(2)}, u32[]{:S(2)}) %all-to-all-start) | async-done | bytes 131104 | tf_op jit(solution)/shard_map/all_to_all | solution.py:163
  50.0 0.0 copy-start.1
  50.0 0.6 %copy-done.1 = f32[32,8,128]{2,1,0:T(8,128)} copy-done((f32[32,8,128]{2,1,0:T(8,128)}, f32[32,8,128]{2,1,0:T(8,128)S(1)}, u32[]{:S(2)}) %copy-start.1) | copy-done | bytes 131096
  50.7 2.1 %shard_map.88 = (f32[256,128]{1,0:T(8,128)}, f32[256,128]{1,0:T(8,128)}) custom-call(f32[32,8,128]{2,1,0:T(8,128)} %copy-done.1, f32[1,128]{1,0:T(1,128)} %dynamic-slice_bitcast_fusion.4.init_ref, f32[256,128]{1,0:T(8,128)} %get-tuple-element.13.pf_ref, f32[256,128]{1,0:T(8,128)} %get-tuple-element.14.lf_ref, f32[256,128]{1,0:T(8,128)} %get-tuple-element.15.pb_ref, ...), custom_call_target="tpu_custom_call" | custom-call | flops 163840 | bytes 917504 | tf_op jit(solution)/shard_map/pallas_call | solution.py:96
  (3 shorter events, 0.0 us)
Async XLA Ops:
  0.6 20.5 %copy-start = (f32[256,1024]{1,0:T(8,128)S(1)}, f32[256,1024]{1,0:T(8,128)}, u32[]{:S(2)}) copy-start(f32[256,1024]{1,0:T(8,128)} %param.10) | copy-start | bytes 3145732
  10.6 2.1 %collective-permute-start = (f32[4,256,128]{2,1,0:T(8,128)}, f32[4,256,128]{2,1,0:T(8,128)S(1)}, u32[]{:S(2)}, u32[]{:S(2)}) collective-permute-start(f32[4,256,128]{2,1,0:T(8,128)} %get-tuple-element.11), channel_id=1, source_target_pairs={{0,1},{1,0},{2,3},{3,2},{4,5},{5,4},{6,7},{7,6},{8,9},{9,8},{10,11... | collective-permute-start | bytes 1572872 | tf_op jit(solution)/shard_map/ppermute | solution.py:153
  14.5 7.3 %collective-permute-start.1 = (f32[256,128]{1,0:T(8,128)S(1)}, f32[256,128]{1,0:T(8,128)S(1)}, u32[]{:S(2)}, u32[]{:S(2)}) collective-permute-start(f32[256,128]{1,0:T(8,128)S(1)} %get-tuple-element.22), channel_id=1, source_target_pairs={{0,2},{1,3},{2,4},{3,5},{4,6},{5,7},{6,0},{7,1},{8,10},{9,11},{10,... | collective-permute-start | bytes 393224 | tf_op jit(solution)/shard_map/ppermute | solution.py:158
  16.1 7.9 %collective-permute-start.2 = (f32[256,128]{1,0:T(8,128)S(1)}, f32[256,128]{1,0:T(8,128)S(1)}, u32[]{:S(2)}, u32[]{:S(2)}) collective-permute-start(f32[256,128]{1,0:T(8,128)S(1)} %get-tuple-element.21), channel_id=1, source_target_pairs={{0,4},{1,5},{2,6},{3,7},{4,0},{5,1},{6,2},{7,3},{8,12},{9,13},{10,... | collective-permute-start | bytes 393224 | tf_op jit(solution)/shard_map/ppermute | solution.py:158
  18.7 6.9 %collective-permute-start.3 = (f32[256,128]{1,0:T(8,128)S(1)}, f32[256,128]{1,0:T(8,128)S(1)}, u32[]{:S(2)}, u32[]{:S(2)}) collective-permute-start(f32[256,128]{1,0:T(8,128)S(1)} %get-tuple-element.20), channel_id=1, source_target_pairs={{0,6},{1,7},{2,0},{3,1},{4,2},{5,3},{6,4},{7,5},{8,14},{9,15},{10,... | collective-permute-start | bytes 393224 | tf_op jit(solution)/shard_map/ppermute | solution.py:158
  21.8 3.8 %copy-start.2 = (f32[256,128]{1,0:T(8,128)}, f32[256,128]{1,0:T(8,128)S(1)}, u32[]{:S(2)}) copy-start(f32[256,128]{1,0:T(8,128)S(1)} %collective-permute-done.1.r1_ref) | copy-start | bytes 393220
  23.9 1.7 %copy-start.3 = (f32[256,128]{1,0:T(8,128)}, f32[256,128]{1,0:T(8,128)S(1)}, u32[]{:S(2)}) copy-start(f32[256,128]{1,0:T(8,128)S(1)} %collective-permute-done.2.r2_ref) | copy-start | bytes 393220
  25.6 0.6 %copy-start.4 = (f32[256,128]{1,0:T(8,128)}, f32[256,128]{1,0:T(8,128)S(1)}, u32[]{:S(2)}) copy-start(f32[256,128]{1,0:T(8,128)S(1)} %collective-permute-done.3.r3_ref) | copy-start | bytes 393220
  29.0 21.1 %all-to-all-start = ((f32[32,8,128]{2,1,0:T(8,128)}), f32[32,8,128]{2,1,0:T(8,128)S(1)}, u32[]{:S(2)}, u32[]{:S(2)}) async-start(f32[32,8,128]{2,1,0:T(8,128)} %get-tuple-element.12), calls=%async_computation | async-start | bytes 262144 | tf_op jit(solution)/shard_map/all_to_all | solution.py:163
  50.0 0.7 %copy-start.1 = (f32[32,8,128]{2,1,0:T(8,128)}, f32[32,8,128]{2,1,0:T(8,128)S(1)}, u32[]{:S(2)}) copy-start(f32[32,8,128]{2,1,0:T(8,128)S(1)} %all-to-all-done.every_ref) | copy-start | bytes 393220

commit v8 on v7

--- a/solution.py
+++ b/solution.py
@@ -145,17 +145,32 @@
     )(core, observations, listed, gain_rows)
 
 
+def chip_sum_kernel(keep_ref, recv_ref, *out_refs):
+    chips = keep_ref.shape[0]
+    chip = lax.axis_index("sensor") // 2
+    for shift, out_ref in enumerate(out_refs):
+        index = (chip + shift) % chips
+        out_ref[...] = keep_ref[index] + recv_ref[index]
+
+
+def chip_sum(keep, recv):
+    chips, rows, cols = keep.shape
+    shape = jax.ShapeDtypeStruct((rows, cols), jnp.float32)
+    return pl.pallas_call(
+        chip_sum_kernel,
+        out_shape=[shape] * chips,
+        cost_estimate=pl.CostEstimate(flops=chips * rows * cols, bytes_accessed=12 * chips * rows * cols, transcendentals=0),
+    )(keep, recv)
+
+
 def sensor_reduce_scatter(keep, send):
     count = lax.axis_size("sensor")
     chips = count // 2
-    j = lax.axis_index("sensor")
-    chip = j // 2
-    chip_sum = keep + lax.ppermute(send, "sensor", [(i, i ^ 1) for i in range(count)])
-    parts = [lax.dynamic_index_in_dim(chip_sum, chip, 0, False)]
+    summed = chip_sum(keep, lax.ppermute(send, "sensor", [(i, i ^ 1) for i in range(count)]))
+    parts = [summed[0]]
     for shift in range(1, chips):
-        part = lax.dynamic_index_in_dim(chip_sum, (chip + shift) % chips, 0, False)
         perm = [(i, (((i // 2) + shift) % chips) * 2 + i % 2) for i in range(count)]
-        parts.append(lax.ppermute(part, "sensor", perm))
+        parts.append(lax.ppermute(summed[shift], "sensor", perm))
     return parts
 
 

time: 53.2 us -> 54.3 us (1.021)
  Pallas kernels: 12.9 us -> 15 us
  waiting for transfers between devices: 14.5 us -> 15.9 us
  local copies, waits for them, and re-layouts: 5.44 us -> 4.21 us
  other arithmetic: 3.78 us -> 2.68 us
    pallas_call x0 -> x1, Pallas kernels: none -> 2.08 us  [chip_sum(): pl.pallas_call(chip_sum_kernel, out_shape=[shape] * chips, cost_estimate=...]
    add x1 -> x0, other arithmetic: 1.1 us -> none  [sensor_reduce_scatter(): keep + lax.ppermute(send, 'sensor', [(i, i ^ 1) for i in range(count)])]
    ppermute x3, waiting for transfers between devices: 3.82 us -> 4.62 us  [sensor_reduce_scatter(): parts.append(lax.ppermute(summed[shift], 'sensor', perm))]
    unnamed x10 -> x12, local copies, waits for them, and re-layouts: 1.31 us -> 2.09 us
    squeeze x1 -> x0, local copies, waits for them, and re-layouts: 0.7 us -> none  [sensor_reduce_scatter(): part = lax.dynamic_index_in_dim(chip_sum, (chip + shift) % chips, 0, False)]
    dynamic_slice x1 -> x0, local copies, waits for them, and re-layouts: 0.67 us -> none  [per_device(): factors = lax.dynamic_slice_in_dim(decay, start_col, width, 1)]
    broadcast_in_dim x1, local copies, waits for them, and re-layouts: 1.25 us -> 0.6 us  [per_device(): initial[None, :]]
    all_to_all x1, waiting for transfers between devices: 9.29 us -> 9.93 us  [gather_tm(): return lax.all_to_all(copies, 'tm', 0, 0, tiled=True)]
  transfers between devices with their start and end apart: 5 -> 5, of which waited for: 4 -> 4; matrix products, arithmetic and copies ran while one was open for 8% -> 6% of each run, Pallas kernels for 0% -> 0%
where the time goes in v8:
time: 54.3 us; the launch traced here: 53.9 us
  waiting for transfers between devices  15.9 us (29%)
  starting transfers between devices  15.5 us (29%)
  Pallas kernels  15 us (28%)
  local copies, waits for them, and re-layouts  4.21 us (8%)
  other arithmetic  2.68 us (5%)
  between operations  0.7 us (1%)
    all_to_all x1, starting transfers between devices, gather_tm(): return lax.all_to_all(copies, 'tm', 0, 0, tiled=True)  10.5 us
    all_to_all x1, waiting for transfers between devices, gather_tm(): return lax.all_to_all(copies, 'tm', 0, 0, tiled=True)  9.93 us
    pallas_call x1, Pallas kernels, listed_matmul(): pl.pallas_call(matmul_kernel, grid=(tiles,), in_specs=[pl.BlockSpec(memor...  8.19 us
    ppermute x3, starting transfers between devices, sensor_reduce_scatter(): parts.append(lax.ppermute(summed[shift], 'sensor', perm))  4.93 us
    ppermute x3, waiting for transfers between devices, sensor_reduce_scatter(): parts.append(lax.ppermute(summed[shift], 'sensor', perm))  4.62 us
    pallas_call x1, Pallas kernels, local_scans(): pl.pallas_call(scan_kernel, out_shape=[shape] * 5 + [jax.ShapeDtypeStruct...  2.65 us
    unnamed x12, local copies, waits for them, and re-layouts  2.09 us
    pallas_call x1, Pallas kernels, combine(): pl.pallas_call(combine_kernel, out_shape=[shape, shape], cost_estimate=pl...  2.08 us
  transfers between devices with their start and end apart: 5, of which 4 were waited for; matrix products, arithmetic and copies ran while one was open for 6% of the time, Pallas kernels for 0%

profile of v8, /device:TPU:8, one launch (start us, length us, event | category | flops | bytes accessed | tf_op | source)
XLA Modules:
  0.0 53.9 jit_solution(18370636986619615881)
XLA Ops:
  0.6 0.0 copy-start
  0.7 0.9 %compare_reduce_fusion = pred[256,32]{0,1:T(8,128)(4,1)S(1)} fusion(s32[256,16]{0,1:T(8,128)} %param.8, s32[32]{0:T(128)S(1)} %iota_add_fusion), kind=kLoop, calls=%fused_computation | loop fusion | flops 253952 | bytes 24704 | tf_op jit(solution)/shard_map/reduce_or | solution.py:189
  1.5 0.8 %copy.11.listed_ref = f32[256,32]{1,0:T(8,128)} copy(f32[256,32]{0,1:T(8,128)S(1)} %convert_element_type.3) | data formatting | bytes 65536 | tf_op jit(solution)/shard_map/convert_element_type | solution.py:189
  2.3 8.2 %shard_map.86 = (f32[4,256,128]{2,1,0:T(8,128)}, f32[4,256,128]{2,1,0:T(8,128)}) custom-call(s32[1]{0:T(128)} %bitcast.core_ref, bf16[256,4096]{1,0:T(8,128)(2,1)} %obs_ref.1, f32[256,32]{1,0:T(8,128)} %copy.11.listed_ref, bf16[4096,1024]{1,0:T(8,128)(2,1)} %gain_ref.1), custom_call_target="tpu_custom_call" | custom-call | flops 2147483648 | bytes 11534336 | tf_op jit(solution)/shard_map/pallas_call | solution.py:124
  10.5 0.0 collective-permute-start
  10.5 0.8 %dynamic_slice.14 = f32[128]{0:T(128)S(1)} dynamic-slice(f32[1024]{0:T(1024)} %param.12, s32[]{:T(128)S(6)} %select_n.17), dynamic_slice_sizes={128} | dynamic-slice | bytes 1028 | tf_op jit(solution)/shard_map/dynamic_slice | solution.py:197
  11.3 1.4 %collective-permute-done.recv_ref = f32[4,256,128]{2,1,0:T(8,128)S(1)} collective-permute-done((f32[4,256,128]{2,1,0:T(8,128)}, f32[4,256,128]{2,1,0:T(8,128)S(1)}, u32[]{:S(2)}, u32[]{:S(2)}) %collective-permute-start) | collective-permute-done | bytes 524320 | tf_op jit(solution)/shard_map/ppermute | solution.py:169
  12.6 0.0 copy-start.1
  12.6 0.8 %copy-done.1 = f32[4,256,128]{2,1,0:T(8,128)} copy-done((f32[4,256,128]{2,1,0:T(8,128)}, f32[4,256,128]{2,1,0:T(8,128)S(1)}, u32[]{:S(2)}) %copy-start.1) | copy-done | bytes 524312
  13.4 2.1 %shard_map.87 = (f32[256,128]{1,0:T(8,128)}, f32[256,128]{1,0:T(8,128)}, f32[256,128]{1,0:T(8,128)}, f32[256,128]{1,0:T(8,128)}) custom-call(f32[4,256,128]{2,1,0:T(8,128)} %get-tuple-element.14.keep_ref, f32[4,256,128]{2,1,0:T(8,128)} %copy-done.1), custom_call_target="tpu_custom_call" | custom-call | flops 131072 | bytes 1572864 | tf_op jit(solution)/shard_map/pallas_call | solution.py:159
  15.5 1.6 %collective-permute-start.1 = (f32[256,128]{1,0:T(8,128)}, f32[256,128]{1,0:T(8,128)S(1)}, u32[]{:S(2)}, u32[]{:S(2)}) collective-permute-start(f32[256,128]{1,0:T(8,128)} %get-tuple-element.17), channel_id=1, source_target_pairs={{0,2},{1,3},{2,4},{3,5},{4,6},{5,7},{6,0},{7,1},{8,10},{9,11},{10,... | collective-permute-start | bytes 393224 | tf_op jit(solution)/shard_map/ppermute | solution.py:173
  17.1 2.6 %collective-permute-start.2 = (f32[256,128]{1,0:T(8,128)}, f32[256,128]{1,0:T(8,128)S(1)}, u32[]{:S(2)}, u32[]{:S(2)}) collective-permute-start(f32[256,128]{1,0:T(8,128)} %get-tuple-element.18), channel_id=1, source_target_pairs={{0,4},{1,5},{2,6},{3,7},{4,0},{5,1},{6,2},{7,3},{8,12},{9,13},{10,... | collective-permute-start | bytes 393224 | tf_op jit(solution)/shard_map/ppermute | solution.py:173
  19.7 0.7 %collective-permute-start.3 = (f32[256,128]{1,0:T(8,128)}, f32[256,128]{1,0:T(8,128)S(1)}, u32[]{:S(2)}, u32[]{:S(2)}) collective-permute-start(f32[256,128]{1,0:T(8,128)} %get-tuple-element.19), channel_id=1, source_target_pairs={{0,6},{1,7},{2,0},{3,1},{4,2},{5,3},{6,4},{7,5},{8,14},{9,15},{10,... | collective-permute-start | bytes 393224 | tf_op jit(solution)/shard_map/ppermute | solution.py:173
  20.4 1.8 %broadcast_multiply_fusion = (f32[256,128]{1,0:T(8,128)}, f32[256,128]{1,0:T(8,128)}, f32[256,128]{1,0:T(8,128)}) fusion(f32[128]{0:T(128)S(1)} %dynamic_slice.14, f32[256,1024]{1,0:T(8,128)} %param.11, s32[]{:T(128)S(6)} %select_n.17, pred[256]{0:T(512)(128)(4,1)S(1)} %add_compare_fusion, f32[256,1024]{1,0:T(8,128)} %param.10), kind=kLoop, calls=%fused_computation.2 | loop fusion | flops 65536 | bytes 656132 | tf_op jit(solution)/shard_map/mul | solution.py:202
  22.2 0.0 collective-permute-done.1.r1_ref
  22.2 0.0 copy-start.3
  22.2 2.9 %collective-permute-done.2.r2_ref = f32[256,128]{1,0:T(8,128)S(1)} collective-permute-done((f32[256,128]{1,0:T(8,128)}, f32[256,128]{1,0:T(8,128)S(1)}, u32[]{:S(2)}, u32[]{:S(2)}) %collective-permute-start.2) | collective-permute-done | bytes 131104 | tf_op jit(solution)/shard_map/ppermute | solution.py:173
  25.1 0.0 copy-start.4
  25.1 1.7 %collective-permute-done.3.r3_ref = f32[256,128]{1,0:T(8,128)S(1)} collective-permute-done((f32[256,128]{1,0:T(8,128)}, f32[256,128]{1,0:T(8,128)S(1)}, u32[]{:S(2)}, u32[]{:S(2)}) %collective-permute-start.3) | collective-permute-done | bytes 131104 | tf_op jit(solution)/shard_map/ppermute | solution.py:173
  26.8 0.0 copy-start.5
  26.8 0.0 copy-done.3
  26.8 0.0 copy-done.4
  26.8 0.6 %copy-done.5 = f32[256,128]{1,0:T(8,128)} copy-done((f32[256,128]{1,0:T(8,128)}, f32[256,128]{1,0:T(8,128)S(1)}, u32[]{:S(2)}) %copy-start.5) | copy-done | bytes 131096
  27.5 2.7 %shard_map.88 = (f32[256,128]{1,0:T(8,128)}, f32[256,128]{1,0:T(8,128)}, f32[256,128]{1,0:T(8,128)}, f32[256,128]{1,0:T(8,128)}, f32[256,128]{1,0:T(8,128)}, /*index=5*/f32[32,8,128]{2,1,0:T(8,128)}) custom-call(f32[256,128]{1,0:T(8,128)} %get-tuple-element.28.a_ref, f32[256,128]{1,0:T(8,128)} %get-tuple-element.16.own_ref, f32[256,128]{1,0:T(8,128)} %copy-done.3, ...), custom_call_target="tpu_custom_call" | custom-call | flops 1310720 | bytes 1572864 | tf_op jit(solution)/shard_map/pallas_call | solution.py:67
  30.1 10.5 %all-to-all-start = ((f32[32,8,128]{2,1,0:T(8,128)}), f32[32,8,128]{2,1,0:T(8,128)S(1)}, u32[]{:S(2)}, u32[]{:S(2)}) async-start(f32[32,8,128]{2,1,0:T(8,128)} %get-tuple-element.20), calls=%async_computation | async-start | bytes 262144 | tf_op jit(solution)/shard_map/all_to_all | solution.py:178
  40.7 0.0 copy-done
  40.7 0.6 %dynamic-slice_bitcast_fusion.init_ref = f32[1,128]{1,0:T(1,128)} fusion(f32[1024]{0:T(1024)S(1)} %copy-done, s32[]{:T(128)S(6)} %select_n.17), kind=kLoop, calls=%fused_computation.4 | loop fusion | bytes 1028 | tf_op jit(solution)/shard_map/broadcast_in_dim | solution.py:209
  41.3 9.9 %all-to-all-done.every_ref = f32[32,8,128]{2,1,0:T(8,128)S(1)} async-done(((f32[32,8,128]{2,1,0:T(8,128)}), f32[32,8,128]{2,1,0:T(8,128)S(1)}, u32[]{:S(2)}, u32[]{:S(2)}) %all-to-all-start) | async-done | bytes 131104 | tf_op jit(solution)/shard_map/all_to_all | solution.py:178
  51.2 0.0 copy-start.2
  51.2 0.6 %copy-done.2 = f32[32,8,128]{2,1,0:T(8,128)} copy-done((f32[32,8,128]{2,1,0:T(8,128)}, f32[32,8,128]{2,1,0:T(8,128)S(1)}, u32[]{:S(2)}) %copy-start.2) | copy-done | bytes 131096
  51.9 2.1 %shard_map.89 = (f32[256,128]{1,0:T(8,128)}, f32[256,128]{1,0:T(8,128)}) custom-call(f32[32,8,128]{2,1,0:T(8,128)} %copy-done.2, f32[1,128]{1,0:T(1,128)} %dynamic-slice_bitcast_fusion.init_ref, f32[256,128]{1,0:T(8,128)} %get-tuple-element.21.pf_ref, f32[256,128]{1,0:T(8,128)} %get-tuple-element.22.lf_ref, f32[256,128]{1,0:T(8,128)} %get-tuple-element.23.pb_ref, ...), custom_call_target="tpu_custom_call" | custom-call | flops 163840 | bytes 917504 | tf_op jit(solution)/shard_map/pallas_call | solution.py:96
  (3 shorter events, 0.0 us)
Async XLA Ops:
  0.6 40.0 %copy-start = (f32[1024]{0:T(1024)S(1)}, f32[1024]{0:T(1024)}, u32[]{:S(2)}) copy-start(f32[1024]{0:T(1024)} %param.13) | copy-start | bytes 12292
  10.5 2.1 %collective-permute-start = (f32[4,256,128]{2,1,0:T(8,128)}, f32[4,256,128]{2,1,0:T(8,128)S(1)}, u32[]{:S(2)}, u32[]{:S(2)}) collective-permute-start(f32[4,256,128]{2,1,0:T(8,128)} %get-tuple-element.15), channel_id=1, source_target_pairs={{0,1},{1,0},{2,3},{3,2},{4,5},{5,4},{6,7},{7,6},{8,9},{9,8},{10,11... | collective-permute-start | bytes 1572872 | tf_op jit(solution)/shard_map/ppermute | solution.py:169
  12.6 0.8 %copy-start.1 = (f32[4,256,128]{2,1,0:T(8,128)}, f32[4,256,128]{2,1,0:T(8,128)S(1)}, u32[]{:S(2)}) copy-start(f32[4,256,128]{2,1,0:T(8,128)S(1)} %collective-permute-done.recv_ref) | copy-start | bytes 1572868
  15.5 6.7 %collective-permute-start.1 = (f32[256,128]{1,0:T(8,128)}, f32[256,128]{1,0:T(8,128)S(1)}, u32[]{:S(2)}, u32[]{:S(2)}) collective-permute-start(f32[256,128]{1,0:T(8,128)} %get-tuple-element.17), channel_id=1, source_target_pairs={{0,2},{1,3},{2,4},{3,5},{4,6},{5,7},{6,0},{7,1},{8,10},{9,11},{10,... | collective-permute-start | bytes 393224 | tf_op jit(solution)/shard_map/ppermute | solution.py:173
  17.1 8.1 %collective-permute-start.2 = (f32[256,128]{1,0:T(8,128)}, f32[256,128]{1,0:T(8,128)S(1)}, u32[]{:S(2)}, u32[]{:S(2)}) collective-permute-start(f32[256,128]{1,0:T(8,128)} %get-tuple-element.18), channel_id=1, source_target_pairs={{0,4},{1,5},{2,6},{3,7},{4,0},{5,1},{6,2},{7,3},{8,12},{9,13},{10,... | collective-permute-start | bytes 393224 | tf_op jit(solution)/shard_map/ppermute | solution.py:173
  19.7 7.1 %collective-permute-start.3 = (f32[256,128]{1,0:T(8,128)}, f32[256,128]{1,0:T(8,128)S(1)}, u32[]{:S(2)}, u32[]{:S(2)}) collective-permute-start(f32[256,128]{1,0:T(8,128)} %get-tuple-element.19), channel_id=1, source_target_pairs={{0,6},{1,7},{2,0},{3,1},{4,2},{5,3},{6,4},{7,5},{8,14},{9,15},{10,... | collective-permute-start | bytes 393224 | tf_op jit(solution)/shard_map/ppermute | solution.py:173
  22.2 4.6 %copy-start.3 = (f32[256,128]{1,0:T(8,128)}, f32[256,128]{1,0:T(8,128)S(1)}, u32[]{:S(2)}) copy-start(f32[256,128]{1,0:T(8,128)S(1)} %collective-permute-done.1.r1_ref) | copy-start | bytes 393220
  25.1 1.7 %copy-start.4 = (f32[256,128]{1,0:T(8,128)}, f32[256,128]{1,0:T(8,128)S(1)}, u32[]{:S(2)}) copy-start(f32[256,128]{1,0:T(8,128)S(1)} %collective-permute-done.2.r2_ref) | copy-start | bytes 393220
  26.8 0.6 %copy-start.5 = (f32[256,128]{1,0:T(8,128)}, f32[256,128]{1,0:T(8,128)S(1)}, u32[]{:S(2)}) copy-start(f32[256,128]{1,0:T(8,128)S(1)} %collective-permute-done.3.r3_ref) | copy-start | bytes 393220
  30.1 21.1 %all-to-all-start = ((f32[32,8,128]{2,1,0:T(8,128)}), f32[32,8,128]{2,1,0:T(8,128)S(1)}, u32[]{:S(2)}, u32[]{:S(2)}) async-start(f32[32,8,128]{2,1,0:T(8,128)} %get-tuple-element.20), calls=%async_computation | async-start | bytes 262144 | tf_op jit(solution)/shard_map/all_to_all | solution.py:178
  51.2 0.7 %copy-start.2 = (f32[32,8,128]{2,1,0:T(8,128)}, f32[32,8,128]{2,1,0:T(8,128)S(1)}, u32[]{:S(2)}) copy-start(f32[32,8,128]{2,1,0:T(8,128)S(1)} %all-to-all-done.every_ref) | copy-start | bytes 393220

commit v9 on v7

--- a/solution.py
+++ b/solution.py
@@ -100,22 +100,32 @@
     )(every, initial, pf, lf, pb, bl, bp)
 
 
-def matmul_kernel(core_ref, obs_ref, listed_ref, gain_ref, keep_ref, send_ref, lhs_ref):
+def matmul_kernel(ids_ref, slots_ref, obs_ref, gain_ref, keep_ref, send_ref, lhs_ref):
+    blocks = obs_ref.shape[1] // 128
+
     @pl.when(pl.program_id(0) == 0)
     def _():
-        for b in range(listed_ref.shape[1]):
+        slots = slots_ref[...]
+        shape = (128, slots.shape[1])
+        block_of = lax.broadcasted_iota(jnp.int32, shape, 0)
+        wanted = jnp.where(block_of < blocks, ids_ref[1] + block_of, -2)
+        listed_t = jnp.zeros(shape, jnp.float32)
+        for s in range(slots.shape[0]):
+            listed_t = jnp.maximum(listed_t, (slots[s:s + 1, :] == wanted).astype(jnp.float32))
+        listed = listed_t.T
+        for b in range(blocks):
             cols = pl.ds(128 * b, 128)
             block = obs_ref[:, cols]
-            lhs_ref[:, cols] = jnp.where(listed_ref[:, b:b + 1] > 0, block, jnp.zeros_like(block))
+            lhs_ref[:, cols] = jnp.where(listed[:, b:b + 1] > 0, block, jnp.zeros_like(block))
 
     prod = jnp.dot(lhs_ref[...], gain_ref[...], preferred_element_type=jnp.float32)
     half = prod.shape[1] // 2
-    even = core_ref[0] == 0
+    even = ids_ref[0] == 0
     keep_ref[0] = jnp.where(even, prod[:, :half], prod[:, half:])
     send_ref[0] = jnp.where(even, prod[:, half:], prod[:, :half])
 
 
-def listed_matmul(core, observations, listed, gain_rows):
+def listed_matmul(ids, slots, observations, gain_rows):
     rows, depth = observations.shape
     modes = gain_rows.shape[1]
     tile = 256
@@ -126,8 +136,8 @@
         grid=(tiles,),
         in_specs=[
             pl.BlockSpec(memory_space=pltpu.SMEM),
+            pl.BlockSpec(slots.shape, lambda j: (0, 0)),
             pl.BlockSpec((rows, depth), lambda j: (0, 0)),
-            pl.BlockSpec((rows, listed.shape[1]), lambda j: (0, 0)),
             pl.BlockSpec((depth, tile), lambda j: (0, j)),
         ],
         out_specs=[
@@ -142,7 +152,7 @@
             bytes_accessed=2 * rows * depth + 2 * depth * modes + 4 * rows * modes,
             transcendentals=0,
         ),
-    )(core, observations, listed, gain_rows)
+    )(ids, slots, observations, gain_rows)
 
 
 def sensor_reduce_scatter(keep, send):
@@ -170,10 +180,8 @@
     time_count = lax.axis_size("tm")
     rows_here = observations.shape[0]
     block_count = observations.shape[1] // 128
-    own_blocks = sensor_index * block_count + jnp.arange(block_count, dtype=jnp.int32)
-    listed = jnp.any(obs_list[:, :, None] == own_blocks[None, None, :], axis=1).astype(jnp.float32)
-    core = (sensor_index % 2).astype(jnp.int32)[None]
-    keep, send = listed_matmul(core, observations, listed, gain_rows)
+    ids = jnp.stack([sensor_index % 2, sensor_index * block_count]).astype(jnp.int32)
+    keep, send = listed_matmul(ids, obs_list.T, observations, gain_rows)
     width = gain_rows.shape[1] // sensor_count
     parts = sensor_reduce_scatter(keep, send)
     start_col = sensor_index * width

time: 53.2 us -> 52.3 us (0.983)
  local copies, waits for them, and re-layouts: 5.44 us -> 4.81 us
    reduce_or x1 -> x0, other arithmetic: 0.94 us -> none  [per_device(): jnp.any(obs_list[:, :, None] == own_blocks[None, None, :], axis=1)]
    convert_element_type x1 -> x0, local copies, waits for them, and re-layouts: 0.76 us -> none  [per_device(): jnp.any(obs_list[:, :, None] == own_blocks[None, None, :], axis=1)]
    another operation x0 -> x1, other arithmetic: none -> 0.67 us  [per_device(): jnp.stack([sensor_index % 2, sensor_index * block_count]).astype(jnp.int32)]
  transfers between devices with their start and end apart: 5 -> 5, of which waited for: 4 -> 4; matrix products, arithmetic and copies ran while one was open for 8% -> 9% of each run, Pallas kernels for 0% -> 0%
where the time goes in v9:
time: 52.3 us; the launch traced here: 51.9 us
  starting transfers between devices  15.5 us (30%)
  waiting for transfers between devices  14.3 us (27%)
  Pallas kernels  13.2 us (25%)
  local copies, waits for them, and re-layouts  4.81 us (9%)
  other arithmetic  3.48 us (7%)
  between operations  0.72 us (1%)
    all_to_all x1, starting transfers between devices, gather_tm(): return lax.all_to_all(copies, 'tm', 0, 0, tiled=True)  10.5 us
    all_to_all x1, waiting for transfers between devices, gather_tm(): return lax.all_to_all(copies, 'tm', 0, 0, tiled=True)  9.19 us
    pallas_call x1, Pallas kernels, listed_matmul(): pl.pallas_call(matmul_kernel, grid=(tiles,), in_specs=[pl.BlockSpec(memor...  8.4 us
    ppermute x3, starting transfers between devices, sensor_reduce_scatter(): parts.append(lax.ppermute(part, 'sensor', perm))  4.92 us
    ppermute x3, waiting for transfers between devices, sensor_reduce_scatter(): parts.append(lax.ppermute(part, 'sensor', perm))  3.83 us
    pallas_call x1, Pallas kernels, local_scans(): pl.pallas_call(scan_kernel, out_shape=[shape] * 5 + [jax.ShapeDtypeStruct...  2.68 us
    pallas_call x1, Pallas kernels, combine(): pl.pallas_call(combine_kernel, out_shape=[shape, shape], cost_estimate=pl...  2.08 us
    mul x1, other arithmetic, per_device(): scale = step_gain * rates[None, :]  1.71 us
  transfers between devices with their start and end apart: 5, of which 4 were waited for; matrix products, arithmetic and copies ran while one was open for 9% of the time, Pallas kernels for 0%

profile of v9, /device:TPU:8, one launch (start us, length us, event | category | flops | bytes accessed | tf_op | source)
XLA Modules:
  0.0 51.9 jit_solution(18239011040708304615)
XLA Ops:
  0.6 0.0 copy-start
  0.7 0.7 %pad_add_fusion.ids_ref = s32[2]{0:T(128)} fusion(s32[1]{0:T(128)} %bitcast.1, s32[1]{0:T(128)} %bitcast), kind=kLoop, calls=%fused_computation.8 | loop fusion | flops 2 | bytes 16 | tf_op jit(solution)/shard_map/stack | solution.py:183
  1.3 8.4 %shard_map.86 = (f32[4,256,128]{2,1,0:T(8,128)}, f32[4,256,128]{2,1,0:T(8,128)}) custom-call(s32[2]{0:T(128)} %pad_add_fusion.ids_ref, s32[16,256]{1,0:T(8,128)} %bitcast.13, bf16[256,4096]{1,0:T(8,128)(2,1)} %obs_ref.1, bf16[4096,1024]{1,0:T(8,128)(2,1)} %gain_ref.1), custom_call_target="tpu_custom_call" | custom-call | flops 2147483648 | bytes 11534336 | tf_op jit(solution)/shard_map/pallas_call | solution.py:134
  9.7 0.0 collective-permute-start
  9.8 0.8 %dynamic_slice.31 = f32[128]{0:T(128)S(1)} dynamic-slice(f32[1024]{0:T(1024)} %param.12, s32[]{:T(128)S(6)} %select_n.46), dynamic_slice_sizes={128} | dynamic-slice | bytes 1028 | tf_op jit(solution)/shard_map/dynamic_slice | solution.py:190
  10.5 1.3 %collective-permute-done = f32[4,256,128]{2,1,0:T(8,128)S(1)} collective-permute-done((f32[4,256,128]{2,1,0:T(8,128)}, f32[4,256,128]{2,1,0:T(8,128)S(1)}, u32[]{:S(2)}, u32[]{:S(2)}) %collective-permute-start) | collective-permute-done | bytes 524320 | tf_op jit(solution)/shard_map/ppermute | solution.py:163
  11.8 1.1 %add.57 = f32[4,256,128]{2,1,0:T(8,128)S(1)} add(f32[4,256,128]{2,1,0:T(8,128)} %get-tuple-element.10, f32[4,256,128]{2,1,0:T(8,128)S(1)} %collective-permute-done) | non-fusion elementwise | flops 131072 | bytes 1572864 | tf_op jit(solution)/shard_map/add | solution.py:163
  12.9 0.7 %dynamic-slice_bitcast_fusion = (f32[256,128]{1,0:T(8,128)S(1)}, f32[256,128]{1,0:T(8,128)S(1)}, f32[256,128]{1,0:T(8,128)S(1)}, f32[256,128]{1,0:T(8,128)}) fusion(f32[4,256,128]{2,1,0:T(8,128)S(1)} %add.57, s32[]{:T(128)S(6)} %select_n.55, s32[]{:T(128)S(6)} %select_n.53, s32[]{:T(128)S(6)} %select_n.51, s32[]{:T(128)S(6)} %select_n.49), kind=kLoop, calls=%fused_computation.1 | loop fusion | bytes 1048592 | tf_op jit(solution)/shard_map/jit(dynamic_index_in_dim)/squeeze | solution.py:166
  13.6 1.6 %collective-permute-start.1 = (f32[256,128]{1,0:T(8,128)S(1)}, f32[256,128]{1,0:T(8,128)S(1)}, u32[]{:S(2)}, u32[]{:S(2)}) collective-permute-start(f32[256,128]{1,0:T(8,128)S(1)} %get-tuple-element.22), channel_id=1, source_target_pairs={{0,2},{1,3},{2,4},{3,5},{4,6},{5,7},{6,0},{7,1},{8,10},{9,11},{10,... | collective-permute-start | bytes 393224 | tf_op jit(solution)/shard_map/ppermute | solution.py:168
  15.2 2.6 %collective-permute-start.2 = (f32[256,128]{1,0:T(8,128)S(1)}, f32[256,128]{1,0:T(8,128)S(1)}, u32[]{:S(2)}, u32[]{:S(2)}) collective-permute-start(f32[256,128]{1,0:T(8,128)S(1)} %get-tuple-element.21), channel_id=1, source_target_pairs={{0,4},{1,5},{2,6},{3,7},{4,0},{5,1},{6,2},{7,3},{8,12},{9,13},{10,... | collective-permute-start | bytes 393224 | tf_op jit(solution)/shard_map/ppermute | solution.py:168
  17.9 0.7 %collective-permute-start.3 = (f32[256,128]{1,0:T(8,128)S(1)}, f32[256,128]{1,0:T(8,128)S(1)}, u32[]{:S(2)}, u32[]{:S(2)}) collective-permute-start(f32[256,128]{1,0:T(8,128)S(1)} %get-tuple-element.20), channel_id=1, source_target_pairs={{0,6},{1,7},{2,0},{3,1},{4,2},{5,3},{6,4},{7,5},{8,14},{9,15},{10,... | collective-permute-start | bytes 393224 | tf_op jit(solution)/shard_map/ppermute | solution.py:168
  18.6 1.7 %broadcast_multiply_fusion = (f32[256,128]{1,0:T(8,128)}, f32[256,128]{1,0:T(8,128)}) fusion(f32[128]{0:T(128)S(1)} %dynamic_slice.31, f32[256,1024]{1,0:T(8,128)} %param.11, s32[]{:T(128)S(6)} %select_n.46, pred[256]{0:T(512)(128)(4,1)S(1)} %add_compare_fusion), kind=kLoop, calls=%fused_computation.5 | loop fusion | flops 65536 | bytes 393988 | tf_op jit(solution)/shard_map/mul | solution.py:195
  20.3 0.0 copy-done
  20.3 0.7 %constant_dynamic-slice_fusion.a_ref = f32[256,128]{1,0:T(8,128)} fusion(f32[256,1024]{1,0:T(8,128)S(1)} %copy-done, s32[]{:T(128)S(6)} %select_n.46), kind=kLoop, calls=%fused_computation.6 | loop fusion | bytes 262148 | tf_op jit(solution)/shard_map/dynamic_slice | solution.py:188
  21.0 0.0 collective-permute-done.1.r1_ref
  21.0 0.0 copy-start.2
  21.0 2.1 %collective-permute-done.2.r2_ref = f32[256,128]{1,0:T(8,128)S(1)} collective-permute-done((f32[256,128]{1,0:T(8,128)S(1)}, f32[256,128]{1,0:T(8,128)S(1)}, u32[]{:S(2)}, u32[]{:S(2)}) %collective-permute-start.2) | collective-permute-done | bytes 131104 | tf_op jit(solution)/shard_map/ppermute | solution.py:168
  23.1 0.0 copy-start.3
  23.1 1.7 %collective-permute-done.3.r3_ref = f32[256,128]{1,0:T(8,128)S(1)} collective-permute-done((f32[256,128]{1,0:T(8,128)S(1)}, f32[256,128]{1,0:T(8,128)S(1)}, u32[]{:S(2)}, u32[]{:S(2)}) %collective-permute-start.3) | collective-permute-done | bytes 131104 | tf_op jit(solution)/shard_map/ppermute | solution.py:168
  24.8 0.0 copy-start.4
  24.8 0.0 copy-done.2
  24.8 0.0 copy-done.3
  24.8 0.6 %copy-done.4 = f32[256,128]{1,0:T(8,128)} copy-done((f32[256,128]{1,0:T(8,128)}, f32[256,128]{1,0:T(8,128)S(1)}, u32[]{:S(2)}) %copy-start.4) | copy-done | bytes 131096
  25.4 2.7 %shard_map.87 = (f32[256,128]{1,0:T(8,128)}, f32[256,128]{1,0:T(8,128)}, f32[256,128]{1,0:T(8,128)}, f32[256,128]{1,0:T(8,128)}, f32[256,128]{1,0:T(8,128)}, /*index=5*/f32[32,8,128]{2,1,0:T(8,128)}) custom-call(f32[256,128]{1,0:T(8,128)} %constant_dynamic-slice_fusion.a_ref, f32[256,128]{1,0:T(8,128)} %get-tuple-element.23.own_ref, f32[256,128]{1,0:T(8,128)} %copy-done.2, ...), custom_call_target="tpu_custom_call" | custom-call | flops 1310720 | bytes 1572864 | tf_op jit(solution)/shard_map/pallas_call | solution.py:67
  28.1 10.5 %all-to-all-start = ((f32[32,8,128]{2,1,0:T(8,128)}), f32[32,8,128]{2,1,0:T(8,128)S(1)}, u32[]{:S(2)}, u32[]{:S(2)}) async-start(f32[32,8,128]{2,1,0:T(8,128)} %get-tuple-element.12), calls=%async_computation | async-start | bytes 262144 | tf_op jit(solution)/shard_map/all_to_all | solution.py:173
  38.7 1.4 %dynamic-slice_bitcast_fusion.4.init_ref = f32[1,128]{1,0:T(1,128)} fusion(f32[1024]{0:T(1024)} %param.13, s32[]{:T(128)S(6)} %select_n.46), kind=kLoop, calls=%fused_computation.9 | loop fusion | bytes 1028 | tf_op jit(solution)/shard_map/broadcast_in_dim | solution.py:202
  40.0 9.2 %all-to-all-done.every_ref = f32[32,8,128]{2,1,0:T(8,128)S(1)} async-done(((f32[32,8,128]{2,1,0:T(8,128)}), f32[32,8,128]{2,1,0:T(8,128)S(1)}, u32[]{:S(2)}, u32[]{:S(2)}) %all-to-all-start) | async-done | bytes 131104 | tf_op jit(solution)/shard_map/all_to_all | solution.py:173
  49.2 0.0 copy-start.1
  49.2 0.7 %copy-done.1 = f32[32,8,128]{2,1,0:T(8,128)} copy-done((f32[32,8,128]{2,1,0:T(8,128)}, f32[32,8,128]{2,1,0:T(8,128)S(1)}, u32[]{:S(2)}) %copy-start.1) | copy-done | bytes 131096
  49.9 2.1 %shard_map.88 = (f32[256,128]{1,0:T(8,128)}, f32[256,128]{1,0:T(8,128)}) custom-call(f32[32,8,128]{2,1,0:T(8,128)} %copy-done.1, f32[1,128]{1,0:T(1,128)} %dynamic-slice_bitcast_fusion.4.init_ref, f32[256,128]{1,0:T(8,128)} %get-tuple-element.13.pf_ref, f32[256,128]{1,0:T(8,128)} %get-tuple-element.14.lf_ref, f32[256,128]{1,0:T(8,128)} %get-tuple-element.15.pb_ref, ...), custom_call_target="tpu_custom_call" | custom-call | flops 163840 | bytes 917504 | tf_op jit(solution)/shard_map/pallas_call | solution.py:96
  (1 shorter events, 0.0 us)
Async XLA Ops:
  0.6 19.7 %copy-start = (f32[256,1024]{1,0:T(8,128)S(1)}, f32[256,1024]{1,0:T(8,128)}, u32[]{:S(2)}) copy-start(f32[256,1024]{1,0:T(8,128)} %param.10) | copy-start | bytes 3145732
  9.7 2.1 %collective-permute-start = (f32[4,256,128]{2,1,0:T(8,128)}, f32[4,256,128]{2,1,0:T(8,128)S(1)}, u32[]{:S(2)}, u32[]{:S(2)}) collective-permute-start(f32[4,256,128]{2,1,0:T(8,128)} %get-tuple-element.11), channel_id=1, source_target_pairs={{0,1},{1,0},{2,3},{3,2},{4,5},{5,4},{6,7},{7,6},{8,9},{9,8},{10,11... | collective-permute-start | bytes 1572872 | tf_op jit(solution)/shard_map/ppermute | solution.py:163
  13.6 7.3 %collective-permute-start.1 = (f32[256,128]{1,0:T(8,128)S(1)}, f32[256,128]{1,0:T(8,128)S(1)}, u32[]{:S(2)}, u32[]{:S(2)}) collective-permute-start(f32[256,128]{1,0:T(8,128)S(1)} %get-tuple-element.22), channel_id=1, source_target_pairs={{0,2},{1,3},{2,4},{3,5},{4,6},{5,7},{6,0},{7,1},{8,10},{9,11},{10,... | collective-permute-start | bytes 393224 | tf_op jit(solution)/shard_map/ppermute | solution.py:168
  15.2 7.9 %collective-permute-start.2 = (f32[256,128]{1,0:T(8,128)S(1)}, f32[256,128]{1,0:T(8,128)S(1)}, u32[]{:S(2)}, u32[]{:S(2)}) collective-permute-start(f32[256,128]{1,0:T(8,128)S(1)} %get-tuple-element.21), channel_id=1, source_target_pairs={{0,4},{1,5},{2,6},{3,7},{4,0},{5,1},{6,2},{7,3},{8,12},{9,13},{10,... | collective-permute-start | bytes 393224 | tf_op jit(solution)/shard_map/ppermute | solution.py:168
  17.9 6.9 %collective-permute-start.3 = (f32[256,128]{1,0:T(8,128)S(1)}, f32[256,128]{1,0:T(8,128)S(1)}, u32[]{:S(2)}, u32[]{:S(2)}) collective-permute-start(f32[256,128]{1,0:T(8,128)S(1)} %get-tuple-element.20), channel_id=1, source_target_pairs={{0,6},{1,7},{2,0},{3,1},{4,2},{5,3},{6,4},{7,5},{8,14},{9,15},{10,... | collective-permute-start | bytes 393224 | tf_op jit(solution)/shard_map/ppermute | solution.py:168
  21.0 3.8 %copy-start.2 = (f32[256,128]{1,0:T(8,128)}, f32[256,128]{1,0:T(8,128)S(1)}, u32[]{:S(2)}) copy-start(f32[256,128]{1,0:T(8,128)S(1)} %collective-permute-done.1.r1_ref) | copy-start | bytes 393220
  23.1 1.7 %copy-start.3 = (f32[256,128]{1,0:T(8,128)}, f32[256,128]{1,0:T(8,128)S(1)}, u32[]{:S(2)}) copy-start(f32[256,128]{1,0:T(8,128)S(1)} %collective-permute-done.2.r2_ref) | copy-start | bytes 393220
  24.8 0.7 %copy-start.4 = (f32[256,128]{1,0:T(8,128)}, f32[256,128]{1,0:T(8,128)S(1)}, u32[]{:S(2)}) copy-start(f32[256,128]{1,0:T(8,128)S(1)} %collective-permute-done.3.r3_ref) | copy-start | bytes 393220
  28.1 21.1 %all-to-all-start = ((f32[32,8,128]{2,1,0:T(8,128)}), f32[32,8,128]{2,1,0:T(8,128)S(1)}, u32[]{:S(2)}, u32[]{:S(2)}) async-start(f32[32,8,128]{2,1,0:T(8,128)} %get-tuple-element.12), calls=%async_computation | async-start | bytes 262144 | tf_op jit(solution)/shard_map/all_to_all | solution.py:173
  49.2 0.7 %copy-start.1 = (f32[32,8,128]{2,1,0:T(8,128)}, f32[32,8,128]{2,1,0:T(8,128)S(1)}, u32[]{:S(2)}) copy-start(f32[32,8,128]{2,1,0:T(8,128)S(1)} %all-to-all-done.every_ref) | copy-start | bytes 393220

commit v10 on v9

--- a/solution.py
+++ b/solution.py
@@ -100,15 +100,16 @@
     )(every, initial, pf, lf, pb, bl, bp)
 
 
-def matmul_kernel(ids_ref, slots_ref, obs_ref, gain_ref, keep_ref, send_ref, lhs_ref):
+def matmul_kernel(slots_ref, obs_ref, gain_ref, keep_ref, send_ref, lhs_ref):
     blocks = obs_ref.shape[1] // 128
+    sensor = lax.axis_index("sensor")
 
     @pl.when(pl.program_id(0) == 0)
     def _():
         slots = slots_ref[...]
         shape = (128, slots.shape[1])
         block_of = lax.broadcasted_iota(jnp.int32, shape, 0)
-        wanted = jnp.where(block_of < blocks, ids_ref[1] + block_of, -2)
+        wanted = jnp.where(block_of < blocks, sensor * blocks + block_of, -2)
         listed_t = jnp.zeros(shape, jnp.float32)
         for s in range(slots.shape[0]):
             listed_t = jnp.maximum(listed_t, (slots[s:s + 1, :] == wanted).astype(jnp.float32))
@@ -120,12 +121,12 @@
 
     prod = jnp.dot(lhs_ref[...], gain_ref[...], preferred_element_type=jnp.float32)
     half = prod.shape[1] // 2
-    even = ids_ref[0] == 0
+    even = sensor % 2 == 0
     keep_ref[0] = jnp.where(even, prod[:, :half], prod[:, half:])
     send_ref[0] = jnp.where(even, prod[:, half:], prod[:, :half])
 
 
-def listed_matmul(ids, slots, observations, gain_rows):
+def listed_matmul(slots, observations, gain_rows):
     rows, depth = observations.shape
     modes = gain_rows.shape[1]
     tile = 256
@@ -135,7 +136,6 @@
         matmul_kernel,
         grid=(tiles,),
         in_specs=[
-            pl.BlockSpec(memory_space=pltpu.SMEM),
             pl.BlockSpec(slots.shape, lambda j: (0, 0)),
             pl.BlockSpec((rows, depth), lambda j: (0, 0)),
             pl.BlockSpec((depth, tile), lambda j: (0, j)),
@@ -152,7 +152,7 @@
             bytes_accessed=2 * rows * depth + 2 * depth * modes + 4 * rows * modes,
             transcendentals=0,
         ),
-    )(ids, slots, observations, gain_rows)
+    )(slots, observations, gain_rows)
 
 
 def sensor_reduce_scatter(keep, send):
@@ -179,9 +179,7 @@
     time_index = lax.axis_index("tm")
     time_count = lax.axis_size("tm")
     rows_here = observations.shape[0]
-    block_count = observations.shape[1] // 128
-    ids = jnp.stack([sensor_index % 2, sensor_index * block_count]).astype(jnp.int32)
-    keep, send = listed_matmul(ids, obs_list.T, observations, gain_rows)
+    keep, send = listed_matmul(obs_list.T, observations, gain_rows)
     width = gain_rows.shape[1] // sensor_count
     parts = sensor_reduce_scatter(keep, send)
     start_col = sensor_index * width

time: 52.3 us -> 51.7 us (0.989)
  other arithmetic: 3.48 us -> 2.81 us
    another operation x1 -> x0, other arithmetic: 0.67 us -> none  [per_device(): jnp.stack([sensor_index % 2, sensor_index * block_count]).astype(jnp.int32)]
where the time goes in v10:
time: 51.7 us; the launch traced here: 51.3 us
  starting transfers between devices  15.5 us (30%)
  waiting for transfers between devices  14.4 us (28%)
  Pallas kernels  13.2 us (26%)
  local copies, waits for them, and re-layouts  4.8 us (9%)
  other arithmetic  2.81 us (5%)
  between operations  0.66 us (1%)
    all_to_all x1, starting transfers between devices, gather_tm(): return lax.all_to_all(copies, 'tm', 0, 0, tiled=True)  10.5 us
    all_to_all x1, waiting for transfers between devices, gather_tm(): return lax.all_to_all(copies, 'tm', 0, 0, tiled=True)  9.19 us
    pallas_call x1, Pallas kernels, listed_matmul(): pl.pallas_call(matmul_kernel, grid=(tiles,), in_specs=[pl.BlockSpec(slots...  8.45 us
    ppermute x3, starting transfers between devices, sensor_reduce_scatter(): parts.append(lax.ppermute(part, 'sensor', perm))  4.93 us
    ppermute x3, waiting for transfers between devices, sensor_reduce_scatter(): parts.append(lax.ppermute(part, 'sensor', perm))  3.83 us
    pallas_call x1, Pallas kernels, local_scans(): pl.pallas_call(scan_kernel, out_shape=[shape] * 5 + [jax.ShapeDtypeStruct...  2.68 us
    pallas_call x1, Pallas kernels, combine(): pl.pallas_call(combine_kernel, out_shape=[shape, shape], cost_estimate=pl...  2.08 us
    mul x1, other arithmetic, per_device(): scale = step_gain * rates[None, :]  1.71 us
  transfers between devices with their start and end apart: 5, of which 4 were waited for; matrix products, arithmetic and copies ran while one was open for 9% of the time, Pallas kernels for 0%

profile of v10, /device:TPU:8, one launch (start us, length us, event | category | flops | bytes accessed | tf_op | source)
XLA Modules:
  0.0 51.3 jit_solution(16004855825205485552)
XLA Ops:
  0.6 0.0 copy-start
  0.6 8.4 %shard_map.86 = (f32[4,256,128]{2,1,0:T(8,128)}, f32[4,256,128]{2,1,0:T(8,128)}) custom-call(s32[16,256]{1,0:T(8,128)} %bitcast.11, bf16[256,4096]{1,0:T(8,128)(2,1)} %obs_ref.1, bf16[4096,1024]{1,0:T(8,128)(2,1)} %gain_ref.1), custom_call_target="tpu_custom_call" | custom-call | flops 2147483648 | bytes 11534336 | tf_op jit(solution)/shard_map/pallas_call | solution.py:135
  9.1 0.0 collective-permute-start
  9.1 0.8 %dynamic_slice.31 = f32[128]{0:T(128)S(1)} dynamic-slice(f32[1024]{0:T(1024)} %param.12, s32[]{:T(128)S(6)} %select_n.42), dynamic_slice_sizes={128} | dynamic-slice | bytes 1028 | tf_op jit(solution)/shard_map/dynamic_slice | solution.py:188
  9.9 1.4 %collective-permute-done = f32[4,256,128]{2,1,0:T(8,128)S(1)} collective-permute-done((f32[4,256,128]{2,1,0:T(8,128)}, f32[4,256,128]{2,1,0:T(8,128)S(1)}, u32[]{:S(2)}, u32[]{:S(2)}) %collective-permute-start) | collective-permute-done | bytes 524320 | tf_op jit(solution)/shard_map/ppermute | solution.py:163
  11.2 1.1 %add.53 = f32[4,256,128]{2,1,0:T(8,128)S(1)} add(f32[4,256,128]{2,1,0:T(8,128)} %get-tuple-element.10, f32[4,256,128]{2,1,0:T(8,128)S(1)} %collective-permute-done) | non-fusion elementwise | flops 131072 | bytes 1572864 | tf_op jit(solution)/shard_map/add | solution.py:163
  12.3 0.7 %dynamic-slice_bitcast_fusion = (f32[256,128]{1,0:T(8,128)S(1)}, f32[256,128]{1,0:T(8,128)S(1)}, f32[256,128]{1,0:T(8,128)S(1)}, f32[256,128]{1,0:T(8,128)}) fusion(f32[4,256,128]{2,1,0:T(8,128)S(1)} %add.53, s32[]{:T(128)S(6)} %select_n.50, s32[]{:T(128)S(6)} %select_n.48, s32[]{:T(128)S(6)} %select_n.46, s32[]{:T(128)S(6)} %select_n.44), kind=kLoop, calls=%fused_computation.1 | loop fusion | bytes 1048592 | tf_op jit(solution)/shard_map/jit(dynamic_index_in_dim)/squeeze | solution.py:166
  13.0 1.6 %collective-permute-start.1 = (f32[256,128]{1,0:T(8,128)S(1)}, f32[256,128]{1,0:T(8,128)S(1)}, u32[]{:S(2)}, u32[]{:S(2)}) collective-permute-start(f32[256,128]{1,0:T(8,128)S(1)} %get-tuple-element.22), channel_id=1, source_target_pairs={{0,2},{1,3},{2,4},{3,5},{4,6},{5,7},{6,0},{7,1},{8,10},{9,11},{10,... | collective-permute-start | bytes 393224 | tf_op jit(solution)/shard_map/ppermute | solution.py:168
  14.6 2.6 %collective-permute-start.2 = (f32[256,128]{1,0:T(8,128)S(1)}, f32[256,128]{1,0:T(8,128)S(1)}, u32[]{:S(2)}, u32[]{:S(2)}) collective-permute-start(f32[256,128]{1,0:T(8,128)S(1)} %get-tuple-element.21), channel_id=1, source_target_pairs={{0,4},{1,5},{2,6},{3,7},{4,0},{5,1},{6,2},{7,3},{8,12},{9,13},{10,... | collective-permute-start | bytes 393224 | tf_op jit(solution)/shard_map/ppermute | solution.py:168
  17.2 0.7 %collective-permute-start.3 = (f32[256,128]{1,0:T(8,128)S(1)}, f32[256,128]{1,0:T(8,128)S(1)}, u32[]{:S(2)}, u32[]{:S(2)}) collective-permute-start(f32[256,128]{1,0:T(8,128)S(1)} %get-tuple-element.20), channel_id=1, source_target_pairs={{0,6},{1,7},{2,0},{3,1},{4,2},{5,3},{6,4},{7,5},{8,14},{9,15},{10,... | collective-permute-start | bytes 393224 | tf_op jit(solution)/shard_map/ppermute | solution.py:168
  17.9 1.7 %broadcast_multiply_fusion = (f32[256,128]{1,0:T(8,128)}, f32[256,128]{1,0:T(8,128)}) fusion(f32[128]{0:T(128)S(1)} %dynamic_slice.31, f32[256,1024]{1,0:T(8,128)} %param.11, s32[]{:T(128)S(6)} %select_n.42, pred[256]{0:T(512)(128)(4,1)S(1)} %add_compare_fusion), kind=kLoop, calls=%fused_computation.5 | loop fusion | flops 65536 | bytes 393988 | tf_op jit(solution)/shard_map/mul | solution.py:193
  19.7 0.0 copy-done
  19.7 0.7 %constant_dynamic-slice_fusion.a_ref = f32[256,128]{1,0:T(8,128)} fusion(f32[256,1024]{1,0:T(8,128)S(1)} %copy-done, s32[]{:T(128)S(6)} %select_n.42), kind=kLoop, calls=%fused_computation.6 | loop fusion | bytes 262148 | tf_op jit(solution)/shard_map/dynamic_slice | solution.py:186
  20.3 0.0 collective-permute-done.1.r1_ref
  20.3 0.0 copy-start.2
  20.3 2.1 %collective-permute-done.2.r2_ref = f32[256,128]{1,0:T(8,128)S(1)} collective-permute-done((f32[256,128]{1,0:T(8,128)S(1)}, f32[256,128]{1,0:T(8,128)S(1)}, u32[]{:S(2)}, u32[]{:S(2)}) %collective-permute-start.2) | collective-permute-done | bytes 131104 | tf_op jit(solution)/shard_map/ppermute | solution.py:168
  22.5 0.0 copy-start.3
  22.5 1.7 %collective-permute-done.3.r3_ref = f32[256,128]{1,0:T(8,128)S(1)} collective-permute-done((f32[256,128]{1,0:T(8,128)S(1)}, f32[256,128]{1,0:T(8,128)S(1)}, u32[]{:S(2)}, u32[]{:S(2)}) %collective-permute-start.3) | collective-permute-done | bytes 131104 | tf_op jit(solution)/shard_map/ppermute | solution.py:168
  24.2 0.0 copy-start.4
  24.2 0.0 copy-done.2
  24.2 0.0 copy-done.3
  24.2 0.6 %copy-done.4 = f32[256,128]{1,0:T(8,128)} copy-done((f32[256,128]{1,0:T(8,128)}, f32[256,128]{1,0:T(8,128)S(1)}, u32[]{:S(2)}) %copy-start.4) | copy-done | bytes 131096
  24.8 2.7 %shard_map.87 = (f32[256,128]{1,0:T(8,128)}, f32[256,128]{1,0:T(8,128)}, f32[256,128]{1,0:T(8,128)}, f32[256,128]{1,0:T(8,128)}, f32[256,128]{1,0:T(8,128)}, /*index=5*/f32[32,8,128]{2,1,0:T(8,128)}) custom-call(f32[256,128]{1,0:T(8,128)} %constant_dynamic-slice_fusion.a_ref, f32[256,128]{1,0:T(8,128)} %get-tuple-element.23.own_ref, f32[256,128]{1,0:T(8,128)} %copy-done.2, ...), custom_call_target="tpu_custom_call" | custom-call | flops 1310720 | bytes 1572864 | tf_op jit(solution)/shard_map/pallas_call | solution.py:67
  27.5 10.5 %all-to-all-start = ((f32[32,8,128]{2,1,0:T(8,128)}), f32[32,8,128]{2,1,0:T(8,128)S(1)}, u32[]{:S(2)}, u32[]{:S(2)}) async-start(f32[32,8,128]{2,1,0:T(8,128)} %get-tuple-element.12), calls=%async_computation | async-start | bytes 262144 | tf_op jit(solution)/shard_map/all_to_all | solution.py:173
  38.0 1.4 %dynamic-slice_bitcast_fusion.4.init_ref = f32[1,128]{1,0:T(1,128)} fusion(f32[1024]{0:T(1024)} %param.13, s32[]{:T(128)S(6)} %select_n.42), kind=kLoop, calls=%fused_computation.8 | loop fusion | bytes 1028 | tf_op jit(solution)/shard_map/broadcast_in_dim | solution.py:200
  39.4 9.2 %all-to-all-done.every_ref = f32[32,8,128]{2,1,0:T(8,128)S(1)} async-done(((f32[32,8,128]{2,1,0:T(8,128)}), f32[32,8,128]{2,1,0:T(8,128)S(1)}, u32[]{:S(2)}, u32[]{:S(2)}) %all-to-all-start) | async-done | bytes 131104 | tf_op jit(solution)/shard_map/all_to_all | solution.py:173
  48.6 0.0 copy-start.1
  48.6 0.7 %copy-done.1 = f32[32,8,128]{2,1,0:T(8,128)} copy-done((f32[32,8,128]{2,1,0:T(8,128)}, f32[32,8,128]{2,1,0:T(8,128)S(1)}, u32[]{:S(2)}) %copy-start.1) | copy-done | bytes 131096
  49.2 2.1 %shard_map.88 = (f32[256,128]{1,0:T(8,128)}, f32[256,128]{1,0:T(8,128)}) custom-call(f32[32,8,128]{2,1,0:T(8,128)} %copy-done.1, f32[1,128]{1,0:T(1,128)} %dynamic-slice_bitcast_fusion.4.init_ref, f32[256,128]{1,0:T(8,128)} %get-tuple-element.13.pf_ref, f32[256,128]{1,0:T(8,128)} %get-tuple-element.14.lf_ref, f32[256,128]{1,0:T(8,128)} %get-tuple-element.15.pb_ref, ...), custom_call_target="tpu_custom_call" | custom-call | flops 163840 | bytes 917504 | tf_op jit(solution)/shard_map/pallas_call | solution.py:96
  (1 shorter events, 0.0 us)
Async XLA Ops:
  0.6 19.0 %copy-start = (f32[256,1024]{1,0:T(8,128)S(1)}, f32[256,1024]{1,0:T(8,128)}, u32[]{:S(2)}) copy-start(f32[256,1024]{1,0:T(8,128)} %param.10) | copy-start | bytes 3145732
  9.1 2.1 %collective-permute-start = (f32[4,256,128]{2,1,0:T(8,128)}, f32[4,256,128]{2,1,0:T(8,128)S(1)}, u32[]{:S(2)}, u32[]{:S(2)}) collective-permute-start(f32[4,256,128]{2,1,0:T(8,128)} %get-tuple-element.11), channel_id=1, source_target_pairs={{0,1},{1,0},{2,3},{3,2},{4,5},{5,4},{6,7},{7,6},{8,9},{9,8},{10,11... | collective-permute-start | bytes 1572872 | tf_op jit(solution)/shard_map/ppermute | solution.py:163
  13.0 7.3 %collective-permute-start.1 = (f32[256,128]{1,0:T(8,128)S(1)}, f32[256,128]{1,0:T(8,128)S(1)}, u32[]{:S(2)}, u32[]{:S(2)}) collective-permute-start(f32[256,128]{1,0:T(8,128)S(1)} %get-tuple-element.22), channel_id=1, source_target_pairs={{0,2},{1,3},{2,4},{3,5},{4,6},{5,7},{6,0},{7,1},{8,10},{9,11},{10,... | collective-permute-start | bytes 393224 | tf_op jit(solution)/shard_map/ppermute | solution.py:168
  14.6 7.9 %collective-permute-start.2 = (f32[256,128]{1,0:T(8,128)S(1)}, f32[256,128]{1,0:T(8,128)S(1)}, u32[]{:S(2)}, u32[]{:S(2)}) collective-permute-start(f32[256,128]{1,0:T(8,128)S(1)} %get-tuple-element.21), channel_id=1, source_target_pairs={{0,4},{1,5},{2,6},{3,7},{4,0},{5,1},{6,2},{7,3},{8,12},{9,13},{10,... | collective-permute-start | bytes 393224 | tf_op jit(solution)/shard_map/ppermute | solution.py:168
  17.2 6.9 %collective-permute-start.3 = (f32[256,128]{1,0:T(8,128)S(1)}, f32[256,128]{1,0:T(8,128)S(1)}, u32[]{:S(2)}, u32[]{:S(2)}) collective-permute-start(f32[256,128]{1,0:T(8,128)S(1)} %get-tuple-element.20), channel_id=1, source_target_pairs={{0,6},{1,7},{2,0},{3,1},{4,2},{5,3},{6,4},{7,5},{8,14},{9,15},{10,... | collective-permute-start | bytes 393224 | tf_op jit(solution)/shard_map/ppermute | solution.py:168
  20.3 3.8 %copy-start.2 = (f32[256,128]{1,0:T(8,128)}, f32[256,128]{1,0:T(8,128)S(1)}, u32[]{:S(2)}) copy-start(f32[256,128]{1,0:T(8,128)S(1)} %collective-permute-done.1.r1_ref) | copy-start | bytes 393220
  22.5 1.7 %copy-start.3 = (f32[256,128]{1,0:T(8,128)}, f32[256,128]{1,0:T(8,128)S(1)}, u32[]{:S(2)}) copy-start(f32[256,128]{1,0:T(8,128)S(1)} %collective-permute-done.2.r2_ref) | copy-start | bytes 393220
  24.2 0.7 %copy-start.4 = (f32[256,128]{1,0:T(8,128)}, f32[256,128]{1,0:T(8,128)S(1)}, u32[]{:S(2)}) copy-start(f32[256,128]{1,0:T(8,128)S(1)} %collective-permute-done.3.r3_ref) | copy-start | bytes 393220
  27.5 21.1 %all-to-all-start = ((f32[32,8,128]{2,1,0:T(8,128)}), f32[32,8,128]{2,1,0:T(8,128)S(1)}, u32[]{:S(2)}, u32[]{:S(2)}) async-start(f32[32,8,128]{2,1,0:T(8,128)} %get-tuple-element.12), calls=%async_computation | async-start | bytes 262144 | tf_op jit(solution)/shard_map/all_to_all | solution.py:173
  48.6 0.7 %copy-start.1 = (f32[32,8,128]{2,1,0:T(8,128)}, f32[32,8,128]{2,1,0:T(8,128)S(1)}, u32[]{:S(2)}) copy-start(f32[32,8,128]{2,1,0:T(8,128)S(1)} %all-to-all-done.every_ref) | copy-start | bytes 393220

commit v11 on v10

--- a/solution.py
+++ b/solution.py
@@ -160,10 +160,14 @@
     chips = count // 2
     j = lax.axis_index("sensor")
     chip = j // 2
-    chip_sum = keep + lax.ppermute(send, "sensor", [(i, i ^ 1) for i in range(count)])
-    parts = [lax.dynamic_index_in_dim(chip_sum, chip, 0, False)]
+    recv = lax.ppermute(send, "sensor", [(i, i ^ 1) for i in range(count)])
+
+    def chip_sum(index):
+        return lax.dynamic_index_in_dim(keep, index, 0, False) + lax.dynamic_index_in_dim(recv, index, 0, False)
+
+    parts = [chip_sum(chip)]
     for shift in range(1, chips):
-        part = lax.dynamic_index_in_dim(chip_sum, (chip + shift) % chips, 0, False)
+        part = chip_sum((chip + shift) % chips)
         perm = [(i, (((i // 2) + shift) % chips) * 2 + i % 2) for i in range(count)]
         parts.append(lax.ppermute(part, "sensor", perm))
     return parts

time: 51.7 us -> 51.6 us (level)
  local copies, waits for them, and re-layouts: 4.8 us -> 2.69 us
  waiting for transfers between devices: 14.4 us -> 15.7 us
  other arithmetic: 2.81 us -> 3.66 us
    add x1, other arithmetic: 1.1 us -> 1.84 us  [chip_sum(): lax.dynamic_index_in_dim(keep, index, 0, False)]
    broadcast_in_dim x1, local copies, waits for them, and re-layouts: 1.35 us -> 0.61 us  [per_device(): initial[None, :]]
    all_to_all x1, waiting for transfers between devices: 9.19 us -> 9.92 us  [gather_tm(): return lax.all_to_all(copies, 'tm', 0, 0, tiled=True)]
    squeeze x1 -> x0, local copies, waits for them, and re-layouts: 0.7 us -> none  [sensor_reduce_scatter(): part = lax.dynamic_index_in_dim(chip_sum, (chip + shift) % chips, 0, False)]
    dynamic_slice x1 -> x0, local copies, waits for them, and re-layouts: 0.67 us -> none  [per_device(): factors = lax.dynamic_slice_in_dim(decay, start_col, width, 1)]
    ppermute x3, waiting for transfers between devices: 3.83 us -> 4.4 us  [sensor_reduce_scatter(): parts.append(lax.ppermute(part, 'sensor', perm))]
  transfers between devices with their start and end apart: 5 -> 5, of which waited for: 4 -> 4; matrix products, arithmetic and copies ran while one was open for 9% -> 6% of each run, Pallas kernels for 0% -> 0%
where the time goes in v11:
time: 51.6 us; the launch traced here: 51.3 us
  waiting for transfers between devices  15.7 us (30%)
  starting transfers between devices  15.5 us (30%)
  Pallas kernels  13.1 us (25%)
  other arithmetic  3.66 us (7%)
  local copies, waits for them, and re-layouts  2.69 us (5%)
  between operations  0.67 us (1%)
    all_to_all x1, starting transfers between devices, gather_tm(): return lax.all_to_all(copies, 'tm', 0, 0, tiled=True)  10.5 us
    all_to_all x1, waiting for transfers between devices, gather_tm(): return lax.all_to_all(copies, 'tm', 0, 0, tiled=True)  9.92 us
    pallas_call x1, Pallas kernels, listed_matmul(): pl.pallas_call(matmul_kernel, grid=(tiles,), in_specs=[pl.BlockSpec(slots...  8.37 us
    ppermute x3, starting transfers between devices, sensor_reduce_scatter(): parts.append(lax.ppermute(part, 'sensor', perm))  4.93 us
    ppermute x3, waiting for transfers between devices, sensor_reduce_scatter(): parts.append(lax.ppermute(part, 'sensor', perm))  4.4 us
    pallas_call x1, Pallas kernels, local_scans(): pl.pallas_call(scan_kernel, out_shape=[shape] * 5 + [jax.ShapeDtypeStruct...  2.68 us
    pallas_call x1, Pallas kernels, combine(): pl.pallas_call(combine_kernel, out_shape=[shape, shape], cost_estimate=pl...  2.08 us
    add x1, other arithmetic, chip_sum(): lax.dynamic_index_in_dim(keep, index, 0, False)  1.84 us
  transfers between devices with their start and end apart: 5, of which 4 were waited for; matrix products, arithmetic and copies ran while one was open for 6% of the time, Pallas kernels for 0%

profile of v11, /device:TPU:8, one launch (start us, length us, event | category | flops | bytes accessed | tf_op | source)
XLA Modules:
  0.0 51.3 jit_solution(3604700419941692218)
XLA Ops:
  0.6 0.0 copy-start
  0.6 8.4 %shard_map.86 = (f32[4,256,128]{2,1,0:T(8,128)}, f32[4,256,128]{2,1,0:T(8,128)}) custom-call(s32[16,256]{1,0:T(8,128)} %bitcast.11, bf16[256,4096]{1,0:T(8,128)(2,1)} %obs_ref.1, bf16[4096,1024]{1,0:T(8,128)(2,1)} %gain_ref.1), custom_call_target="tpu_custom_call" | custom-call | flops 2147483648 | bytes 11534336 | tf_op jit(solution)/shard_map/pallas_call | solution.py:135
  9.0 0.0 collective-permute-start
  9.0 0.8 %dynamic_slice.47 = f32[128]{0:T(128)S(1)} dynamic-slice(f32[1024]{0:T(1024)} %param.12, s32[]{:T(128)S(6)} %select_n.46), dynamic_slice_sizes={128} | dynamic-slice | bytes 1028 | tf_op jit(solution)/shard_map/dynamic_slice | solution.py:192
  9.8 1.4 %collective-permute-done = f32[4,256,128]{2,1,0:T(8,128)S(1)} collective-permute-done((f32[4,256,128]{2,1,0:T(8,128)}, f32[4,256,128]{2,1,0:T(8,128)S(1)}, u32[]{:S(2)}, u32[]{:S(2)}) %collective-permute-start) | collective-permute-done | bytes 524320 | tf_op jit(solution)/shard_map/ppermute | solution.py:163
  11.1 1.8 %add_bitcast_fusion = (f32[256,128]{1,0:T(8,128)S(1)}, f32[256,128]{1,0:T(8,128)S(1)}, f32[256,128]{1,0:T(8,128)S(1)}, f32[256,128]{1,0:T(8,128)}) fusion(f32[4,256,128]{2,1,0:T(8,128)S(1)} %collective-permute-done, s32[]{:T(128)S(6)} %select_n.54, f32[4,256,128]{2,1,0:T(8,128)} %get-tuple-element.10, s32[]{:T(128)S(6)} %select_n.52, s32[]{:T(128)S(6)} %select_n.50, ...), kind=kLoop, calls=%fused_computation.1 | loop fusion | flops 131072 | bytes 1572880 | tf_op jit(solution)/shard_map/add | solution.py:166
  13.0 1.6 %collective-permute-start.1 = (f32[256,128]{1,0:T(8,128)S(1)}, f32[256,128]{1,0:T(8,128)S(1)}, u32[]{:S(2)}, u32[]{:S(2)}) collective-permute-start(f32[256,128]{1,0:T(8,128)S(1)} %get-tuple-element.22), channel_id=1, source_target_pairs={{0,2},{1,3},{2,4},{3,5},{4,6},{5,7},{6,0},{7,1},{8,10},{9,11},{10,... | collective-permute-start | bytes 393224 | tf_op jit(solution)/shard_map/ppermute | solution.py:172
  14.6 2.6 %collective-permute-start.2 = (f32[256,128]{1,0:T(8,128)S(1)}, f32[256,128]{1,0:T(8,128)S(1)}, u32[]{:S(2)}, u32[]{:S(2)}) collective-permute-start(f32[256,128]{1,0:T(8,128)S(1)} %get-tuple-element.21), channel_id=1, source_target_pairs={{0,4},{1,5},{2,6},{3,7},{4,0},{5,1},{6,2},{7,3},{8,12},{9,13},{10,... | collective-permute-start | bytes 393224 | tf_op jit(solution)/shard_map/ppermute | solution.py:172
  17.2 0.7 %collective-permute-start.3 = (f32[256,128]{1,0:T(8,128)S(1)}, f32[256,128]{1,0:T(8,128)S(1)}, u32[]{:S(2)}, u32[]{:S(2)}) collective-permute-start(f32[256,128]{1,0:T(8,128)S(1)} %get-tuple-element.20), channel_id=1, source_target_pairs={{0,6},{1,7},{2,0},{3,1},{4,2},{5,3},{6,4},{7,5},{8,14},{9,15},{10,... | collective-permute-start | bytes 393224 | tf_op jit(solution)/shard_map/ppermute | solution.py:172
  17.9 1.8 %broadcast_multiply_fusion = (f32[256,128]{1,0:T(8,128)}, f32[256,128]{1,0:T(8,128)}, f32[256,128]{1,0:T(8,128)}) fusion(f32[128]{0:T(128)S(1)} %dynamic_slice.47, f32[256,1024]{1,0:T(8,128)} %param.11, s32[]{:T(128)S(6)} %select_n.46, pred[256]{0:T(512)(128)(4,1)S(1)} %add_compare_fusion, f32[256,1024]{1,0:T(8,128)} %param.10), kind=kLoop, calls=%fused_computation.5 | loop fusion | flops 65536 | bytes 656132 | tf_op jit(solution)/shard_map/mul | solution.py:197
  19.7 0.0 collective-permute-done.1.r1_ref
  19.7 0.0 copy-start.2
  19.7 2.7 %collective-permute-done.2.r2_ref = f32[256,128]{1,0:T(8,128)S(1)} collective-permute-done((f32[256,128]{1,0:T(8,128)S(1)}, f32[256,128]{1,0:T(8,128)S(1)}, u32[]{:S(2)}, u32[]{:S(2)}) %collective-permute-start.2) | collective-permute-done | bytes 131104 | tf_op jit(solution)/shard_map/ppermute | solution.py:172
  22.4 0.0 copy-start.3
  22.4 1.7 %collective-permute-done.3.r3_ref = f32[256,128]{1,0:T(8,128)S(1)} collective-permute-done((f32[256,128]{1,0:T(8,128)S(1)}, f32[256,128]{1,0:T(8,128)S(1)}, u32[]{:S(2)}, u32[]{:S(2)}) %collective-permute-start.3) | collective-permute-done | bytes 131104 | tf_op jit(solution)/shard_map/ppermute | solution.py:172
  24.1 0.0 copy-start.4
  24.1 0.0 copy-done.2
  24.1 0.0 copy-done.3
  24.1 0.6 %copy-done.4 = f32[256,128]{1,0:T(8,128)} copy-done((f32[256,128]{1,0:T(8,128)}, f32[256,128]{1,0:T(8,128)S(1)}, u32[]{:S(2)}) %copy-start.4) | copy-done | bytes 131096
  24.8 2.7 %shard_map.87 = (f32[256,128]{1,0:T(8,128)}, f32[256,128]{1,0:T(8,128)}, f32[256,128]{1,0:T(8,128)}, f32[256,128]{1,0:T(8,128)}, f32[256,128]{1,0:T(8,128)}, /*index=5*/f32[32,8,128]{2,1,0:T(8,128)}) custom-call(f32[256,128]{1,0:T(8,128)} %get-tuple-element.24.a_ref, f32[256,128]{1,0:T(8,128)} %get-tuple-element.23.own_ref, f32[256,128]{1,0:T(8,128)} %copy-done.2, ...), custom_call_target="tpu_custom_call" | custom-call | flops 1310720 | bytes 1572864 | tf_op jit(solution)/shard_map/pallas_call | solution.py:67
  27.5 10.5 %all-to-all-start = ((f32[32,8,128]{2,1,0:T(8,128)}), f32[32,8,128]{2,1,0:T(8,128)S(1)}, u32[]{:S(2)}, u32[]{:S(2)}) async-start(f32[32,8,128]{2,1,0:T(8,128)} %get-tuple-element.12), calls=%async_computation | async-start | bytes 262144 | tf_op jit(solution)/shard_map/all_to_all | solution.py:177
  38.0 0.0 copy-done
  38.0 0.6 %dynamic-slice_bitcast_fusion.init_ref = f32[1,128]{1,0:T(1,128)} fusion(f32[1024]{0:T(1024)S(1)} %copy-done, s32[]{:T(128)S(6)} %select_n.46), kind=kLoop, calls=%fused_computation.8 | loop fusion | bytes 1028 | tf_op jit(solution)/shard_map/broadcast_in_dim | solution.py:204
  38.6 9.9 %all-to-all-done.every_ref = f32[32,8,128]{2,1,0:T(8,128)S(1)} async-done(((f32[32,8,128]{2,1,0:T(8,128)}), f32[32,8,128]{2,1,0:T(8,128)S(1)}, u32[]{:S(2)}, u32[]{:S(2)}) %all-to-all-start) | async-done | bytes 131104 | tf_op jit(solution)/shard_map/all_to_all | solution.py:177
  48.5 0.0 copy-start.1
  48.5 0.7 %copy-done.1 = f32[32,8,128]{2,1,0:T(8,128)} copy-done((f32[32,8,128]{2,1,0:T(8,128)}, f32[32,8,128]{2,1,0:T(8,128)S(1)}, u32[]{:S(2)}) %copy-start.1) | copy-done | bytes 131096
  49.2 2.1 %shard_map.88 = (f32[256,128]{1,0:T(8,128)}, f32[256,128]{1,0:T(8,128)}) custom-call(f32[32,8,128]{2,1,0:T(8,128)} %copy-done.1, f32[1,128]{1,0:T(1,128)} %dynamic-slice_bitcast_fusion.init_ref, f32[256,128]{1,0:T(8,128)} %get-tuple-element.13.pf_ref, f32[256,128]{1,0:T(8,128)} %get-tuple-element.14.lf_ref, f32[256,128]{1,0:T(8,128)} %get-tuple-element.15.pb_ref, ...), custom_call_target="tpu_custom_call" | custom-call | flops 163840 | bytes 917504 | tf_op jit(solution)/shard_map/pallas_call | solution.py:96
  (1 shorter events, 0.0 us)
Async XLA Ops:
  0.6 37.4 %copy-start = (f32[1024]{0:T(1024)S(1)}, f32[1024]{0:T(1024)}, u32[]{:S(2)}) copy-start(f32[1024]{0:T(1024)} %param.13) | copy-start | bytes 12292
  9.0 2.1 %collective-permute-start = (f32[4,256,128]{2,1,0:T(8,128)}, f32[4,256,128]{2,1,0:T(8,128)S(1)}, u32[]{:S(2)}, u32[]{:S(2)}) collective-permute-start(f32[4,256,128]{2,1,0:T(8,128)} %get-tuple-element.11), channel_id=1, source_target_pairs={{0,1},{1,0},{2,3},{3,2},{4,5},{5,4},{6,7},{7,6},{8,9},{9,8},{10,11... | collective-permute-start | bytes 1572872 | tf_op jit(solution)/shard_map/ppermute | solution.py:163
  13.0 6.7 %collective-permute-start.1 = (f32[256,128]{1,0:T(8,128)S(1)}, f32[256,128]{1,0:T(8,128)S(1)}, u32[]{:S(2)}, u32[]{:S(2)}) collective-permute-start(f32[256,128]{1,0:T(8,128)S(1)} %get-tuple-element.22), channel_id=1, source_target_pairs={{0,2},{1,3},{2,4},{3,5},{4,6},{5,7},{6,0},{7,1},{8,10},{9,11},{10,... | collective-permute-start | bytes 393224 | tf_op jit(solution)/shard_map/ppermute | solution.py:172
  14.6 7.9 %collective-permute-start.2 = (f32[256,128]{1,0:T(8,128)S(1)}, f32[256,128]{1,0:T(8,128)S(1)}, u32[]{:S(2)}, u32[]{:S(2)}) collective-permute-start(f32[256,128]{1,0:T(8,128)S(1)} %get-tuple-element.21), channel_id=1, source_target_pairs={{0,4},{1,5},{2,6},{3,7},{4,0},{5,1},{6,2},{7,3},{8,12},{9,13},{10,... | collective-permute-start | bytes 393224 | tf_op jit(solution)/shard_map/ppermute | solution.py:172
  17.2 6.9 %collective-permute-start.3 = (f32[256,128]{1,0:T(8,128)S(1)}, f32[256,128]{1,0:T(8,128)S(1)}, u32[]{:S(2)}, u32[]{:S(2)}) collective-permute-start(f32[256,128]{1,0:T(8,128)S(1)} %get-tuple-element.20), channel_id=1, source_target_pairs={{0,6},{1,7},{2,0},{3,1},{4,2},{5,3},{6,4},{7,5},{8,14},{9,15},{10,... | collective-permute-start | bytes 393224 | tf_op jit(solution)/shard_map/ppermute | solution.py:172
  19.7 4.4 %copy-start.2 = (f32[256,128]{1,0:T(8,128)}, f32[256,128]{1,0:T(8,128)S(1)}, u32[]{:S(2)}) copy-start(f32[256,128]{1,0:T(8,128)S(1)} %collective-permute-done.1.r1_ref) | copy-start | bytes 393220
  22.4 1.7 %copy-start.3 = (f32[256,128]{1,0:T(8,128)}, f32[256,128]{1,0:T(8,128)S(1)}, u32[]{:S(2)}) copy-start(f32[256,128]{1,0:T(8,128)S(1)} %collective-permute-done.2.r2_ref) | copy-start | bytes 393220
  24.1 0.7 %copy-start.4 = (f32[256,128]{1,0:T(8,128)}, f32[256,128]{1,0:T(8,128)S(1)}, u32[]{:S(2)}) copy-start(f32[256,128]{1,0:T(8,128)S(1)} %collective-permute-done.3.r3_ref) | copy-start | bytes 393220
  27.5 21.1 %all-to-all-start = ((f32[32,8,128]{2,1,0:T(8,128)}), f32[32,8,128]{2,1,0:T(8,128)S(1)}, u32[]{:S(2)}, u32[]{:S(2)}) async-start(f32[32,8,128]{2,1,0:T(8,128)} %get-tuple-element.12), calls=%async_computation | async-start | bytes 262144 | tf_op jit(solution)/shard_map/all_to_all | solution.py:177
  48.5 0.7 %copy-start.1 = (f32[32,8,128]{2,1,0:T(8,128)}, f32[32,8,128]{2,1,0:T(8,128)S(1)}, u32[]{:S(2)}) copy-start(f32[32,8,128]{2,1,0:T(8,128)S(1)} %all-to-all-done.every_ref) | copy-start | bytes 393220

commit v12 on v10

--- a/solution.py
+++ b/solution.py
@@ -40,35 +40,64 @@
         carry_x = [jnp.broadcast_to(v[edge:edge + 1], v.shape) for v in cx]
 
 
-def scan_kernel(a_ref, own_ref, r1_ref, r2_ref, r3_ref, g_ref, s_ref, pf_ref, lf_ref, pb_ref, bl_ref,
-                bp_ref, sum_ref):
-    rows = a_ref.shape[0]
+def _summary_tile(rows_by_slot, cols):
+    sub = lax.broadcasted_iota(jnp.int32, (SUB, cols), 0)
+    tile = jnp.zeros((SUB, cols), jnp.float32)
+    for row, value in rows_by_slot:
+        tile = jnp.where(sub == row, jnp.broadcast_to(value, tile.shape), tile)
+    return tile
+
+
+def gain_scan_kernel(a_ref, g_ref, s_ref, pf_ref, pb_ref, bp_ref, part_ref):
+    rows, cols = a_ref.shape
+    a, _ = _chunk_scan(a_ref[...], [], rows, False)
+    _carry(a, [], pf_ref, [], rows, False)
+    scale = s_ref[...]
+    pf = pf_ref[...]
+    g, (op,) = _chunk_scan(g_ref[...], [pf - scale * pf], rows, True)
+    _carry(g, [op], pb_ref, [bp_ref], rows, True)
+    part_ref[...] = _summary_tile(
+        [(0, pf_ref[rows - 1:rows, :]), (2, pb_ref[0:1, :]), (4, bp_ref[0:1, :])], cols
+    )
+
+
+def gain_scans(factors, step_gain, scale):
+    shape = jax.ShapeDtypeStruct(factors.shape, jnp.float32)
+    rows, cols = factors.shape
+    return pl.pallas_call(
+        gain_scan_kernel,
+        out_shape=[shape] * 3 + [jax.ShapeDtypeStruct((SUB, cols), jnp.float32)],
+        cost_estimate=pl.CostEstimate(flops=20 * rows * cols, bytes_accessed=24 * rows * cols, transcendentals=0),
+    )(factors, step_gain, scale)
+
+
+def scan_kernel(a_ref, own_ref, r1_ref, r2_ref, r3_ref, g_ref, s_ref, part_ref, lf_ref, bl_ref, sum_ref):
+    rows, cols = a_ref.shape
     inflow = ((own_ref[...] + r1_ref[...]) + r2_ref[...]) + r3_ref[...]
     a, (u,) = _chunk_scan(a_ref[...], [inflow], rows, False)
-    _carry(a, [u], pf_ref, [lf_ref], rows, False)
+    _carry(a, [u], None, [lf_ref], rows, False)
     scale = s_ref[...]
     lf = lf_ref[...]
-    pf = pf_ref[...]
-    g, (ol, op) = _chunk_scan(g_ref[...], [lf - scale * lf, pf - scale * pf], rows, True)
-    _carry(g, [ol, op], pb_ref, [bl_ref, bp_ref], rows, True)
-    sub = lax.broadcasted_iota(jnp.int32, (SUB, pf_ref.shape[1]), 0)
-    tile = jnp.zeros((SUB, pf_ref.shape[1]), jnp.float32)
-    for row, value in enumerate(
-        [pf_ref[rows - 1:rows, :], lf_ref[rows - 1:rows, :], pb_ref[0:1, :], bl_ref[0:1, :], bp_ref[0:1, :]]
-    ):
-        tile = jnp.where(sub == row, jnp.broadcast_to(value, tile.shape), tile)
+    g, (ol,) = _chunk_scan(g_ref[...], [lf - scale * lf], rows, True)
+    _carry(g, [ol], None, [bl_ref], rows, True)
+    sub = lax.broadcasted_iota(jnp.int32, (SUB, cols), 0)
+    tile = jnp.where(
+        sub == 1,
+        jnp.broadcast_to(lf_ref[rows - 1:rows, :], (SUB, cols)),
+        jnp.where(sub == 3, jnp.broadcast_to(bl_ref[0:1, :], (SUB, cols)), part_ref[...]),
+    )
     for k in range(sum_ref.shape[0]):
         sum_ref[k] = tile
 
 
-def local_scans(factors, parts, step_gain, scale, blocks):
+def local_scans(factors, parts, step_gain, scale, part, blocks):
     shape = jax.ShapeDtypeStruct(factors.shape, jnp.float32)
     rows, cols = factors.shape
     return pl.pallas_call(
         scan_kernel,
-        out_shape=[shape] * 5 + [jax.ShapeDtypeStruct((blocks, SUB, cols), jnp.float32)],
-        cost_estimate=pl.CostEstimate(flops=40 * rows * cols, bytes_accessed=48 * rows * cols, transcendentals=0),
-    )(factors, *parts, step_gain, scale)
+        out_shape=[shape] * 2 + [jax.ShapeDtypeStruct((blocks, SUB, cols), jnp.float32)],
+        cost_estimate=pl.CostEstimate(flops=20 * rows * cols, bytes_accessed=40 * rows * cols, transcendentals=0),
+    )(factors, *parts, step_gain, scale, part)
 
 
 def combine_kernel(every_ref, init_ref, pf_ref, lf_ref, pb_ref, bl_ref, bp_ref, f_ref, s_ref):
@@ -192,9 +221,8 @@
     step_gain = jnp.where((hour_ids == total_hours - 1)[:, None], jnp.float32(0.0), gains)
     scale = step_gain * rates[None, :]
 
-    prod_fwd, local_fwd, prod_back, back_local, back_prod, summary = local_scans(
-        factors, parts, step_gain, scale, time_count
-    )
+    prod_fwd, prod_back, back_prod, part = gain_scans(factors, step_gain, scale)
+    local_fwd, back_local, summary = local_scans(factors, parts, step_gain, scale, part, time_count)
     every = gather_tm(summary)
     filtered, smoothed = combine(
         every, initial[None, :], prod_fwd, local_fwd, prod_back, back_local, back_prod

time: 51.7 us -> 51.5 us (level)
  waiting for transfers between devices: 14.4 us -> 12.3 us
  Pallas kernels: 13.2 us -> 15 us
    ppermute x3, waiting for transfers between devices: 3.83 us -> 1.77 us  [sensor_reduce_scatter(): parts.append(lax.ppermute(part, 'sensor', perm))]
    pallas_call x1 -> x2, Pallas kernels: 2.68 us -> 4.52 us  [the longest x1 2.47 us: local_scans(): pl.pallas_call(scan_kernel, out_shape=[shape] * 2 + [jax.ShapeDtypeStruct...]
  transfers between devices with their start and end apart: 5 -> 5, of which waited for: 4 -> 4; matrix products, arithmetic and copies ran while one was open for 9% -> 9% of each run, Pallas kernels for 0% -> 4%
where the time goes in v12:
time: 51.5 us; the launch traced here: 51.1 us
  starting transfers between devices  15.5 us (30%)
  Pallas kernels  15 us (29%)
  waiting for transfers between devices  12.3 us (24%)
  local copies, waits for them, and re-layouts  4.8 us (9%)
  other arithmetic  2.81 us (5%)
  between operations  0.67 us (1%)
    all_to_all x1, starting transfers between devices, gather_tm(): return lax.all_to_all(copies, 'tm', 0, 0, tiled=True)  10.5 us
    all_to_all x1, waiting for transfers between devices, gather_tm(): return lax.all_to_all(copies, 'tm', 0, 0, tiled=True)  9.19 us
    pallas_call x1, Pallas kernels, listed_matmul(): pl.pallas_call(matmul_kernel, grid=(tiles,), in_specs=[pl.BlockSpec(slots...  8.44 us
    ppermute x3, starting transfers between devices, sensor_reduce_scatter(): parts.append(lax.ppermute(part, 'sensor', perm))  4.93 us
    pallas_call x1, Pallas kernels, local_scans(): pl.pallas_call(scan_kernel, out_shape=[shape] * 2 + [jax.ShapeDtypeStruct...  2.47 us
    pallas_call x1, Pallas kernels, combine(): pl.pallas_call(combine_kernel, out_shape=[shape, shape], cost_estimate=pl...  2.08 us
    pallas_call x1, Pallas kernels, gain_scans(): pl.pallas_call(gain_scan_kernel, out_shape=[shape] * 3 + [jax.ShapeDtypeS...  2.05 us
    ppermute x3, waiting for transfers between devices, sensor_reduce_scatter(): parts.append(lax.ppermute(part, 'sensor', perm))  1.77 us
  transfers between devices with their start and end apart: 5, of which 4 were waited for; matrix products, arithmetic and copies ran while one was open for 9% of the time, Pallas kernels for 4%

profile of v12, /device:TPU:8, one launch (start us, length us, event | category | flops | bytes accessed | tf_op | source)
XLA Modules:
  0.0 51.1 jit_solution(1734828942348590601)
XLA Ops:
  0.6 0.0 copy-start
  0.6 8.4 %shard_map.86 = (f32[4,256,128]{2,1,0:T(8,128)}, f32[4,256,128]{2,1,0:T(8,128)}) custom-call(s32[16,256]{1,0:T(8,128)} %bitcast.11, bf16[256,4096]{1,0:T(8,128)(2,1)} %obs_ref.1, bf16[4096,1024]{1,0:T(8,128)(2,1)} %gain_ref.1), custom_call_target="tpu_custom_call" | custom-call | flops 2147483648 | bytes 11534336 | tf_op jit(solution)/shard_map/pallas_call | solution.py:164
  9.1 0.0 collective-permute-start
  9.1 0.8 %dynamic_slice.31 = f32[128]{0:T(128)S(1)} dynamic-slice(f32[1024]{0:T(1024)} %param.12, s32[]{:T(128)S(6)} %select_n.42), dynamic_slice_sizes={128} | dynamic-slice | bytes 1028 | tf_op jit(solution)/shard_map/dynamic_slice | solution.py:217
  9.9 1.4 %collective-permute-done = f32[4,256,128]{2,1,0:T(8,128)S(1)} collective-permute-done((f32[4,256,128]{2,1,0:T(8,128)}, f32[4,256,128]{2,1,0:T(8,128)S(1)}, u32[]{:S(2)}, u32[]{:S(2)}) %collective-permute-start) | collective-permute-done | bytes 524320 | tf_op jit(solution)/shard_map/ppermute | solution.py:192
  11.2 1.1 %add.53 = f32[4,256,128]{2,1,0:T(8,128)S(1)} add(f32[4,256,128]{2,1,0:T(8,128)} %get-tuple-element.11, f32[4,256,128]{2,1,0:T(8,128)S(1)} %collective-permute-done) | non-fusion elementwise | flops 131072 | bytes 1572864 | tf_op jit(solution)/shard_map/add | solution.py:192
  12.3 0.7 %dynamic-slice_bitcast_fusion = (f32[256,128]{1,0:T(8,128)S(1)}, f32[256,128]{1,0:T(8,128)S(1)}, f32[256,128]{1,0:T(8,128)S(1)}, f32[256,128]{1,0:T(8,128)}) fusion(f32[4,256,128]{2,1,0:T(8,128)S(1)} %add.53, s32[]{:T(128)S(6)} %select_n.50, s32[]{:T(128)S(6)} %select_n.48, s32[]{:T(128)S(6)} %select_n.46, s32[]{:T(128)S(6)} %select_n.44), kind=kLoop, calls=%fused_computation.1 | loop fusion | bytes 1048592 | tf_op jit(solution)/shard_map/jit(dynamic_index_in_dim)/squeeze | solution.py:195
  13.0 1.6 %collective-permute-start.1 = (f32[256,128]{1,0:T(8,128)S(1)}, f32[256,128]{1,0:T(8,128)S(1)}, u32[]{:S(2)}, u32[]{:S(2)}) collective-permute-start(f32[256,128]{1,0:T(8,128)S(1)} %get-tuple-element.24), channel_id=1, source_target_pairs={{0,2},{1,3},{2,4},{3,5},{4,6},{5,7},{6,0},{7,1},{8,10},{9,11},{10,... | collective-permute-start | bytes 393224 | tf_op jit(solution)/shard_map/ppermute | solution.py:197
  14.6 2.6 %collective-permute-start.2 = (f32[256,128]{1,0:T(8,128)S(1)}, f32[256,128]{1,0:T(8,128)S(1)}, u32[]{:S(2)}, u32[]{:S(2)}) collective-permute-start(f32[256,128]{1,0:T(8,128)S(1)} %get-tuple-element.23), channel_id=1, source_target_pairs={{0,4},{1,5},{2,6},{3,7},{4,0},{5,1},{6,2},{7,3},{8,12},{9,13},{10,... | collective-permute-start | bytes 393224 | tf_op jit(solution)/shard_map/ppermute | solution.py:197
  17.2 0.7 %collective-permute-start.3 = (f32[256,128]{1,0:T(8,128)S(1)}, f32[256,128]{1,0:T(8,128)S(1)}, u32[]{:S(2)}, u32[]{:S(2)}) collective-permute-start(f32[256,128]{1,0:T(8,128)S(1)} %get-tuple-element.22), channel_id=1, source_target_pairs={{0,6},{1,7},{2,0},{3,1},{4,2},{5,3},{6,4},{7,5},{8,14},{9,15},{10,... | collective-permute-start | bytes 393224 | tf_op jit(solution)/shard_map/ppermute | solution.py:197
  17.9 1.7 %broadcast_multiply_fusion = (f32[256,128]{1,0:T(8,128)}, f32[256,128]{1,0:T(8,128)}) fusion(f32[128]{0:T(128)S(1)} %dynamic_slice.31, f32[256,1024]{1,0:T(8,128)} %param.11, s32[]{:T(128)S(6)} %select_n.42, pred[256]{0:T(512)(128)(4,1)S(1)} %add_compare_fusion), kind=kLoop, calls=%fused_computation.5 | loop fusion | flops 65536 | bytes 393988 | tf_op jit(solution)/shard_map/mul | solution.py:222
  19.6 0.0 copy-done
  19.7 0.7 %constant_dynamic-slice_fusion.a_ref = f32[256,128]{1,0:T(8,128)} fusion(f32[256,1024]{1,0:T(8,128)S(1)} %copy-done, s32[]{:T(128)S(6)} %select_n.42), kind=kLoop, calls=%fused_computation.6 | loop fusion | bytes 262148 | tf_op jit(solution)/shard_map/dynamic_slice | solution.py:215
  20.3 2.1 %shard_map.87 = (f32[256,128]{1,0:T(8,128)}, f32[256,128]{1,0:T(8,128)}, f32[256,128]{1,0:T(8,128)}, f32[8,128]{1,0:T(8,128)}) custom-call(f32[256,128]{1,0:T(8,128)} %constant_dynamic-slice_fusion.a_ref, f32[256,128]{1,0:T(8,128)} %get-tuple-element.21.g_ref, f32[256,128]{1,0:T(8,128)} %get-tuple-element.20.s_ref), custom_call_target="tpu_custom_call" | custom-call | flops 655360 | bytes 786432 | tf_op jit(solution)/shard_map/pallas_call | solution.py:67
  22.4 0.0 collective-permute-done.1.r1_ref
  22.4 0.0 copy-start.2
  22.4 0.1 collective-permute-done.2.r2_ref
  22.5 0.0 copy-start.3
  22.5 1.7 %collective-permute-done.3.r3_ref = f32[256,128]{1,0:T(8,128)S(1)} collective-permute-done((f32[256,128]{1,0:T(8,128)S(1)}, f32[256,128]{1,0:T(8,128)S(1)}, u32[]{:S(2)}, u32[]{:S(2)}) %collective-permute-start.3) | collective-permute-done | bytes 131104 | tf_op jit(solution)/shard_map/ppermute | solution.py:197
  24.2 0.0 copy-start.4
  24.2 0.0 copy-done.2
  24.2 0.0 copy-done.3
  24.2 0.6 %copy-done.4 = f32[256,128]{1,0:T(8,128)} copy-done((f32[256,128]{1,0:T(8,128)}, f32[256,128]{1,0:T(8,128)S(1)}, u32[]{:S(2)}) %copy-start.4) | copy-done | bytes 131096
  24.8 2.5 %shard_map.88 = (f32[256,128]{1,0:T(8,128)}, f32[256,128]{1,0:T(8,128)}, f32[32,8,128]{2,1,0:T(8,128)}) custom-call(f32[256,128]{1,0:T(8,128)} %constant_dynamic-slice_fusion.a_ref, f32[256,128]{1,0:T(8,128)} %get-tuple-element.25.own_ref, f32[256,128]{1,0:T(8,128)} %copy-done.2, f32[256,128]{1,0:T(8,128)} %copy-done.3, f32[256,128]{1,0:T(8,128)} %copy-done.4, ...), custom_call_target="tpu_custom_call" | custom-call | flops 655360 | bytes 1310720 | tf_op jit(solution)/shard_map/pallas_call | solution.py:96
  27.3 10.5 %all-to-all-start = ((f32[32,8,128]{2,1,0:T(8,128)}), f32[32,8,128]{2,1,0:T(8,128)S(1)}, u32[]{:S(2)}, u32[]{:S(2)}) async-start(f32[32,8,128]{2,1,0:T(8,128)} %get-tuple-element.14), calls=%async_computation | async-start | bytes 262144 | tf_op jit(solution)/shard_map/all_to_all | solution.py:202
  37.8 1.4 %dynamic-slice_bitcast_fusion.4.init_ref = f32[1,128]{1,0:T(1,128)} fusion(f32[1024]{0:T(1024)} %param.13, s32[]{:T(128)S(6)} %select_n.42), kind=kLoop, calls=%fused_computation.8 | loop fusion | bytes 1028 | tf_op jit(solution)/shard_map/broadcast_in_dim | solution.py:228
  39.2 9.2 %all-to-all-done.every_ref = f32[32,8,128]{2,1,0:T(8,128)S(1)} async-done(((f32[32,8,128]{2,1,0:T(8,128)}), f32[32,8,128]{2,1,0:T(8,128)S(1)}, u32[]{:S(2)}, u32[]{:S(2)}) %all-to-all-start) | async-done | bytes 131104 | tf_op jit(solution)/shard_map/all_to_all | solution.py:202
  48.4 0.0 copy-start.1
  48.4 0.7 %copy-done.1 = f32[32,8,128]{2,1,0:T(8,128)} copy-done((f32[32,8,128]{2,1,0:T(8,128)}, f32[32,8,128]{2,1,0:T(8,128)S(1)}, u32[]{:S(2)}) %copy-start.1) | copy-done | bytes 131096
  49.0 2.1 %shard_map.89 = (f32[256,128]{1,0:T(8,128)}, f32[256,128]{1,0:T(8,128)}) custom-call(f32[32,8,128]{2,1,0:T(8,128)} %copy-done.1, f32[1,128]{1,0:T(1,128)} %dynamic-slice_bitcast_fusion.4.init_ref, f32[256,128]{1,0:T(8,128)} %get-tuple-element.15.pf_ref, f32[256,128]{1,0:T(8,128)} %get-tuple-element.16.lf_ref, f32[256,128]{1,0:T(8,128)} %get-tuple-element.17.pb_ref, ...), custom_call_target="tpu_custom_call" | custom-call | flops 163840 | bytes 917504 | tf_op jit(solution)/shard_map/pallas_call | solution.py:125
  (1 shorter events, 0.0 us)
Async XLA Ops:
  0.6 19.0 %copy-start = (f32[256,1024]{1,0:T(8,128)S(1)}, f32[256,1024]{1,0:T(8,128)}, u32[]{:S(2)}) copy-start(f32[256,1024]{1,0:T(8,128)} %param.10) | copy-start | bytes 3145732
  9.1 2.1 %collective-permute-start = (f32[4,256,128]{2,1,0:T(8,128)}, f32[4,256,128]{2,1,0:T(8,128)S(1)}, u32[]{:S(2)}, u32[]{:S(2)}) collective-permute-start(f32[4,256,128]{2,1,0:T(8,128)} %get-tuple-element.12), channel_id=1, source_target_pairs={{0,1},{1,0},{2,3},{3,2},{4,5},{5,4},{6,7},{7,6},{8,9},{9,8},{10,11... | collective-permute-start | bytes 1572872 | tf_op jit(solution)/shard_map/ppermute | solution.py:192
  13.0 9.4 %collective-permute-start.1 = (f32[256,128]{1,0:T(8,128)S(1)}, f32[256,128]{1,0:T(8,128)S(1)}, u32[]{:S(2)}, u32[]{:S(2)}) collective-permute-start(f32[256,128]{1,0:T(8,128)S(1)} %get-tuple-element.24), channel_id=1, source_target_pairs={{0,2},{1,3},{2,4},{3,5},{4,6},{5,7},{6,0},{7,1},{8,10},{9,11},{10,... | collective-permute-start | bytes 393224 | tf_op jit(solution)/shard_map/ppermute | solution.py:197
  14.6 7.9 %collective-permute-start.2 = (f32[256,128]{1,0:T(8,128)S(1)}, f32[256,128]{1,0:T(8,128)S(1)}, u32[]{:S(2)}, u32[]{:S(2)}) collective-permute-start(f32[256,128]{1,0:T(8,128)S(1)} %get-tuple-element.23), channel_id=1, source_target_pairs={{0,4},{1,5},{2,6},{3,7},{4,0},{5,1},{6,2},{7,3},{8,12},{9,13},{10,... | collective-permute-start | bytes 393224 | tf_op jit(solution)/shard_map/ppermute | solution.py:197
  17.2 6.9 %collective-permute-start.3 = (f32[256,128]{1,0:T(8,128)S(1)}, f32[256,128]{1,0:T(8,128)S(1)}, u32[]{:S(2)}, u32[]{:S(2)}) collective-permute-start(f32[256,128]{1,0:T(8,128)S(1)} %get-tuple-element.22), channel_id=1, source_target_pairs={{0,6},{1,7},{2,0},{3,1},{4,2},{5,3},{6,4},{7,5},{8,14},{9,15},{10,... | collective-permute-start | bytes 393224 | tf_op jit(solution)/shard_map/ppermute | solution.py:197
  22.4 1.8 %copy-start.2 = (f32[256,128]{1,0:T(8,128)}, f32[256,128]{1,0:T(8,128)S(1)}, u32[]{:S(2)}) copy-start(f32[256,128]{1,0:T(8,128)S(1)} %collective-permute-done.1.r1_ref) | copy-start | bytes 393220
  22.5 1.7 %copy-start.3 = (f32[256,128]{1,0:T(8,128)}, f32[256,128]{1,0:T(8,128)S(1)}, u32[]{:S(2)}) copy-start(f32[256,128]{1,0:T(8,128)S(1)} %collective-permute-done.2.r2_ref) | copy-start | bytes 393220
  24.2 0.6 %copy-start.4 = (f32[256,128]{1,0:T(8,128)}, f32[256,128]{1,0:T(8,128)S(1)}, u32[]{:S(2)}) copy-start(f32[256,128]{1,0:T(8,128)S(1)} %collective-permute-done.3.r3_ref) | copy-start | bytes 393220
  27.3 21.1 %all-to-all-start = ((f32[32,8,128]{2,1,0:T(8,128)}), f32[32,8,128]{2,1,0:T(8,128)S(1)}, u32[]{:S(2)}, u32[]{:S(2)}) async-start(f32[32,8,128]{2,1,0:T(8,128)} %get-tuple-element.14), calls=%async_computation | async-start | bytes 262144 | tf_op jit(solution)/shard_map/all_to_all | solution.py:202
  48.4 0.7 %copy-start.1 = (f32[32,8,128]{2,1,0:T(8,128)}, f32[32,8,128]{2,1,0:T(8,128)S(1)}, u32[]{:S(2)}) copy-start(f32[32,8,128]{2,1,0:T(8,128)S(1)} %all-to-all-done.every_ref) | copy-start | bytes 393220

commit v13 on v12

--- a/solution.py
+++ b/solution.py
@@ -7,35 +7,36 @@
 
 
 SUB = 8
+CHUNK = 64
 
 
 def _chunk_scan(a, x, rows, reverse):
-    sub = lax.broadcasted_iota(jnp.int32, a.shape, 0) % SUB
-    for k in (1, 2, 4):
+    sub = lax.broadcasted_iota(jnp.int32, a.shape, 0) % CHUNK
+    for k in (1, 2, 4, 8, 16, 32):
         shift = rows - k if reverse else k
         prev_a = pltpu.roll(a, shift, 0)
         prev_x = [pltpu.roll(v, shift, 0) for v in x]
-        inside = sub < SUB - k if reverse else sub >= k
+        inside = sub < CHUNK - k if reverse else sub >= k
         x = [jnp.where(inside, a * p + v, v) for p, v in zip(prev_x, x)]
         a = jnp.where(inside, a * prev_a, a)
     return a, x
 
 
 def _carry(a, x, out_a, out_x, rows, reverse):
-    chunks = rows // SUB
+    chunks = rows // CHUNK
     order = range(chunks - 1, -1, -1) if reverse else range(chunks)
-    edge = 0 if reverse else SUB - 1
+    edge = 0 if reverse else CHUNK - 1
     carry_a = None
     for i in order:
-        ca = a[i * SUB:(i + 1) * SUB]
-        cx = [v[i * SUB:(i + 1) * SUB] for v in x]
+        ca = a[i * CHUNK:(i + 1) * CHUNK]
+        cx = [v[i * CHUNK:(i + 1) * CHUNK] for v in x]
         if carry_a is not None:
             cx = [c * px + v for c, px, v in zip([ca] * len(cx), carry_x, cx)]
             ca = ca * carry_a
         if out_a is not None:
-            out_a[i * SUB:(i + 1) * SUB, :] = ca
+            out_a[i * CHUNK:(i + 1) * CHUNK, :] = ca
         for o, v in zip(out_x, cx):
-            o[i * SUB:(i + 1) * SUB, :] = v
+            o[i * CHUNK:(i + 1) * CHUNK, :] = v
         carry_a = jnp.broadcast_to(ca[edge:edge + 1], ca.shape)
         carry_x = [jnp.broadcast_to(v[edge:edge + 1], v.shape) for v in cx]
 

time: 51.5 us -> 51.3 us (level)
  no operation moved by 1% of the time
where the time goes in v13:
time: 51.3 us; the launch traced here: 51 us
  starting transfers between devices  15.5 us (30%)
  Pallas kernels  14.8 us (29%)
  waiting for transfers between devices  12.5 us (24%)
  local copies, waits for them, and re-layouts  4.8 us (9%)
  other arithmetic  2.81 us (5%)
  between operations  0.67 us (1%)
    all_to_all x1, starting transfers between devices, gather_tm(): return lax.all_to_all(copies, 'tm', 0, 0, tiled=True)  10.5 us
    all_to_all x1, waiting for transfers between devices, gather_tm(): return lax.all_to_all(copies, 'tm', 0, 0, tiled=True)  9.19 us
    pallas_call x1, Pallas kernels, listed_matmul(): pl.pallas_call(matmul_kernel, grid=(tiles,), in_specs=[pl.BlockSpec(slots...  8.44 us
    ppermute x3, starting transfers between devices, sensor_reduce_scatter(): parts.append(lax.ppermute(part, 'sensor', perm))  4.93 us
    pallas_call x1, Pallas kernels, local_scans(): pl.pallas_call(scan_kernel, out_shape=[shape] * 2 + [jax.ShapeDtypeStruct...  2.33 us
    pallas_call x1, Pallas kernels, combine(): pl.pallas_call(combine_kernel, out_shape=[shape, shape], cost_estimate=pl...  2.08 us
    ppermute x3, waiting for transfers between devices, sensor_reduce_scatter(): parts.append(lax.ppermute(part, 'sensor', perm))  1.92 us
    pallas_call x1, Pallas kernels, gain_scans(): pl.pallas_call(gain_scan_kernel, out_shape=[shape] * 3 + [jax.ShapeDtypeS...  1.91 us
  transfers between devices with their start and end apart: 5, of which 4 were waited for; matrix products, arithmetic and copies ran while one was open for 9% of the time, Pallas kernels for 4%

profile of v13, /device:TPU:8, one launch (start us, length us, event | category | flops | bytes accessed | tf_op | source)
XLA Modules:
  0.0 51.0 jit_solution(17185271939097026293)
XLA Ops:
  0.6 0.0 copy-start
  0.6 8.4 %shard_map.86 = (f32[4,256,128]{2,1,0:T(8,128)}, f32[4,256,128]{2,1,0:T(8,128)}) custom-call(s32[16,256]{1,0:T(8,128)} %bitcast.11, bf16[256,4096]{1,0:T(8,128)(2,1)} %obs_ref.1, bf16[4096,1024]{1,0:T(8,128)(2,1)} %gain_ref.1), custom_call_target="tpu_custom_call" | custom-call | flops 2147483648 | bytes 11534336 | tf_op jit(solution)/shard_map/pallas_call | solution.py:165
  9.1 0.0 collective-permute-start
  9.1 0.8 %dynamic_slice.31 = f32[128]{0:T(128)S(1)} dynamic-slice(f32[1024]{0:T(1024)} %param.12, s32[]{:T(128)S(6)} %select_n.42), dynamic_slice_sizes={128} | dynamic-slice | bytes 1028 | tf_op jit(solution)/shard_map/dynamic_slice | solution.py:218
  9.9 1.4 %collective-permute-done = f32[4,256,128]{2,1,0:T(8,128)S(1)} collective-permute-done((f32[4,256,128]{2,1,0:T(8,128)}, f32[4,256,128]{2,1,0:T(8,128)S(1)}, u32[]{:S(2)}, u32[]{:S(2)}) %collective-permute-start) | collective-permute-done | bytes 524320 | tf_op jit(solution)/shard_map/ppermute | solution.py:193
  11.2 1.1 %add.53 = f32[4,256,128]{2,1,0:T(8,128)S(1)} add(f32[4,256,128]{2,1,0:T(8,128)} %get-tuple-element.11, f32[4,256,128]{2,1,0:T(8,128)S(1)} %collective-permute-done) | non-fusion elementwise | flops 131072 | bytes 1572864 | tf_op jit(solution)/shard_map/add | solution.py:193
  12.3 0.7 %dynamic-slice_bitcast_fusion = (f32[256,128]{1,0:T(8,128)S(1)}, f32[256,128]{1,0:T(8,128)S(1)}, f32[256,128]{1,0:T(8,128)S(1)}, f32[256,128]{1,0:T(8,128)}) fusion(f32[4,256,128]{2,1,0:T(8,128)S(1)} %add.53, s32[]{:T(128)S(6)} %select_n.50, s32[]{:T(128)S(6)} %select_n.48, s32[]{:T(128)S(6)} %select_n.46, s32[]{:T(128)S(6)} %select_n.44), kind=kLoop, calls=%fused_computation.1 | loop fusion | bytes 1048592 | tf_op jit(solution)/shard_map/jit(dynamic_index_in_dim)/squeeze | solution.py:196
  13.0 1.6 %collective-permute-start.1 = (f32[256,128]{1,0:T(8,128)S(1)}, f32[256,128]{1,0:T(8,128)S(1)}, u32[]{:S(2)}, u32[]{:S(2)}) collective-permute-start(f32[256,128]{1,0:T(8,128)S(1)} %get-tuple-element.24), channel_id=1, source_target_pairs={{0,2},{1,3},{2,4},{3,5},{4,6},{5,7},{6,0},{7,1},{8,10},{9,11},{10,... | collective-permute-start | bytes 393224 | tf_op jit(solution)/shard_map/ppermute | solution.py:198
  14.6 2.6 %collective-permute-start.2 = (f32[256,128]{1,0:T(8,128)S(1)}, f32[256,128]{1,0:T(8,128)S(1)}, u32[]{:S(2)}, u32[]{:S(2)}) collective-permute-start(f32[256,128]{1,0:T(8,128)S(1)} %get-tuple-element.23), channel_id=1, source_target_pairs={{0,4},{1,5},{2,6},{3,7},{4,0},{5,1},{6,2},{7,3},{8,12},{9,13},{10,... | collective-permute-start | bytes 393224 | tf_op jit(solution)/shard_map/ppermute | solution.py:198
  17.2 0.7 %collective-permute-start.3 = (f32[256,128]{1,0:T(8,128)S(1)}, f32[256,128]{1,0:T(8,128)S(1)}, u32[]{:S(2)}, u32[]{:S(2)}) collective-permute-start(f32[256,128]{1,0:T(8,128)S(1)} %get-tuple-element.22), channel_id=1, source_target_pairs={{0,6},{1,7},{2,0},{3,1},{4,2},{5,3},{6,4},{7,5},{8,14},{9,15},{10,... | collective-permute-start | bytes 393224 | tf_op jit(solution)/shard_map/ppermute | solution.py:198
  17.9 1.7 %broadcast_multiply_fusion = (f32[256,128]{1,0:T(8,128)}, f32[256,128]{1,0:T(8,128)}) fusion(f32[128]{0:T(128)S(1)} %dynamic_slice.31, f32[256,1024]{1,0:T(8,128)} %param.11, s32[]{:T(128)S(6)} %select_n.42, pred[256]{0:T(512)(128)(4,1)S(1)} %add_compare_fusion), kind=kLoop, calls=%fused_computation.5 | loop fusion | flops 65536 | bytes 393988 | tf_op jit(solution)/shard_map/mul | solution.py:223
  19.6 0.0 copy-done
  19.7 0.7 %constant_dynamic-slice_fusion.a_ref = f32[256,128]{1,0:T(8,128)} fusion(f32[256,1024]{1,0:T(8,128)S(1)} %copy-done, s32[]{:T(128)S(6)} %select_n.42), kind=kLoop, calls=%fused_computation.6 | loop fusion | bytes 262148 | tf_op jit(solution)/shard_map/dynamic_slice | solution.py:216
  20.3 1.9 %shard_map.87 = (f32[256,128]{1,0:T(8,128)}, f32[256,128]{1,0:T(8,128)}, f32[256,128]{1,0:T(8,128)}, f32[8,128]{1,0:T(8,128)}) custom-call(f32[256,128]{1,0:T(8,128)} %constant_dynamic-slice_fusion.a_ref, f32[256,128]{1,0:T(8,128)} %get-tuple-element.21.g_ref, f32[256,128]{1,0:T(8,128)} %get-tuple-element.20.s_ref), custom_call_target="tpu_custom_call" | custom-call | flops 655360 | bytes 786432 | tf_op jit(solution)/shard_map/pallas_call | solution.py:68
  22.2 0.0 collective-permute-done.1.r1_ref
  22.2 0.0 copy-start.2
  22.2 0.2 collective-permute-done.2.r2_ref
  22.5 0.0 copy-start.3
  22.5 1.7 %collective-permute-done.3.r3_ref = f32[256,128]{1,0:T(8,128)S(1)} collective-permute-done((f32[256,128]{1,0:T(8,128)S(1)}, f32[256,128]{1,0:T(8,128)S(1)}, u32[]{:S(2)}, u32[]{:S(2)}) %collective-permute-start.3) | collective-permute-done | bytes 131104 | tf_op jit(solution)/shard_map/ppermute | solution.py:198
  24.2 0.0 copy-start.4
  24.2 0.0 copy-done.2
  24.2 0.0 copy-done.3
  24.2 0.6 %copy-done.4 = f32[256,128]{1,0:T(8,128)} copy-done((f32[256,128]{1,0:T(8,128)}, f32[256,128]{1,0:T(8,128)S(1)}, u32[]{:S(2)}) %copy-start.4) | copy-done | bytes 131096
  24.8 2.3 %shard_map.88 = (f32[256,128]{1,0:T(8,128)}, f32[256,128]{1,0:T(8,128)}, f32[32,8,128]{2,1,0:T(8,128)}) custom-call(f32[256,128]{1,0:T(8,128)} %constant_dynamic-slice_fusion.a_ref, f32[256,128]{1,0:T(8,128)} %get-tuple-element.25.own_ref, f32[256,128]{1,0:T(8,128)} %copy-done.2, f32[256,128]{1,0:T(8,128)} %copy-done.3, f32[256,128]{1,0:T(8,128)} %copy-done.4, ...), custom_call_target="tpu_custom_call" | custom-call | flops 655360 | bytes 1310720 | tf_op jit(solution)/shard_map/pallas_call | solution.py:97
  27.1 10.5 %all-to-all-start = ((f32[32,8,128]{2,1,0:T(8,128)}), f32[32,8,128]{2,1,0:T(8,128)S(1)}, u32[]{:S(2)}, u32[]{:S(2)}) async-start(f32[32,8,128]{2,1,0:T(8,128)} %get-tuple-element.14), calls=%async_computation | async-start | bytes 262144 | tf_op jit(solution)/shard_map/all_to_all | solution.py:203
  37.7 1.4 %dynamic-slice_bitcast_fusion.4.init_ref = f32[1,128]{1,0:T(1,128)} fusion(f32[1024]{0:T(1024)} %param.13, s32[]{:T(128)S(6)} %select_n.42), kind=kLoop, calls=%fused_computation.8 | loop fusion | bytes 1028 | tf_op jit(solution)/shard_map/broadcast_in_dim | solution.py:229
  39.0 9.2 %all-to-all-done.every_ref = f32[32,8,128]{2,1,0:T(8,128)S(1)} async-done(((f32[32,8,128]{2,1,0:T(8,128)}), f32[32,8,128]{2,1,0:T(8,128)S(1)}, u32[]{:S(2)}, u32[]{:S(2)}) %all-to-all-start) | async-done | bytes 131104 | tf_op jit(solution)/shard_map/all_to_all | solution.py:203
  48.2 0.0 copy-start.1
  48.2 0.7 %copy-done.1 = f32[32,8,128]{2,1,0:T(8,128)} copy-done((f32[32,8,128]{2,1,0:T(8,128)}, f32[32,8,128]{2,1,0:T(8,128)S(1)}, u32[]{:S(2)}) %copy-start.1) | copy-done | bytes 131096
  48.9 2.1 %shard_map.89 = (f32[256,128]{1,0:T(8,128)}, f32[256,128]{1,0:T(8,128)}) custom-call(f32[32,8,128]{2,1,0:T(8,128)} %copy-done.1, f32[1,128]{1,0:T(1,128)} %dynamic-slice_bitcast_fusion.4.init_ref, f32[256,128]{1,0:T(8,128)} %get-tuple-element.15.pf_ref, f32[256,128]{1,0:T(8,128)} %get-tuple-element.16.lf_ref, f32[256,128]{1,0:T(8,128)} %get-tuple-element.17.pb_ref, ...), custom_call_target="tpu_custom_call" | custom-call | flops 163840 | bytes 917504 | tf_op jit(solution)/shard_map/pallas_call | solution.py:126
  (1 shorter events, 0.0 us)
Async XLA Ops:
  0.6 19.0 %copy-start = (f32[256,1024]{1,0:T(8,128)S(1)}, f32[256,1024]{1,0:T(8,128)}, u32[]{:S(2)}) copy-start(f32[256,1024]{1,0:T(8,128)} %param.10) | copy-start | bytes 3145732
  9.1 2.1 %collective-permute-start = (f32[4,256,128]{2,1,0:T(8,128)}, f32[4,256,128]{2,1,0:T(8,128)S(1)}, u32[]{:S(2)}, u32[]{:S(2)}) collective-permute-start(f32[4,256,128]{2,1,0:T(8,128)} %get-tuple-element.12), channel_id=1, source_target_pairs={{0,1},{1,0},{2,3},{3,2},{4,5},{5,4},{6,7},{7,6},{8,9},{9,8},{10,11... | collective-permute-start | bytes 1572872 | tf_op jit(solution)/shard_map/ppermute | solution.py:193
  13.0 9.2 %collective-permute-start.1 = (f32[256,128]{1,0:T(8,128)S(1)}, f32[256,128]{1,0:T(8,128)S(1)}, u32[]{:S(2)}, u32[]{:S(2)}) collective-permute-start(f32[256,128]{1,0:T(8,128)S(1)} %get-tuple-element.24), channel_id=1, source_target_pairs={{0,2},{1,3},{2,4},{3,5},{4,6},{5,7},{6,0},{7,1},{8,10},{9,11},{10,... | collective-permute-start | bytes 393224 | tf_op jit(solution)/shard_map/ppermute | solution.py:198
  14.6 7.9 %collective-permute-start.2 = (f32[256,128]{1,0:T(8,128)S(1)}, f32[256,128]{1,0:T(8,128)S(1)}, u32[]{:S(2)}, u32[]{:S(2)}) collective-permute-start(f32[256,128]{1,0:T(8,128)S(1)} %get-tuple-element.23), channel_id=1, source_target_pairs={{0,4},{1,5},{2,6},{3,7},{4,0},{5,1},{6,2},{7,3},{8,12},{9,13},{10,... | collective-permute-start | bytes 393224 | tf_op jit(solution)/shard_map/ppermute | solution.py:198
  17.2 6.9 %collective-permute-start.3 = (f32[256,128]{1,0:T(8,128)S(1)}, f32[256,128]{1,0:T(8,128)S(1)}, u32[]{:S(2)}, u32[]{:S(2)}) collective-permute-start(f32[256,128]{1,0:T(8,128)S(1)} %get-tuple-element.22), channel_id=1, source_target_pairs={{0,6},{1,7},{2,0},{3,1},{4,2},{5,3},{6,4},{7,5},{8,14},{9,15},{10,... | collective-permute-start | bytes 393224 | tf_op jit(solution)/shard_map/ppermute | solution.py:198
  22.2 1.9 %copy-start.2 = (f32[256,128]{1,0:T(8,128)}, f32[256,128]{1,0:T(8,128)S(1)}, u32[]{:S(2)}) copy-start(f32[256,128]{1,0:T(8,128)S(1)} %collective-permute-done.1.r1_ref) | copy-start | bytes 393220
  22.5 1.7 %copy-start.3 = (f32[256,128]{1,0:T(8,128)}, f32[256,128]{1,0:T(8,128)S(1)}, u32[]{:S(2)}) copy-start(f32[256,128]{1,0:T(8,128)S(1)} %collective-permute-done.2.r2_ref) | copy-start | bytes 393220
  24.2 0.6 %copy-start.4 = (f32[256,128]{1,0:T(8,128)}, f32[256,128]{1,0:T(8,128)S(1)}, u32[]{:S(2)}) copy-start(f32[256,128]{1,0:T(8,128)S(1)} %collective-permute-done.3.r3_ref) | copy-start | bytes 393220
  27.1 21.1 %all-to-all-start = ((f32[32,8,128]{2,1,0:T(8,128)}), f32[32,8,128]{2,1,0:T(8,128)S(1)}, u32[]{:S(2)}, u32[]{:S(2)}) async-start(f32[32,8,128]{2,1,0:T(8,128)} %get-tuple-element.14), calls=%async_computation | async-start | bytes 262144 | tf_op jit(solution)/shard_map/all_to_all | solution.py:203
  48.2 0.7 %copy-start.1 = (f32[32,8,128]{2,1,0:T(8,128)}, f32[32,8,128]{2,1,0:T(8,128)S(1)}, u32[]{:S(2)}) copy-start(f32[32,8,128]{2,1,0:T(8,128)S(1)} %all-to-all-done.every_ref) | copy-start | bytes 393220

commit v14 on v13

--- a/solution.py
+++ b/solution.py
@@ -130,11 +130,13 @@
     )(every, initial, pf, lf, pb, bl, bp)
 
 
-def matmul_kernel(slots_ref, obs_ref, gain_ref, keep_ref, send_ref, lhs_ref):
-    blocks = obs_ref.shape[1] // 128
+def matmul_kernel(slots_ref, obs_ref, gain_ref, keep_ref, send_ref, mask_ref, acc_ref):
+    step = pl.program_id(0)
+    per_step = obs_ref.shape[1] // 128
+    blocks = mask_ref.shape[0]
     sensor = lax.axis_index("sensor")
 
-    @pl.when(pl.program_id(0) == 0)
+    @pl.when(step == 0)
     def _():
         slots = slots_ref[...]
         shape = (128, slots.shape[1])
@@ -145,37 +147,54 @@
             listed_t = jnp.maximum(listed_t, (slots[s:s + 1, :] == wanted).astype(jnp.float32))
         listed = listed_t.T
         for b in range(blocks):
-            cols = pl.ds(128 * b, 128)
-            block = obs_ref[:, cols]
-            lhs_ref[:, cols] = jnp.where(listed[:, b:b + 1] > 0, block, jnp.zeros_like(block))
-
-    prod = jnp.dot(lhs_ref[...], gain_ref[...], preferred_element_type=jnp.float32)
-    half = prod.shape[1] // 2
-    even = sensor % 2 == 0
-    keep_ref[0] = jnp.where(even, prod[:, :half], prod[:, half:])
-    send_ref[0] = jnp.where(even, prod[:, half:], prod[:, :half])
+            mask_ref[b] = jnp.broadcast_to(listed[:, b:b + 1], mask_ref.shape[1:])
+
+    pieces = []
+    for b in range(per_step):
+        block = obs_ref[:, pl.ds(128 * b, 128)]
+        pieces.append(jnp.where(mask_ref[step * per_step + b] > 0, block, jnp.zeros_like(block)))
+    prod = jnp.dot(jnp.concatenate(pieces, 1), gain_ref[...], preferred_element_type=jnp.float32)
+
+    @pl.when(step == 0)
+    def _():
+        acc_ref[...] = prod
+
+    @pl.when(step > 0)
+    def _():
+        acc_ref[...] += prod
+
+    @pl.when(step == pl.num_programs(0) - 1)
+    def _():
+        even = sensor % 2 == 0
+        for j in range(keep_ref.shape[0]):
+            left = acc_ref[:, pl.ds(256 * j, 128)]
+            right = acc_ref[:, pl.ds(256 * j + 128, 128)]
+            keep_ref[j] = jnp.where(even, left, right)
+            send_ref[j] = jnp.where(even, right, left)
 
 
 def listed_matmul(slots, observations, gain_rows):
     rows, depth = observations.shape
     modes = gain_rows.shape[1]
-    tile = 256
-    tiles = modes // tile
-    piece = jax.ShapeDtypeStruct((tiles, rows, tile // 2), jnp.float32)
+    slab = 512
+    piece = jax.ShapeDtypeStruct((modes // 256, rows, 128), jnp.float32)
     return pl.pallas_call(
         matmul_kernel,
-        grid=(tiles,),
+        grid=(depth // slab,),
         in_specs=[
-            pl.BlockSpec(slots.shape, lambda j: (0, 0)),
-            pl.BlockSpec((rows, depth), lambda j: (0, 0)),
-            pl.BlockSpec((depth, tile), lambda j: (0, j)),
+            pl.BlockSpec(slots.shape, lambda k: (0, 0)),
+            pl.BlockSpec((rows, slab), lambda k: (0, k)),
+            pl.BlockSpec((slab, modes), lambda k: (k, 0)),
         ],
         out_specs=[
-            pl.BlockSpec((1, rows, tile // 2), lambda j: (j, 0, 0)),
-            pl.BlockSpec((1, rows, tile // 2), lambda j: (j, 0, 0)),
+            pl.BlockSpec(piece.shape, lambda k: (0, 0, 0)),
+            pl.BlockSpec(piece.shape, lambda k: (0, 0, 0)),
         ],
         out_shape=[piece, piece],
-        scratch_shapes=[pltpu.VMEM((rows, depth), jnp.bfloat16)],
+        scratch_shapes=[
+            pltpu.VMEM((depth // 128, rows, 128), jnp.float32),
+            pltpu.VMEM((rows, modes), jnp.float32),
+        ],
         compiler_params=pltpu.CompilerParams(dimension_semantics=("arbitrary",)),
         cost_estimate=pl.CostEstimate(
             flops=2 * rows * depth * modes,

time: 51.3 us -> 53.2 us (1.037)
  Pallas kernels: 14.8 us -> 16.6 us
    pallas_call x1, Pallas kernels: 8.44 us -> 10.2 us  [listed_matmul(): pl.pallas_call(matmul_kernel, grid=(depth // slab,), in_specs=[pl.BlockSp...]
where the time goes in v14:
time: 53.2 us; the launch traced here: 52.8 us
  Pallas kernels  16.6 us (31%)
  starting transfers between devices  15.5 us (29%)
  waiting for transfers between devices  12.5 us (23%)
  local copies, waits for them, and re-layouts  4.8 us (9%)
  other arithmetic  2.81 us (5%)
  between operations  0.67 us (1%)
    all_to_all x1, starting transfers between devices, gather_tm(): return lax.all_to_all(copies, 'tm', 0, 0, tiled=True)  10.5 us
    pallas_call x1, Pallas kernels, listed_matmul(): pl.pallas_call(matmul_kernel, grid=(depth // slab,), in_specs=[pl.BlockSp...  10.2 us
    all_to_all x1, waiting for transfers between devices, gather_tm(): return lax.all_to_all(copies, 'tm', 0, 0, tiled=True)  9.19 us
    ppermute x3, starting transfers between devices, sensor_reduce_scatter(): parts.append(lax.ppermute(part, 'sensor', perm))  4.93 us
    pallas_call x1, Pallas kernels, local_scans(): pl.pallas_call(scan_kernel, out_shape=[shape] * 2 + [jax.ShapeDtypeStruct...  2.33 us
    pallas_call x1, Pallas kernels, combine(): pl.pallas_call(combine_kernel, out_shape=[shape, shape], cost_estimate=pl...  2.08 us
    ppermute x3, waiting for transfers between devices, sensor_reduce_scatter(): parts.append(lax.ppermute(part, 'sensor', perm))  1.92 us
    pallas_call x1, Pallas kernels, gain_scans(): pl.pallas_call(gain_scan_kernel, out_shape=[shape] * 3 + [jax.ShapeDtypeS...  1.91 us
  transfers between devices with their start and end apart: 5, of which 4 were waited for; matrix products, arithmetic and copies ran while one was open for 9% of the time, Pallas kernels for 4%

profile of v14, /device:TPU:8, one launch (start us, length us, event | category | flops | bytes accessed | tf_op | source)
XLA Modules:
  0.0 52.8 jit_solution(15275575446258587754)
XLA Ops:
  0.6 0.0 copy-start
  0.6 10.2 %shard_map.86 = (f32[4,256,128]{2,1,0:T(8,128)}, f32[4,256,128]{2,1,0:T(8,128)}) custom-call(s32[16,256]{1,0:T(8,128)} %bitcast.11, bf16[256,4096]{1,0:T(8,128)(2,1)} %obs_ref.1, bf16[4096,1024]{1,0:T(8,128)(2,1)} %gain_ref.1), custom_call_target="tpu_custom_call" | custom-call | flops 2147483648 | bytes 11534336 | tf_op jit(solution)/shard_map/pallas_call | solution.py:181
  10.9 0.0 collective-permute-start
  10.9 0.8 %dynamic_slice.31 = f32[128]{0:T(128)S(1)} dynamic-slice(f32[1024]{0:T(1024)} %param.12, s32[]{:T(128)S(6)} %select_n.42), dynamic_slice_sizes={128} | dynamic-slice | bytes 1028 | tf_op jit(solution)/shard_map/dynamic_slice | solution.py:237
  11.7 1.4 %collective-permute-done = f32[4,256,128]{2,1,0:T(8,128)S(1)} collective-permute-done((f32[4,256,128]{2,1,0:T(8,128)}, f32[4,256,128]{2,1,0:T(8,128)S(1)}, u32[]{:S(2)}, u32[]{:S(2)}) %collective-permute-start) | collective-permute-done | bytes 524320 | tf_op jit(solution)/shard_map/ppermute | solution.py:212
  13.0 1.1 %add.53 = f32[4,256,128]{2,1,0:T(8,128)S(1)} add(f32[4,256,128]{2,1,0:T(8,128)} %get-tuple-element.11, f32[4,256,128]{2,1,0:T(8,128)S(1)} %collective-permute-done) | non-fusion elementwise | flops 131072 | bytes 1572864 | tf_op jit(solution)/shard_map/add | solution.py:212
  14.1 0.7 %dynamic-slice_bitcast_fusion = (f32[256,128]{1,0:T(8,128)S(1)}, f32[256,128]{1,0:T(8,128)S(1)}, f32[256,128]{1,0:T(8,128)S(1)}, f32[256,128]{1,0:T(8,128)}) fusion(f32[4,256,128]{2,1,0:T(8,128)S(1)} %add.53, s32[]{:T(128)S(6)} %select_n.50, s32[]{:T(128)S(6)} %select_n.48, s32[]{:T(128)S(6)} %select_n.46, s32[]{:T(128)S(6)} %select_n.44), kind=kLoop, calls=%fused_computation.1 | loop fusion | bytes 1048592 | tf_op jit(solution)/shard_map/jit(dynamic_index_in_dim)/squeeze | solution.py:215
  14.8 1.6 %collective-permute-start.1 = (f32[256,128]{1,0:T(8,128)S(1)}, f32[256,128]{1,0:T(8,128)S(1)}, u32[]{:S(2)}, u32[]{:S(2)}) collective-permute-start(f32[256,128]{1,0:T(8,128)S(1)} %get-tuple-element.24), channel_id=1, source_target_pairs={{0,2},{1,3},{2,4},{3,5},{4,6},{5,7},{6,0},{7,1},{8,10},{9,11},{10,... | collective-permute-start | bytes 393224 | tf_op jit(solution)/shard_map/ppermute | solution.py:217
  16.4 2.6 %collective-permute-start.2 = (f32[256,128]{1,0:T(8,128)S(1)}, f32[256,128]{1,0:T(8,128)S(1)}, u32[]{:S(2)}, u32[]{:S(2)}) collective-permute-start(f32[256,128]{1,0:T(8,128)S(1)} %get-tuple-element.23), channel_id=1, source_target_pairs={{0,4},{1,5},{2,6},{3,7},{4,0},{5,1},{6,2},{7,3},{8,12},{9,13},{10,... | collective-permute-start | bytes 393224 | tf_op jit(solution)/shard_map/ppermute | solution.py:217
  19.0 0.7 %collective-permute-start.3 = (f32[256,128]{1,0:T(8,128)S(1)}, f32[256,128]{1,0:T(8,128)S(1)}, u32[]{:S(2)}, u32[]{:S(2)}) collective-permute-start(f32[256,128]{1,0:T(8,128)S(1)} %get-tuple-element.22), channel_id=1, source_target_pairs={{0,6},{1,7},{2,0},{3,1},{4,2},{5,3},{6,4},{7,5},{8,14},{9,15},{10,... | collective-permute-start | bytes 393224 | tf_op jit(solution)/shard_map/ppermute | solution.py:217
  19.7 1.7 %broadcast_multiply_fusion = (f32[256,128]{1,0:T(8,128)}, f32[256,128]{1,0:T(8,128)}) fusion(f32[128]{0:T(128)S(1)} %dynamic_slice.31, f32[256,1024]{1,0:T(8,128)} %param.11, s32[]{:T(128)S(6)} %select_n.42, pred[256]{0:T(512)(128)(4,1)S(1)} %add_compare_fusion), kind=kLoop, calls=%fused_computation.5 | loop fusion | flops 65536 | bytes 393988 | tf_op jit(solution)/shard_map/mul | solution.py:242
  21.4 0.0 copy-done
  21.4 0.7 %constant_dynamic-slice_fusion.a_ref = f32[256,128]{1,0:T(8,128)} fusion(f32[256,1024]{1,0:T(8,128)S(1)} %copy-done, s32[]{:T(128)S(6)} %select_n.42), kind=kLoop, calls=%fused_computation.6 | loop fusion | bytes 262148 | tf_op jit(solution)/shard_map/dynamic_slice | solution.py:235
  22.1 1.9 %shard_map.87 = (f32[256,128]{1,0:T(8,128)}, f32[256,128]{1,0:T(8,128)}, f32[256,128]{1,0:T(8,128)}, f32[8,128]{1,0:T(8,128)}) custom-call(f32[256,128]{1,0:T(8,128)} %constant_dynamic-slice_fusion.a_ref, f32[256,128]{1,0:T(8,128)} %get-tuple-element.21.g_ref, f32[256,128]{1,0:T(8,128)} %get-tuple-element.20.s_ref), custom_call_target="tpu_custom_call" | custom-call | flops 655360 | bytes 786432 | tf_op jit(solution)/shard_map/pallas_call | solution.py:68
  24.0 0.0 collective-permute-done.1.r1_ref
  24.0 0.0 copy-start.2
  24.0 0.2 collective-permute-done.2.r2_ref
  24.3 0.0 copy-start.3
  24.3 1.7 %collective-permute-done.3.r3_ref = f32[256,128]{1,0:T(8,128)S(1)} collective-permute-done((f32[256,128]{1,0:T(8,128)S(1)}, f32[256,128]{1,0:T(8,128)S(1)}, u32[]{:S(2)}, u32[]{:S(2)}) %collective-permute-start.3) | collective-permute-done | bytes 131104 | tf_op jit(solution)/shard_map/ppermute | solution.py:217
  26.0 0.0 copy-start.4
  26.0 0.0 copy-done.2
  26.0 0.0 copy-done.3
  26.0 0.6 %copy-done.4 = f32[256,128]{1,0:T(8,128)} copy-done((f32[256,128]{1,0:T(8,128)}, f32[256,128]{1,0:T(8,128)S(1)}, u32[]{:S(2)}) %copy-start.4) | copy-done | bytes 131096
  26.6 2.3 %shard_map.88 = (f32[256,128]{1,0:T(8,128)}, f32[256,128]{1,0:T(8,128)}, f32[32,8,128]{2,1,0:T(8,128)}) custom-call(f32[256,128]{1,0:T(8,128)} %constant_dynamic-slice_fusion.a_ref, f32[256,128]{1,0:T(8,128)} %get-tuple-element.25.own_ref, f32[256,128]{1,0:T(8,128)} %copy-done.2, f32[256,128]{1,0:T(8,128)} %copy-done.3, f32[256,128]{1,0:T(8,128)} %copy-done.4, ...), custom_call_target="tpu_custom_call" | custom-call | flops 655360 | bytes 1310720 | tf_op jit(solution)/shard_map/pallas_call | solution.py:97
  28.9 10.5 %all-to-all-start = ((f32[32,8,128]{2,1,0:T(8,128)}), f32[32,8,128]{2,1,0:T(8,128)S(1)}, u32[]{:S(2)}, u32[]{:S(2)}) async-start(f32[32,8,128]{2,1,0:T(8,128)} %get-tuple-element.14), calls=%async_computation | async-start | bytes 262144 | tf_op jit(solution)/shard_map/all_to_all | solution.py:222
  39.5 1.4 %dynamic-slice_bitcast_fusion.4.init_ref = f32[1,128]{1,0:T(1,128)} fusion(f32[1024]{0:T(1024)} %param.13, s32[]{:T(128)S(6)} %select_n.42), kind=kLoop, calls=%fused_computation.8 | loop fusion | bytes 1028 | tf_op jit(solution)/shard_map/broadcast_in_dim | solution.py:248
  40.8 9.2 %all-to-all-done.every_ref = f32[32,8,128]{2,1,0:T(8,128)S(1)} async-done(((f32[32,8,128]{2,1,0:T(8,128)}), f32[32,8,128]{2,1,0:T(8,128)S(1)}, u32[]{:S(2)}, u32[]{:S(2)}) %all-to-all-start) | async-done | bytes 131104 | tf_op jit(solution)/shard_map/all_to_all | solution.py:222
  50.0 0.0 copy-start.1
  50.0 0.7 %copy-done.1 = f32[32,8,128]{2,1,0:T(8,128)} copy-done((f32[32,8,128]{2,1,0:T(8,128)}, f32[32,8,128]{2,1,0:T(8,128)S(1)}, u32[]{:S(2)}) %copy-start.1) | copy-done | bytes 131096
  50.7 2.1 %shard_map.89 = (f32[256,128]{1,0:T(8,128)}, f32[256,128]{1,0:T(8,128)}) custom-call(f32[32,8,128]{2,1,0:T(8,128)} %copy-done.1, f32[1,128]{1,0:T(1,128)} %dynamic-slice_bitcast_fusion.4.init_ref, f32[256,128]{1,0:T(8,128)} %get-tuple-element.15.pf_ref, f32[256,128]{1,0:T(8,128)} %get-tuple-element.16.lf_ref, f32[256,128]{1,0:T(8,128)} %get-tuple-element.17.pb_ref, ...), custom_call_target="tpu_custom_call" | custom-call | flops 163840 | bytes 917504 | tf_op jit(solution)/shard_map/pallas_call | solution.py:126
  (1 shorter events, 0.0 us)
Async XLA Ops:
  0.6 20.8 %copy-start = (f32[256,1024]{1,0:T(8,128)S(1)}, f32[256,1024]{1,0:T(8,128)}, u32[]{:S(2)}) copy-start(f32[256,1024]{1,0:T(8,128)} %param.10) | copy-start | bytes 3145732
  10.9 2.1 %collective-permute-start = (f32[4,256,128]{2,1,0:T(8,128)}, f32[4,256,128]{2,1,0:T(8,128)S(1)}, u32[]{:S(2)}, u32[]{:S(2)}) collective-permute-start(f32[4,256,128]{2,1,0:T(8,128)} %get-tuple-element.12), channel_id=1, source_target_pairs={{0,1},{1,0},{2,3},{3,2},{4,5},{5,4},{6,7},{7,6},{8,9},{9,8},{10,11... | collective-permute-start | bytes 1572872 | tf_op jit(solution)/shard_map/ppermute | solution.py:212
  14.8 9.2 %collective-permute-start.1 = (f32[256,128]{1,0:T(8,128)S(1)}, f32[256,128]{1,0:T(8,128)S(1)}, u32[]{:S(2)}, u32[]{:S(2)}) collective-permute-start(f32[256,128]{1,0:T(8,128)S(1)} %get-tuple-element.24), channel_id=1, source_target_pairs={{0,2},{1,3},{2,4},{3,5},{4,6},{5,7},{6,0},{7,1},{8,10},{9,11},{10,... | collective-permute-start | bytes 393224 | tf_op jit(solution)/shard_map/ppermute | solution.py:217
  16.4 7.9 %collective-permute-start.2 = (f32[256,128]{1,0:T(8,128)S(1)}, f32[256,128]{1,0:T(8,128)S(1)}, u32[]{:S(2)}, u32[]{:S(2)}) collective-permute-start(f32[256,128]{1,0:T(8,128)S(1)} %get-tuple-element.23), channel_id=1, source_target_pairs={{0,4},{1,5},{2,6},{3,7},{4,0},{5,1},{6,2},{7,3},{8,12},{9,13},{10,... | collective-permute-start | bytes 393224 | tf_op jit(solution)/shard_map/ppermute | solution.py:217
  19.0 6.9 %collective-permute-start.3 = (f32[256,128]{1,0:T(8,128)S(1)}, f32[256,128]{1,0:T(8,128)S(1)}, u32[]{:S(2)}, u32[]{:S(2)}) collective-permute-start(f32[256,128]{1,0:T(8,128)S(1)} %get-tuple-element.22), channel_id=1, source_target_pairs={{0,6},{1,7},{2,0},{3,1},{4,2},{5,3},{6,4},{7,5},{8,14},{9,15},{10,... | collective-permute-start | bytes 393224 | tf_op jit(solution)/shard_map/ppermute | solution.py:217
  24.0 1.9 %copy-start.2 = (f32[256,128]{1,0:T(8,128)}, f32[256,128]{1,0:T(8,128)S(1)}, u32[]{:S(2)}) copy-start(f32[256,128]{1,0:T(8,128)S(1)} %collective-permute-done.1.r1_ref) | copy-start | bytes 393220
  24.3 1.7 %copy-start.3 = (f32[256,128]{1,0:T(8,128)}, f32[256,128]{1,0:T(8,128)S(1)}, u32[]{:S(2)}) copy-start(f32[256,128]{1,0:T(8,128)S(1)} %collective-permute-done.2.r2_ref) | copy-start | bytes 393220
  26.0 0.6 %copy-start.4 = (f32[256,128]{1,0:T(8,128)}, f32[256,128]{1,0:T(8,128)S(1)}, u32[]{:S(2)}) copy-start(f32[256,128]{1,0:T(8,128)S(1)} %collective-permute-done.3.r3_ref) | copy-start | bytes 393220
  28.9 21.1 %all-to-all-start = ((f32[32,8,128]{2,1,0:T(8,128)}), f32[32,8,128]{2,1,0:T(8,128)S(1)}, u32[]{:S(2)}, u32[]{:S(2)}) async-start(f32[32,8,128]{2,1,0:T(8,128)} %get-tuple-element.14), calls=%async_computation | async-start | bytes 262144 | tf_op jit(solution)/shard_map/all_to_all | solution.py:222
  50.0 0.7 %copy-start.1 = (f32[32,8,128]{2,1,0:T(8,128)}, f32[32,8,128]{2,1,0:T(8,128)S(1)}, u32[]{:S(2)}) copy-start(f32[32,8,128]{2,1,0:T(8,128)S(1)} %all-to-all-done.every_ref) | copy-start | bytes 393220

commit v15 on v13

--- a/solution.py
+++ b/solution.py
@@ -104,18 +104,29 @@
 def combine_kernel(every_ref, init_ref, pf_ref, lf_ref, pb_ref, bl_ref, bp_ref, f_ref, s_ref):
     count = every_ref.shape[0]
     place = lax.axis_index("tm")
-    entering = [init_ref[...]]
-    for k in range(count - 1):
-        tile = every_ref[k]
-        entering.append(tile[0:1] * entering[-1] + tile[1:2])
-    after = jnp.zeros_like(entering[0])
-    e_here = jnp.where(place == count - 1, entering[count - 1], 0.0)
-    y_here = jnp.zeros_like(after)
-    for k in range(count - 1, 0, -1):
-        tile = every_ref[k]
-        after = tile[3:4] + tile[4:5] * entering[k] + tile[2:3] * after
-        e_here = jnp.where(place == k - 1, entering[k - 1], e_here)
-        y_here = jnp.where(place == k - 1, after, y_here)
+    prod, local, back_gain, back_local, back_prod = (every_ref[:, r, :] for r in range(5))
+    row = lax.broadcasted_iota(jnp.int32, prod.shape, 0)
+    step = 1
+    while step < count:
+        earlier_a = pltpu.roll(prod, step, 0)
+        earlier_x = pltpu.roll(local, step, 0)
+        inside = row >= step
+        local = jnp.where(inside, prod * earlier_x + local, local)
+        prod = jnp.where(inside, prod * earlier_a, prod)
+        step *= 2
+    initial = init_ref[...]
+    entering = jnp.where(row == 0, initial, pltpu.roll(prod * initial + local, 1, 0))
+    gain, after = back_gain, back_local + back_prod * entering
+    step = 1
+    while step < count:
+        later_a = pltpu.roll(gain, count - step, 0)
+        later_x = pltpu.roll(after, count - step, 0)
+        inside = row < count - step
+        after = jnp.where(inside, gain * later_x + after, after)
+        gain = jnp.where(inside, gain * later_a, gain)
+        step *= 2
+    e_here = jnp.sum(jnp.where(row == place, entering, 0.0), axis=0, keepdims=True)
+    y_here = jnp.sum(jnp.where(row == place + 1, after, 0.0), axis=0, keepdims=True)
     f_ref[...] = lf_ref[...] + pf_ref[...] * e_here
     s_ref[...] = bl_ref[...] + bp_ref[...] * e_here + pb_ref[...] * y_here
 

time: 51.3 us -> 51.2 us (level)
  no operation moved by 1% of the time
where the time goes in v15:
time: 51.2 us; the launch traced here: 50.9 us
  starting transfers between devices  15.5 us (30%)
  Pallas kernels  14.7 us (29%)
  waiting for transfers between devices  12.5 us (24%)
  local copies, waits for them, and re-layouts  4.8 us (9%)
  other arithmetic  2.81 us (5%)
  between operations  0.67 us (1%)
    all_to_all x1, starting transfers between devices, gather_tm(): return lax.all_to_all(copies, 'tm', 0, 0, tiled=True)  10.5 us
    all_to_all x1, waiting for transfers between devices, gather_tm(): return lax.all_to_all(copies, 'tm', 0, 0, tiled=True)  9.19 us
    pallas_call x1, Pallas kernels, listed_matmul(): pl.pallas_call(matmul_kernel, grid=(tiles,), in_specs=[pl.BlockSpec(slots...  8.44 us
    ppermute x3, starting transfers between devices, sensor_reduce_scatter(): parts.append(lax.ppermute(part, 'sensor', perm))  4.93 us
    pallas_call x1, Pallas kernels, local_scans(): pl.pallas_call(scan_kernel, out_shape=[shape] * 2 + [jax.ShapeDtypeStruct...  2.33 us
    pallas_call x1, Pallas kernels, combine(): pl.pallas_call(combine_kernel, out_shape=[shape, shape], cost_estimate=pl...  1.98 us
    ppermute x3, waiting for transfers between devices, sensor_reduce_scatter(): parts.append(lax.ppermute(part, 'sensor', perm))  1.92 us
    pallas_call x1, Pallas kernels, gain_scans(): pl.pallas_call(gain_scan_kernel, out_shape=[shape] * 3 + [jax.ShapeDtypeS...  1.91 us
  transfers between devices with their start and end apart: 5, of which 4 were waited for; matrix products, arithmetic and copies ran while one was open for 9% of the time, Pallas kernels for 4%

profile of v15, /device:TPU:8, one launch (start us, length us, event | category | flops | bytes accessed | tf_op | source)
XLA Modules:
  0.0 50.9 jit_solution(5064661444045794575)
XLA Ops:
  0.6 0.0 copy-start
  0.6 8.4 %shard_map.86 = (f32[4,256,128]{2,1,0:T(8,128)}, f32[4,256,128]{2,1,0:T(8,128)}) custom-call(s32[16,256]{1,0:T(8,128)} %bitcast.11, bf16[256,4096]{1,0:T(8,128)(2,1)} %obs_ref.1, bf16[4096,1024]{1,0:T(8,128)(2,1)} %gain_ref.1), custom_call_target="tpu_custom_call" | custom-call | flops 2147483648 | bytes 11534336 | tf_op jit(solution)/shard_map/pallas_call | solution.py:176
  9.1 0.0 collective-permute-start
  9.1 0.8 %dynamic_slice.31 = f32[128]{0:T(128)S(1)} dynamic-slice(f32[1024]{0:T(1024)} %param.12, s32[]{:T(128)S(6)} %select_n.42), dynamic_slice_sizes={128} | dynamic-slice | bytes 1028 | tf_op jit(solution)/shard_map/dynamic_slice | solution.py:229
  9.9 1.4 %collective-permute-done = f32[4,256,128]{2,1,0:T(8,128)S(1)} collective-permute-done((f32[4,256,128]{2,1,0:T(8,128)}, f32[4,256,128]{2,1,0:T(8,128)S(1)}, u32[]{:S(2)}, u32[]{:S(2)}) %collective-permute-start) | collective-permute-done | bytes 524320 | tf_op jit(solution)/shard_map/ppermute | solution.py:204
  11.2 1.1 %add.53 = f32[4,256,128]{2,1,0:T(8,128)S(1)} add(f32[4,256,128]{2,1,0:T(8,128)} %get-tuple-element.11, f32[4,256,128]{2,1,0:T(8,128)S(1)} %collective-permute-done) | non-fusion elementwise | flops 131072 | bytes 1572864 | tf_op jit(solution)/shard_map/add | solution.py:204
  12.3 0.7 %dynamic-slice_bitcast_fusion = (f32[256,128]{1,0:T(8,128)S(1)}, f32[256,128]{1,0:T(8,128)S(1)}, f32[256,128]{1,0:T(8,128)S(1)}, f32[256,128]{1,0:T(8,128)}) fusion(f32[4,256,128]{2,1,0:T(8,128)S(1)} %add.53, s32[]{:T(128)S(6)} %select_n.50, s32[]{:T(128)S(6)} %select_n.48, s32[]{:T(128)S(6)} %select_n.46, s32[]{:T(128)S(6)} %select_n.44), kind=kLoop, calls=%fused_computation.1 | loop fusion | bytes 1048592 | tf_op jit(solution)/shard_map/jit(dynamic_index_in_dim)/squeeze | solution.py:207
  13.0 1.6 %collective-permute-start.1 = (f32[256,128]{1,0:T(8,128)S(1)}, f32[256,128]{1,0:T(8,128)S(1)}, u32[]{:S(2)}, u32[]{:S(2)}) collective-permute-start(f32[256,128]{1,0:T(8,128)S(1)} %get-tuple-element.24), channel_id=1, source_target_pairs={{0,2},{1,3},{2,4},{3,5},{4,6},{5,7},{6,0},{7,1},{8,10},{9,11},{10,... | collective-permute-start | bytes 393224 | tf_op jit(solution)/shard_map/ppermute | solution.py:209
  14.6 2.6 %collective-permute-start.2 = (f32[256,128]{1,0:T(8,128)S(1)}, f32[256,128]{1,0:T(8,128)S(1)}, u32[]{:S(2)}, u32[]{:S(2)}) collective-permute-start(f32[256,128]{1,0:T(8,128)S(1)} %get-tuple-element.23), channel_id=1, source_target_pairs={{0,4},{1,5},{2,6},{3,7},{4,0},{5,1},{6,2},{7,3},{8,12},{9,13},{10,... | collective-permute-start | bytes 393224 | tf_op jit(solution)/shard_map/ppermute | solution.py:209
  17.2 0.7 %collective-permute-start.3 = (f32[256,128]{1,0:T(8,128)S(1)}, f32[256,128]{1,0:T(8,128)S(1)}, u32[]{:S(2)}, u32[]{:S(2)}) collective-permute-start(f32[256,128]{1,0:T(8,128)S(1)} %get-tuple-element.22), channel_id=1, source_target_pairs={{0,6},{1,7},{2,0},{3,1},{4,2},{5,3},{6,4},{7,5},{8,14},{9,15},{10,... | collective-permute-start | bytes 393224 | tf_op jit(solution)/shard_map/ppermute | solution.py:209
  17.9 1.7 %broadcast_multiply_fusion = (f32[256,128]{1,0:T(8,128)}, f32[256,128]{1,0:T(8,128)}) fusion(f32[128]{0:T(128)S(1)} %dynamic_slice.31, f32[256,1024]{1,0:T(8,128)} %param.11, s32[]{:T(128)S(6)} %select_n.42, pred[256]{0:T(512)(128)(4,1)S(1)} %add_compare_fusion), kind=kLoop, calls=%fused_computation.5 | loop fusion | flops 65536 | bytes 393988 | tf_op jit(solution)/shard_map/mul | solution.py:234
  19.6 0.0 copy-done
  19.7 0.7 %constant_dynamic-slice_fusion.a_ref = f32[256,128]{1,0:T(8,128)} fusion(f32[256,1024]{1,0:T(8,128)S(1)} %copy-done, s32[]{:T(128)S(6)} %select_n.42), kind=kLoop, calls=%fused_computation.6 | loop fusion | bytes 262148 | tf_op jit(solution)/shard_map/dynamic_slice | solution.py:227
  20.3 1.9 %shard_map.87 = (f32[256,128]{1,0:T(8,128)}, f32[256,128]{1,0:T(8,128)}, f32[256,128]{1,0:T(8,128)}, f32[8,128]{1,0:T(8,128)}) custom-call(f32[256,128]{1,0:T(8,128)} %constant_dynamic-slice_fusion.a_ref, f32[256,128]{1,0:T(8,128)} %get-tuple-element.21.g_ref, f32[256,128]{1,0:T(8,128)} %get-tuple-element.20.s_ref), custom_call_target="tpu_custom_call" | custom-call | flops 655360 | bytes 786432 | tf_op jit(solution)/shard_map/pallas_call | solution.py:68
  22.2 0.0 collective-permute-done.1.r1_ref
  22.2 0.0 copy-start.2
  22.2 0.2 collective-permute-done.2.r2_ref
  22.5 0.0 copy-start.3
  22.5 1.7 %collective-permute-done.3.r3_ref = f32[256,128]{1,0:T(8,128)S(1)} collective-permute-done((f32[256,128]{1,0:T(8,128)S(1)}, f32[256,128]{1,0:T(8,128)S(1)}, u32[]{:S(2)}, u32[]{:S(2)}) %collective-permute-start.3) | collective-permute-done | bytes 131104 | tf_op jit(solution)/shard_map/ppermute | solution.py:209
  24.2 0.0 copy-start.4
  24.2 0.0 copy-done.2
  24.2 0.0 copy-done.3
  24.2 0.6 %copy-done.4 = f32[256,128]{1,0:T(8,128)} copy-done((f32[256,128]{1,0:T(8,128)}, f32[256,128]{1,0:T(8,128)S(1)}, u32[]{:S(2)}) %copy-start.4) | copy-done | bytes 131096
  24.8 2.3 %shard_map.88 = (f32[256,128]{1,0:T(8,128)}, f32[256,128]{1,0:T(8,128)}, f32[32,8,128]{2,1,0:T(8,128)}) custom-call(f32[256,128]{1,0:T(8,128)} %constant_dynamic-slice_fusion.a_ref, f32[256,128]{1,0:T(8,128)} %get-tuple-element.25.own_ref, f32[256,128]{1,0:T(8,128)} %copy-done.2, f32[256,128]{1,0:T(8,128)} %copy-done.3, f32[256,128]{1,0:T(8,128)} %copy-done.4, ...), custom_call_target="tpu_custom_call" | custom-call | flops 655360 | bytes 1310720 | tf_op jit(solution)/shard_map/pallas_call | solution.py:97
  27.1 10.5 %all-to-all-start = ((f32[32,8,128]{2,1,0:T(8,128)}), f32[32,8,128]{2,1,0:T(8,128)S(1)}, u32[]{:S(2)}, u32[]{:S(2)}) async-start(f32[32,8,128]{2,1,0:T(8,128)} %get-tuple-element.14), calls=%async_computation | async-start | bytes 262144 | tf_op jit(solution)/shard_map/all_to_all | solution.py:214
  37.7 1.4 %dynamic-slice_bitcast_fusion.4.init_ref = f32[1,128]{1,0:T(1,128)} fusion(f32[1024]{0:T(1024)} %param.13, s32[]{:T(128)S(6)} %select_n.42), kind=kLoop, calls=%fused_computation.8 | loop fusion | bytes 1028 | tf_op jit(solution)/shard_map/broadcast_in_dim | solution.py:240
  39.0 9.2 %all-to-all-done.every_ref = f32[32,8,128]{2,1,0:T(8,128)S(1)} async-done(((f32[32,8,128]{2,1,0:T(8,128)}), f32[32,8,128]{2,1,0:T(8,128)S(1)}, u32[]{:S(2)}, u32[]{:S(2)}) %all-to-all-start) | async-done | bytes 131104 | tf_op jit(solution)/shard_map/all_to_all | solution.py:214
  48.2 0.0 copy-start.1
  48.2 0.7 %copy-done.1 = f32[32,8,128]{2,1,0:T(8,128)} copy-done((f32[32,8,128]{2,1,0:T(8,128)}, f32[32,8,128]{2,1,0:T(8,128)S(1)}, u32[]{:S(2)}) %copy-start.1) | copy-done | bytes 131096
  48.9 2.0 %shard_map.89 = (f32[256,128]{1,0:T(8,128)}, f32[256,128]{1,0:T(8,128)}) custom-call(f32[32,8,128]{2,1,0:T(8,128)} %copy-done.1, f32[1,128]{1,0:T(1,128)} %dynamic-slice_bitcast_fusion.4.init_ref, f32[256,128]{1,0:T(8,128)} %get-tuple-element.15.pf_ref, f32[256,128]{1,0:T(8,128)} %get-tuple-element.16.lf_ref, f32[256,128]{1,0:T(8,128)} %get-tuple-element.17.pb_ref, ...), custom_call_target="tpu_custom_call" | custom-call | flops 163840 | bytes 917504 | tf_op jit(solution)/shard_map/pallas_call | solution.py:137
  (1 shorter events, 0.0 us)
Async XLA Ops:
  0.6 19.0 %copy-start = (f32[256,1024]{1,0:T(8,128)S(1)}, f32[256,1024]{1,0:T(8,128)}, u32[]{:S(2)}) copy-start(f32[256,1024]{1,0:T(8,128)} %param.10) | copy-start | bytes 3145732
  9.1 2.1 %collective-permute-start = (f32[4,256,128]{2,1,0:T(8,128)}, f32[4,256,128]{2,1,0:T(8,128)S(1)}, u32[]{:S(2)}, u32[]{:S(2)}) collective-permute-start(f32[4,256,128]{2,1,0:T(8,128)} %get-tuple-element.12), channel_id=1, source_target_pairs={{0,1},{1,0},{2,3},{3,2},{4,5},{5,4},{6,7},{7,6},{8,9},{9,8},{10,11... | collective-permute-start | bytes 1572872 | tf_op jit(solution)/shard_map/ppermute | solution.py:204
  13.0 9.2 %collective-permute-start.1 = (f32[256,128]{1,0:T(8,128)S(1)}, f32[256,128]{1,0:T(8,128)S(1)}, u32[]{:S(2)}, u32[]{:S(2)}) collective-permute-start(f32[256,128]{1,0:T(8,128)S(1)} %get-tuple-element.24), channel_id=1, source_target_pairs={{0,2},{1,3},{2,4},{3,5},{4,6},{5,7},{6,0},{7,1},{8,10},{9,11},{10,... | collective-permute-start | bytes 393224 | tf_op jit(solution)/shard_map/ppermute | solution.py:209
  14.6 7.9 %collective-permute-start.2 = (f32[256,128]{1,0:T(8,128)S(1)}, f32[256,128]{1,0:T(8,128)S(1)}, u32[]{:S(2)}, u32[]{:S(2)}) collective-permute-start(f32[256,128]{1,0:T(8,128)S(1)} %get-tuple-element.23), channel_id=1, source_target_pairs={{0,4},{1,5},{2,6},{3,7},{4,0},{5,1},{6,2},{7,3},{8,12},{9,13},{10,... | collective-permute-start | bytes 393224 | tf_op jit(solution)/shard_map/ppermute | solution.py:209
  17.2 6.9 %collective-permute-start.3 = (f32[256,128]{1,0:T(8,128)S(1)}, f32[256,128]{1,0:T(8,128)S(1)}, u32[]{:S(2)}, u32[]{:S(2)}) collective-permute-start(f32[256,128]{1,0:T(8,128)S(1)} %get-tuple-element.22), channel_id=1, source_target_pairs={{0,6},{1,7},{2,0},{3,1},{4,2},{5,3},{6,4},{7,5},{8,14},{9,15},{10,... | collective-permute-start | bytes 393224 | tf_op jit(solution)/shard_map/ppermute | solution.py:209
  22.2 1.9 %copy-start.2 = (f32[256,128]{1,0:T(8,128)}, f32[256,128]{1,0:T(8,128)S(1)}, u32[]{:S(2)}) copy-start(f32[256,128]{1,0:T(8,128)S(1)} %collective-permute-done.1.r1_ref) | copy-start | bytes 393220
  22.5 1.7 %copy-start.3 = (f32[256,128]{1,0:T(8,128)}, f32[256,128]{1,0:T(8,128)S(1)}, u32[]{:S(2)}) copy-start(f32[256,128]{1,0:T(8,128)S(1)} %collective-permute-done.2.r2_ref) | copy-start | bytes 393220
  24.2 0.6 %copy-start.4 = (f32[256,128]{1,0:T(8,128)}, f32[256,128]{1,0:T(8,128)S(1)}, u32[]{:S(2)}) copy-start(f32[256,128]{1,0:T(8,128)S(1)} %collective-permute-done.3.r3_ref) | copy-start | bytes 393220
  27.1 21.1 %all-to-all-start = ((f32[32,8,128]{2,1,0:T(8,128)}), f32[32,8,128]{2,1,0:T(8,128)S(1)}, u32[]{:S(2)}, u32[]{:S(2)}) async-start(f32[32,8,128]{2,1,0:T(8,128)} %get-tuple-element.14), calls=%async_computation | async-start | bytes 262144 | tf_op jit(solution)/shard_map/all_to_all | solution.py:214
  48.2 0.7 %copy-start.1 = (f32[32,8,128]{2,1,0:T(8,128)}, f32[32,8,128]{2,1,0:T(8,128)S(1)}, u32[]{:S(2)}) copy-start(f32[32,8,128]{2,1,0:T(8,128)S(1)} %all-to-all-done.every_ref) | copy-start | bytes 393220

commit v16 on v13

--- a/solution.py
+++ b/solution.py
@@ -99,35 +99,6 @@
         out_shape=[shape] * 2 + [jax.ShapeDtypeStruct((blocks, SUB, cols), jnp.float32)],
         cost_estimate=pl.CostEstimate(flops=20 * rows * cols, bytes_accessed=40 * rows * cols, transcendentals=0),
     )(factors, *parts, step_gain, scale, part)
-
-
-def combine_kernel(every_ref, init_ref, pf_ref, lf_ref, pb_ref, bl_ref, bp_ref, f_ref, s_ref):
-    count = every_ref.shape[0]
-    place = lax.axis_index("tm")
-    entering = [init_ref[...]]
-    for k in range(count - 1):
-        tile = every_ref[k]
-        entering.append(tile[0:1] * entering[-1] + tile[1:2])
-    after = jnp.zeros_like(entering[0])
-    e_here = jnp.where(place == count - 1, entering[count - 1], 0.0)
-    y_here = jnp.zeros_like(after)
-    for k in range(count - 1, 0, -1):
-        tile = every_ref[k]
-        after = tile[3:4] + tile[4:5] * entering[k] + tile[2:3] * after
-        e_here = jnp.where(place == k - 1, entering[k - 1], e_here)
-        y_here = jnp.where(place == k - 1, after, y_here)
-    f_ref[...] = lf_ref[...] + pf_ref[...] * e_here
-    s_ref[...] = bl_ref[...] + bp_ref[...] * e_here + pb_ref[...] * y_here
-
-
-def combine(every, initial, pf, lf, pb, bl, bp):
-    rows, cols = pf.shape
-    shape = jax.ShapeDtypeStruct(pf.shape, jnp.float32)
-    return pl.pallas_call(
-        combine_kernel,
-        out_shape=[shape, shape],
-        cost_estimate=pl.CostEstimate(flops=5 * rows * cols, bytes_accessed=28 * rows * cols, transcendentals=0),
-    )(every, initial, pf, lf, pb, bl, bp)
 
 
 def matmul_kernel(slots_ref, obs_ref, gain_ref, keep_ref, send_ref, lhs_ref):
@@ -225,9 +196,17 @@
     prod_fwd, prod_back, back_prod, part = gain_scans(factors, step_gain, scale)
     local_fwd, back_local, summary = local_scans(factors, parts, step_gain, scale, part, time_count)
     every = gather_tm(summary)
-    filtered, smoothed = combine(
-        every, initial[None, :], prod_fwd, local_fwd, prod_back, back_local, back_prod
-    )
+    entering = [initial]
+    for k in range(time_count - 1):
+        entering.append(every[k, 0] * entering[-1] + every[k, 1])
+    after = [jnp.zeros_like(initial)]
+    for k in range(time_count - 1, 0, -1):
+        after.append(every[k, 3] + every[k, 4] * entering[k] + every[k, 2] * after[-1])
+    after = after[::-1]
+    entering_here = lax.dynamic_index_in_dim(jnp.stack(entering, 0), time_index, 0, False)
+    after_here = lax.dynamic_index_in_dim(jnp.stack(after, 0), time_index, 0, False)
+    filtered = local_fwd + prod_fwd * entering_here[None, :]
+    smoothed = back_local + back_prod * entering_here[None, :] + prod_back * after_here[None, :]
     return (filtered, smoothed)
 
 

time: 51.3 us -> 51.6 us (level)
  other arithmetic: 2.81 us -> 5.6 us
  Pallas kernels: 14.8 us -> 12.7 us
  local copies, waits for them, and re-layouts: 4.8 us -> 3.75 us
    pallas_call x1 -> x0, Pallas kernels: 2.08 us -> none  [combine(): pl.pallas_call(combine_kernel, out_shape=[shape, shape], cost_estimate=pl...]
    add x0 -> x1, other arithmetic: none -> 1.9 us  [per_device(): back_local + back_prod * entering_here[None, :]]
    broadcast_in_dim x1 -> x0, local copies, waits for them, and re-layouts: 1.35 us -> none  [per_device(): initial[None, :]]
    another operation x0 -> x4, local copies, waits for them, and re-layouts: none -> 0.95 us  [the longest x2 0.86 us: per_device(): jnp.stack(entering, 0)]
    another operation x0 -> x1, other arithmetic: none -> 0.89 us  [per_device(): jnp.stack(after, 0)]
    unnamed x10 -> x8, local copies, waits for them, and re-layouts: 1.32 us -> 0.66 us
    all_to_all x1, waiting for transfers between devices: 9.19 us -> 9.77 us  [gather_tm(): return lax.all_to_all(copies, 'tm', 0, 0, tiled=True)]
  transfers between devices with their start and end apart: 5 -> 5, of which waited for: 4 -> 4; matrix products, arithmetic and copies ran while one was open for 9% -> 8% of each run, Pallas kernels for 4% -> 4%
where the time goes in v16:
time: 51.6 us; the launch traced here: 51.2 us
  starting transfers between devices  15.5 us (30%)
  waiting for transfers between devices  13 us (25%)
  Pallas kernels  12.7 us (25%)
  other arithmetic  5.6 us (11%)
  local copies, waits for them, and re-layouts  3.75 us (7%)
  between operations  0.68 us (1%)
    all_to_all x1, starting transfers between devices, gather_tm(): return lax.all_to_all(copies, 'tm', 0, 0, tiled=True)  10.5 us
    all_to_all x1, waiting for transfers between devices, gather_tm(): return lax.all_to_all(copies, 'tm', 0, 0, tiled=True)  9.77 us
    pallas_call x1, Pallas kernels, listed_matmul(): pl.pallas_call(matmul_kernel, grid=(tiles,), in_specs=[pl.BlockSpec(slots...  8.43 us
    ppermute x3, starting transfers between devices, sensor_reduce_scatter(): parts.append(lax.ppermute(part, 'sensor', perm))  4.93 us
    pallas_call x1, Pallas kernels, local_scans(): pl.pallas_call(scan_kernel, out_shape=[shape] * 2 + [jax.ShapeDtypeStruct...  2.31 us
    ppermute x3, waiting for transfers between devices, sensor_reduce_scatter(): parts.append(lax.ppermute(part, 'sensor', perm))  1.92 us
    pallas_call x1, Pallas kernels, gain_scans(): pl.pallas_call(gain_scan_kernel, out_shape=[shape] * 3 + [jax.ShapeDtypeS...  1.91 us
    add x1, other arithmetic, per_device(): back_local + back_prod * entering_here[None, :]  1.9 us
  transfers between devices with their start and end apart: 5, of which 4 were waited for; matrix products, arithmetic and copies ran while one was open for 8% of the time, Pallas kernels for 4%

profile of v16, /device:TPU:8, one launch (start us, length us, event | category | flops | bytes accessed | tf_op | source)
XLA Modules:
  0.0 51.2 jit_solution(2465712699770786593)
XLA Ops:
  0.6 0.0 copy-start
  0.6 8.4 %shard_map.86 = (f32[4,256,128]{2,1,0:T(8,128)}, f32[4,256,128]{2,1,0:T(8,128)}) custom-call(s32[16,256]{1,0:T(8,128)} %bitcast.1102, bf16[256,4096]{1,0:T(8,128)(2,1)} %obs_ref.1, bf16[4096,1024]{1,0:T(8,128)(2,1)} %gain_ref.1), custom_call_target="tpu_custom_call" | custom-call | flops 2147483648 | bytes 11534336 | tf_op jit(solution)/shard_map/pallas_call | solution.py:136
  9.1 0.0 collective-permute-start
  9.1 0.8 %dynamic_slice.38 = f32[128]{0:T(128)S(1)} dynamic-slice(f32[1024]{0:T(1024)} %param.12, s32[]{:T(128)S(6)} %select_n.47), dynamic_slice_sizes={128} | dynamic-slice | bytes 1028 | tf_op jit(solution)/shard_map/dynamic_slice | solution.py:189
  9.8 1.4 %collective-permute-done = f32[4,256,128]{2,1,0:T(8,128)S(1)} collective-permute-done((f32[4,256,128]{2,1,0:T(8,128)}, f32[4,256,128]{2,1,0:T(8,128)S(1)}, u32[]{:S(2)}, u32[]{:S(2)}) %collective-permute-start) | collective-permute-done | bytes 524320 | tf_op jit(solution)/shard_map/ppermute | solution.py:164
  11.2 1.1 %add.346 = f32[4,256,128]{2,1,0:T(8,128)S(1)} add(f32[4,256,128]{2,1,0:T(8,128)} %get-tuple-element.11, f32[4,256,128]{2,1,0:T(8,128)S(1)} %collective-permute-done) | non-fusion elementwise | flops 131072 | bytes 1572864 | tf_op jit(solution)/shard_map/add | solution.py:164
  12.3 0.7 %dynamic-slice_bitcast_fusion = (f32[256,128]{1,0:T(8,128)S(1)}, f32[256,128]{1,0:T(8,128)S(1)}, f32[256,128]{1,0:T(8,128)S(1)}, f32[256,128]{1,0:T(8,128)}) fusion(f32[4,256,128]{2,1,0:T(8,128)S(1)} %add.346, s32[]{:T(128)S(6)} %select_n.55, s32[]{:T(128)S(6)} %select_n.53, s32[]{:T(128)S(6)} %select_n.51, s32[]{:T(128)S(6)} %select_n.49), kind=kLoop, calls=%fused_computation.3 | loop fusion | bytes 1048592 | tf_op jit(solution)/shard_map/jit(dynamic_index_in_dim)/squeeze | solution.py:167
  13.0 1.6 %collective-permute-start.1 = (f32[256,128]{1,0:T(8,128)S(1)}, f32[256,128]{1,0:T(8,128)S(1)}, u32[]{:S(2)}, u32[]{:S(2)}) collective-permute-start(f32[256,128]{1,0:T(8,128)S(1)} %get-tuple-element.86), channel_id=1, source_target_pairs={{0,2},{1,3},{2,4},{3,5},{4,6},{5,7},{6,0},{7,1},{8,10},{9,11},{10,... | collective-permute-start | bytes 393224 | tf_op jit(solution)/shard_map/ppermute | solution.py:169
  14.6 2.6 %collective-permute-start.2 = (f32[256,128]{1,0:T(8,128)S(1)}, f32[256,128]{1,0:T(8,128)S(1)}, u32[]{:S(2)}, u32[]{:S(2)}) collective-permute-start(f32[256,128]{1,0:T(8,128)S(1)} %get-tuple-element.85), channel_id=1, source_target_pairs={{0,4},{1,5},{2,6},{3,7},{4,0},{5,1},{6,2},{7,3},{8,12},{9,13},{10,... | collective-permute-start | bytes 393224 | tf_op jit(solution)/shard_map/ppermute | solution.py:169
  17.2 0.7 %collective-permute-start.3 = (f32[256,128]{1,0:T(8,128)S(1)}, f32[256,128]{1,0:T(8,128)S(1)}, u32[]{:S(2)}, u32[]{:S(2)}) collective-permute-start(f32[256,128]{1,0:T(8,128)S(1)} %get-tuple-element.84), channel_id=1, source_target_pairs={{0,6},{1,7},{2,0},{3,1},{4,2},{5,3},{6,4},{7,5},{8,14},{9,15},{10,... | collective-permute-start | bytes 393224 | tf_op jit(solution)/shard_map/ppermute | solution.py:169
  17.9 1.7 %broadcast_multiply_fusion = (f32[256,128]{1,0:T(8,128)}, f32[256,128]{1,0:T(8,128)}) fusion(f32[128]{0:T(128)S(1)} %dynamic_slice.38, f32[256,1024]{1,0:T(8,128)} %param.11, s32[]{:T(128)S(6)} %select_n.47, pred[256]{0:T(512)(128)(4,1)S(1)} %add_compare_fusion), kind=kLoop, calls=%fused_computation.7 | loop fusion | flops 65536 | bytes 393988 | tf_op jit(solution)/shard_map/mul | solution.py:194
  19.6 0.0 copy-done
  19.6 0.7 %constant_dynamic-slice_fusion.2.a_ref = f32[256,128]{1,0:T(8,128)} fusion(f32[256,1024]{1,0:T(8,128)S(1)} %copy-done, s32[]{:T(128)S(6)} %select_n.47), kind=kLoop, calls=%fused_computation.10 | loop fusion | bytes 262148 | tf_op jit(solution)/shard_map/dynamic_slice | solution.py:187
  20.3 1.9 %shard_map.87 = (f32[256,128]{1,0:T(8,128)}, f32[256,128]{1,0:T(8,128)}, f32[256,128]{1,0:T(8,128)}, f32[8,128]{1,0:T(8,128)}) custom-call(f32[256,128]{1,0:T(8,128)} %constant_dynamic-slice_fusion.2.a_ref, f32[256,128]{1,0:T(8,128)} %get-tuple-element.83.g_ref, f32[256,128]{1,0:T(8,128)} %get-tuple-element.82.s_ref), custom_call_target="tpu_custom_call" | custom-call | flops 655360 | bytes 786432 | tf_op jit(solution)/shard_map/pallas_call | solution.py:68
  22.2 0.0 collective-permute-done.1.r1_ref
  22.2 0.0 copy-start.1
  22.2 0.2 collective-permute-done.2.r2_ref
  22.4 0.0 copy-start.2
  22.5 1.7 %collective-permute-done.3.r3_ref = f32[256,128]{1,0:T(8,128)S(1)} collective-permute-done((f32[256,128]{1,0:T(8,128)S(1)}, f32[256,128]{1,0:T(8,128)S(1)}, u32[]{:S(2)}, u32[]{:S(2)}) %collective-permute-start.3) | collective-permute-done | bytes 131104 | tf_op jit(solution)/shard_map/ppermute | solution.py:169
  24.1 0.0 copy-start.3
  24.1 0.0 copy-done.1
  24.1 0.0 copy-done.2
  24.2 0.6 %copy-done.3 = f32[256,128]{1,0:T(8,128)} copy-done((f32[256,128]{1,0:T(8,128)}, f32[256,128]{1,0:T(8,128)S(1)}, u32[]{:S(2)}) %copy-start.3) | copy-done | bytes 131096
  24.8 2.3 %shard_map.88 = (f32[256,128]{1,0:T(8,128)}, f32[256,128]{1,0:T(8,128)}, f32[32,8,128]{2,1,0:T(8,128)}) custom-call(f32[256,128]{1,0:T(8,128)} %constant_dynamic-slice_fusion.2.a_ref, f32[256,128]{1,0:T(8,128)} %get-tuple-element.87.own_ref, f32[256,128]{1,0:T(8,128)} %copy-done.1, f32[256,128]{1,0:T(8,128)} %copy-done.2, f32[256,128]{1,0:T(8,128)} %copy-done.3, ...), custom_call_target="tpu_custom_call" | custom-call | flops 655360 | bytes 1310720 | tf_op jit(solution)/shard_map/pallas_call | solution.py:97
  27.1 10.5 %all-to-all-start = ((f32[32,8,128]{2,1,0:T(8,128)}), f32[32,8,128]{2,1,0:T(8,128)S(1)}, u32[]{:S(2)}, u32[]{:S(2)}) async-start(f32[32,8,128]{2,1,0:T(8,128)} %get-tuple-element.16), calls=%async_computation | async-start | bytes 262144 | tf_op jit(solution)/shard_map/all_to_all | solution.py:174
  37.6 0.8 %dynamic-slice_bitcast_fusion.4 = f32[1,128]{1,0:T(1,128)S(1)} fusion(f32[1024]{0:T(1024)} %param.13, s32[]{:T(128)S(6)} %select_n.47), kind=kLoop, calls=%fused_computation.356 | loop fusion | bytes 1028 | tf_op jit(solution)/shard_map/stack | solution.py:206
  38.4 9.8 %all-to-all-done = f32[32,8,128]{2,1,0:T(8,128)S(1)} async-done(((f32[32,8,128]{2,1,0:T(8,128)}), f32[32,8,128]{2,1,0:T(8,128)S(1)}, u32[]{:S(2)}, u32[]{:S(2)}) %all-to-all-start) | async-done | bytes 131104 | tf_op jit(solution)/shard_map/all_to_all | solution.py:174
  48.2 0.9 %fusion.188 = (f32[1,128]{1,0:T(1,128)S(1)}, f32[128]{0:T(128)S(1)}, f32[128]{0:T(128)S(1)}, f32[128]{0:T(128)S(1)}, f32[128]{0:T(128)S(1)}, /*index=5*/f32[128]...) fusion(f32[32,8,128]{2,1,0:T(8,128)S(1)} %all-to-all-done, ...), kind=kLoop, calls=%fused_computation.355 | loop fusion | flops 23808 | bytes 111620 | tf_op jit(solution)/shard_map/stack | solution.py:207
  49.1 0.1 stack.259
  49.2 0.1 stack.227
  49.3 1.9 %multiply_add_fusion = (f32[256,128]{1,0:T(8,128)}, f32[256,128]{1,0:T(8,128)}) fusion(f32[256,128]{1,0:T(8,128)} %get-tuple-element.19, f32[256,128]{1,0:T(8,128)} %get-tuple-element.17, f32[256,128]{1,0:T(8,128)} %get-tuple-element.18, f32[128]{0:T(128)S(1)} %get-tuple-element.91, f32[128]{0:T(128)S(1)} %get-tuple-element.90, ...), kind=kLoop, calls=%fused_computation | loop fusion | flops 196608 | bytes 918528 | tf_op jit(solution)/shard_map/add | solution.py:209
  (3 shorter events, 0.0 us)
Async XLA Ops:
  0.6 19.0 %copy-start = (f32[256,1024]{1,0:T(8,128)S(1)}, f32[256,1024]{1,0:T(8,128)}, u32[]{:S(2)}) copy-start(f32[256,1024]{1,0:T(8,128)} %param.10) | copy-start | bytes 3145732
  9.1 2.1 %collective-permute-start = (f32[4,256,128]{2,1,0:T(8,128)}, f32[4,256,128]{2,1,0:T(8,128)S(1)}, u32[]{:S(2)}, u32[]{:S(2)}) collective-permute-start(f32[4,256,128]{2,1,0:T(8,128)} %get-tuple-element.12), channel_id=1, source_target_pairs={{0,1},{1,0},{2,3},{3,2},{4,5},{5,4},{6,7},{7,6},{8,9},{9,8},{10,11... | collective-permute-start | bytes 1572872 | tf_op jit(solution)/shard_map/ppermute | solution.py:164
  13.0 9.2 %collective-permute-start.1 = (f32[256,128]{1,0:T(8,128)S(1)}, f32[256,128]{1,0:T(8,128)S(1)}, u32[]{:S(2)}, u32[]{:S(2)}) collective-permute-start(f32[256,128]{1,0:T(8,128)S(1)} %get-tuple-element.86), channel_id=1, source_target_pairs={{0,2},{1,3},{2,4},{3,5},{4,6},{5,7},{6,0},{7,1},{8,10},{9,11},{10,... | collective-permute-start | bytes 393224 | tf_op jit(solution)/shard_map/ppermute | solution.py:169
  14.6 7.9 %collective-permute-start.2 = (f32[256,128]{1,0:T(8,128)S(1)}, f32[256,128]{1,0:T(8,128)S(1)}, u32[]{:S(2)}, u32[]{:S(2)}) collective-permute-start(f32[256,128]{1,0:T(8,128)S(1)} %get-tuple-element.85), channel_id=1, source_target_pairs={{0,4},{1,5},{2,6},{3,7},{4,0},{5,1},{6,2},{7,3},{8,12},{9,13},{10,... | collective-permute-start | bytes 393224 | tf_op jit(solution)/shard_map/ppermute | solution.py:169
  17.2 6.9 %collective-permute-start.3 = (f32[256,128]{1,0:T(8,128)S(1)}, f32[256,128]{1,0:T(8,128)S(1)}, u32[]{:S(2)}, u32[]{:S(2)}) collective-permute-start(f32[256,128]{1,0:T(8,128)S(1)} %get-tuple-element.84), channel_id=1, source_target_pairs={{0,6},{1,7},{2,0},{3,1},{4,2},{5,3},{6,4},{7,5},{8,14},{9,15},{10,... | collective-permute-start | bytes 393224 | tf_op jit(solution)/shard_map/ppermute | solution.py:169
  22.2 1.9 %copy-start.1 = (f32[256,128]{1,0:T(8,128)}, f32[256,128]{1,0:T(8,128)S(1)}, u32[]{:S(2)}) copy-start(f32[256,128]{1,0:T(8,128)S(1)} %collective-permute-done.1.r1_ref) | copy-start | bytes 393220
  22.4 1.7 %copy-start.2 = (f32[256,128]{1,0:T(8,128)}, f32[256,128]{1,0:T(8,128)S(1)}, u32[]{:S(2)}) copy-start(f32[256,128]{1,0:T(8,128)S(1)} %collective-permute-done.2.r2_ref) | copy-start | bytes 393220
  24.1 0.6 %copy-start.3 = (f32[256,128]{1,0:T(8,128)}, f32[256,128]{1,0:T(8,128)S(1)}, u32[]{:S(2)}) copy-start(f32[256,128]{1,0:T(8,128)S(1)} %collective-permute-done.3.r3_ref) | copy-start | bytes 393220
  27.1 21.1 %all-to-all-start = ((f32[32,8,128]{2,1,0:T(8,128)}), f32[32,8,128]{2,1,0:T(8,128)S(1)}, u32[]{:S(2)}, u32[]{:S(2)}) async-start(f32[32,8,128]{2,1,0:T(8,128)} %get-tuple-element.16), calls=%async_computation | async-start | bytes 262144 | tf_op jit(solution)/shard_map/all_to_all | solution.py:174

commit v17 on v13

--- a/solution.py
+++ b/solution.py
@@ -150,18 +150,21 @@
             lhs_ref[:, cols] = jnp.where(listed[:, b:b + 1] > 0, block, jnp.zeros_like(block))
 
     prod = jnp.dot(lhs_ref[...], gain_ref[...], preferred_element_type=jnp.float32)
-    half = prod.shape[1] // 2
     even = sensor % 2 == 0
-    keep_ref[0] = jnp.where(even, prod[:, :half], prod[:, half:])
-    send_ref[0] = jnp.where(even, prod[:, half:], prod[:, :half])
+    for c in range(keep_ref.shape[0]):
+        left = prod[:, 256 * c:256 * c + 128]
+        right = prod[:, 256 * c + 128:256 * c + 256]
+        keep_ref[c] = jnp.where(even, left, right)
+        send_ref[c] = jnp.where(even, right, left)
 
 
 def listed_matmul(slots, observations, gain_rows):
     rows, depth = observations.shape
     modes = gain_rows.shape[1]
-    tile = 256
+    tile = 512
     tiles = modes // tile
-    piece = jax.ShapeDtypeStruct((tiles, rows, tile // 2), jnp.float32)
+    chips_per_tile = tile // 256
+    piece = jax.ShapeDtypeStruct((modes // 256, rows, 128), jnp.float32)
     return pl.pallas_call(
         matmul_kernel,
         grid=(tiles,),
@@ -171,8 +174,8 @@
             pl.BlockSpec((depth, tile), lambda j: (0, j)),
         ],
         out_specs=[
-            pl.BlockSpec((1, rows, tile // 2), lambda j: (j, 0, 0)),
-            pl.BlockSpec((1, rows, tile // 2), lambda j: (j, 0, 0)),
+            pl.BlockSpec((chips_per_tile, rows, 128), lambda j: (j, 0, 0)),
+            pl.BlockSpec((chips_per_tile, rows, 128), lambda j: (j, 0, 0)),
         ],
         out_shape=[piece, piece],
         scratch_shapes=[pltpu.VMEM((rows, depth), jnp.bfloat16)],

time: 51.3 us -> 50.5 us (0.984)
  Pallas kernels: 14.8 us -> 14 us
    pallas_call x1, Pallas kernels: 8.44 us -> 7.68 us  [listed_matmul(): pl.pallas_call(matmul_kernel, grid=(tiles,), in_specs=[pl.BlockSpec(slots...]
where the time goes in v17:
time: 50.5 us; the launch traced here: 50.2 us
  starting transfers between devices  15.5 us (31%)
  Pallas kernels  14 us (28%)
  waiting for transfers between devices  12.5 us (25%)
  local copies, waits for them, and re-layouts  4.8 us (10%)
  other arithmetic  2.81 us (6%)
  between operations  0.67 us (1%)
    all_to_all x1, starting transfers between devices, gather_tm(): return lax.all_to_all(copies, 'tm', 0, 0, tiled=True)  10.5 us
    all_to_all x1, waiting for transfers between devices, gather_tm(): return lax.all_to_all(copies, 'tm', 0, 0, tiled=True)  9.19 us
    pallas_call x1, Pallas kernels, listed_matmul(): pl.pallas_call(matmul_kernel, grid=(tiles,), in_specs=[pl.BlockSpec(slots...  7.68 us
    ppermute x3, starting transfers between devices, sensor_reduce_scatter(): parts.append(lax.ppermute(part, 'sensor', perm))  4.93 us
    pallas_call x1, Pallas kernels, local_scans(): pl.pallas_call(scan_kernel, out_shape=[shape] * 2 + [jax.ShapeDtypeStruct...  2.33 us
    pallas_call x1, Pallas kernels, combine(): pl.pallas_call(combine_kernel, out_shape=[shape, shape], cost_estimate=pl...  2.08 us
    ppermute x3, waiting for transfers between devices, sensor_reduce_scatter(): parts.append(lax.ppermute(part, 'sensor', perm))  1.92 us
    pallas_call x1, Pallas kernels, gain_scans(): pl.pallas_call(gain_scan_kernel, out_shape=[shape] * 3 + [jax.ShapeDtypeS...  1.91 us
  transfers between devices with their start and end apart: 5, of which 4 were waited for; matrix products, arithmetic and copies ran while one was open for 9% of the time, Pallas kernels for 4%

profile of v17, /device:TPU:8, one launch (start us, length us, event | category | flops | bytes accessed | tf_op | source)
XLA Modules:
  0.0 50.2 jit_solution(6347009109939818694)
XLA Ops:
  0.6 0.0 copy-start
  0.6 7.7 %shard_map.86 = (f32[4,256,128]{2,1,0:T(8,128)}, f32[4,256,128]{2,1,0:T(8,128)}) custom-call(s32[16,256]{1,0:T(8,128)} %bitcast.11, bf16[256,4096]{1,0:T(8,128)(2,1)} %obs_ref.1, bf16[4096,1024]{1,0:T(8,128)(2,1)} %gain_ref.1), custom_call_target="tpu_custom_call" | custom-call | flops 2147483648 | bytes 11534336 | tf_op jit(solution)/shard_map/pallas_call | solution.py:168
  8.3 0.0 collective-permute-start
  8.3 0.8 %dynamic_slice.31 = f32[128]{0:T(128)S(1)} dynamic-slice(f32[1024]{0:T(1024)} %param.12, s32[]{:T(128)S(6)} %select_n.42), dynamic_slice_sizes={128} | dynamic-slice | bytes 1028 | tf_op jit(solution)/shard_map/dynamic_slice | solution.py:221
  9.1 1.4 %collective-permute-done = f32[4,256,128]{2,1,0:T(8,128)S(1)} collective-permute-done((f32[4,256,128]{2,1,0:T(8,128)}, f32[4,256,128]{2,1,0:T(8,128)S(1)}, u32[]{:S(2)}, u32[]{:S(2)}) %collective-permute-start) | collective-permute-done | bytes 524320 | tf_op jit(solution)/shard_map/ppermute | solution.py:196
  10.5 1.1 %add.53 = f32[4,256,128]{2,1,0:T(8,128)S(1)} add(f32[4,256,128]{2,1,0:T(8,128)} %get-tuple-element.11, f32[4,256,128]{2,1,0:T(8,128)S(1)} %collective-permute-done) | non-fusion elementwise | flops 131072 | bytes 1572864 | tf_op jit(solution)/shard_map/add | solution.py:196
  11.5 0.7 %dynamic-slice_bitcast_fusion = (f32[256,128]{1,0:T(8,128)S(1)}, f32[256,128]{1,0:T(8,128)S(1)}, f32[256,128]{1,0:T(8,128)S(1)}, f32[256,128]{1,0:T(8,128)}) fusion(f32[4,256,128]{2,1,0:T(8,128)S(1)} %add.53, s32[]{:T(128)S(6)} %select_n.50, s32[]{:T(128)S(6)} %select_n.48, s32[]{:T(128)S(6)} %select_n.46, s32[]{:T(128)S(6)} %select_n.44), kind=kLoop, calls=%fused_computation.1 | loop fusion | bytes 1048592 | tf_op jit(solution)/shard_map/jit(dynamic_index_in_dim)/squeeze | solution.py:199
  12.3 1.6 %collective-permute-start.1 = (f32[256,128]{1,0:T(8,128)S(1)}, f32[256,128]{1,0:T(8,128)S(1)}, u32[]{:S(2)}, u32[]{:S(2)}) collective-permute-start(f32[256,128]{1,0:T(8,128)S(1)} %get-tuple-element.24), channel_id=1, source_target_pairs={{0,2},{1,3},{2,4},{3,5},{4,6},{5,7},{6,0},{7,1},{8,10},{9,11},{10,... | collective-permute-start | bytes 393224 | tf_op jit(solution)/shard_map/ppermute | solution.py:201
  13.8 2.6 %collective-permute-start.2 = (f32[256,128]{1,0:T(8,128)S(1)}, f32[256,128]{1,0:T(8,128)S(1)}, u32[]{:S(2)}, u32[]{:S(2)}) collective-permute-start(f32[256,128]{1,0:T(8,128)S(1)} %get-tuple-element.23), channel_id=1, source_target_pairs={{0,4},{1,5},{2,6},{3,7},{4,0},{5,1},{6,2},{7,3},{8,12},{9,13},{10,... | collective-permute-start | bytes 393224 | tf_op jit(solution)/shard_map/ppermute | solution.py:201
  16.5 0.7 %collective-permute-start.3 = (f32[256,128]{1,0:T(8,128)S(1)}, f32[256,128]{1,0:T(8,128)S(1)}, u32[]{:S(2)}, u32[]{:S(2)}) collective-permute-start(f32[256,128]{1,0:T(8,128)S(1)} %get-tuple-element.22), channel_id=1, source_target_pairs={{0,6},{1,7},{2,0},{3,1},{4,2},{5,3},{6,4},{7,5},{8,14},{9,15},{10,... | collective-permute-start | bytes 393224 | tf_op jit(solution)/shard_map/ppermute | solution.py:201
  17.2 1.7 %broadcast_multiply_fusion = (f32[256,128]{1,0:T(8,128)}, f32[256,128]{1,0:T(8,128)}) fusion(f32[128]{0:T(128)S(1)} %dynamic_slice.31, f32[256,1024]{1,0:T(8,128)} %param.11, s32[]{:T(128)S(6)} %select_n.42, pred[256]{0:T(512)(128)(4,1)S(1)} %add_compare_fusion), kind=kLoop, calls=%fused_computation.5 | loop fusion | flops 65536 | bytes 393988 | tf_op jit(solution)/shard_map/mul | solution.py:226
  18.9 0.0 copy-done
  18.9 0.7 %constant_dynamic-slice_fusion.a_ref = f32[256,128]{1,0:T(8,128)} fusion(f32[256,1024]{1,0:T(8,128)S(1)} %copy-done, s32[]{:T(128)S(6)} %select_n.42), kind=kLoop, calls=%fused_computation.6 | loop fusion | bytes 262148 | tf_op jit(solution)/shard_map/dynamic_slice | solution.py:219
  19.6 1.9 %shard_map.87 = (f32[256,128]{1,0:T(8,128)}, f32[256,128]{1,0:T(8,128)}, f32[256,128]{1,0:T(8,128)}, f32[8,128]{1,0:T(8,128)}) custom-call(f32[256,128]{1,0:T(8,128)} %constant_dynamic-slice_fusion.a_ref, f32[256,128]{1,0:T(8,128)} %get-tuple-element.21.g_ref, f32[256,128]{1,0:T(8,128)} %get-tuple-element.20.s_ref), custom_call_target="tpu_custom_call" | custom-call | flops 655360 | bytes 786432 | tf_op jit(solution)/shard_map/pallas_call | solution.py:68
  21.5 0.0 collective-permute-done.1.r1_ref
  21.5 0.0 copy-start.2
  21.5 0.2 collective-permute-done.2.r2_ref
  21.7 0.0 copy-start.3
  21.7 1.7 %collective-permute-done.3.r3_ref = f32[256,128]{1,0:T(8,128)S(1)} collective-permute-done((f32[256,128]{1,0:T(8,128)S(1)}, f32[256,128]{1,0:T(8,128)S(1)}, u32[]{:S(2)}, u32[]{:S(2)}) %collective-permute-start.3) | collective-permute-done | bytes 131104 | tf_op jit(solution)/shard_map/ppermute | solution.py:201
  23.4 0.0 copy-start.4
  23.4 0.0 copy-done.2
  23.4 0.0 copy-done.3
  23.4 0.6 %copy-done.4 = f32[256,128]{1,0:T(8,128)} copy-done((f32[256,128]{1,0:T(8,128)}, f32[256,128]{1,0:T(8,128)S(1)}, u32[]{:S(2)}) %copy-start.4) | copy-done | bytes 131096
  24.0 2.3 %shard_map.88 = (f32[256,128]{1,0:T(8,128)}, f32[256,128]{1,0:T(8,128)}, f32[32,8,128]{2,1,0:T(8,128)}) custom-call(f32[256,128]{1,0:T(8,128)} %constant_dynamic-slice_fusion.a_ref, f32[256,128]{1,0:T(8,128)} %get-tuple-element.25.own_ref, f32[256,128]{1,0:T(8,128)} %copy-done.2, f32[256,128]{1,0:T(8,128)} %copy-done.3, f32[256,128]{1,0:T(8,128)} %copy-done.4, ...), custom_call_target="tpu_custom_call" | custom-call | flops 655360 | bytes 1310720 | tf_op jit(solution)/shard_map/pallas_call | solution.py:97
  26.4 10.5 %all-to-all-start = ((f32[32,8,128]{2,1,0:T(8,128)}), f32[32,8,128]{2,1,0:T(8,128)S(1)}, u32[]{:S(2)}, u32[]{:S(2)}) async-start(f32[32,8,128]{2,1,0:T(8,128)} %get-tuple-element.14), calls=%async_computation | async-start | bytes 262144 | tf_op jit(solution)/shard_map/all_to_all | solution.py:206
  36.9 1.4 %dynamic-slice_bitcast_fusion.4.init_ref = f32[1,128]{1,0:T(1,128)} fusion(f32[1024]{0:T(1024)} %param.13, s32[]{:T(128)S(6)} %select_n.42), kind=kLoop, calls=%fused_computation.8 | loop fusion | bytes 1028 | tf_op jit(solution)/shard_map/broadcast_in_dim | solution.py:232
  38.3 9.2 %all-to-all-done.every_ref = f32[32,8,128]{2,1,0:T(8,128)S(1)} async-done(((f32[32,8,128]{2,1,0:T(8,128)}), f32[32,8,128]{2,1,0:T(8,128)S(1)}, u32[]{:S(2)}, u32[]{:S(2)}) %all-to-all-start) | async-done | bytes 131104 | tf_op jit(solution)/shard_map/all_to_all | solution.py:206
  47.5 0.0 copy-start.1
  47.5 0.7 %copy-done.1 = f32[32,8,128]{2,1,0:T(8,128)} copy-done((f32[32,8,128]{2,1,0:T(8,128)}, f32[32,8,128]{2,1,0:T(8,128)S(1)}, u32[]{:S(2)}) %copy-start.1) | copy-done | bytes 131096
  48.1 2.1 %shard_map.89 = (f32[256,128]{1,0:T(8,128)}, f32[256,128]{1,0:T(8,128)}) custom-call(f32[32,8,128]{2,1,0:T(8,128)} %copy-done.1, f32[1,128]{1,0:T(1,128)} %dynamic-slice_bitcast_fusion.4.init_ref, f32[256,128]{1,0:T(8,128)} %get-tuple-element.15.pf_ref, f32[256,128]{1,0:T(8,128)} %get-tuple-element.16.lf_ref, f32[256,128]{1,0:T(8,128)} %get-tuple-element.17.pb_ref, ...), custom_call_target="tpu_custom_call" | custom-call | flops 163840 | bytes 917504 | tf_op jit(solution)/shard_map/pallas_call | solution.py:126
  (1 shorter events, 0.0 us)
Async XLA Ops:
  0.6 18.3 %copy-start = (f32[256,1024]{1,0:T(8,128)S(1)}, f32[256,1024]{1,0:T(8,128)}, u32[]{:S(2)}) copy-start(f32[256,1024]{1,0:T(8,128)} %param.10) | copy-start | bytes 3145732
  8.3 2.1 %collective-permute-start = (f32[4,256,128]{2,1,0:T(8,128)}, f32[4,256,128]{2,1,0:T(8,128)S(1)}, u32[]{:S(2)}, u32[]{:S(2)}) collective-permute-start(f32[4,256,128]{2,1,0:T(8,128)} %get-tuple-element.12), channel_id=1, source_target_pairs={{0,1},{1,0},{2,3},{3,2},{4,5},{5,4},{6,7},{7,6},{8,9},{9,8},{10,11... | collective-permute-start | bytes 1572872 | tf_op jit(solution)/shard_map/ppermute | solution.py:196
  12.3 9.2 %collective-permute-start.1 = (f32[256,128]{1,0:T(8,128)S(1)}, f32[256,128]{1,0:T(8,128)S(1)}, u32[]{:S(2)}, u32[]{:S(2)}) collective-permute-start(f32[256,128]{1,0:T(8,128)S(1)} %get-tuple-element.24), channel_id=1, source_target_pairs={{0,2},{1,3},{2,4},{3,5},{4,6},{5,7},{6,0},{7,1},{8,10},{9,11},{10,... | collective-permute-start | bytes 393224 | tf_op jit(solution)/shard_map/ppermute | solution.py:201
  13.8 7.9 %collective-permute-start.2 = (f32[256,128]{1,0:T(8,128)S(1)}, f32[256,128]{1,0:T(8,128)S(1)}, u32[]{:S(2)}, u32[]{:S(2)}) collective-permute-start(f32[256,128]{1,0:T(8,128)S(1)} %get-tuple-element.23), channel_id=1, source_target_pairs={{0,4},{1,5},{2,6},{3,7},{4,0},{5,1},{6,2},{7,3},{8,12},{9,13},{10,... | collective-permute-start | bytes 393224 | tf_op jit(solution)/shard_map/ppermute | solution.py:201
  16.5 6.9 %collective-permute-start.3 = (f32[256,128]{1,0:T(8,128)S(1)}, f32[256,128]{1,0:T(8,128)S(1)}, u32[]{:S(2)}, u32[]{:S(2)}) collective-permute-start(f32[256,128]{1,0:T(8,128)S(1)} %get-tuple-element.22), channel_id=1, source_target_pairs={{0,6},{1,7},{2,0},{3,1},{4,2},{5,3},{6,4},{7,5},{8,14},{9,15},{10,... | collective-permute-start | bytes 393224 | tf_op jit(solution)/shard_map/ppermute | solution.py:201
  21.5 1.9 %copy-start.2 = (f32[256,128]{1,0:T(8,128)}, f32[256,128]{1,0:T(8,128)S(1)}, u32[]{:S(2)}) copy-start(f32[256,128]{1,0:T(8,128)S(1)} %collective-permute-done.1.r1_ref) | copy-start | bytes 393220
  21.7 1.7 %copy-start.3 = (f32[256,128]{1,0:T(8,128)}, f32[256,128]{1,0:T(8,128)S(1)}, u32[]{:S(2)}) copy-start(f32[256,128]{1,0:T(8,128)S(1)} %collective-permute-done.2.r2_ref) | copy-start | bytes 393220
  23.4 0.6 %copy-start.4 = (f32[256,128]{1,0:T(8,128)}, f32[256,128]{1,0:T(8,128)S(1)}, u32[]{:S(2)}) copy-start(f32[256,128]{1,0:T(8,128)S(1)} %collective-permute-done.3.r3_ref) | copy-start | bytes 393220
  26.4 21.1 %all-to-all-start = ((f32[32,8,128]{2,1,0:T(8,128)}), f32[32,8,128]{2,1,0:T(8,128)S(1)}, u32[]{:S(2)}, u32[]{:S(2)}) async-start(f32[32,8,128]{2,1,0:T(8,128)} %get-tuple-element.14), calls=%async_computation | async-start | bytes 262144 | tf_op jit(solution)/shard_map/all_to_all | solution.py:206
  47.5 0.7 %copy-start.1 = (f32[32,8,128]{2,1,0:T(8,128)}, f32[32,8,128]{2,1,0:T(8,128)S(1)}, u32[]{:S(2)}) copy-start(f32[32,8,128]{2,1,0:T(8,128)S(1)} %all-to-all-done.every_ref) | copy-start | bytes 393220

commit v18 on v17

--- a/solution.py
+++ b/solution.py
@@ -161,7 +161,7 @@
 def listed_matmul(slots, observations, gain_rows):
     rows, depth = observations.shape
     modes = gain_rows.shape[1]
-    tile = 512
+    tile = 1024
     tiles = modes // tile
     chips_per_tile = tile // 256
     piece = jax.ShapeDtypeStruct((modes // 256, rows, 128), jnp.float32)

time: 50.5 us -> 51.4 us (1.018)
  Pallas kernels: 14 us -> 14.9 us
    pallas_call x1, Pallas kernels: 7.68 us -> 8.59 us  [listed_matmul(): pl.pallas_call(matmul_kernel, grid=(tiles,), in_specs=[pl.BlockSpec(slots...]
where the time goes in v18:
time: 51.4 us; the launch traced here: 51.1 us
  starting transfers between devices  15.5 us (30%)
  Pallas kernels  14.9 us (29%)
  waiting for transfers between devices  12.5 us (24%)
  local copies, waits for them, and re-layouts  4.8 us (9%)
  other arithmetic  2.81 us (5%)
  between operations  0.67 us (1%)
    all_to_all x1, starting transfers between devices, gather_tm(): return lax.all_to_all(copies, 'tm', 0, 0, tiled=True)  10.5 us
    all_to_all x1, waiting for transfers between devices, gather_tm(): return lax.all_to_all(copies, 'tm', 0, 0, tiled=True)  9.19 us
    pallas_call x1, Pallas kernels, listed_matmul(): pl.pallas_call(matmul_kernel, grid=(tiles,), in_specs=[pl.BlockSpec(slots...  8.59 us
    ppermute x3, starting transfers between devices, sensor_reduce_scatter(): parts.append(lax.ppermute(part, 'sensor', perm))  4.92 us
    pallas_call x1, Pallas kernels, local_scans(): pl.pallas_call(scan_kernel, out_shape=[shape] * 2 + [jax.ShapeDtypeStruct...  2.33 us
    pallas_call x1, Pallas kernels, combine(): pl.pallas_call(combine_kernel, out_shape=[shape, shape], cost_estimate=pl...  2.08 us
    ppermute x3, waiting for transfers between devices, sensor_reduce_scatter(): parts.append(lax.ppermute(part, 'sensor', perm))  1.92 us
    pallas_call x1, Pallas kernels, gain_scans(): pl.pallas_call(gain_scan_kernel, out_shape=[shape] * 3 + [jax.ShapeDtypeS...  1.91 us
  transfers between devices with their start and end apart: 5, of which 4 were waited for; matrix products, arithmetic and copies ran while one was open for 9% of the time, Pallas kernels for 4%

profile of v18, /device:TPU:8, one launch (start us, length us, event | category | flops | bytes accessed | tf_op | source)
XLA Modules:
  0.0 51.1 jit_solution(6077081223551896810)
XLA Ops:
  0.6 0.0 copy-start
  0.6 8.6 %shard_map.86 = (f32[4,256,128]{2,1,0:T(8,128)}, f32[4,256,128]{2,1,0:T(8,128)}) custom-call(s32[16,256]{1,0:T(8,128)} %bitcast.11, bf16[256,4096]{1,0:T(8,128)(2,1)} %obs_ref.1, bf16[4096,1024]{1,0:T(8,128)(2,1)} %gain_ref.1), custom_call_target="tpu_custom_call" | custom-call | flops 2147483648 | bytes 11534336 | tf_op jit(solution)/shard_map/pallas_call | solution.py:168
  9.2 0.0 collective-permute-start
  9.2 0.8 %dynamic_slice.31 = f32[128]{0:T(128)S(1)} dynamic-slice(f32[1024]{0:T(1024)} %param.12, s32[]{:T(128)S(6)} %select_n.42), dynamic_slice_sizes={128} | dynamic-slice | bytes 1028 | tf_op jit(solution)/shard_map/dynamic_slice | solution.py:221
  10.0 1.4 %collective-permute-done = f32[4,256,128]{2,1,0:T(8,128)S(1)} collective-permute-done((f32[4,256,128]{2,1,0:T(8,128)}, f32[4,256,128]{2,1,0:T(8,128)S(1)}, u32[]{:S(2)}, u32[]{:S(2)}) %collective-permute-start) | collective-permute-done | bytes 524320 | tf_op jit(solution)/shard_map/ppermute | solution.py:196
  11.4 1.1 %add.53 = f32[4,256,128]{2,1,0:T(8,128)S(1)} add(f32[4,256,128]{2,1,0:T(8,128)} %get-tuple-element.11, f32[4,256,128]{2,1,0:T(8,128)S(1)} %collective-permute-done) | non-fusion elementwise | flops 131072 | bytes 1572864 | tf_op jit(solution)/shard_map/add | solution.py:196
  12.5 0.7 %dynamic-slice_bitcast_fusion = (f32[256,128]{1,0:T(8,128)S(1)}, f32[256,128]{1,0:T(8,128)S(1)}, f32[256,128]{1,0:T(8,128)S(1)}, f32[256,128]{1,0:T(8,128)}) fusion(f32[4,256,128]{2,1,0:T(8,128)S(1)} %add.53, s32[]{:T(128)S(6)} %select_n.50, s32[]{:T(128)S(6)} %select_n.48, s32[]{:T(128)S(6)} %select_n.46, s32[]{:T(128)S(6)} %select_n.44), kind=kLoop, calls=%fused_computation.1 | loop fusion | bytes 1048592 | tf_op jit(solution)/shard_map/jit(dynamic_index_in_dim)/squeeze | solution.py:199
  13.2 1.6 %collective-permute-start.1 = (f32[256,128]{1,0:T(8,128)S(1)}, f32[256,128]{1,0:T(8,128)S(1)}, u32[]{:S(2)}, u32[]{:S(2)}) collective-permute-start(f32[256,128]{1,0:T(8,128)S(1)} %get-tuple-element.24), channel_id=1, source_target_pairs={{0,2},{1,3},{2,4},{3,5},{4,6},{5,7},{6,0},{7,1},{8,10},{9,11},{10,... | collective-permute-start | bytes 393224 | tf_op jit(solution)/shard_map/ppermute | solution.py:201
  14.7 2.6 %collective-permute-start.2 = (f32[256,128]{1,0:T(8,128)S(1)}, f32[256,128]{1,0:T(8,128)S(1)}, u32[]{:S(2)}, u32[]{:S(2)}) collective-permute-start(f32[256,128]{1,0:T(8,128)S(1)} %get-tuple-element.23), channel_id=1, source_target_pairs={{0,4},{1,5},{2,6},{3,7},{4,0},{5,1},{6,2},{7,3},{8,12},{9,13},{10,... | collective-permute-start | bytes 393224 | tf_op jit(solution)/shard_map/ppermute | solution.py:201
  17.4 0.7 %collective-permute-start.3 = (f32[256,128]{1,0:T(8,128)S(1)}, f32[256,128]{1,0:T(8,128)S(1)}, u32[]{:S(2)}, u32[]{:S(2)}) collective-permute-start(f32[256,128]{1,0:T(8,128)S(1)} %get-tuple-element.22), channel_id=1, source_target_pairs={{0,6},{1,7},{2,0},{3,1},{4,2},{5,3},{6,4},{7,5},{8,14},{9,15},{10,... | collective-permute-start | bytes 393224 | tf_op jit(solution)/shard_map/ppermute | solution.py:201
  18.1 1.7 %broadcast_multiply_fusion = (f32[256,128]{1,0:T(8,128)}, f32[256,128]{1,0:T(8,128)}) fusion(f32[128]{0:T(128)S(1)} %dynamic_slice.31, f32[256,1024]{1,0:T(8,128)} %param.11, s32[]{:T(128)S(6)} %select_n.42, pred[256]{0:T(512)(128)(4,1)S(1)} %add_compare_fusion), kind=kLoop, calls=%fused_computation.5 | loop fusion | flops 65536 | bytes 393988 | tf_op jit(solution)/shard_map/mul | solution.py:226
  19.8 0.0 copy-done
  19.8 0.7 %constant_dynamic-slice_fusion.a_ref = f32[256,128]{1,0:T(8,128)} fusion(f32[256,1024]{1,0:T(8,128)S(1)} %copy-done, s32[]{:T(128)S(6)} %select_n.42), kind=kLoop, calls=%fused_computation.6 | loop fusion | bytes 262148 | tf_op jit(solution)/shard_map/dynamic_slice | solution.py:219
  20.5 1.9 %shard_map.87 = (f32[256,128]{1,0:T(8,128)}, f32[256,128]{1,0:T(8,128)}, f32[256,128]{1,0:T(8,128)}, f32[8,128]{1,0:T(8,128)}) custom-call(f32[256,128]{1,0:T(8,128)} %constant_dynamic-slice_fusion.a_ref, f32[256,128]{1,0:T(8,128)} %get-tuple-element.21.g_ref, f32[256,128]{1,0:T(8,128)} %get-tuple-element.20.s_ref), custom_call_target="tpu_custom_call" | custom-call | flops 655360 | bytes 786432 | tf_op jit(solution)/shard_map/pallas_call | solution.py:68
  22.4 0.0 collective-permute-done.1.r1_ref
  22.4 0.0 copy-start.2
  22.4 0.2 collective-permute-done.2.r2_ref
  22.6 0.0 copy-start.3
  22.6 1.7 %collective-permute-done.3.r3_ref = f32[256,128]{1,0:T(8,128)S(1)} collective-permute-done((f32[256,128]{1,0:T(8,128)S(1)}, f32[256,128]{1,0:T(8,128)S(1)}, u32[]{:S(2)}, u32[]{:S(2)}) %collective-permute-start.3) | collective-permute-done | bytes 131104 | tf_op jit(solution)/shard_map/ppermute | solution.py:201
  24.3 0.0 copy-start.4
  24.3 0.0 copy-done.2
  24.3 0.0 copy-done.3
  24.3 0.6 %copy-done.4 = f32[256,128]{1,0:T(8,128)} copy-done((f32[256,128]{1,0:T(8,128)}, f32[256,128]{1,0:T(8,128)S(1)}, u32[]{:S(2)}) %copy-start.4) | copy-done | bytes 131096
  24.9 2.3 %shard_map.88 = (f32[256,128]{1,0:T(8,128)}, f32[256,128]{1,0:T(8,128)}, f32[32,8,128]{2,1,0:T(8,128)}) custom-call(f32[256,128]{1,0:T(8,128)} %constant_dynamic-slice_fusion.a_ref, f32[256,128]{1,0:T(8,128)} %get-tuple-element.25.own_ref, f32[256,128]{1,0:T(8,128)} %copy-done.2, f32[256,128]{1,0:T(8,128)} %copy-done.3, f32[256,128]{1,0:T(8,128)} %copy-done.4, ...), custom_call_target="tpu_custom_call" | custom-call | flops 655360 | bytes 1310720 | tf_op jit(solution)/shard_map/pallas_call | solution.py:97
  27.3 10.5 %all-to-all-start = ((f32[32,8,128]{2,1,0:T(8,128)}), f32[32,8,128]{2,1,0:T(8,128)S(1)}, u32[]{:S(2)}, u32[]{:S(2)}) async-start(f32[32,8,128]{2,1,0:T(8,128)} %get-tuple-element.14), calls=%async_computation | async-start | bytes 262144 | tf_op jit(solution)/shard_map/all_to_all | solution.py:206
  37.8 1.4 %dynamic-slice_bitcast_fusion.4.init_ref = f32[1,128]{1,0:T(1,128)} fusion(f32[1024]{0:T(1024)} %param.13, s32[]{:T(128)S(6)} %select_n.42), kind=kLoop, calls=%fused_computation.8 | loop fusion | bytes 1028 | tf_op jit(solution)/shard_map/broadcast_in_dim | solution.py:232
  39.2 9.2 %all-to-all-done.every_ref = f32[32,8,128]{2,1,0:T(8,128)S(1)} async-done(((f32[32,8,128]{2,1,0:T(8,128)}), f32[32,8,128]{2,1,0:T(8,128)S(1)}, u32[]{:S(2)}, u32[]{:S(2)}) %all-to-all-start) | async-done | bytes 131104 | tf_op jit(solution)/shard_map/all_to_all | solution.py:206
  48.4 0.0 copy-start.1
  48.4 0.7 %copy-done.1 = f32[32,8,128]{2,1,0:T(8,128)} copy-done((f32[32,8,128]{2,1,0:T(8,128)}, f32[32,8,128]{2,1,0:T(8,128)S(1)}, u32[]{:S(2)}) %copy-start.1) | copy-done | bytes 131096
  49.0 2.1 %shard_map.89 = (f32[256,128]{1,0:T(8,128)}, f32[256,128]{1,0:T(8,128)}) custom-call(f32[32,8,128]{2,1,0:T(8,128)} %copy-done.1, f32[1,128]{1,0:T(1,128)} %dynamic-slice_bitcast_fusion.4.init_ref, f32[256,128]{1,0:T(8,128)} %get-tuple-element.15.pf_ref, f32[256,128]{1,0:T(8,128)} %get-tuple-element.16.lf_ref, f32[256,128]{1,0:T(8,128)} %get-tuple-element.17.pb_ref, ...), custom_call_target="tpu_custom_call" | custom-call | flops 163840 | bytes 917504 | tf_op jit(solution)/shard_map/pallas_call | solution.py:126
  (1 shorter events, 0.0 us)
Async XLA Ops:
  0.6 19.2 %copy-start = (f32[256,1024]{1,0:T(8,128)S(1)}, f32[256,1024]{1,0:T(8,128)}, u32[]{:S(2)}) copy-start(f32[256,1024]{1,0:T(8,128)} %param.10) | copy-start | bytes 3145732
  9.2 2.1 %collective-permute-start = (f32[4,256,128]{2,1,0:T(8,128)}, f32[4,256,128]{2,1,0:T(8,128)S(1)}, u32[]{:S(2)}, u32[]{:S(2)}) collective-permute-start(f32[4,256,128]{2,1,0:T(8,128)} %get-tuple-element.12), channel_id=1, source_target_pairs={{0,1},{1,0},{2,3},{3,2},{4,5},{5,4},{6,7},{7,6},{8,9},{9,8},{10,11... | collective-permute-start | bytes 1572872 | tf_op jit(solution)/shard_map/ppermute | solution.py:196
  13.2 9.2 %collective-permute-start.1 = (f32[256,128]{1,0:T(8,128)S(1)}, f32[256,128]{1,0:T(8,128)S(1)}, u32[]{:S(2)}, u32[]{:S(2)}) collective-permute-start(f32[256,128]{1,0:T(8,128)S(1)} %get-tuple-element.24), channel_id=1, source_target_pairs={{0,2},{1,3},{2,4},{3,5},{4,6},{5,7},{6,0},{7,1},{8,10},{9,11},{10,... | collective-permute-start | bytes 393224 | tf_op jit(solution)/shard_map/ppermute | solution.py:201
  14.7 7.9 %collective-permute-start.2 = (f32[256,128]{1,0:T(8,128)S(1)}, f32[256,128]{1,0:T(8,128)S(1)}, u32[]{:S(2)}, u32[]{:S(2)}) collective-permute-start(f32[256,128]{1,0:T(8,128)S(1)} %get-tuple-element.23), channel_id=1, source_target_pairs={{0,4},{1,5},{2,6},{3,7},{4,0},{5,1},{6,2},{7,3},{8,12},{9,13},{10,... | collective-permute-start | bytes 393224 | tf_op jit(solution)/shard_map/ppermute | solution.py:201
  17.4 6.9 %collective-permute-start.3 = (f32[256,128]{1,0:T(8,128)S(1)}, f32[256,128]{1,0:T(8,128)S(1)}, u32[]{:S(2)}, u32[]{:S(2)}) collective-permute-start(f32[256,128]{1,0:T(8,128)S(1)} %get-tuple-element.22), channel_id=1, source_target_pairs={{0,6},{1,7},{2,0},{3,1},{4,2},{5,3},{6,4},{7,5},{8,14},{9,15},{10,... | collective-permute-start | bytes 393224 | tf_op jit(solution)/shard_map/ppermute | solution.py:201
  22.4 1.9 %copy-start.2 = (f32[256,128]{1,0:T(8,128)}, f32[256,128]{1,0:T(8,128)S(1)}, u32[]{:S(2)}) copy-start(f32[256,128]{1,0:T(8,128)S(1)} %collective-permute-done.1.r1_ref) | copy-start | bytes 393220
  22.6 1.7 %copy-start.3 = (f32[256,128]{1,0:T(8,128)}, f32[256,128]{1,0:T(8,128)S(1)}, u32[]{:S(2)}) copy-start(f32[256,128]{1,0:T(8,128)S(1)} %collective-permute-done.2.r2_ref) | copy-start | bytes 393220
  24.3 0.6 %copy-start.4 = (f32[256,128]{1,0:T(8,128)}, f32[256,128]{1,0:T(8,128)S(1)}, u32[]{:S(2)}) copy-start(f32[256,128]{1,0:T(8,128)S(1)} %collective-permute-done.3.r3_ref) | copy-start | bytes 393220
  27.3 21.1 %all-to-all-start = ((f32[32,8,128]{2,1,0:T(8,128)}), f32[32,8,128]{2,1,0:T(8,128)S(1)}, u32[]{:S(2)}, u32[]{:S(2)}) async-start(f32[32,8,128]{2,1,0:T(8,128)} %get-tuple-element.14), calls=%async_computation | async-start | bytes 262144 | tf_op jit(solution)/shard_map/all_to_all | solution.py:206
  48.4 0.7 %copy-start.1 = (f32[32,8,128]{2,1,0:T(8,128)}, f32[32,8,128]{2,1,0:T(8,128)S(1)}, u32[]{:S(2)}) copy-start(f32[32,8,128]{2,1,0:T(8,128)S(1)} %all-to-all-done.every_ref) | copy-start | bytes 393220

commit v19 on v15

--- a/solution.py
+++ b/solution.py
@@ -161,18 +161,21 @@
             lhs_ref[:, cols] = jnp.where(listed[:, b:b + 1] > 0, block, jnp.zeros_like(block))
 
     prod = jnp.dot(lhs_ref[...], gain_ref[...], preferred_element_type=jnp.float32)
-    half = prod.shape[1] // 2
     even = sensor % 2 == 0
-    keep_ref[0] = jnp.where(even, prod[:, :half], prod[:, half:])
-    send_ref[0] = jnp.where(even, prod[:, half:], prod[:, :half])
+    for c in range(keep_ref.shape[0]):
+        left = prod[:, 256 * c:256 * c + 128]
+        right = prod[:, 256 * c + 128:256 * c + 256]
+        keep_ref[c] = jnp.where(even, left, right)
+        send_ref[c] = jnp.where(even, right, left)
 
 
 def listed_matmul(slots, observations, gain_rows):
     rows, depth = observations.shape
     modes = gain_rows.shape[1]
-    tile = 256
+    tile = 512
     tiles = modes // tile
-    piece = jax.ShapeDtypeStruct((tiles, rows, tile // 2), jnp.float32)
+    chips_per_tile = tile // 256
+    piece = jax.ShapeDtypeStruct((modes // 256, rows, 128), jnp.float32)
     return pl.pallas_call(
         matmul_kernel,
         grid=(tiles,),
@@ -182,8 +185,8 @@
             pl.BlockSpec((depth, tile), lambda j: (0, j)),
         ],
         out_specs=[
-            pl.BlockSpec((1, rows, tile // 2), lambda j: (j, 0, 0)),
-            pl.BlockSpec((1, rows, tile // 2), lambda j: (j, 0, 0)),
+            pl.BlockSpec((chips_per_tile, rows, 128), lambda j: (j, 0, 0)),
+            pl.BlockSpec((chips_per_tile, rows, 128), lambda j: (j, 0, 0)),
         ],
         out_shape=[piece, piece],
         scratch_shapes=[pltpu.VMEM((rows, depth), jnp.bfloat16)],

time: 51.2 us -> 50.4 us (0.984)
  Pallas kernels: 14.7 us -> 13.9 us
    pallas_call x1, Pallas kernels: 8.44 us -> 7.68 us  [listed_matmul(): pl.pallas_call(matmul_kernel, grid=(tiles,), in_specs=[pl.BlockSpec(slots...]
where the time goes in v19:
time: 50.4 us; the launch traced here: 50.1 us
  starting transfers between devices  15.5 us (31%)
  Pallas kernels  13.9 us (28%)
  waiting for transfers between devices  12.5 us (25%)
  local copies, waits for them, and re-layouts  4.8 us (10%)
  other arithmetic  2.81 us (6%)
  between operations  0.67 us (1%)
    all_to_all x1, starting transfers between devices, gather_tm(): return lax.all_to_all(copies, 'tm', 0, 0, tiled=True)  10.5 us
    all_to_all x1, waiting for transfers between devices, gather_tm(): return lax.all_to_all(copies, 'tm', 0, 0, tiled=True)  9.19 us
    pallas_call x1, Pallas kernels, listed_matmul(): pl.pallas_call(matmul_kernel, grid=(tiles,), in_specs=[pl.BlockSpec(slots...  7.68 us
    ppermute x3, starting transfers between devices, sensor_reduce_scatter(): parts.append(lax.ppermute(part, 'sensor', perm))  4.93 us
    pallas_call x1, Pallas kernels, local_scans(): pl.pallas_call(scan_kernel, out_shape=[shape] * 2 + [jax.ShapeDtypeStruct...  2.33 us
    pallas_call x1, Pallas kernels, combine(): pl.pallas_call(combine_kernel, out_shape=[shape, shape], cost_estimate=pl...  1.98 us
    ppermute x3, waiting for transfers between devices, sensor_reduce_scatter(): parts.append(lax.ppermute(part, 'sensor', perm))  1.92 us
    pallas_call x1, Pallas kernels, gain_scans(): pl.pallas_call(gain_scan_kernel, out_shape=[shape] * 3 + [jax.ShapeDtypeS...  1.91 us
  transfers between devices with their start and end apart: 5, of which 4 were waited for; matrix products, arithmetic and copies ran while one was open for 9% of the time, Pallas kernels for 4%

profile of v19, /device:TPU:8, one launch (start us, length us, event | category | flops | bytes accessed | tf_op | source)
XLA Modules:
  0.0 50.1 jit_solution(8730375678784874408)
XLA Ops:
  0.6 0.0 copy-start
  0.6 7.7 %shard_map.86 = (f32[4,256,128]{2,1,0:T(8,128)}, f32[4,256,128]{2,1,0:T(8,128)}) custom-call(s32[16,256]{1,0:T(8,128)} %bitcast.11, bf16[256,4096]{1,0:T(8,128)(2,1)} %obs_ref.1, bf16[4096,1024]{1,0:T(8,128)(2,1)} %gain_ref.1), custom_call_target="tpu_custom_call" | custom-call | flops 2147483648 | bytes 11534336 | tf_op jit(solution)/shard_map/pallas_call | solution.py:179
  8.3 0.0 collective-permute-start
  8.3 0.8 %dynamic_slice.31 = f32[128]{0:T(128)S(1)} dynamic-slice(f32[1024]{0:T(1024)} %param.12, s32[]{:T(128)S(6)} %select_n.42), dynamic_slice_sizes={128} | dynamic-slice | bytes 1028 | tf_op jit(solution)/shard_map/dynamic_slice | solution.py:232
  9.1 1.4 %collective-permute-done = f32[4,256,128]{2,1,0:T(8,128)S(1)} collective-permute-done((f32[4,256,128]{2,1,0:T(8,128)}, f32[4,256,128]{2,1,0:T(8,128)S(1)}, u32[]{:S(2)}, u32[]{:S(2)}) %collective-permute-start) | collective-permute-done | bytes 524320 | tf_op jit(solution)/shard_map/ppermute | solution.py:207
  10.5 1.1 %add.53 = f32[4,256,128]{2,1,0:T(8,128)S(1)} add(f32[4,256,128]{2,1,0:T(8,128)} %get-tuple-element.11, f32[4,256,128]{2,1,0:T(8,128)S(1)} %collective-permute-done) | non-fusion elementwise | flops 131072 | bytes 1572864 | tf_op jit(solution)/shard_map/add | solution.py:207
  11.5 0.7 %dynamic-slice_bitcast_fusion = (f32[256,128]{1,0:T(8,128)S(1)}, f32[256,128]{1,0:T(8,128)S(1)}, f32[256,128]{1,0:T(8,128)S(1)}, f32[256,128]{1,0:T(8,128)}) fusion(f32[4,256,128]{2,1,0:T(8,128)S(1)} %add.53, s32[]{:T(128)S(6)} %select_n.50, s32[]{:T(128)S(6)} %select_n.48, s32[]{:T(128)S(6)} %select_n.46, s32[]{:T(128)S(6)} %select_n.44), kind=kLoop, calls=%fused_computation.1 | loop fusion | bytes 1048592 | tf_op jit(solution)/shard_map/jit(dynamic_index_in_dim)/squeeze | solution.py:210
  12.3 1.6 %collective-permute-start.1 = (f32[256,128]{1,0:T(8,128)S(1)}, f32[256,128]{1,0:T(8,128)S(1)}, u32[]{:S(2)}, u32[]{:S(2)}) collective-permute-start(f32[256,128]{1,0:T(8,128)S(1)} %get-tuple-element.24), channel_id=1, source_target_pairs={{0,2},{1,3},{2,4},{3,5},{4,6},{5,7},{6,0},{7,1},{8,10},{9,11},{10,... | collective-permute-start | bytes 393224 | tf_op jit(solution)/shard_map/ppermute | solution.py:212
  13.8 2.6 %collective-permute-start.2 = (f32[256,128]{1,0:T(8,128)S(1)}, f32[256,128]{1,0:T(8,128)S(1)}, u32[]{:S(2)}, u32[]{:S(2)}) collective-permute-start(f32[256,128]{1,0:T(8,128)S(1)} %get-tuple-element.23), channel_id=1, source_target_pairs={{0,4},{1,5},{2,6},{3,7},{4,0},{5,1},{6,2},{7,3},{8,12},{9,13},{10,... | collective-permute-start | bytes 393224 | tf_op jit(solution)/shard_map/ppermute | solution.py:212
  16.5 0.7 %collective-permute-start.3 = (f32[256,128]{1,0:T(8,128)S(1)}, f32[256,128]{1,0:T(8,128)S(1)}, u32[]{:S(2)}, u32[]{:S(2)}) collective-permute-start(f32[256,128]{1,0:T(8,128)S(1)} %get-tuple-element.22), channel_id=1, source_target_pairs={{0,6},{1,7},{2,0},{3,1},{4,2},{5,3},{6,4},{7,5},{8,14},{9,15},{10,... | collective-permute-start | bytes 393224 | tf_op jit(solution)/shard_map/ppermute | solution.py:212
  17.2 1.7 %broadcast_multiply_fusion = (f32[256,128]{1,0:T(8,128)}, f32[256,128]{1,0:T(8,128)}) fusion(f32[128]{0:T(128)S(1)} %dynamic_slice.31, f32[256,1024]{1,0:T(8,128)} %param.11, s32[]{:T(128)S(6)} %select_n.42, pred[256]{0:T(512)(128)(4,1)S(1)} %add_compare_fusion), kind=kLoop, calls=%fused_computation.5 | loop fusion | flops 65536 | bytes 393988 | tf_op jit(solution)/shard_map/mul | solution.py:237
  18.9 0.0 copy-done
  18.9 0.7 %constant_dynamic-slice_fusion.a_ref = f32[256,128]{1,0:T(8,128)} fusion(f32[256,1024]{1,0:T(8,128)S(1)} %copy-done, s32[]{:T(128)S(6)} %select_n.42), kind=kLoop, calls=%fused_computation.6 | loop fusion | bytes 262148 | tf_op jit(solution)/shard_map/dynamic_slice | solution.py:230
  19.6 1.9 %shard_map.87 = (f32[256,128]{1,0:T(8,128)}, f32[256,128]{1,0:T(8,128)}, f32[256,128]{1,0:T(8,128)}, f32[8,128]{1,0:T(8,128)}) custom-call(f32[256,128]{1,0:T(8,128)} %constant_dynamic-slice_fusion.a_ref, f32[256,128]{1,0:T(8,128)} %get-tuple-element.21.g_ref, f32[256,128]{1,0:T(8,128)} %get-tuple-element.20.s_ref), custom_call_target="tpu_custom_call" | custom-call | flops 655360 | bytes 786432 | tf_op jit(solution)/shard_map/pallas_call | solution.py:68
  21.5 0.0 collective-permute-done.1.r1_ref
  21.5 0.0 copy-start.2
  21.5 0.2 collective-permute-done.2.r2_ref
  21.7 0.0 copy-start.3
  21.7 1.7 %collective-permute-done.3.r3_ref = f32[256,128]{1,0:T(8,128)S(1)} collective-permute-done((f32[256,128]{1,0:T(8,128)S(1)}, f32[256,128]{1,0:T(8,128)S(1)}, u32[]{:S(2)}, u32[]{:S(2)}) %collective-permute-start.3) | collective-permute-done | bytes 131104 | tf_op jit(solution)/shard_map/ppermute | solution.py:212
  23.4 0.0 copy-start.4
  23.4 0.0 copy-done.2
  23.4 0.0 copy-done.3
  23.4 0.6 %copy-done.4 = f32[256,128]{1,0:T(8,128)} copy-done((f32[256,128]{1,0:T(8,128)}, f32[256,128]{1,0:T(8,128)S(1)}, u32[]{:S(2)}) %copy-start.4) | copy-done | bytes 131096
  24.0 2.3 %shard_map.88 = (f32[256,128]{1,0:T(8,128)}, f32[256,128]{1,0:T(8,128)}, f32[32,8,128]{2,1,0:T(8,128)}) custom-call(f32[256,128]{1,0:T(8,128)} %constant_dynamic-slice_fusion.a_ref, f32[256,128]{1,0:T(8,128)} %get-tuple-element.25.own_ref, f32[256,128]{1,0:T(8,128)} %copy-done.2, f32[256,128]{1,0:T(8,128)} %copy-done.3, f32[256,128]{1,0:T(8,128)} %copy-done.4, ...), custom_call_target="tpu_custom_call" | custom-call | flops 655360 | bytes 1310720 | tf_op jit(solution)/shard_map/pallas_call | solution.py:97
  26.4 10.5 %all-to-all-start = ((f32[32,8,128]{2,1,0:T(8,128)}), f32[32,8,128]{2,1,0:T(8,128)S(1)}, u32[]{:S(2)}, u32[]{:S(2)}) async-start(f32[32,8,128]{2,1,0:T(8,128)} %get-tuple-element.14), calls=%async_computation | async-start | bytes 262144 | tf_op jit(solution)/shard_map/all_to_all | solution.py:217
  36.9 1.4 %dynamic-slice_bitcast_fusion.4.init_ref = f32[1,128]{1,0:T(1,128)} fusion(f32[1024]{0:T(1024)} %param.13, s32[]{:T(128)S(6)} %select_n.42), kind=kLoop, calls=%fused_computation.8 | loop fusion | bytes 1028 | tf_op jit(solution)/shard_map/broadcast_in_dim | solution.py:243
  38.3 9.2 %all-to-all-done.every_ref = f32[32,8,128]{2,1,0:T(8,128)S(1)} async-done(((f32[32,8,128]{2,1,0:T(8,128)}), f32[32,8,128]{2,1,0:T(8,128)S(1)}, u32[]{:S(2)}, u32[]{:S(2)}) %all-to-all-start) | async-done | bytes 131104 | tf_op jit(solution)/shard_map/all_to_all | solution.py:217
  47.5 0.0 copy-start.1
  47.5 0.7 %copy-done.1 = f32[32,8,128]{2,1,0:T(8,128)} copy-done((f32[32,8,128]{2,1,0:T(8,128)}, f32[32,8,128]{2,1,0:T(8,128)S(1)}, u32[]{:S(2)}) %copy-start.1) | copy-done | bytes 131096
  48.1 2.0 %shard_map.89 = (f32[256,128]{1,0:T(8,128)}, f32[256,128]{1,0:T(8,128)}) custom-call(f32[32,8,128]{2,1,0:T(8,128)} %copy-done.1, f32[1,128]{1,0:T(1,128)} %dynamic-slice_bitcast_fusion.4.init_ref, f32[256,128]{1,0:T(8,128)} %get-tuple-element.15.pf_ref, f32[256,128]{1,0:T(8,128)} %get-tuple-element.16.lf_ref, f32[256,128]{1,0:T(8,128)} %get-tuple-element.17.pb_ref, ...), custom_call_target="tpu_custom_call" | custom-call | flops 163840 | bytes 917504 | tf_op jit(solution)/shard_map/pallas_call | solution.py:137
  (1 shorter events, 0.0 us)
Async XLA Ops:
  0.6 18.3 %copy-start = (f32[256,1024]{1,0:T(8,128)S(1)}, f32[256,1024]{1,0:T(8,128)}, u32[]{:S(2)}) copy-start(f32[256,1024]{1,0:T(8,128)} %param.10) | copy-start | bytes 3145732
  8.3 2.1 %collective-permute-start = (f32[4,256,128]{2,1,0:T(8,128)}, f32[4,256,128]{2,1,0:T(8,128)S(1)}, u32[]{:S(2)}, u32[]{:S(2)}) collective-permute-start(f32[4,256,128]{2,1,0:T(8,128)} %get-tuple-element.12), channel_id=1, source_target_pairs={{0,1},{1,0},{2,3},{3,2},{4,5},{5,4},{6,7},{7,6},{8,9},{9,8},{10,11... | collective-permute-start | bytes 1572872 | tf_op jit(solution)/shard_map/ppermute | solution.py:207
  12.3 9.2 %collective-permute-start.1 = (f32[256,128]{1,0:T(8,128)S(1)}, f32[256,128]{1,0:T(8,128)S(1)}, u32[]{:S(2)}, u32[]{:S(2)}) collective-permute-start(f32[256,128]{1,0:T(8,128)S(1)} %get-tuple-element.24), channel_id=1, source_target_pairs={{0,2},{1,3},{2,4},{3,5},{4,6},{5,7},{6,0},{7,1},{8,10},{9,11},{10,... | collective-permute-start | bytes 393224 | tf_op jit(solution)/shard_map/ppermute | solution.py:212
  13.8 7.9 %collective-permute-start.2 = (f32[256,128]{1,0:T(8,128)S(1)}, f32[256,128]{1,0:T(8,128)S(1)}, u32[]{:S(2)}, u32[]{:S(2)}) collective-permute-start(f32[256,128]{1,0:T(8,128)S(1)} %get-tuple-element.23), channel_id=1, source_target_pairs={{0,4},{1,5},{2,6},{3,7},{4,0},{5,1},{6,2},{7,3},{8,12},{9,13},{10,... | collective-permute-start | bytes 393224 | tf_op jit(solution)/shard_map/ppermute | solution.py:212
  16.5 6.9 %collective-permute-start.3 = (f32[256,128]{1,0:T(8,128)S(1)}, f32[256,128]{1,0:T(8,128)S(1)}, u32[]{:S(2)}, u32[]{:S(2)}) collective-permute-start(f32[256,128]{1,0:T(8,128)S(1)} %get-tuple-element.22), channel_id=1, source_target_pairs={{0,6},{1,7},{2,0},{3,1},{4,2},{5,3},{6,4},{7,5},{8,14},{9,15},{10,... | collective-permute-start | bytes 393224 | tf_op jit(solution)/shard_map/ppermute | solution.py:212
  21.5 1.9 %copy-start.2 = (f32[256,128]{1,0:T(8,128)}, f32[256,128]{1,0:T(8,128)S(1)}, u32[]{:S(2)}) copy-start(f32[256,128]{1,0:T(8,128)S(1)} %collective-permute-done.1.r1_ref) | copy-start | bytes 393220
  21.7 1.7 %copy-start.3 = (f32[256,128]{1,0:T(8,128)}, f32[256,128]{1,0:T(8,128)S(1)}, u32[]{:S(2)}) copy-start(f32[256,128]{1,0:T(8,128)S(1)} %collective-permute-done.2.r2_ref) | copy-start | bytes 393220
  23.4 0.6 %copy-start.4 = (f32[256,128]{1,0:T(8,128)}, f32[256,128]{1,0:T(8,128)S(1)}, u32[]{:S(2)}) copy-start(f32[256,128]{1,0:T(8,128)S(1)} %collective-permute-done.3.r3_ref) | copy-start | bytes 393220
  26.4 21.1 %all-to-all-start = ((f32[32,8,128]{2,1,0:T(8,128)}), f32[32,8,128]{2,1,0:T(8,128)S(1)}, u32[]{:S(2)}, u32[]{:S(2)}) async-start(f32[32,8,128]{2,1,0:T(8,128)} %get-tuple-element.14), calls=%async_computation | async-start | bytes 262144 | tf_op jit(solution)/shard_map/all_to_all | solution.py:217
  47.5 0.7 %copy-start.1 = (f32[32,8,128]{2,1,0:T(8,128)}, f32[32,8,128]{2,1,0:T(8,128)S(1)}, u32[]{:S(2)}) copy-start(f32[32,8,128]{2,1,0:T(8,128)S(1)} %all-to-all-done.every_ref) | copy-start | bytes 393220

commit v20 on v17

--- a/solution.py
+++ b/solution.py
@@ -7,12 +7,12 @@
 
 
 SUB = 8
-CHUNK = 64
+CHUNK = 128
 
 
 def _chunk_scan(a, x, rows, reverse):
     sub = lax.broadcasted_iota(jnp.int32, a.shape, 0) % CHUNK
-    for k in (1, 2, 4, 8, 16, 32):
+    for k in (1, 2, 4, 8, 16, 32, 64):
         shift = rows - k if reverse else k
         prev_a = pltpu.roll(a, shift, 0)
         prev_x = [pltpu.roll(v, shift, 0) for v in x]

time: 50.5 us -> 50.6 us (level)
  no operation moved by 1% of the time
where the time goes in v20:
time: 50.6 us; the launch traced here: 50.2 us
  starting transfers between devices  15.5 us (31%)
  Pallas kernels  14 us (28%)
  waiting for transfers between devices  12.4 us (25%)
  local copies, waits for them, and re-layouts  4.8 us (9%)
  other arithmetic  2.81 us (6%)
  between operations  0.67 us (1%)
    all_to_all x1, starting transfers between devices, gather_tm(): return lax.all_to_all(copies, 'tm', 0, 0, tiled=True)  10.5 us
    all_to_all x1, waiting for transfers between devices, gather_tm(): return lax.all_to_all(copies, 'tm', 0, 0, tiled=True)  9.19 us
    pallas_call x1, Pallas kernels, listed_matmul(): pl.pallas_call(matmul_kernel, grid=(tiles,), in_specs=[pl.BlockSpec(slots...  7.68 us
    ppermute x3, starting transfers between devices, sensor_reduce_scatter(): parts.append(lax.ppermute(part, 'sensor', perm))  4.93 us
    pallas_call x1, Pallas kernels, local_scans(): pl.pallas_call(scan_kernel, out_shape=[shape] * 2 + [jax.ShapeDtypeStruct...  2.35 us
    pallas_call x1, Pallas kernels, combine(): pl.pallas_call(combine_kernel, out_shape=[shape, shape], cost_estimate=pl...  2.08 us
    pallas_call x1, Pallas kernels, gain_scans(): pl.pallas_call(gain_scan_kernel, out_shape=[shape] * 3 + [jax.ShapeDtypeS...  1.92 us
    ppermute x3, waiting for transfers between devices, sensor_reduce_scatter(): parts.append(lax.ppermute(part, 'sensor', perm))  1.91 us
  transfers between devices with their start and end apart: 5, of which 4 were waited for; matrix products, arithmetic and copies ran while one was open for 9% of the time, Pallas kernels for 4%

profile of v20, /device:TPU:8, one launch (start us, length us, event | category | flops | bytes accessed | tf_op | source)
XLA Modules:
  0.0 50.2 jit_solution(16456745364364149329)
XLA Ops:
  0.6 0.0 copy-start
  0.6 7.7 %shard_map.86 = (f32[4,256,128]{2,1,0:T(8,128)}, f32[4,256,128]{2,1,0:T(8,128)}) custom-call(s32[16,256]{1,0:T(8,128)} %bitcast.11, bf16[256,4096]{1,0:T(8,128)(2,1)} %obs_ref.1, bf16[4096,1024]{1,0:T(8,128)(2,1)} %gain_ref.1), custom_call_target="tpu_custom_call" | custom-call | flops 2147483648 | bytes 11534336 | tf_op jit(solution)/shard_map/pallas_call | solution.py:168
  8.3 0.0 collective-permute-start
  8.3 0.8 %dynamic_slice.31 = f32[128]{0:T(128)S(1)} dynamic-slice(f32[1024]{0:T(1024)} %param.12, s32[]{:T(128)S(6)} %select_n.42), dynamic_slice_sizes={128} | dynamic-slice | bytes 1028 | tf_op jit(solution)/shard_map/dynamic_slice | solution.py:221
  9.1 1.4 %collective-permute-done = f32[4,256,128]{2,1,0:T(8,128)S(1)} collective-permute-done((f32[4,256,128]{2,1,0:T(8,128)}, f32[4,256,128]{2,1,0:T(8,128)S(1)}, u32[]{:S(2)}, u32[]{:S(2)}) %collective-permute-start) | collective-permute-done | bytes 524320 | tf_op jit(solution)/shard_map/ppermute | solution.py:196
  10.5 1.1 %add.53 = f32[4,256,128]{2,1,0:T(8,128)S(1)} add(f32[4,256,128]{2,1,0:T(8,128)} %get-tuple-element.11, f32[4,256,128]{2,1,0:T(8,128)S(1)} %collective-permute-done) | non-fusion elementwise | flops 131072 | bytes 1572864 | tf_op jit(solution)/shard_map/add | solution.py:196
  11.5 0.7 %dynamic-slice_bitcast_fusion = (f32[256,128]{1,0:T(8,128)S(1)}, f32[256,128]{1,0:T(8,128)S(1)}, f32[256,128]{1,0:T(8,128)S(1)}, f32[256,128]{1,0:T(8,128)}) fusion(f32[4,256,128]{2,1,0:T(8,128)S(1)} %add.53, s32[]{:T(128)S(6)} %select_n.50, s32[]{:T(128)S(6)} %select_n.48, s32[]{:T(128)S(6)} %select_n.46, s32[]{:T(128)S(6)} %select_n.44), kind=kLoop, calls=%fused_computation.1 | loop fusion | bytes 1048592 | tf_op jit(solution)/shard_map/jit(dynamic_index_in_dim)/squeeze | solution.py:199
  12.3 1.6 %collective-permute-start.1 = (f32[256,128]{1,0:T(8,128)S(1)}, f32[256,128]{1,0:T(8,128)S(1)}, u32[]{:S(2)}, u32[]{:S(2)}) collective-permute-start(f32[256,128]{1,0:T(8,128)S(1)} %get-tuple-element.24), channel_id=1, source_target_pairs={{0,2},{1,3},{2,4},{3,5},{4,6},{5,7},{6,0},{7,1},{8,10},{9,11},{10,... | collective-permute-start | bytes 393224 | tf_op jit(solution)/shard_map/ppermute | solution.py:201
  13.8 2.6 %collective-permute-start.2 = (f32[256,128]{1,0:T(8,128)S(1)}, f32[256,128]{1,0:T(8,128)S(1)}, u32[]{:S(2)}, u32[]{:S(2)}) collective-permute-start(f32[256,128]{1,0:T(8,128)S(1)} %get-tuple-element.23), channel_id=1, source_target_pairs={{0,4},{1,5},{2,6},{3,7},{4,0},{5,1},{6,2},{7,3},{8,12},{9,13},{10,... | collective-permute-start | bytes 393224 | tf_op jit(solution)/shard_map/ppermute | solution.py:201
  16.5 0.7 %collective-permute-start.3 = (f32[256,128]{1,0:T(8,128)S(1)}, f32[256,128]{1,0:T(8,128)S(1)}, u32[]{:S(2)}, u32[]{:S(2)}) collective-permute-start(f32[256,128]{1,0:T(8,128)S(1)} %get-tuple-element.22), channel_id=1, source_target_pairs={{0,6},{1,7},{2,0},{3,1},{4,2},{5,3},{6,4},{7,5},{8,14},{9,15},{10,... | collective-permute-start | bytes 393224 | tf_op jit(solution)/shard_map/ppermute | solution.py:201
  17.2 1.7 %broadcast_multiply_fusion = (f32[256,128]{1,0:T(8,128)}, f32[256,128]{1,0:T(8,128)}) fusion(f32[128]{0:T(128)S(1)} %dynamic_slice.31, f32[256,1024]{1,0:T(8,128)} %param.11, s32[]{:T(128)S(6)} %select_n.42, pred[256]{0:T(512)(128)(4,1)S(1)} %add_compare_fusion), kind=kLoop, calls=%fused_computation.5 | loop fusion | flops 65536 | bytes 393988 | tf_op jit(solution)/shard_map/mul | solution.py:226
  18.9 0.0 copy-done
  18.9 0.7 %constant_dynamic-slice_fusion.a_ref = f32[256,128]{1,0:T(8,128)} fusion(f32[256,1024]{1,0:T(8,128)S(1)} %copy-done, s32[]{:T(128)S(6)} %select_n.42), kind=kLoop, calls=%fused_computation.6 | loop fusion | bytes 262148 | tf_op jit(solution)/shard_map/dynamic_slice | solution.py:219
  19.6 1.9 %shard_map.87 = (f32[256,128]{1,0:T(8,128)}, f32[256,128]{1,0:T(8,128)}, f32[256,128]{1,0:T(8,128)}, f32[8,128]{1,0:T(8,128)}) custom-call(f32[256,128]{1,0:T(8,128)} %constant_dynamic-slice_fusion.a_ref, f32[256,128]{1,0:T(8,128)} %get-tuple-element.21.g_ref, f32[256,128]{1,0:T(8,128)} %get-tuple-element.20.s_ref), custom_call_target="tpu_custom_call" | custom-call | flops 655360 | bytes 786432 | tf_op jit(solution)/shard_map/pallas_call | solution.py:68
  21.5 0.0 collective-permute-done.1.r1_ref
  21.5 0.0 copy-start.2
  21.5 0.2 collective-permute-done.2.r2_ref
  21.7 0.0 copy-start.3
  21.7 1.7 %collective-permute-done.3.r3_ref = f32[256,128]{1,0:T(8,128)S(1)} collective-permute-done((f32[256,128]{1,0:T(8,128)S(1)}, f32[256,128]{1,0:T(8,128)S(1)}, u32[]{:S(2)}, u32[]{:S(2)}) %collective-permute-start.3) | collective-permute-done | bytes 131104 | tf_op jit(solution)/shard_map/ppermute | solution.py:201
  23.4 0.0 copy-start.4
  23.4 0.0 copy-done.2
  23.4 0.0 copy-done.3
  23.4 0.6 %copy-done.4 = f32[256,128]{1,0:T(8,128)} copy-done((f32[256,128]{1,0:T(8,128)}, f32[256,128]{1,0:T(8,128)S(1)}, u32[]{:S(2)}) %copy-start.4) | copy-done | bytes 131096
  24.0 2.3 %shard_map.88 = (f32[256,128]{1,0:T(8,128)}, f32[256,128]{1,0:T(8,128)}, f32[32,8,128]{2,1,0:T(8,128)}) custom-call(f32[256,128]{1,0:T(8,128)} %constant_dynamic-slice_fusion.a_ref, f32[256,128]{1,0:T(8,128)} %get-tuple-element.25.own_ref, f32[256,128]{1,0:T(8,128)} %copy-done.2, f32[256,128]{1,0:T(8,128)} %copy-done.3, f32[256,128]{1,0:T(8,128)} %copy-done.4, ...), custom_call_target="tpu_custom_call" | custom-call | flops 655360 | bytes 1310720 | tf_op jit(solution)/shard_map/pallas_call | solution.py:97
  26.4 10.5 %all-to-all-start = ((f32[32,8,128]{2,1,0:T(8,128)}), f32[32,8,128]{2,1,0:T(8,128)S(1)}, u32[]{:S(2)}, u32[]{:S(2)}) async-start(f32[32,8,128]{2,1,0:T(8,128)} %get-tuple-element.14), calls=%async_computation | async-start | bytes 262144 | tf_op jit(solution)/shard_map/all_to_all | solution.py:206
  36.9 1.4 %dynamic-slice_bitcast_fusion.4.init_ref = f32[1,128]{1,0:T(1,128)} fusion(f32[1024]{0:T(1024)} %param.13, s32[]{:T(128)S(6)} %select_n.42), kind=kLoop, calls=%fused_computation.8 | loop fusion | bytes 1028 | tf_op jit(solution)/shard_map/broadcast_in_dim | solution.py:232
  38.3 9.2 %all-to-all-done.every_ref = f32[32,8,128]{2,1,0:T(8,128)S(1)} async-done(((f32[32,8,128]{2,1,0:T(8,128)}), f32[32,8,128]{2,1,0:T(8,128)S(1)}, u32[]{:S(2)}, u32[]{:S(2)}) %all-to-all-start) | async-done | bytes 131104 | tf_op jit(solution)/shard_map/all_to_all | solution.py:206
  47.5 0.0 copy-start.1
  47.5 0.7 %copy-done.1 = f32[32,8,128]{2,1,0:T(8,128)} copy-done((f32[32,8,128]{2,1,0:T(8,128)}, f32[32,8,128]{2,1,0:T(8,128)S(1)}, u32[]{:S(2)}) %copy-start.1) | copy-done | bytes 131096
  48.1 2.1 %shard_map.89 = (f32[256,128]{1,0:T(8,128)}, f32[256,128]{1,0:T(8,128)}) custom-call(f32[32,8,128]{2,1,0:T(8,128)} %copy-done.1, f32[1,128]{1,0:T(1,128)} %dynamic-slice_bitcast_fusion.4.init_ref, f32[256,128]{1,0:T(8,128)} %get-tuple-element.15.pf_ref, f32[256,128]{1,0:T(8,128)} %get-tuple-element.16.lf_ref, f32[256,128]{1,0:T(8,128)} %get-tuple-element.17.pb_ref, ...), custom_call_target="tpu_custom_call" | custom-call | flops 163840 | bytes 917504 | tf_op jit(solution)/shard_map/pallas_call | solution.py:126
  (1 shorter events, 0.0 us)
Async XLA Ops:
  0.6 18.3 %copy-start = (f32[256,1024]{1,0:T(8,128)S(1)}, f32[256,1024]{1,0:T(8,128)}, u32[]{:S(2)}) copy-start(f32[256,1024]{1,0:T(8,128)} %param.10) | copy-start | bytes 3145732
  8.3 2.1 %collective-permute-start = (f32[4,256,128]{2,1,0:T(8,128)}, f32[4,256,128]{2,1,0:T(8,128)S(1)}, u32[]{:S(2)}, u32[]{:S(2)}) collective-permute-start(f32[4,256,128]{2,1,0:T(8,128)} %get-tuple-element.12), channel_id=1, source_target_pairs={{0,1},{1,0},{2,3},{3,2},{4,5},{5,4},{6,7},{7,6},{8,9},{9,8},{10,11... | collective-permute-start | bytes 1572872 | tf_op jit(solution)/shard_map/ppermute | solution.py:196
  12.3 9.2 %collective-permute-start.1 = (f32[256,128]{1,0:T(8,128)S(1)}, f32[256,128]{1,0:T(8,128)S(1)}, u32[]{:S(2)}, u32[]{:S(2)}) collective-permute-start(f32[256,128]{1,0:T(8,128)S(1)} %get-tuple-element.24), channel_id=1, source_target_pairs={{0,2},{1,3},{2,4},{3,5},{4,6},{5,7},{6,0},{7,1},{8,10},{9,11},{10,... | collective-permute-start | bytes 393224 | tf_op jit(solution)/shard_map/ppermute | solution.py:201
  13.8 7.9 %collective-permute-start.2 = (f32[256,128]{1,0:T(8,128)S(1)}, f32[256,128]{1,0:T(8,128)S(1)}, u32[]{:S(2)}, u32[]{:S(2)}) collective-permute-start(f32[256,128]{1,0:T(8,128)S(1)} %get-tuple-element.23), channel_id=1, source_target_pairs={{0,4},{1,5},{2,6},{3,7},{4,0},{5,1},{6,2},{7,3},{8,12},{9,13},{10,... | collective-permute-start | bytes 393224 | tf_op jit(solution)/shard_map/ppermute | solution.py:201
  16.5 6.9 %collective-permute-start.3 = (f32[256,128]{1,0:T(8,128)S(1)}, f32[256,128]{1,0:T(8,128)S(1)}, u32[]{:S(2)}, u32[]{:S(2)}) collective-permute-start(f32[256,128]{1,0:T(8,128)S(1)} %get-tuple-element.22), channel_id=1, source_target_pairs={{0,6},{1,7},{2,0},{3,1},{4,2},{5,3},{6,4},{7,5},{8,14},{9,15},{10,... | collective-permute-start | bytes 393224 | tf_op jit(solution)/shard_map/ppermute | solution.py:201
  21.5 1.9 %copy-start.2 = (f32[256,128]{1,0:T(8,128)}, f32[256,128]{1,0:T(8,128)S(1)}, u32[]{:S(2)}) copy-start(f32[256,128]{1,0:T(8,128)S(1)} %collective-permute-done.1.r1_ref) | copy-start | bytes 393220
  21.7 1.7 %copy-start.3 = (f32[256,128]{1,0:T(8,128)}, f32[256,128]{1,0:T(8,128)S(1)}, u32[]{:S(2)}) copy-start(f32[256,128]{1,0:T(8,128)S(1)} %collective-permute-done.2.r2_ref) | copy-start | bytes 393220
  23.4 0.6 %copy-start.4 = (f32[256,128]{1,0:T(8,128)}, f32[256,128]{1,0:T(8,128)S(1)}, u32[]{:S(2)}) copy-start(f32[256,128]{1,0:T(8,128)S(1)} %collective-permute-done.3.r3_ref) | copy-start | bytes 393220
  26.4 21.1 %all-to-all-start = ((f32[32,8,128]{2,1,0:T(8,128)}), f32[32,8,128]{2,1,0:T(8,128)S(1)}, u32[]{:S(2)}, u32[]{:S(2)}) async-start(f32[32,8,128]{2,1,0:T(8,128)} %get-tuple-element.14), calls=%async_computation | async-start | bytes 262144 | tf_op jit(solution)/shard_map/all_to_all | solution.py:206
  47.5 0.7 %copy-start.1 = (f32[32,8,128]{2,1,0:T(8,128)}, f32[32,8,128]{2,1,0:T(8,128)S(1)}, u32[]{:S(2)}) copy-start(f32[32,8,128]{2,1,0:T(8,128)S(1)} %all-to-all-done.every_ref) | copy-start | bytes 393220
